TPU v7x, 32 devices: a whole 2x2x4 slice. The times are simulated.
32 devices in a mesh: shots: 4 (over x, core), depth: 8 (over z, y).
Axes of the slice: x: 2, y: 2, z: 4, core: 2. Of those that a mesh axis runs over, the one named last changes fastest.
Arguments:
- forward_prev: float32 [4, 64, 128, 256], P('shots', 'depth'), may hold values from -3 to 3
- forward_now: float32 [4, 64, 128, 256], P('shots', 'depth'), may hold values from -3 to 3
- adjoint_prev: float32 [4, 64, 128, 256], P('shots', 'depth'), may hold values from -3 to 3
- adjoint_now: float32 [4, 64, 128, 256], P('shots', 'depth'), may hold values from -3 to 3
- courant: float32 [64, 128, 256], P('depth'), may hold values from 0.05 to 0.18
- wavelet: float32 [2, 512], replicated, may hold values from -5 to 5
- sign_bits: int32 [4, 512], P('shots'), may hold values from 0 to 1
- source_depth: int32 [512], replicated, may hold values from 0 to 63
- source_cell: int32 [512], replicated, may hold values from 0 to 32767
- receiver_depth: int32 [4096], replicated, may hold values from 0 to 63
- receiver_cell: int32 [4096], replicated, may hold values from 0 to 32767
- residual_traces: float32 [4, 2, 4096], P('shots'), may hold values from -5 to 5
Outputs:
- forward_older: float32 [4, 64, 128, 256], P('shots', 'depth')
- forward_newer: float32 [4, 64, 128, 256], P('shots', 'depth')
- adjoint_older: float32 [4, 64, 128, 256], P('shots', 'depth')
- adjoint_newer: float32 [4, 64, 128, 256], P('shots', 'depth')
- gradient: float32 [64, 128, 256], P(None, ('shots', 'depth'))
All inputs are finite; a program needn't handle non-finite values.
Results may differ from a plain program's by a relative error of at most 0.00002.
Values sent between devices are 32-bit elements; how exact they have to be, the bound alone decides.
No kernel may reach another device: no remote copies, remote signals or barrier semaphores. Data moves between devices by JAX's collectives and lax.ppermute only.
A program may use at most 128 MiB of HBM per device.

v0:
```python
import jax
import jax.numpy as jnp
from jax import lax
from jax.sharding import PartitionSpec as P

STEPS = 2


COEFFS = (-205.0 / 72.0, 8.0 / 5.0, -1.0 / 5.0, 8.0 / 315.0, -1.0 / 560.0)
KERNEL = (1.0 / 16.0, 4.0 / 16.0, 6.0 / 16.0, 4.0 / 16.0, 1.0 / 16.0)


def extended_2(shard, sides, width):
    for axis, dim in sides:
        devices, length = (lax.axis_size(axis), shard.shape[dim])
        up = [(i, (i + 1) % devices) for i in range(devices - 1)]
        down = [(j, i) for i, j in up]
        last = lax.slice_in_dim(shard, length - width, length, axis=dim)
        leading = lax.slice_in_dim(shard, 0, width, axis=dim)
        before = lax.ppermute(last, axis, up)
        after = lax.ppermute(leading, axis, down)
        shard = jnp.concatenate([before, shard, after], axis=dim)
    return shard


def shifted(values, axis, offset):
    size = values.shape[axis]
    width = abs(offset)
    filler = jnp.zeros_like(lax.slice_in_dim(values, 0, width, axis=axis))
    if offset > 0:
        kept = lax.slice_in_dim(values, offset, size, axis=axis)
        return jnp.concatenate([kept, filler], axis=axis)
    kept = lax.slice_in_dim(values, 0, size - width, axis=axis)
    return jnp.concatenate([filler, kept], axis=axis)


def laplace(extended):
    zaxis = extended.ndim - 3
    planes = extended.shape[zaxis] - 8
    core = lax.slice_in_dim(extended, 4, 4 + planes, axis=zaxis)
    total = 3.0 * COEFFS[0] * core
    for k in range(1, 5):
        near = lax.slice_in_dim(extended, 4 + k, 4 + k + planes, axis=zaxis) + lax.slice_in_dim(
            extended, 4 - k, 4 - k + planes, axis=zaxis
        )
        near = near + shifted(core, zaxis + 1, k) + shifted(core, zaxis + 1, -k)
        near = near + shifted(core, zaxis + 2, k) + shifted(core, zaxis + 2, -k)
        total = total + COEFFS[k] * near
    return total


def smooth(values, axis):
    total = KERNEL[2] * values
    for k in (1, 2):
        total = total + KERNEL[2 + k] * (shifted(values, axis, k) + shifted(values, axis, -k))
    return total


def spread(flat, values, first_plane, planes, rows, cols):
    lateral = rows * cols
    limit = planes * lateral
    local = flat - first_plane * lateral
    local = jnp.where((local >= 0) & (local < limit), local, limit)
    grid = jnp.zeros((values.shape[0], limit), jnp.float32).at[:, local].add(values, mode="drop")
    return grid.reshape(values.shape[0], planes, rows, cols)


def on_device(
    forward_prev,
    forward_now,
    adjoint_prev,
    adjoint_now,
    courant,
    wavelet,
    sign_bits,
    source_depth,
    source_cell,
    receiver_depth,
    receiver_cell,
    residual_traces,
):
    planes, rows, cols = courant.shape
    lateral = rows * cols
    source_flat = source_depth * lateral + source_cell
    receiver_flat = receiver_depth * lateral + receiver_cell
    signs = (2 * sign_bits - 1).astype(jnp.float32)
    position = lax.axis_index("depth")
    earlier = jnp.stack([forward_prev, adjoint_prev])
    current = jnp.stack([forward_now, adjoint_now])
    correlation = jnp.zeros((planes, rows, cols), jnp.float32)
    for step in range(STEPS):
        extended = extended_2(current, (("depth", 2),), 4)
        first_plane = position * planes
        forward_part = spread(
            source_flat, signs * wavelet[step][None, :], first_plane, planes, rows, cols
        )
        adjoint_part = spread(
            receiver_flat, residual_traces[:, step, :], first_plane, planes, rows, cols
        )
        fresh = (
            2.0 * current
            - earlier
            + courant * laplace(extended)
            + jnp.stack([forward_part, adjoint_part])
        )
        correlation = correlation + jnp.sum(fresh[0] * fresh[1], axis=0)
        earlier, current = (current, fresh)
    lateral_smooth = smooth(smooth(correlation, 1), 2)
    summed = lax.psum_scatter(lateral_smooth, "shots", scatter_dimension=1, tiled=True)
    columns = lax.all_to_all(summed, "depth", split_axis=1, concat_axis=0, tiled=True)
    gradient = smooth(columns, 0)
    return (earlier[0], current[0], earlier[1], current[1], gradient)


def solution(mesh):
    in_specs = (
        P("shots", "depth", None, None),
        P("shots", "depth", None, None),
        P("shots", "depth", None, None),
        P("shots", "depth", None, None),
        P("depth", None, None),
        P(),
        P("shots", None),
        P(),
        P(),
        P(),
        P(),
        P("shots", None, None),
    )
    out_specs = (
        P("shots", "depth", None, None),
        P("shots", "depth", None, None),
        P("shots", "depth", None, None),
        P("shots", "depth", None, None),
        P(None, ("shots", "depth"), None),
    )
    return jax.shard_map(
        on_device, mesh=mesh, in_specs=in_specs, out_specs=out_specs, check_vma=False
    )
```

profile of v0, /device:TPU:0, one launch (start us, length us, event | category | flops | bytes accessed | tf_op | source)
XLA Modules:
  0.0 237.2 jit_solution(1340536631924805276)
XLA Ops:
  7.2 3.2 %fusion.80 = (f32[2,1,4,128,256]{4,3,2,1,0:T(8,128)}, f32[2,1,4,128,256]{4,3,2,1,0:T(8,128)}) fusion(f32[1,1,8,128,256]{4,3,2,1,0:T(8,128)} %bitcast.23, f32[1,1,8,128,256]{4,3,2,1,0:T(8,128)} %bitcast.35), kind=kLoop, calls=%fused_computation.142 | loop fusion | flops 524288 | bytes 4194304 | tf_op jit(solution)/shard_map/stack | solution.py:89
  10.4 1.3 collective-permute-start
  11.7 6.5 %collective-permute-start.1 = (f32[2,1,4,128,256]{4,3,2,1,0:T(8,128)}, f32[2,1,4,128,256]{4,3,2,1,0:T(8,128)}, u32[]{:S(2)}, u32[]{:S(2)}) collective-permute-start(f32[2,1,4,128,256]{4,3,2,1,0:T(8,128)} %get-tuple-element.52), channel_id=1, source_target_pairs={{0,1},{1,2},{2,3},{3,4},{4,5},{5,6},{6,7},{8,9},{9,10},{10,11},{11... | collective-permute-start | bytes 3145736 | tf_op jit(solution)/shard_map/ppermute | solution.py:20
  18.2 2.4 %fusion.31 = (f32[2,1,8,127,256]{4,3,2,1,0:T(8,128)}, f32[2,1,8,127,256]{4,3,2,1,0:T(8,128)}) fusion(f32[1,1,8,128,256]{4,3,2,1,0:T(8,128)S(1)} %bitcast.24, f32[1,1,8,128,256]{4,3,2,1,0:T(8,128)S(1)} %bitcast.36), kind=kLoop, calls=%fused_computation.86 | loop fusion | flops 1040384 | bytes 6258688 | tf_op jit(solution)/shard_map/stack | solution.py:89
  20.6 2.7 %fusion.33 = (f32[2,1,8,128,255]{4,3,2,1,0:T(8,128)}, f32[2,1,8,128,255]{4,3,2,1,0:T(8,128)}) fusion(f32[1,1,8,128,256]{4,3,2,1,0:T(8,128)S(1)} %bitcast.25, f32[1,1,8,128,256]{4,3,2,1,0:T(8,128)S(1)} %bitcast.37), kind=kLoop, calls=%fused_computation.88 | loop fusion | flops 1044480 | bytes 6275072 | tf_op jit(solution)/shard_map/stack | solution.py:89
  23.4 2.4 %fusion.35 = (f32[2,1,8,126,256]{4,3,2,1,0:T(8,128)}, f32[2,1,8,126,256]{4,3,2,1,0:T(8,128)}) fusion(f32[1,1,8,128,256]{4,3,2,1,0:T(8,128)S(1)} %bitcast.26, f32[1,1,8,128,256]{4,3,2,1,0:T(8,128)S(1)} %bitcast.38), kind=kLoop, calls=%fused_computation.90 | loop fusion | flops 1032192 | bytes 6225920 | tf_op jit(solution)/shard_map/stack | solution.py:89
  25.9 22.2 %scatter_custom_fusion.1 = f32[262144]{0:T(1024)S(1)} fusion(s32[4096]{0:T(1024)S(1)} %compare_select_fusion, f32[4096]{0:T(1024)S(1)} %bitcast.53, f32[]{:T(128)} %constant.18.clone.1), kind=kCustom, calls=%fused_computation.155 | custom fusion | flops 4096 | bytes 1048580 | tf_op jit(solution)/shard_map/scatter-add | solution.py:64
  49.4 3.5 %scatter_custom_fusion = f32[262144]{0:T(1024)S(1)} fusion(s32[512]{0:T(512)S(1)} %compare_select_fusion.1, f32[512]{0:T(512)S(1)} %bitcast.55, f32[]{:T(128)} %constant.18.clone.1), kind=kCustom, calls=%fused_computation.157 | custom fusion | flops 512 | bytes 1048580 | tf_op jit(solution)/shard_map/scatter-add | solution.py:64
  54.2 22.2 %scatter_custom_fusion.3 = f32[262144]{0:T(1024)S(1)} fusion(s32[4096]{0:T(1024)S(1)} %compare_select_fusion, f32[4096]{0:T(1024)S(1)} %bitcast.52, f32[]{:T(128)} %constant.18.clone.1), kind=kCustom, calls=%fused_computation.151 | custom fusion | flops 4096 | bytes 1048580 | tf_op jit(solution)/shard_map/scatter-add | solution.py:64
  77.6 3.7 %scatter_custom_fusion.2 = f32[262144]{0:T(1024)S(1)} fusion(s32[512]{0:T(512)S(1)} %compare_select_fusion.1, f32[512]{0:T(512)S(1)} %bitcast.54, f32[]{:T(128)} %constant.18.clone.1), kind=kCustom, calls=%fused_computation.153 | custom fusion | flops 512 | bytes 1048580 | tf_op jit(solution)/shard_map/scatter-add | solution.py:64
  81.3 1.3 stack_reshape.14
  82.6 2.7 %fusion.37 = (f32[2,1,8,128,254]{4,3,2,1,0:T(8,128)}, f32[2,1,8,128,254]{4,3,2,1,0:T(8,128)}) fusion(f32[1,1,8,128,256]{4,3,2,1,0:T(8,128)S(1)} %bitcast.27, f32[1,1,8,128,256]{4,3,2,1,0:T(8,128)S(1)} %bitcast.39), kind=kLoop, calls=%fused_computation.92 | loop fusion | flops 1040384 | bytes 6258688 | tf_op jit(solution)/shard_map/stack | solution.py:89
  85.2 2.4 %fusion.39 = (f32[2,1,8,125,256]{4,3,2,1,0:T(8,128)}, f32[2,1,8,125,256]{4,3,2,1,0:T(8,128)}) fusion(f32[1,1,8,128,256]{4,3,2,1,0:T(8,128)S(1)} %bitcast.28, f32[1,1,8,128,256]{4,3,2,1,0:T(8,128)S(1)} %bitcast.40), kind=kLoop, calls=%fused_computation.94 | loop fusion | flops 1024000 | bytes 6193152 | tf_op jit(solution)/shard_map/stack | solution.py:89
  87.7 2.7 %fusion.41 = (f32[2,1,8,128,253]{4,3,2,1,0:T(8,128)}, f32[2,1,8,128,253]{4,3,2,1,0:T(8,128)}) fusion(f32[1,1,8,128,256]{4,3,2,1,0:T(8,128)S(1)} %bitcast.29, f32[1,1,8,128,256]{4,3,2,1,0:T(8,128)S(1)} %bitcast.41), kind=kLoop, calls=%fused_computation.96 | loop fusion | flops 1036288 | bytes 6242304 | tf_op jit(solution)/shard_map/stack | solution.py:89
  90.4 2.4 %fusion.43 = (f32[2,1,8,124,256]{4,3,2,1,0:T(8,128)}, f32[2,1,8,124,256]{4,3,2,1,0:T(8,128)}) fusion(f32[1,1,8,128,256]{4,3,2,1,0:T(8,128)S(1)} %bitcast.30, f32[1,1,8,128,256]{4,3,2,1,0:T(8,128)S(1)} %bitcast.42), kind=kLoop, calls=%fused_computation.98 | loop fusion | flops 1015808 | bytes 6160384 | tf_op jit(solution)/shard_map/stack | solution.py:89
  92.8 2.6 %fusion.45 = (f32[2,1,8,128,252]{4,3,2,1,0:T(8,128)}, f32[2,1,8,128,252]{4,3,2,1,0:T(8,128)}) fusion(f32[1,1,8,128,256]{4,3,2,1,0:T(8,128)S(1)} %bitcast.31, f32[1,1,8,128,256]{4,3,2,1,0:T(8,128)S(1)} %bitcast.43), kind=kLoop, calls=%fused_computation.100 | loop fusion | flops 1032192 | bytes 6225920 | tf_op jit(solution)/shard_map/stack | solution.py:89
  95.5 2.2 pad_maximum_fusion.1
  100.2 11.1 %fusion.61 = f32[2,1,8,128,256]{4,3,2,1,0:T(8,128)S(1)} fusion(f32[2,1,12,128,256]{4,3,2,1,0:T(8,128)S(1)} %get-tuple-element.50, f32[2,1,12,128,256]{4,3,2,1,0:T(8,128)S(1)} %get-tuple-element.49, f32[1,1,8,128,256]{4,3,2,1,0:T(8,128)} %bitcast.49, f32[1,1,8,128,256]{4,3,2,1,0:T(8,128)} %bitcast.50, f32[1,1,8,128,256]{4,3,2,1,0:T(8,128)S(1)} %copy-done.8, ...), kind=kLoop, calls=%fused_computation.119 | loop fusion | flops 19398656 | bytes 59277312 | tf_op jit(solution)/shard_map/add | solution.py:101
  113.0 2.7 %fusion.93 = (f32[2,1,8,128,254]{4,3,2,1,0:T(8,128)}, f32[2,1,8,128,254]{4,3,2,1,0:T(8,128)}) fusion(f32[2,1,8,128,256]{4,3,2,1,0:T(8,128)S(1)} %fusion.61), kind=kLoop, calls=%fused_computation.170 | loop fusion | bytes 8323072 | tf_op jit(solution)/shard_map/slice | solution.py:31
  115.7 2.4 %fusion.94 = (f32[2,1,8,125,256]{4,3,2,1,0:T(8,128)}, f32[2,1,8,125,256]{4,3,2,1,0:T(8,128)}) fusion(f32[2,1,8,128,256]{4,3,2,1,0:T(8,128)S(1)} %fusion.61), kind=kLoop, calls=%fused_computation.171 | loop fusion | bytes 8192000 | tf_op jit(solution)/shard_map/slice | solution.py:31
  118.2 1.3 collective-permute-start.2
  119.5 5.5 %collective-permute-start.3 = (f32[2,1,4,128,256]{4,3,2,1,0:T(8,128)S(1)}, f32[2,1,4,128,256]{4,3,2,1,0:T(8,128)}, u32[]{:S(2)}, u32[]{:S(2)}) collective-permute-start(f32[2,1,4,128,256]{4,3,2,1,0:T(8,128)S(1)} %get-tuple-element.32), channel_id=1, source_target_pairs={{0,1},{1,2},{2,3},{3,4},{4,5},{5,6},{6,7},{8,9},{9,10},{10,11},{11... | collective-permute-start | bytes 3145736 | tf_op jit(solution)/shard_map/ppermute | solution.py:20
  125.1 2.7 %fusion.95 = (f32[2,1,8,128,253]{4,3,2,1,0:T(8,128)}, f32[2,1,8,128,253]{4,3,2,1,0:T(8,128)}) fusion(f32[2,1,8,128,256]{4,3,2,1,0:T(8,128)S(1)} %fusion.61), kind=kLoop, calls=%fused_computation.172 | loop fusion | bytes 8290304 | tf_op jit(solution)/shard_map/slice | solution.py:31
  127.8 2.4 %fusion.96 = (f32[2,1,8,124,256]{4,3,2,1,0:T(8,128)}, f32[2,1,8,124,256]{4,3,2,1,0:T(8,128)}) fusion(f32[2,1,8,128,256]{4,3,2,1,0:T(8,128)S(1)} %fusion.61), kind=kLoop, calls=%fused_computation.173 | loop fusion | bytes 8126464 | tf_op jit(solution)/shard_map/slice | solution.py:31
  130.2 2.7 %fusion.97 = (f32[2,1,8,128,252]{4,3,2,1,0:T(8,128)}, f32[2,1,8,128,252]{4,3,2,1,0:T(8,128)}) fusion(f32[2,1,8,128,256]{4,3,2,1,0:T(8,128)S(1)} %fusion.61), kind=kLoop, calls=%fused_computation.174 | loop fusion | bytes 8257536 | tf_op jit(solution)/shard_map/slice | solution.py:31
  132.9 11.9 %collective-permute-done.2 = f32[2,1,4,128,256]{4,3,2,1,0:T(8,128)} collective-permute-done((f32[2,1,4,128,256]{4,3,2,1,0:T(8,128)S(1)}, f32[2,1,4,128,256]{4,3,2,1,0:T(8,128)}, u32[]{:S(2)}, u32[]{:S(2)}) %collective-permute-start.2) | collective-permute-done | bytes 1048608 | tf_op jit(solution)/shard_map/ppermute | solution.py:21
  144.9 22.5 %collective-permute-done.3 = f32[2,1,4,128,256]{4,3,2,1,0:T(8,128)} collective-permute-done((f32[2,1,4,128,256]{4,3,2,1,0:T(8,128)S(1)}, f32[2,1,4,128,256]{4,3,2,1,0:T(8,128)}, u32[]{:S(2)}, u32[]{:S(2)}) %collective-permute-start.3) | collective-permute-done | bytes 1048608 | tf_op jit(solution)/shard_map/ppermute | solution.py:20
  167.3 13.1 %fusion.11 = f32[2,1,8,128,256]{4,3,2,1,0:T(8,128)} fusion(f32[2,1,8,128,256]{4,3,2,1,0:T(8,128)S(1)} %fusion.61, f32[2,1,4,128,256]{4,3,2,1,0:T(8,128)} %collective-permute-done.3, f32[2,1,4,128,256]{4,3,2,1,0:T(8,128)} %collective-permute-done.2, f32[1,1,8,128,256]{4,3,2,1,0:T(8,128)S(1)} %copy-done.9, f32[1,1,8,128,256]{4,3,2,1,0:T(8,128)} %stack_reshape.14, ...), kind=kLoop, calls=%fused_computation.66 | loop fusion | flops 23068672 | bytes 44597248 | tf_op jit(solution)/shard_map/add | solution.py:101
  180.4 3.8 %add_bitcast_fusion = (f32[8,128,256]{2,1,0:T(8,128)S(1)}, f32[1,8,128,256]{3,2,1,0:T(8,128)}, f32[1,8,128,256]{3,2,1,0:T(8,128)}, f32[1,8,128,256]{3,2,1,0:T(8,128)}, f32[1,8,128,256]{3,2,1,0:T(8,128)}) fusion(f32[2,1,8,128,256]{4,3,2,1,0:T(8,128)} %fusion.11, f32[2,1,8,128,256]{4,3,2,1,0:T(8,128)S(1)} %fusion.61), kind=kLoop, calls=%fused_computation.146 | loop fusion | flops 786432 | bytes 9437184 | tf_op jit(solution)/shard_map/add | solution.py:106
  185.8 1.6 multiply_add_fusion
  187.4 26.4 %reduce-scatter.2.cloned.1.call-done = f32[8,32,256]{2,1,0:T(8,128)} async-done(((f32[8,128,256]{2,1,0:T(8,128)}), f32[8,32,256]{2,1,0:T(8,128)}) %reduce-scatter.2.cloned.1.call-update) | async-done | bytes 262160 | tf_op jit(solution)/shard_map/reduce_scatter | solution.py:109
  214.9 14.2 %all_to_all.18 = f32[8,32,256]{2,0,1:T(8,128)S(1)} all-to-all(f32[8,32,256]{2,0,1:T(8,128)S(1)} %copy.28), channel_id=1, replica_groups=mesh['shots'=4,'depth'=8] {'depth'}, dimensions={1} | all-to-all | bytes 524288 | tf_op jit(solution)/shard_map/all_to_all | solution.py:110
  (59 shorter events, 12.0 us)
Async XLA Ops:
  7.2 206.6 %reduce-scatter.2.cloned.1.call-start = ((), (), s32[]{:S(2)}) async-start(), calls=%async_computation.2 | async-start | bytes 1310720 | tf_op jit(solution)/shard_map/reduce_scatter | solution.py:109
  7.2 11.0 %copy-start = (f32[1,8,128,256]{3,2,1,0:T(8,128)S(1)}, f32[1,8,128,256]{3,2,1,0:T(8,128)}, u32[]{:S(2)}) copy-start(f32[1,8,128,256]{3,2,1,0:T(8,128)} %param.13) | copy-start | bytes 3145732
  7.2 11.0 %copy-start.1 = (f32[1,8,128,256]{3,2,1,0:T(8,128)S(1)}, f32[1,8,128,256]{3,2,1,0:T(8,128)}, u32[]{:S(2)}) copy-start(f32[1,8,128,256]{3,2,1,0:T(8,128)} %param.15) | copy-start | bytes 3145732
  10.4 85.1 %collective-permute-start = (f32[2,1,4,128,256]{4,3,2,1,0:T(8,128)}, f32[2,1,4,128,256]{4,3,2,1,0:T(8,128)}, u32[]{:S(2)}, u32[]{:S(2)}) collective-permute-start(f32[2,1,4,128,256]{4,3,2,1,0:T(8,128)} %get-tuple-element.51), channel_id=1, source_target_pairs={{1,0},{2,1},{3,2},{4,3},{5,4},{6,5},{7,6},{9,8},{10,9},{11,10},{12... | collective-permute-start | bytes 3145736 | tf_op jit(solution)/shard_map/ppermute | solution.py:21
  11.7 83.8 %collective-permute-start.1 = (f32[2,1,4,128,256]{4,3,2,1,0:T(8,128)}, f32[2,1,4,128,256]{4,3,2,1,0:T(8,128)}, u32[]{:S(2)}, u32[]{:S(2)}) collective-permute-start(f32[2,1,4,128,256]{4,3,2,1,0:T(8,128)} %get-tuple-element.52), channel_id=1, source_target_pairs={{0,1},{1,2},{2,3},{3,4},{4,5},{5,6},{6,7},{8,9},{9,10},{10,11},{11... | collective-permute-start | bytes 3145736 | tf_op jit(solution)/shard_map/ppermute | solution.py:20
  23.4 2.4 %copy-start.10 = (f32[1,2,4096]{2,1,0:T(2,128)S(1)}, f32[1,2,4096]{2,1,0:T(2,128)}, u32[]{:S(2)}) copy-start(f32[1,2,4096]{2,1,0:T(2,128)} %param.23) | copy-start | bytes 98308
  23.4 2.5 %copy-start.11 = (s32[4096]{0:T(1024)S(1)}, s32[4096]{0:T(1024)}, u32[]{:S(2)}) copy-start(s32[4096]{0:T(1024)} %param.22) | copy-start | bytes 49156
  23.4 2.5 %copy-start.12 = (s32[4096]{0:T(1024)S(1)}, s32[4096]{0:T(1024)}, u32[]{:S(2)}) copy-start(s32[4096]{0:T(1024)} %param.21) | copy-start | bytes 49156
  25.8 23.5 %copy-start.15 = (s32[512]{0:T(512)S(1)}, s32[512]{0:T(512)}, u32[]{:S(2)}) copy-start(s32[512]{0:T(512)} %param.20) | copy-start | bytes 6148
  25.8 23.5 %copy-start.16 = (s32[512]{0:T(512)S(1)}, s32[512]{0:T(512)}, u32[]{:S(2)}) copy-start(s32[512]{0:T(512)} %param.19) | copy-start | bytes 6148
  25.8 23.6 %copy-start.13 = (f32[2,512]{1,0:T(2,128)S(1)}, f32[2,512]{1,0:T(2,128)}, u32[]{:S(2)}) copy-start(f32[2,512]{1,0:T(2,128)} %param.17) | copy-start | bytes 12292
  25.8 23.6 %copy-start.14 = (s32[1,512]{1,0:T(1,128)S(1)}, s32[1,512]{1,0:T(1,128)}, u32[]{:S(2)}) copy-start(s32[1,512]{1,0:T(1,128)} %param.18) | copy-start | bytes 6148
  92.8 4.9 %copy-start.7 = (f32[8,128,256]{2,1,0:T(8,128)S(1)}, f32[8,128,256]{2,1,0:T(8,128)}, u32[]{:S(2)}) copy-start(f32[8,128,256]{2,1,0:T(8,128)} %param.16) | copy-start | bytes 3145732
  92.8 4.9 %copy-start.8 = (f32[1,1,8,128,256]{4,3,2,1,0:T(8,128)S(1)}, f32[1,1,8,128,256]{4,3,2,1,0:T(8,128)}, u32[]{:S(2)}) copy-start(f32[1,1,8,128,256]{4,3,2,1,0:T(8,128)} %stack_reshape.13) | copy-start | bytes 3145732
  95.5 2.3 copy-start.2
  95.5 2.9 %copy-start.3 = (f32[2,1,8,127,256]{4,3,2,1,0:T(8,128)S(1)}, f32[2,1,8,127,256]{4,3,2,1,0:T(8,128)}, u32[]{:S(2)}) copy-start(f32[2,1,8,127,256]{4,3,2,1,0:T(8,128)} %get-tuple-element.34) | copy-start | bytes 6242308
  95.5 3.5 %copy-start.4 = (f32[2,1,8,128,255]{4,3,2,1,0:T(8,128)S(1)}, f32[2,1,8,128,255]{4,3,2,1,0:T(8,128)}, u32[]{:S(2)}) copy-start(f32[2,1,8,128,255]{4,3,2,1,0:T(8,128)} %get-tuple-element.35) | copy-start | bytes 6266884
  95.5 4.1 %copy-start.5 = (f32[2,1,8,128,255]{4,3,2,1,0:T(8,128)S(1)}, f32[2,1,8,128,255]{4,3,2,1,0:T(8,128)}, u32[]{:S(2)}) copy-start(f32[2,1,8,128,255]{4,3,2,1,0:T(8,128)} %get-tuple-element.36) | copy-start | bytes 6266884
  95.5 4.7 %copy-start.6 = (f32[2,1,8,126,256]{4,3,2,1,0:T(8,128)S(1)}, f32[2,1,8,126,256]{4,3,2,1,0:T(8,128)}, u32[]{:S(2)}) copy-start(f32[2,1,8,126,256]{4,3,2,1,0:T(8,128)} %get-tuple-element.37) | copy-start | bytes 6193156
  118.2 26.6 %collective-permute-start.2 = (f32[2,1,4,128,256]{4,3,2,1,0:T(8,128)S(1)}, f32[2,1,4,128,256]{4,3,2,1,0:T(8,128)}, u32[]{:S(2)}, u32[]{:S(2)}) collective-permute-start(f32[2,1,4,128,256]{4,3,2,1,0:T(8,128)S(1)} %get-tuple-element.31), channel_id=1, source_target_pairs={{1,0},{2,1},{3,2},{4,3},{5,4},{6,5},{7,6},{9,8},{10,9},{11,10},{12... | collective-permute-start | bytes 3145736 | tf_op jit(solution)/shard_map/ppermute | solution.py:21
  119.5 47.8 %collective-permute-start.3 = (f32[2,1,4,128,256]{4,3,2,1,0:T(8,128)S(1)}, f32[2,1,4,128,256]{4,3,2,1,0:T(8,128)}, u32[]{:S(2)}, u32[]{:S(2)}) collective-permute-start(f32[2,1,4,128,256]{4,3,2,1,0:T(8,128)S(1)} %get-tuple-element.32), channel_id=1, source_target_pairs={{0,1},{1,2},{2,3},{3,4},{4,5},{5,6},{6,7},{8,9},{9,10},{10,11},{11... | collective-permute-start | bytes 3145736 | tf_op jit(solution)/shard_map/ppermute | solution.py:20
  130.2 37.1 %copy-start.9 = (f32[1,1,8,128,256]{4,3,2,1,0:T(8,128)S(1)}, f32[1,1,8,128,256]{4,3,2,1,0:T(8,128)}, u32[]{:S(2)}) copy-start(f32[1,1,8,128,256]{4,3,2,1,0:T(8,128)} %stack_reshape.15) | copy-start | bytes 3145732
Sparse Core Ops, SparseCore 0:
  187.5 26.1 reduce-scatter.1
where the time goes:
time: 237 us
  other arithmetic  108 us (46%)
  waiting for transfers between devices  60.8 us (26%)
  local copies, waits for them, and re-layouts  24.8 us (10%)
  starting transfers between devices  14.6 us (6%)
  between operations  14.3 us (6%)
  blocking collectives  14.2 us (6%)
    scatter-add x4, other arithmetic, spread(): jnp.zeros((values.shape[0], limit), jnp.float32).at[:, local]  51.5 us
    reduce_scatter x1, waiting for transfers between devices, on_device(): lax.psum_scatter(lateral_smooth, 'shots', scatter_dimension=1, tiled=True)  26.4 us
    add x2, other arithmetic, on_device(): 2.0 * current - earlier + courant * laplace(extended)  24.2 us
    another operation x9, other arithmetic, on_device(): current = jnp.stack([forward_now, adjoint_now])  23.7 us
    ppermute x2, waiting for transfers between devices, extended_2(): before = lax.ppermute(last, axis, up)  22.5 us
    slice x14, local copies, waits for them, and re-layouts, shifted(): kept = lax.slice_in_dim(values, offset, size, axis=axis)  15.8 us
    all_to_all x1, blocking collectives, on_device(): lax.all_to_all(summed, 'depth', split_axis=1, concat_axis=0, tiled=True)  14.2 us
    ppermute x2, starting transfers between devices, extended_2(): before = lax.ppermute(last, axis, up)  12 us
  transfers between devices with their start and end apart: 5, of which 3 were waited for; matrix products, arithmetic and copies ran while one was open for 36% of the time, Pallas kernels for 0%

commit v1 on v0

v1 whole, which is shorter than its diff:
```python
import jax
import jax.numpy as jnp
from jax import lax
from jax.sharding import PartitionSpec as P

STEPS = 2
HALO = 4


COEFFS = (-205.0 / 72.0, 8.0 / 5.0, -1.0 / 5.0, 8.0 / 315.0, -1.0 / 560.0)
KERNEL = (1.0 / 16.0, 4.0 / 16.0, 6.0 / 16.0, 4.0 / 16.0, 1.0 / 16.0)


def shifted(values, axis, offset):
    size = values.shape[axis]
    width = abs(offset)
    pads = [(0, 0, 0)] * values.ndim
    if offset > 0:
        kept = lax.slice_in_dim(values, offset, size, axis=axis)
        pads[axis] = (0, width, 0)
    else:
        kept = lax.slice_in_dim(values, 0, size - width, axis=axis)
        pads[axis] = (width, 0, 0)
    return lax.pad(kept, jnp.array(0.0, values.dtype), pads)


def local_laplace(core, zaxis):
    total = 3.0 * COEFFS[0] * core
    for k in range(1, 5):
        near = shifted(core, zaxis, k) + shifted(core, zaxis, -k)
        near = near + shifted(core, zaxis + 1, k) + shifted(core, zaxis + 1, -k)
        near = near + shifted(core, zaxis + 2, k) + shifted(core, zaxis + 2, -k)
        total = total + COEFFS[k] * near
    return total


def halo_laplace(below, above, planes, zaxis):
    parts = []
    for p in range(planes):
        term = None
        for k in range(1, 5):
            for q in (p - k, p + k):
                if q < 0:
                    piece = lax.index_in_dim(below, HALO + q, axis=zaxis, keepdims=True)
                elif q >= planes:
                    piece = lax.index_in_dim(above, q - planes, axis=zaxis, keepdims=True)
                else:
                    continue
                piece = COEFFS[k] * piece
                term = piece if term is None else term + piece
        parts.append(term)
    return jnp.concatenate(parts, axis=zaxis)


def smooth(values, axis):
    total = KERNEL[2] * values
    for k in (1, 2):
        total = total + KERNEL[2 + k] * (shifted(values, axis, k) + shifted(values, axis, -k))
    return total


def exchange(current, dim):
    devices = lax.axis_size("depth")
    length = current.shape[dim]
    up = [(i, i + 1) for i in range(devices - 1)]
    down = [(i + 1, i) for i in range(devices - 1)]
    last = lax.slice_in_dim(current, length - HALO, length, axis=dim)
    leading = lax.slice_in_dim(current, 0, HALO, axis=dim)
    below = lax.ppermute(last, "depth", up)
    above = lax.ppermute(leading, "depth", down)
    return below, above


def spread_all(source_flat, receiver_flat, source_values, receiver_values, first_plane, planes, rows, cols):
    lateral = rows * cols
    limit = planes * lateral
    total = 2 * limit

    def local_of(flat, field):
        local = flat - first_plane * lateral
        inside = (local >= 0) & (local < limit)
        return jnp.where(inside, local + field * limit, total)

    index = jnp.concatenate([local_of(source_flat, 0), local_of(receiver_flat, 1)])
    values = jnp.concatenate([source_values, receiver_values], axis=1)
    grid = jnp.zeros((values.shape[0], total), jnp.float32).at[:, index].add(values, mode="drop")
    return grid.reshape(values.shape[0], 2, 1, planes, rows, cols)


def on_device(
    forward_prev,
    forward_now,
    adjoint_prev,
    adjoint_now,
    courant,
    wavelet,
    sign_bits,
    source_depth,
    source_cell,
    receiver_depth,
    receiver_cell,
    residual_traces,
):
    planes, rows, cols = courant.shape
    lateral = rows * cols
    source_flat = source_depth * lateral + source_cell
    receiver_flat = receiver_depth * lateral + receiver_cell
    signs = (2 * sign_bits - 1).astype(jnp.float32)
    position = lax.axis_index("depth")
    earlier = jnp.stack([forward_prev, adjoint_prev])
    current = jnp.stack([forward_now, adjoint_now])
    zaxis = 2
    below, above = exchange(current, zaxis)
    terms = spread_all(
        source_flat,
        receiver_flat,
        signs[0][None, :] * wavelet,
        residual_traces[0],
        position * planes,
        planes,
        rows,
        cols,
    )
    reduced = None
    for step in range(STEPS):
        base = 2.0 * current - earlier + courant * local_laplace(current, zaxis) + terms[step]
        fresh = base + courant * halo_laplace(below, above, planes, zaxis)
        if step + 1 < STEPS:
            below, above = exchange(fresh, zaxis)
        part = smooth(smooth(fresh[0, 0] * fresh[1, 0], 1), 2)
        part = lax.psum_scatter(part, "shots", scatter_dimension=1, tiled=True)
        reduced = part if reduced is None else reduced + part
        earlier, current = (current, fresh)
    columns = lax.all_to_all(reduced, "depth", split_axis=1, concat_axis=0, tiled=True)
    gradient = smooth(columns, 0)
    return (earlier[0], current[0], earlier[1], current[1], gradient)


def solution(mesh):
    in_specs = (
        P("shots", "depth", None, None),
        P("shots", "depth", None, None),
        P("shots", "depth", None, None),
        P("shots", "depth", None, None),
        P("depth", None, None),
        P(),
        P("shots", None),
        P(),
        P(),
        P(),
        P(),
        P("shots", None, None),
    )
    out_specs = (
        P("shots", "depth", None, None),
        P("shots", "depth", None, None),
        P("shots", "depth", None, None),
        P("shots", "depth", None, None),
        P(None, ("shots", "depth"), None),
    )
    return jax.shard_map(
        on_device, mesh=mesh, in_specs=in_specs, out_specs=out_specs, check_vma=False
    )
```

time: 237 us -> 814 us (3.43); the launches traced: 237 us -> 806 us
  other arithmetic: 108 us -> 635 us
  local copies, waits for them, and re-layouts: 24.8 us -> 67.4 us
    scatter-add x4 -> x1, other arithmetic: 51.5 us -> 564 us  [spread_all(): jnp.zeros((values.shape[0], total), jnp.float32).at[:, index]]
    slice x2, local copies, waits for them, and re-layouts: 0.23 us -> 26.2 us  [the longest x1 26.1 us: on_device(): terms[step]]
    slice x14 -> x21, local copies, waits for them, and re-layouts: 15.8 us -> 24.9 us  [shifted(): kept = lax.slice_in_dim(values, offset, size, axis=axis)]
    another operation x9 -> x12, other arithmetic: 23.7 us -> 29.5 us  [on_device(): current = jnp.stack([forward_now, adjoint_now])]
  transfers between devices with their start and end apart: 5 -> 5, of which waited for: 3 -> 2; matrix products, arithmetic and copies ran while one was open for 36% -> 79% of each run, Pallas kernels for 0% -> 0%
where the time goes in v1:
time: 814 us; the launch traced here: 806 us
  other arithmetic  635 us (78%)
  local copies, waits for them, and re-layouts  67.4 us (8%)
  waiting for transfers between devices  60.9 us (7%)
  between operations  14.6 us (2%)
  blocking collectives  14.2 us (2%)
  starting transfers between devices  13.2 us (2%)
    scatter-add x1, other arithmetic, spread_all(): jnp.zeros((values.shape[0], total), jnp.float32).at[:, index]  564 us
    ppermute x2, waiting for transfers between devices, exchange(): below = lax.ppermute(last, 'depth', up)  35.2 us
    another operation x12, other arithmetic, on_device(): current = jnp.stack([forward_now, adjoint_now])  29.5 us
    add x2, other arithmetic, on_device(): fresh = base + courant * halo_laplace(below, above, planes, zaxis)  26.1 us
    slice x1, local copies, waits for them, and re-layouts, on_device(): terms[step]  26.1 us
    reduce_scatter x1, waiting for transfers between devices, on_device(): part = lax.psum_scatter(part, 'shots', scatter_dimension=1, tiled=True)  25.7 us
    slice x21, local copies, waits for them, and re-layouts, shifted(): kept = lax.slice_in_dim(values, offset, size, axis=axis)  24.9 us
  transfers between devices with their start and end apart: 5, of which 2 were waited for; matrix products, arithmetic and copies ran while one was open for 79% of the time, Pallas kernels for 0%

profile of v1, /device:TPU:0, one launch (start us, length us, event | category | flops | bytes accessed | tf_op | source)
XLA Modules:
  0.0 805.6 jit_solution(13231183870164972821)
XLA Ops:
  7.2 3.2 fusion.26
  10.4 4.9 collective-permute-start
  16.6 2.7 fusion.14
  19.4 2.3 fusion.12
  21.7 2.7 fusion.10
  24.4 2.4 fusion.8
  26.8 2.1 fusion.21
  29.0 2.4 fusion.19
  31.6 3.1 broadcast_in_dim.16
  34.7 564.1 %scatter_fusion = f32[2,524288]{1,0:T(2,128)} fusion(f32[2,524288]{1,0:T(2,128)} %broadcast_in_dim.16, s32[4608]{0:T(1024)S(1)} %fusion.35, f32[4608,2]{0,1:T(2,128)S(1)} %maximum_bitcast_fusion), kind=kCustom, calls=%fused_computation | custom fusion | flops 9216 | bytes 129024 | tf_op jit(solution)/shard_map/scatter-add | solution.py:86
  598.8 26.1 %slice_reduce_fusion = (f32[524288]{0:T(1024)}, f32[524288]{0:T(1024)}) fusion(f32[2,524288]{1,0:T(2,128)} %scatter_fusion), kind=kLoop, calls=%fused_computation.66 | loop fusion | bytes 8388608 | tf_op jit(solution)/shard_map/slice | solution.py:126
  624.9 2.9 squeeze.26
  627.8 2.9 squeeze.28
  630.7 2.1 fusion.6
  632.8 2.4 fusion.4
  635.2 2.8 fusion.2
  638.0 2.5 fusion
  640.5 1.9 fusion.23
  645.2 1.8 multiply_dynamic-update-slice_fusion.2
  652.0 12.9 %fusion.18 = f32[2,1,8,128,256]{4,3,2,1,0:T(8,128)S(1)} fusion(f32[2,1,8,128,256]{4,3,2,1,0:T(8,128)} %squeeze.26, f32[1,1,8,128,256]{4,3,2,1,0:T(8,128)} %bitcast.57, f32[1,1,8,128,256]{4,3,2,1,0:T(8,128)} %bitcast.58, f32[2,1,8,128,256]{4,3,2,1,0:T(8,128)} %copy-done.19, f32[2,1,8,128,252]{4,3,2,1,0:T(8,128)S(1)} %copy-done.3, ...), kind=kLoop, calls=%fused_computation.71 | loop fusion | flops 19922944 | bytes 56131584 | tf_op jit(solution)/shard_map/add | solution.py:127
  672.1 2.7 fusion.41
  674.8 2.3 fusion.40
  677.2 2.1 fusion.39
  679.3 2.6 fusion.38
  681.9 5.6 collective-permute-start.2
  690.4 2.3 fusion.36
  692.7 2.4 fusion.37
  696.6 35.2 %collective-permute-done.2 = f32[2,1,4,128,256]{4,3,2,1,0:T(8,128)S(1)} collective-permute-done((f32[2,1,4,128,256]{4,3,2,1,0:T(8,128)S(1)}, f32[2,1,4,128,256]{4,3,2,1,0:T(8,128)S(1)}, u32[]{:S(2)}, u32[]{:S(2)}) %collective-permute-start.2) | collective-permute-done | bytes 1048608 | tf_op jit(solution)/shard_map/ppermute | solution.py:69
  734.4 13.1 %multiply_add_fusion = f32[2,1,8,128,256]{4,3,2,1,0:T(8,128)S(1)} fusion(f32[2,1,8,128,256]{4,3,2,1,0:T(8,128)} %copy-done.20, f32[2,1,8,128,256]{4,3,2,1,0:T(8,128)S(1)} %copy-done.10, f32[2,1,8,128,252]{4,3,2,1,0:T(8,128)S(1)} %get-tuple-element.39, f32[2,1,8,128,252]{4,3,2,1,0:T(8,128)S(1)} %get-tuple-element.38, ...), kind=kLoop, calls=%fused_computation.72 | loop fusion | flops 19398656 | bytes 56131584 | tf_op jit(solution)/shard_map/add | solution.py:127
  754.2 2.3 add_add_fusion
  756.5 25.7 %reduce-scatter.2.cloned.1.call-done = f32[8,32,256]{2,1,0:T(8,128)} async-done(((f32[8,128,256]{2,1,0:T(8,128)}), f32[8,32,256]{2,1,0:T(8,128)}) %reduce-scatter.2.cloned.1.call-update) | async-done | bytes 262160 | tf_op jit(solution)/shard_map/reduce_scatter | solution.py:131
  783.3 14.2 %all_to_all.18 = f32[8,32,256]{2,0,1:T(8,128)S(1)} all-to-all(f32[8,32,256]{2,0,1:T(8,128)S(1)} %copy.35), channel_id=1, replica_groups=mesh['shots'=4,'depth'=8] {'depth'}, dimensions={1} | all-to-all | bytes 524288 | tf_op jit(solution)/shard_map/all_to_all | solution.py:134
  (106 shorter events, 32.0 us)
Async XLA Ops:
  7.2 775.0 %reduce-scatter.2.cloned.1.call-start = ((), (), s32[]{:S(2)}) async-start(), calls=%async_computation.2 | async-start | bytes 1310720 | tf_op jit(solution)/shard_map/reduce_scatter | solution.py:131
  7.2 9.4 %copy-start = (f32[1,8,128,256]{3,2,1,0:T(8,128)S(1)}, f32[1,8,128,256]{3,2,1,0:T(8,128)}, u32[]{:S(2)}) copy-start(f32[1,8,128,256]{3,2,1,0:T(8,128)} %param.13) | copy-start | bytes 3145732
  7.2 9.4 %copy-start.1 = (f32[1,8,128,256]{3,2,1,0:T(8,128)S(1)}, f32[1,8,128,256]{3,2,1,0:T(8,128)}, u32[]{:S(2)}) copy-start(f32[1,8,128,256]{3,2,1,0:T(8,128)} %param.15) | copy-start | bytes 3145732
  10.4 632.0 %collective-permute-start = (f32[2,1,4,128,256]{4,3,2,1,0:T(8,128)}, f32[2,1,4,128,256]{4,3,2,1,0:T(8,128)S(1)}, u32[]{:S(2)}, u32[]{:S(2)}) collective-permute-start(f32[2,1,4,128,256]{4,3,2,1,0:T(8,128)} %get-tuple-element.65), channel_id=1, source_target_pairs={{0,1},{1,2},{2,3},{3,4},{4,5},{5,6},{6,7},{8,9},{9,10},{10,11},{11... | collective-permute-start | bytes 3145736 | tf_op jit(solution)/shard_map/ppermute | solution.py:69
  15.3 629.9 %collective-permute-start.1 = (f32[2,1,4,128,256]{4,3,2,1,0:T(8,128)}, f32[2,1,4,128,256]{4,3,2,1,0:T(8,128)}, u32[]{:S(2)}, u32[]{:S(2)}) collective-permute-start(f32[2,1,4,128,256]{4,3,2,1,0:T(8,128)} %get-tuple-element.64), channel_id=1, source_target_pairs={{1,0},{2,1},{3,2},{4,3},{5,4},{6,5},{7,6},{9,8},{10,9},{11,10},{12... | collective-permute-start | bytes 3145736 | tf_op jit(solution)/shard_map/ppermute | solution.py:70
  28.9 2.4 copy-start.25
  28.9 2.4 copy-start.22
  28.9 2.4 copy-start.23
  28.9 2.5 copy-start.26
  28.9 2.5 copy-start.27
  29.0 2.6 copy-start.24
  29.0 2.6 copy-start.21
  638.0 14.0 %copy-start.7 = (f32[2,1,8,128,253]{4,3,2,1,0:T(8,128)S(1)}, f32[2,1,8,128,253]{4,3,2,1,0:T(8,128)}, u32[]{:S(2)}) copy-start(f32[2,1,8,128,253]{4,3,2,1,0:T(8,128)} %get-tuple-element.59) | copy-start | bytes 6217732
  638.0 14.0 %copy-start.8 = (f32[2,1,8,125,256]{4,3,2,1,0:T(8,128)S(1)}, f32[2,1,8,125,256]{4,3,2,1,0:T(8,128)}, u32[]{:S(2)}) copy-start(f32[2,1,8,125,256]{4,3,2,1,0:T(8,128)} %get-tuple-element.56) | copy-start | bytes 6144004
  638.0 14.0 %copy-start.9 = (f32[2,1,8,125,256]{4,3,2,1,0:T(8,128)S(1)}, f32[2,1,8,125,256]{4,3,2,1,0:T(8,128)}, u32[]{:S(2)}) copy-start(f32[2,1,8,125,256]{4,3,2,1,0:T(8,128)} %get-tuple-element.57) | copy-start | bytes 6144004
  640.5 11.4 %copy-start.5 = (f32[2,1,8,124,256]{4,3,2,1,0:T(8,128)S(1)}, f32[2,1,8,124,256]{4,3,2,1,0:T(8,128)}, u32[]{:S(2)}) copy-start(f32[2,1,8,124,256]{4,3,2,1,0:T(8,128)} %get-tuple-element.61) | copy-start | bytes 6094852
  640.5 11.4 %copy-start.6 = (f32[2,1,8,128,253]{4,3,2,1,0:T(8,128)S(1)}, f32[2,1,8,128,253]{4,3,2,1,0:T(8,128)}, u32[]{:S(2)}) copy-start(f32[2,1,8,128,253]{4,3,2,1,0:T(8,128)} %get-tuple-element.58) | copy-start | bytes 6217732
  642.4 9.6 %copy-start.4 = (f32[2,1,8,124,256]{4,3,2,1,0:T(8,128)S(1)}, f32[2,1,8,124,256]{4,3,2,1,0:T(8,128)}, u32[]{:S(2)}) copy-start(f32[2,1,8,124,256]{4,3,2,1,0:T(8,128)} %get-tuple-element.60) | copy-start | bytes 6094852
  642.5 9.5 %copy-start.12 = (f32[8,128,256]{2,1,0:T(8,128)S(1)}, f32[8,128,256]{2,1,0:T(8,128)}, u32[]{:S(2)}) copy-start(f32[8,128,256]{2,1,0:T(8,128)} %param.16) | copy-start | bytes 3145732
  643.4 8.6 %copy-start.2 = (f32[2,1,8,128,252]{4,3,2,1,0:T(8,128)S(1)}, f32[2,1,8,128,252]{4,3,2,1,0:T(8,128)}, u32[]{:S(2)}) copy-start(f32[2,1,8,128,252]{4,3,2,1,0:T(8,128)} %get-tuple-element.62) | copy-start | bytes 6193156
  643.4 8.6 %copy-start.3 = (f32[2,1,8,128,252]{4,3,2,1,0:T(8,128)S(1)}, f32[2,1,8,128,252]{4,3,2,1,0:T(8,128)}, u32[]{:S(2)}) copy-start(f32[2,1,8,128,252]{4,3,2,1,0:T(8,128)} %get-tuple-element.63) | copy-start | bytes 6193156
  650.6 1.4 copy-start.19
  666.7 15.3 %copy-start.14 = (f32[2,1,4,128,256]{4,3,2,1,0:T(8,128)}, f32[2,1,4,128,256]{4,3,2,1,0:T(8,128)S(1)}, u32[]{:S(2)}) copy-start(f32[2,1,4,128,256]{4,3,2,1,0:T(8,128)S(1)} %get-tuple-element.41) | copy-start | bytes 3145732
  666.7 20.9 %copy-start.13 = (f32[2,1,4,128,256]{4,3,2,1,0:T(8,128)}, f32[2,1,4,128,256]{4,3,2,1,0:T(8,128)S(1)}, u32[]{:S(2)}) copy-start(f32[2,1,4,128,256]{4,3,2,1,0:T(8,128)S(1)} %get-tuple-element.40) | copy-start | bytes 3145732
  681.9 49.9 %collective-permute-start.2 = (f32[2,1,4,128,256]{4,3,2,1,0:T(8,128)S(1)}, f32[2,1,4,128,256]{4,3,2,1,0:T(8,128)S(1)}, u32[]{:S(2)}, u32[]{:S(2)}) collective-permute-start(f32[2,1,4,128,256]{4,3,2,1,0:T(8,128)S(1)} %get-tuple-element.41), channel_id=1, source_target_pairs={{0,1},{1,2},{2,3},{3,4},{4,5},{5,6},{6,7},{8,9},{9,10},{10,11},{11... | collective-permute-start | bytes 3145736 | tf_op jit(solution)/shard_map/ppermute | solution.py:69
  687.6 44.5 %collective-permute-start.3 = (f32[2,1,4,128,256]{4,3,2,1,0:T(8,128)S(1)}, f32[2,1,4,128,256]{4,3,2,1,0:T(8,128)S(1)}, u32[]{:S(2)}, u32[]{:S(2)}) collective-permute-start(f32[2,1,4,128,256]{4,3,2,1,0:T(8,128)S(1)} %get-tuple-element.40), channel_id=1, source_target_pairs={{1,0},{2,1},{3,2},{4,3},{5,4},{6,5},{7,6},{9,8},{10,9},{11,10},{12... | collective-permute-start | bytes 3145736 | tf_op jit(solution)/shard_map/ppermute | solution.py:70
  732.0 2.3 copy-start.10
  732.3 1.3 copy-start.20
  749.3 1.2 copy-start.15
  749.3 1.5 copy-start.16
  749.3 1.8 copy-start.17
  749.3 2.1 copy-start.18
  (1 other events, 1.0 us)
Sparse Core Ops, SparseCore 0:
  756.6 25.5 reduce-scatter.1

commit v2 on v1

--- a/solution.py
+++ b/solution.py
@@ -24,12 +24,23 @@
     return lax.pad(kept, jnp.array(0.0, values.dtype), pads)
 
 
+def band(size):
+    index = jnp.arange(size)
+    gap = jnp.abs(index[:, None] - index[None, :])
+    matrix = jnp.zeros((size, size), jnp.float32)
+    for k in range(1, 5):
+        matrix = jnp.where(gap == k, jnp.float32(COEFFS[k]), matrix)
+    return matrix
+
+
 def local_laplace(core, zaxis):
-    total = 3.0 * COEFFS[0] * core
+    rows, cols = core.shape[zaxis + 1], core.shape[zaxis + 2]
+    high = lax.Precision.HIGHEST
+    along_y = jnp.einsum("...xy,yk->...xk", core, band(cols), precision=high)
+    along_x = jnp.einsum("...xy,kx->...ky", core, band(rows), precision=high)
+    total = 3.0 * COEFFS[0] * core + (along_x + along_y)
     for k in range(1, 5):
         near = shifted(core, zaxis, k) + shifted(core, zaxis, -k)
-        near = near + shifted(core, zaxis + 1, k) + shifted(core, zaxis + 1, -k)
-        near = near + shifted(core, zaxis + 2, k) + shifted(core, zaxis + 2, -k)
         total = total + COEFFS[k] * near
     return total
 
@@ -71,20 +82,32 @@
     return below, above
 
 
-def spread_all(source_flat, receiver_flat, source_values, receiver_values, first_plane, planes, rows, cols):
+def spread(flat, values, first_plane, planes, rows, cols):
     lateral = rows * cols
     limit = planes * lateral
-    total = 2 * limit
+    local = flat - first_plane * lateral
+    local = jnp.where((local >= 0) & (local < limit), local, limit)
+    grid = jnp.zeros((values.shape[0], limit), jnp.float32).at[:, local].add(values, mode="drop")
+    return grid.reshape(values.shape[0], planes, rows, cols)
 
-    def local_of(flat, field):
-        local = flat - first_plane * lateral
-        inside = (local >= 0) & (local < limit)
-        return jnp.where(inside, local + field * limit, total)
 
-    index = jnp.concatenate([local_of(source_flat, 0), local_of(receiver_flat, 1)])
-    values = jnp.concatenate([source_values, receiver_values], axis=1)
-    grid = jnp.zeros((values.shape[0], total), jnp.float32).at[:, index].add(values, mode="drop")
-    return grid.reshape(values.shape[0], 2, 1, planes, rows, cols)
+def reduce_shots(values, dim):
+    devices = lax.axis_size("shots")
+    me = lax.axis_index("shots")
+    length = values.shape[dim]
+    shape = values.shape
+    blocks = values.reshape(shape[:dim] + (devices, length // devices) + shape[dim + 1 :])
+    bit = 1
+    while bit < devices:
+        count = blocks.shape[dim]
+        paired = blocks.reshape(shape[:dim] + (count // 2, 2, length // devices) + shape[dim + 1 :])
+        mine = (me // bit) % 2
+        keep = lax.dynamic_index_in_dim(paired, mine, axis=dim + 1, keepdims=False)
+        send = lax.dynamic_index_in_dim(paired, 1 - mine, axis=dim + 1, keepdims=False)
+        pairs = [(i, i ^ bit) for i in range(devices)]
+        blocks = keep + lax.ppermute(send, "shots", pairs)
+        bit *= 2
+    return blocks.reshape(shape[:dim] + (length // devices,) + shape[dim + 1 :])
 
 
 def on_device(
@@ -111,26 +134,21 @@
     current = jnp.stack([forward_now, adjoint_now])
     zaxis = 2
     below, above = exchange(current, zaxis)
-    terms = spread_all(
-        source_flat,
-        receiver_flat,
-        signs[0][None, :] * wavelet,
-        residual_traces[0],
-        position * planes,
-        planes,
-        rows,
-        cols,
-    )
-    reduced = None
+    first_plane = position * planes
+    correlation = None
     for step in range(STEPS):
-        base = 2.0 * current - earlier + courant * local_laplace(current, zaxis) + terms[step]
+        forward_part = spread(source_flat, signs * wavelet[step][None, :], first_plane, planes, rows, cols)
+        adjoint_part = spread(receiver_flat, residual_traces[:, step, :], first_plane, planes, rows, cols)
+        terms = jnp.stack([forward_part, adjoint_part])
+        base = 2.0 * current - earlier + courant * local_laplace(current, zaxis) + terms
         fresh = base + courant * halo_laplace(below, above, planes, zaxis)
         if step + 1 < STEPS:
             below, above = exchange(fresh, zaxis)
-        part = smooth(smooth(fresh[0, 0] * fresh[1, 0], 1), 2)
-        part = lax.psum_scatter(part, "shots", scatter_dimension=1, tiled=True)
-        reduced = part if reduced is None else reduced + part
+        part = fresh[0, 0] * fresh[1, 0]
+        correlation = part if correlation is None else correlation + part
         earlier, current = (current, fresh)
+    lateral_smooth = smooth(smooth(correlation, 1), 2)
+    reduced = reduce_shots(lateral_smooth, 1)
     columns = lax.all_to_all(reduced, "depth", split_axis=1, concat_axis=0, tiled=True)
     gradient = smooth(columns, 0)
     return (earlier[0], current[0], earlier[1], current[1], gradient)

time: 814 us -> 171 us (0.21); the launches traced: 806 us -> 171 us
  other arithmetic: 635 us -> 65.3 us
  local copies, waits for them, and re-layouts: 67.4 us -> 13.1 us
  matrix products: 0 us -> 14.1 us
  between operations: 14.6 us -> 1.23 us
  waiting for transfers between devices: 60.9 us -> 48.2 us
    scatter-add x1 -> x4, other arithmetic: 564 us -> 52.1 us  [spread(): jnp.zeros((values.shape[0], limit), jnp.float32).at[:, local]]
    slice x1, local copies, waits for them, and re-layouts: 26.1 us -> 0.03 us  [on_device(): residual_traces[:, step, :]]
    add x3 -> x2, other arithmetic: 28.3 us -> 2.6 us  [the longest x1 2.27 us: on_device(): correlation = part if correlation is None else correlation + part]
    reduce_scatter x1 -> x0, waiting for transfers between devices: 25.7 us -> none  [on_device(): part = lax.psum_scatter(part, 'shots', scatter_dimension=1, tiled=True)]
    another operation x12 -> x4, other arithmetic: 29.5 us -> 4.07 us  [on_device(): current = jnp.stack([forward_now, adjoint_now])]
    slice x21 -> x9, local copies, waits for them, and re-layouts: 24.9 us -> 2.42 us  [shifted(): kept = lax.slice_in_dim(values, offset, size, axis=axis)]
    dot_general x0 -> x4, matrix products: none -> 14.1 us  [the longest x2 7.05 us: local_laplace(): along_y = jnp.einsum('...xy,yk->...xk', core, band(cols), precision=high)]
    ppermute x0 -> x2, waiting for transfers between devices: none -> 8.71 us  [reduce_shots(): blocks = keep + lax.ppermute(send, 'shots', pairs)]
  transfers between devices with their start and end apart: 5 -> 6, of which waited for: 2 -> 3; matrix products, arithmetic and copies ran while one was open for 79% -> 41% of each run, Pallas kernels for 0% -> 0%
where the time goes in v2:
time: 171 us
  other arithmetic  65.3 us (38%)
  waiting for transfers between devices  48.2 us (28%)
  starting transfers between devices  15 us (9%)
  matrix products  14.1 us (8%)
  blocking collectives  14.1 us (8%)
  local copies, waits for them, and re-layouts  13.1 us (8%)
    scatter-add x4, other arithmetic, spread(): jnp.zeros((values.shape[0], limit), jnp.float32).at[:, local]  52.1 us
    ppermute x2, waiting for transfers between devices, exchange(): below = lax.ppermute(last, 'depth', up)  39.5 us
    all_to_all x1, blocking collectives, on_device(): lax.all_to_all(reduced, 'depth', split_axis=1, concat_axis=0, tiled=True)  14.1 us
    ppermute x2, starting transfers between devices, exchange(): below = lax.ppermute(last, 'depth', up)  10.6 us
    ppermute x2, waiting for transfers between devices, reduce_shots(): blocks = keep + lax.ppermute(send, 'shots', pairs)  8.71 us
    dot_general x2, matrix products, local_laplace(): along_y = jnp.einsum('...xy,yk->...xk', core, band(cols), precision=high)  7.05 us
    dot_general x2, matrix products, local_laplace(): along_x = jnp.einsum('...xy,kx->...ky', core, band(rows), precision=high)  7.04 us
    another operation x4, local copies, waits for them, and re-layouts, on_device(): terms = jnp.stack([forward_part, adjoint_part])  6.3 us
  transfers between devices with their start and end apart: 6, of which 3 were waited for; matrix products, arithmetic and copies ran while one was open for 41% of the time, Pallas kernels for 0%

profile of v2, /device:TPU:0, one launch (start us, length us, event | category | flops | bytes accessed | tf_op | source)
XLA Modules:
  0.0 171.0 jit_solution(13064640563787606769)
XLA Ops:
  0.7 3.1 %fusion.32 = (f32[2,1,4,128,256]{4,3,2,0,1:T(8,128)}, f32[2,1,4,128,256]{4,3,2,0,1:T(8,128)}) fusion(f32[1,1,8,128,256]{4,3,2,0,1:T(8,128)} %bitcast.113, f32[1,1,8,128,256]{4,3,2,0,1:T(8,128)} %bitcast.106), kind=kLoop, calls=%fused_computation.57 | loop fusion | flops 524288 | bytes 4194304 | tf_op jit(solution)/shard_map/stack | solution.py:134
  3.8 6.0 %collective-permute-start = (f32[2,1,4,128,256]{4,3,2,0,1:T(8,128)}, f32[2,1,4,128,256]{4,3,2,0,1:T(8,128)}, u32[]{:S(2)}, u32[]{:S(2)}) collective-permute-start(f32[2,1,4,128,256]{4,3,2,0,1:T(8,128)} %get-tuple-element.30), channel_id=1, source_target_pairs={{0,1},{1,2},{2,3},{3,4},{4,5},{5,6},{6,7},{8,9},{9,10},{10,11},{11... | collective-permute-start | bytes 3145736 | tf_op jit(solution)/shard_map/ppermute | solution.py:80
  9.7 1.3 collective-permute-start.1
  11.2 22.2 %scatter_custom_fusion.3 = f32[262144]{0:T(1024)S(1)} fusion(s32[4096]{0:T(1024)S(1)} %compare_select_fusion, f32[4096]{0:T(1024)S(1)} %bitcast.129, f32[]{:T(128)} %constant.56.clone.1), kind=kCustom, calls=%fused_computation.67 | custom fusion | flops 4096 | bytes 1048580 | tf_op jit(solution)/shard_map/scatter-add | solution.py:90
  33.3 1.3 stack_reshape.15
  34.6 3.5 %scatter_custom_fusion.2 = f32[262144]{0:T(1024)S(1)} fusion(s32[512]{0:T(512)S(1)} %compare_select_fusion.1, f32[512]{0:T(512)S(1)} %bitcast.131, f32[]{:T(128)} %constant.56.clone.1), kind=kCustom, calls=%fused_computation.69 | custom fusion | flops 512 | bytes 1048580 | tf_op jit(solution)/shard_map/scatter-add | solution.py:90
  38.1 1.3 stack_reshape.14
  39.4 22.2 %scatter_custom_fusion.1 = f32[262144]{0:T(1024)S(1)} fusion(s32[4096]{0:T(1024)S(1)} %compare_select_fusion, f32[4096]{0:T(1024)S(1)} %bitcast.128, f32[]{:T(128)} %constant.56.clone.1), kind=kCustom, calls=%fused_computation.71 | custom fusion | flops 4096 | bytes 1048580 | tf_op jit(solution)/shard_map/scatter-add | solution.py:90
  61.6 1.3 stack_reshape.13
  62.8 4.2 %scatter_custom_fusion = f32[262144]{0:T(1024)} fusion(s32[512]{0:T(512)S(1)} %compare_select_fusion.1, f32[512]{0:T(512)S(1)} %bitcast.130, f32[]{:T(128)} %constant.56.clone.1), kind=kCustom, calls=%fused_computation.73 | custom fusion | flops 512 | bytes 1048580 | tf_op jit(solution)/shard_map/scatter-add | solution.py:90
  67.1 2.5 %stack_reshape.12 = f32[1,1,8,128,256]{4,3,2,0,1:T(8,128)} reshape(f32[262144]{0:T(1024)} %scatter_custom_fusion) | data formatting | bytes 2097152 | tf_op jit(solution)/shard_map/stack;reshape | solution.py:142
  70.6 1.9 %fusion.21 = f32[2,8,128,256]{3,2,1,0:T(8,128)S(1)} fusion(f32[1,1,8,128,256]{4,3,2,0,1:T(8,128)S(1)} %bitcast.110, f32[1,1,8,128,256]{4,3,2,0,1:T(8,128)S(1)} %bitcast.117), kind=kOutput, calls=%fused_computation.46 | convolution fusion | flops 1611792384 | bytes 4194304 | tf_op jit(solution)/shard_map/...xy,yk->...xk/dot_general | solution.py:39
  72.6 1.3 fusion.50
  73.9 1.2 add_dynamic-update-slice_fusion.7
  75.0 1.1 add_dynamic-update-slice_fusion.6
  76.2 1.1 multiply_dynamic-update-slice_fusion.3
  78.4 5.1 %fusion.2 = f32[2,1,8,128,256]{4,3,2,0,1:T(8,128)S(1)} fusion(f32[1,1,8,128,256]{4,3,2,0,1:T(8,128)S(1)} %bitcast.125, f32[1,1,8,128,256]{4,3,2,0,1:T(8,128)} %bitcast.126, f32[1,1,8,128,256]{4,3,2,0,1:T(8,128)S(1)} %copy-done.5, f32[1,1,8,128,256]{4,3,2,0,1:T(8,128)S(1)} %copy-done.6, f32[2,8,128,256]{3,2,1,0:T(8,128)S(1)} %fusion.21, ...), kind=kOutput, calls=%fused_computation.24 | convolution fusion | flops 819101696 | bytes 25165824 | tf_op jit(solution)/shard_map/...xy,kx->...ky/dot_general | solution.py:40
  83.7 4.6 %collective-permute-start.2 = (f32[2,1,4,128,256]{4,3,2,0,1:T(8,128)S(1)}, f32[2,1,4,128,256]{4,3,2,0,1:T(8,128)S(1)}, u32[]{:S(2)}, u32[]{:S(2)}) collective-permute-start(f32[2,1,4,128,256]{4,3,2,0,1:T(8,128)S(1)} %get-tuple-element.22), channel_id=1, source_target_pairs={{0,1},{1,2},{2,3},{3,4},{4,5},{5,6},{6,7},{8,9},{9,10},{10,11},{11... | collective-permute-start | bytes 3145736 | tf_op jit(solution)/shard_map/ppermute | solution.py:80
  88.3 1.9 %fusion.19 = f32[128,2,8,256]{3,0,2,1:T(8,128)S(1)} fusion(f32[2,1,8,128,256]{4,3,2,0,1:T(8,128)S(1)} %fusion.2), kind=kOutput, calls=%fused_computation.44 | convolution fusion | flops 805470208 | bytes 4194304 | tf_op jit(solution)/shard_map/...xy,kx->...ky/dot_general | solution.py:40
  90.2 1.5 collective-permute-start.3
  92.2 0.5 fusion.141
  93.1 39.5 %collective-permute-done.2 = f32[2,1,4,128,256]{4,3,2,0,1:T(8,128)S(1)} collective-permute-done((f32[2,1,4,128,256]{4,3,2,0,1:T(8,128)S(1)}, f32[2,1,4,128,256]{4,3,2,0,1:T(8,128)S(1)}, u32[]{:S(2)}, u32[]{:S(2)}) %collective-permute-start.2) | collective-permute-done | bytes 1048608 | tf_op jit(solution)/shard_map/ppermute | solution.py:80
  133.1 1.3 copy-done.7
  134.4 0.6 copy-done.3
  135.1 5.1 %fusion.3 = f32[2,1,8,128,256]{4,3,2,0,1:T(8,128)S(1)} fusion(f32[1,1,8,128,256]{4,3,2,0,1:T(8,128)S(1)} %copy-done.2, f32[1,1,8,128,256]{4,3,2,0,1:T(8,128)S(1)} %copy-done.3, f32[128,2,8,256]{3,0,2,1:T(8,128)S(1)} %fusion.19, f32[2,1,8,128,256]{4,3,2,0,1:T(8,128)} %copy-done.7, f32[2,1,4,128,256]{4,3,2,0,1:T(8,128)S(1)} %get-tuple-element.21, ...), kind=kOutput, calls=%fused_computation.26 | convolution fusion | flops 1623851008 | bytes 25165824 | tf_op jit(solution)/shard_map/...xy,yk->...xk/dot_general | solution.py:39
  140.2 2.3 %add_bitcast_fusion = (f32[8,128,256]{2,1,0:T(8,128)S(1)}, f32[1,8,128,256]{3,2,1,0:T(8,128)}, f32[1,8,128,256]{3,2,1,0:T(8,128)}, f32[1,8,128,256]{3,2,1,0:T(8,128)}, f32[1,8,128,256]{3,2,1,0:T(8,128)}) fusion(f32[2,1,8,128,256]{4,3,2,0,1:T(8,128)S(1)} %fusion.3, f32[2,1,8,128,256]{4,3,2,0,1:T(8,128)S(1)} %fusion.2), kind=kLoop, calls=%fused_computation.60 | loop fusion | flops 786432 | bytes 9437184 | tf_op jit(solution)/shard_map/add | solution.py:148
  144.0 0.6 multiply_add_fusion
  145.1 1.9 %collective-permute-done.4 = f32[8,2,32,256]{3,0,2,1:T(8,128)S(1)} collective-permute-done((f32[8,2,32,256]{3,0,2,1:T(8,128)S(1)}, f32[8,2,32,256]{3,0,2,1:T(8,128)S(1)}, u32[]{:S(2)}, u32[]{:S(2)}) %collective-permute-start.4) | collective-permute-done | bytes 524320 | tf_op jit(solution)/shard_map/ppermute | solution.py:108
  147.3 1.6 collective-permute-start.5
  148.9 6.8 %collective-permute-done.5 = f32[8,1,32,256]{3,0,2,1:T(8,128)S(1)} collective-permute-done((f32[8,1,32,256]{3,0,2,1:T(8,128)S(1)}, f32[8,1,32,256]{3,0,2,1:T(8,128)S(1)}, u32[]{:S(2)}, u32[]{:S(2)}) %collective-permute-start.5) | collective-permute-done | bytes 262176 | tf_op jit(solution)/shard_map/ppermute | solution.py:108
  155.8 14.1 %all_to_all.18 = f32[8,32,256]{2,0,1:T(8,128)S(1)} all-to-all(f32[8,32,256]{2,0,1:T(8,128)S(1)} %add_bitcast_fusion.1), channel_id=1, replica_groups=mesh['shots'=4,'depth'=8] {'depth'}, dimensions={1} | all-to-all | bytes 524288 | tf_op jit(solution)/shard_map/all_to_all | solution.py:152
  170.1 0.9 copy.22
  (70 shorter events, 6.1 us)
Async XLA Ops:
  0.6 10.4 %copy-start.9 = (f32[1,2,4096]{2,1,0:T(2,128)S(1)}, f32[1,2,4096]{2,1,0:T(2,128)}, u32[]{:S(2)}) copy-start(f32[1,2,4096]{2,1,0:T(2,128)} %param.23) | copy-start | bytes 98308
  0.6 10.4 %copy-start.10 = (s32[4096]{0:T(1024)S(1)}, s32[4096]{0:T(1024)}, u32[]{:S(2)}) copy-start(s32[4096]{0:T(1024)} %param.22) | copy-start | bytes 49156
  0.7 10.4 %copy-start.11 = (s32[4096]{0:T(1024)S(1)}, s32[4096]{0:T(1024)}, u32[]{:S(2)}) copy-start(s32[4096]{0:T(1024)} %param.21) | copy-start | bytes 49156
  0.7 10.4 %copy-start.14 = (s32[512]{0:T(512)S(1)}, s32[512]{0:T(512)}, u32[]{:S(2)}) copy-start(s32[512]{0:T(512)} %param.20) | copy-start | bytes 6148
  0.7 10.4 %copy-start.15 = (s32[512]{0:T(512)S(1)}, s32[512]{0:T(512)}, u32[]{:S(2)}) copy-start(s32[512]{0:T(512)} %param.19) | copy-start | bytes 6148
  3.8 30.8 %copy-start.12 = (f32[2,512]{1,0:T(2,128)S(1)}, f32[2,512]{1,0:T(2,128)}, u32[]{:S(2)}) copy-start(f32[2,512]{1,0:T(2,128)} %param.17) | copy-start | bytes 12292
  3.8 30.8 %copy-start.13 = (s32[1,512]{1,0:T(1,128)S(1)}, s32[1,512]{1,0:T(1,128)}, u32[]{:S(2)}) copy-start(s32[1,512]{1,0:T(1,128)} %param.18) | copy-start | bytes 6148
  3.8 68.8 %collective-permute-start = (f32[2,1,4,128,256]{4,3,2,0,1:T(8,128)}, f32[2,1,4,128,256]{4,3,2,0,1:T(8,128)}, u32[]{:S(2)}, u32[]{:S(2)}) collective-permute-start(f32[2,1,4,128,256]{4,3,2,0,1:T(8,128)} %get-tuple-element.30), channel_id=1, source_target_pairs={{0,1},{1,2},{2,3},{3,4},{4,5},{5,6},{6,7},{8,9},{9,10},{10,11},{11... | collective-permute-start | bytes 3145736 | tf_op jit(solution)/shard_map/ppermute | solution.py:80
  9.7 67.6 %collective-permute-start.1 = (f32[2,1,4,128,256]{4,3,2,0,1:T(8,128)}, f32[2,1,4,128,256]{4,3,2,0,1:T(8,128)S(1)}, u32[]{:S(2)}, u32[]{:S(2)}) collective-permute-start(f32[2,1,4,128,256]{4,3,2,0,1:T(8,128)} %get-tuple-element.29), channel_id=1, source_target_pairs={{1,0},{2,1},{3,2},{4,3},{5,4},{6,5},{7,6},{9,8},{10,9},{11,10},{12... | collective-permute-start | bytes 3145736 | tf_op jit(solution)/shard_map/ppermute | solution.py:81
  62.8 6.8 %copy-start = (f32[1,8,128,256]{3,2,1,0:T(8,128)S(1)}, f32[1,8,128,256]{3,2,1,0:T(8,128)}, u32[]{:S(2)}) copy-start(f32[1,8,128,256]{3,2,1,0:T(8,128)} %param.15) | copy-start | bytes 3145732
  62.8 6.8 %copy-start.1 = (f32[1,8,128,256]{3,2,1,0:T(8,128)S(1)}, f32[1,8,128,256]{3,2,1,0:T(8,128)}, u32[]{:S(2)}) copy-start(f32[1,8,128,256]{3,2,1,0:T(8,128)} %param.13) | copy-start | bytes 3145732
  76.1 1.4 copy-start.4
  76.1 1.6 copy-start.5
  76.1 1.9 %copy-start.6 = (f32[1,1,8,128,256]{4,3,2,0,1:T(8,128)S(1)}, f32[1,1,8,128,256]{4,3,2,0,1:T(8,128)}, u32[]{:S(2)}) copy-start(f32[1,1,8,128,256]{4,3,2,0,1:T(8,128)} %stack_reshape.12) | copy-start | bytes 3145732
  76.2 2.2 %copy-start.8 = (f32[1,8,128,256]{3,2,1,0:T(8,128)S(1)}, f32[1,8,128,256]{3,2,1,0:T(8,128)}, u32[]{:S(2)}) copy-start(f32[1,8,128,256]{3,2,1,0:T(8,128)} %param.14) | copy-start | bytes 3145732
  83.7 48.9 %collective-permute-start.2 = (f32[2,1,4,128,256]{4,3,2,0,1:T(8,128)S(1)}, f32[2,1,4,128,256]{4,3,2,0,1:T(8,128)S(1)}, u32[]{:S(2)}, u32[]{:S(2)}) collective-permute-start(f32[2,1,4,128,256]{4,3,2,0,1:T(8,128)S(1)} %get-tuple-element.22), channel_id=1, source_target_pairs={{0,1},{1,2},{2,3},{3,4},{4,5},{5,6},{6,7},{8,9},{9,10},{10,11},{11... | collective-permute-start | bytes 3145736 | tf_op jit(solution)/shard_map/ppermute | solution.py:80
  90.2 42.6 %collective-permute-start.3 = (f32[2,1,4,128,256]{4,3,2,0,1:T(8,128)S(1)}, f32[2,1,4,128,256]{4,3,2,0,1:T(8,128)S(1)}, u32[]{:S(2)}, u32[]{:S(2)}) collective-permute-start(f32[2,1,4,128,256]{4,3,2,0,1:T(8,128)S(1)} %get-tuple-element.21), channel_id=1, source_target_pairs={{1,0},{2,1},{3,2},{4,3},{5,4},{6,5},{7,6},{9,8},{10,9},{11,10},{12... | collective-permute-start | bytes 3145736 | tf_op jit(solution)/shard_map/ppermute | solution.py:81
  132.8 1.7 copy-start.2
  132.8 2.3 %copy-start.3 = (f32[1,1,8,128,256]{4,3,2,0,1:T(8,128)S(1)}, f32[1,1,8,128,256]{4,3,2,0,1:T(8,128)}, u32[]{:S(2)}) copy-start(f32[1,1,8,128,256]{4,3,2,0,1:T(8,128)} %stack_reshape.14) | copy-start | bytes 3145732
  133.1 1.3 copy-start.7
  145.0 2.0 %collective-permute-start.4 = (f32[8,2,32,256]{3,0,2,1:T(8,128)S(1)}, f32[8,2,32,256]{3,0,2,1:T(8,128)S(1)}, u32[]{:S(2)}, u32[]{:S(2)}) collective-permute-start(f32[8,2,32,256]{3,0,2,1:T(8,128)S(1)} %bitcast.127), channel_id=1, source_target_pairs={{0,8},{8,0},{16,24},{24,16},{1,9},{9,1},{17,25},{25,17},{2,10},{10... | collective-permute-start | bytes 1572872 | tf_op jit(solution)/shard_map/ppermute | solution.py:108
  147.3 8.4 %collective-permute-start.5 = (f32[8,1,32,256]{3,0,2,1:T(8,128)S(1)}, f32[8,1,32,256]{3,0,2,1:T(8,128)S(1)}, u32[]{:S(2)}, u32[]{:S(2)}) collective-permute-start(f32[8,1,32,256]{3,0,2,1:T(8,128)S(1)} %constant_dynamic-slice_fusion), channel_id=1, source_target_pairs={{0,16},{8,24},{16,0},{24,8},{1,17},{9,25},{17,1},{25,9},{2,18},{10... | collective-permute-start | bytes 786440 | tf_op jit(solution)/shard_map/ppermute | solution.py:108

commit v3 on v2

--- a/solution.py
+++ b/solution.py
@@ -136,7 +136,12 @@
     below, above = exchange(current, zaxis)
     first_plane = position * planes
     correlation = None
+    gate = ()
     for step in range(STEPS):
+        if step > 0:
+            gate, (source_flat, receiver_flat, signs, wavelet, residual_traces) = lax.optimization_barrier(
+                (gate, (source_flat, receiver_flat, signs, wavelet, residual_traces))
+            )
         forward_part = spread(source_flat, signs * wavelet[step][None, :], first_plane, planes, rows, cols)
         adjoint_part = spread(receiver_flat, residual_traces[:, step, :], first_plane, planes, rows, cols)
         terms = jnp.stack([forward_part, adjoint_part])
@@ -144,6 +149,7 @@
         fresh = base + courant * halo_laplace(below, above, planes, zaxis)
         if step + 1 < STEPS:
             below, above = exchange(fresh, zaxis)
+            gate = fresh
         part = fresh[0, 0] * fresh[1, 0]
         correlation = part if correlation is None else correlation + part
         earlier, current = (current, fresh)

time: 171 us -> 167 us (0.977)
  waiting for transfers between devices: 48.2 us -> 23.7 us
  other arithmetic: 65.3 us -> 76 us
  local copies, waits for them, and re-layouts: 13.1 us -> 19.7 us
  matrix products: 14.1 us -> 16.4 us
    ppermute x2, waiting for transfers between devices: 39.5 us -> 15 us  [exchange(): below = lax.ppermute(last, 'depth', up)]
    unnamed x14, other arithmetic: 5.16 us -> 13.1 us
    slice x9, local copies, waits for them, and re-layouts: 2.42 us -> 7.21 us  [shifted(): kept = lax.slice_in_dim(values, offset, size, axis=axis)]
    another operation x4, local copies, waits for them, and re-layouts: 6.3 us -> 8.72 us  [on_device(): terms = jnp.stack([forward_part, adjoint_part])]
    unnamed x33 -> x39, local copies, waits for them, and re-layouts: 3.7 us -> 1.75 us
  transfers between devices with their start and end apart: 6 -> 6, of which waited for: 3 -> 4; matrix products, arithmetic and copies ran while one was open for 41% -> 48% of each run, Pallas kernels for 0% -> 0%
where the time goes in v3:
time: 167 us
  other arithmetic  76 us (46%)
  waiting for transfers between devices  23.7 us (14%)
  local copies, waits for them, and re-layouts  19.7 us (12%)
  matrix products  16.4 us (10%)
  starting transfers between devices  15.6 us (9%)
  blocking collectives  14.1 us (8%)
    scatter-add x4, other arithmetic, spread(): jnp.zeros((values.shape[0], limit), jnp.float32).at[:, local]  53.6 us
    ppermute x2, waiting for transfers between devices, exchange(): below = lax.ppermute(last, 'depth', up)  15 us
    all_to_all x1, blocking collectives, on_device(): lax.all_to_all(reduced, 'depth', split_axis=1, concat_axis=0, tiled=True)  14.1 us
    unnamed x14, other arithmetic  13.1 us
    ppermute x2, starting transfers between devices, exchange(): below = lax.ppermute(last, 'depth', up)  11.2 us
    another operation x4, local copies, waits for them, and re-layouts, on_device(): terms = jnp.stack([forward_part, adjoint_part])  8.72 us
    ppermute x2, waiting for transfers between devices, reduce_shots(): blocks = keep + lax.ppermute(send, 'shots', pairs)  8.72 us
    dot_general x2, matrix products, local_laplace(): along_y = jnp.einsum('...xy,yk->...xk', core, band(cols), precision=high)  8.22 us
  transfers between devices with their start and end apart: 6, of which 4 were waited for; matrix products, arithmetic and copies ran while one was open for 48% of the time, Pallas kernels for 0%

profile of v3, /device:TPU:0, one launch (start us, length us, event | category | flops | bytes accessed | tf_op | source)
XLA Modules:
  0.0 166.7 jit_solution(2140955145207473487)
XLA Ops:
  0.7 3.1 %fusion.32 = (f32[2,1,4,128,256]{4,3,2,0,1:T(8,128)}, f32[2,1,4,128,256]{4,3,2,0,1:T(8,128)}) fusion(f32[1,1,8,128,256]{4,3,2,0,1:T(8,128)} %bitcast.113, f32[1,1,8,128,256]{4,3,2,0,1:T(8,128)} %bitcast.106), kind=kLoop, calls=%fused_computation.57 | loop fusion | flops 524288 | bytes 4194304 | tf_op jit(solution)/shard_map/stack | solution.py:134
  3.8 5.8 %collective-permute-start = (f32[2,1,4,128,256]{4,3,2,0,1:T(8,128)}, f32[2,1,4,128,256]{4,3,2,0,1:T(8,128)}, u32[]{:S(2)}, u32[]{:S(2)}) collective-permute-start(f32[2,1,4,128,256]{4,3,2,0,1:T(8,128)} %get-tuple-element.44), channel_id=1, source_target_pairs={{0,1},{1,2},{2,3},{3,4},{4,5},{5,6},{6,7},{8,9},{9,10},{10,11},{11... | collective-permute-start | bytes 3145736 | tf_op jit(solution)/shard_map/ppermute | solution.py:80
  9.6 1.3 collective-permute-start.1
  11.0 22.2 %scatter_custom_fusion.1 = f32[262144]{0:T(1024)S(1)} fusion(s32[4096]{0:T(1024)S(1)} %get-tuple-element.22, f32[4096]{0:T(1024)S(1)} %bitcast.128, f32[]{:T(128)} %constant.56.clone.1), kind=kCustom, calls=%fused_computation.71 | custom fusion | flops 4096 | bytes 1048580 | tf_op jit(solution)/shard_map/scatter-add | solution.py:90
  33.2 1.3 stack_reshape.13
  34.5 4.2 %scatter_custom_fusion = f32[262144]{0:T(1024)} fusion(s32[512]{0:T(512)S(1)} %get-tuple-element.20, f32[512]{0:T(512)S(1)} %bitcast.130, f32[]{:T(128)} %constant.56.clone.1), kind=kCustom, calls=%fused_computation.73 | custom fusion | flops 512 | bytes 1048580 | tf_op jit(solution)/shard_map/scatter-add | solution.py:90
  38.7 2.5 %stack_reshape.12 = f32[1,1,8,128,256]{4,3,2,0,1:T(8,128)} reshape(f32[262144]{0:T(1024)} %scatter_custom_fusion) | data formatting | bytes 2097152 | tf_op jit(solution)/shard_map/stack;reshape | solution.py:147
  42.2 1.9 %fusion.21 = f32[2,8,128,256]{3,2,1,0:T(8,128)S(1)} fusion(f32[1,1,8,128,256]{4,3,2,0,1:T(8,128)S(1)} %bitcast.110, f32[1,1,8,128,256]{4,3,2,0,1:T(8,128)S(1)} %bitcast.117), kind=kOutput, calls=%fused_computation.46 | convolution fusion | flops 1611792384 | bytes 4194304 | tf_op jit(solution)/shard_map/...xy,yk->...xk/dot_general | solution.py:39
  44.2 9.6 %collective-permute-done = f32[2,1,4,128,256]{4,3,2,0,1:T(8,128)} collective-permute-done((f32[2,1,4,128,256]{4,3,2,0,1:T(8,128)}, f32[2,1,4,128,256]{4,3,2,0,1:T(8,128)}, u32[]{:S(2)}, u32[]{:S(2)}) %collective-permute-start) | collective-permute-done | bytes 1048608 | tf_op jit(solution)/shard_map/ppermute | solution.py:80
  53.8 1.4 fusion.50
  55.2 1.3 add_dynamic-update-slice_fusion.7
  59.8 5.0 %fusion.2 = f32[2,1,8,128,256]{4,3,2,0,1:T(8,128)S(1)} fusion(f32[1,1,8,128,256]{4,3,2,0,1:T(8,128)S(1)} %bitcast.125, f32[1,1,8,128,256]{4,3,2,0,1:T(8,128)S(1)} %bitcast.126, f32[1,1,8,128,256]{4,3,2,0,1:T(8,128)S(1)} %copy-done.8, f32[1,1,8,128,256]{4,3,2,0,1:T(8,128)S(1)} %copy-done.9, f32[2,8,128,256]{3,2,1,0:T(8,128)S(1)} %fusion.21, ...), kind=kOutput, calls=%fused_computation.24 | convolution fusion | flops 819101696 | bytes 25165824 | tf_op jit(solution)/shard_map/...xy,kx->...ky/dot_general | solution.py:40
  64.8 1.6 fusion.144
  66.3 1.8 %fusion.143 = (f32[2,1,5,128,256]{4,3,2,0,1:T(8,128)}, f32[2,1,5,128,256]{4,3,2,0,1:T(8,128)}) fusion(f32[2,1,8,128,256]{4,3,2,0,1:T(8,128)S(1)} %fusion.2), kind=kLoop, calls=%fused_computation.206 | loop fusion | bytes 5242880 | tf_op jit(solution)/shard_map/slice | solution.py:19
  68.1 3.3 %fusion.19 = f32[128,2,8,256]{3,0,2,1:T(8,128)} fusion(f32[2,1,8,128,256]{4,3,2,0,1:T(8,128)S(1)} %fusion.2), kind=kOutput, calls=%fused_computation.44 | convolution fusion | flops 805470208 | bytes 4194304 | tf_op jit(solution)/shard_map/...xy,kx->...ky/dot_general | solution.py:40
  71.4 5.4 %collective-permute-start.2 = (f32[2,1,4,128,256]{4,3,2,0,1:T(8,128)}, f32[2,1,4,128,256]{4,3,2,0,1:T(8,128)}, u32[]{:S(2)}, u32[]{:S(2)}) collective-permute-start(f32[2,1,4,128,256]{4,3,2,0,1:T(8,128)} %get-tuple-element.36), channel_id=1, source_target_pairs={{0,1},{1,2},{2,3},{3,4},{4,5},{5,6},{6,7},{8,9},{9,10},{10,11},{11... | collective-permute-start | bytes 3145736 | tf_op jit(solution)/shard_map/ppermute | solution.py:80
  76.7 1.5 collective-permute-start.3
  78.2 2.0 %fusion.142 = (f32[2,1,6,128,256]{4,3,2,0,1:T(8,128)}, f32[2,1,6,128,256]{4,3,2,0,1:T(8,128)}) fusion(f32[2,1,8,128,256]{4,3,2,0,1:T(8,128)S(1)} %fusion.2), kind=kLoop, calls=%fused_computation.205 | loop fusion | bytes 6291456 | tf_op jit(solution)/shard_map/slice | solution.py:19
  80.3 2.3 %fusion.141 = (f32[2,1,7,128,256]{4,3,2,0,1:T(8,128)}, f32[2,1,7,128,256]{4,3,2,0,1:T(8,128)}) fusion(f32[2,1,8,128,256]{4,3,2,0,1:T(8,128)S(1)} %fusion.2), kind=kLoop, calls=%fused_computation.204 | loop fusion | bytes 7340032 | tf_op jit(solution)/shard_map/slice | solution.py:19
  82.5 4.2 %scatter_custom_fusion.2 = f32[262144]{0:T(1024)} fusion(s32[512]{0:T(512)S(1)} %compare_select_fusion.2, f32[512]{0:T(512)S(1)} %bitcast.131, f32[]{:T(128)} %constant.56.clone.1), kind=kCustom, calls=%fused_computation.69 | custom fusion | flops 512 | bytes 1048580 | tf_op jit(solution)/shard_map/scatter-add | solution.py:90
  86.8 2.5 %stack_reshape.14 = f32[1,1,8,128,256]{4,3,2,0,1:T(8,128)} reshape(f32[262144]{0:T(1024)} %scatter_custom_fusion.2) | data formatting | bytes 2097152 | tf_op jit(solution)/shard_map/stack;reshape | solution.py:147
  89.3 22.9 %scatter_custom_fusion.3 = f32[262144]{0:T(1024)} fusion(s32[4096]{0:T(1024)S(1)} %compare_select_fusion, f32[4096]{0:T(1024)S(1)} %bitcast.129, f32[]{:T(128)} %constant.56.clone.1), kind=kCustom, calls=%fused_computation.67 | custom fusion | flops 4096 | bytes 1048580 | tf_op jit(solution)/shard_map/scatter-add | solution.py:90
  112.2 2.5 %stack_reshape.15 = f32[1,1,8,128,256]{4,3,2,0,1:T(8,128)} reshape(f32[262144]{0:T(1024)} %scatter_custom_fusion.3) | data formatting | bytes 2097152 | tf_op jit(solution)/shard_map/stack;reshape | solution.py:147
  114.7 5.4 %collective-permute-done.2 = f32[2,1,4,128,256]{4,3,2,0,1:T(8,128)} collective-permute-done((f32[2,1,4,128,256]{4,3,2,0,1:T(8,128)}, f32[2,1,4,128,256]{4,3,2,0,1:T(8,128)}, u32[]{:S(2)}, u32[]{:S(2)}) %collective-permute-start.2) | collective-permute-done | bytes 1048608 | tf_op jit(solution)/shard_map/ppermute | solution.py:80
  120.1 1.4 fusion.46
  128.3 1.3 fusion.44
  129.6 6.3 %fusion.3 = f32[2,1,8,128,256]{4,3,2,0,1:T(8,128)S(1)} fusion(f32[1,1,8,128,256]{4,3,2,0,1:T(8,128)} %stack_reshape.15, f32[1,1,8,128,256]{4,3,2,0,1:T(8,128)} %stack_reshape.14, f32[128,2,8,256]{3,0,2,1:T(8,128)S(1)} %copy-done.4, f32[2,1,8,128,256]{4,3,2,0,1:T(8,128)S(1)} %fusion.44, f32[2,1,4,128,256]{4,3,2,0,1:T(8,128)} %get-tuple-element.35, ...), kind=kOutput, calls=%fused_computation.26 | convolution fusion | flops 1623851008 | bytes 25165824 | tf_op jit(solution)/shard_map/...xy,yk->...xk/dot_general | solution.py:39
  135.9 2.3 %add_bitcast_fusion = (f32[8,128,256]{2,1,0:T(8,128)S(1)}, f32[1,8,128,256]{3,2,1,0:T(8,128)}, f32[1,8,128,256]{3,2,1,0:T(8,128)}, f32[1,8,128,256]{3,2,1,0:T(8,128)}, f32[1,8,128,256]{3,2,1,0:T(8,128)}) fusion(f32[2,1,8,128,256]{4,3,2,0,1:T(8,128)S(1)} %fusion.3, f32[2,1,8,128,256]{4,3,2,0,1:T(8,128)S(1)} %fusion.2), kind=kLoop, calls=%fused_computation.60 | loop fusion | flops 786432 | bytes 9437184 | tf_op jit(solution)/shard_map/add | solution.py:154
  140.9 1.9 %collective-permute-done.4 = f32[8,2,32,256]{3,0,2,1:T(8,128)S(1)} collective-permute-done((f32[8,2,32,256]{3,0,2,1:T(8,128)S(1)}, f32[8,2,32,256]{3,0,2,1:T(8,128)S(1)}, u32[]{:S(2)}, u32[]{:S(2)}) %collective-permute-start.4) | collective-permute-done | bytes 524320 | tf_op jit(solution)/shard_map/ppermute | solution.py:108
  143.1 1.6 collective-permute-start.5
  144.6 6.9 %collective-permute-done.5 = f32[8,1,32,256]{3,0,2,1:T(8,128)S(1)} collective-permute-done((f32[8,1,32,256]{3,0,2,1:T(8,128)S(1)}, f32[8,1,32,256]{3,0,2,1:T(8,128)S(1)}, u32[]{:S(2)}, u32[]{:S(2)}) %collective-permute-start.5) | collective-permute-done | bytes 262176 | tf_op jit(solution)/shard_map/ppermute | solution.py:108
  151.5 14.1 %all_to_all.18 = f32[8,32,256]{2,0,1:T(8,128)S(1)} all-to-all(f32[8,32,256]{2,0,1:T(8,128)S(1)} %add_bitcast_fusion.1), channel_id=1, replica_groups=mesh['shots'=4,'depth'=8] {'depth'}, dimensions={1} | all-to-all | bytes 524288 | tf_op jit(solution)/shard_map/all_to_all | solution.py:158
  (82 shorter events, 15.2 us)
Async XLA Ops:
  0.6 10.3 %copy-start.13 = (s32[4096]{0:T(1024)S(1)}, s32[4096]{0:T(1024)}, u32[]{:S(2)}) copy-start(s32[4096]{0:T(1024)} %param.22) | copy-start | bytes 49156
  0.6 10.3 %copy-start.14 = (s32[4096]{0:T(1024)S(1)}, s32[4096]{0:T(1024)}, u32[]{:S(2)}) copy-start(s32[4096]{0:T(1024)} %param.21) | copy-start | bytes 49156
  0.7 10.3 %copy-start.17 = (s32[512]{0:T(512)S(1)}, s32[512]{0:T(512)}, u32[]{:S(2)}) copy-start(s32[512]{0:T(512)} %param.20) | copy-start | bytes 6148
  0.7 10.3 %copy-start.18 = (s32[512]{0:T(512)S(1)}, s32[512]{0:T(512)}, u32[]{:S(2)}) copy-start(s32[512]{0:T(512)} %param.19) | copy-start | bytes 6148
  0.7 10.3 %copy-start.15 = (s32[1,512]{1,0:T(1,128)S(1)}, s32[1,512]{1,0:T(1,128)}, u32[]{:S(2)}) copy-start(s32[1,512]{1,0:T(1,128)} %param.18) | copy-start | bytes 6148
  0.7 10.3 %copy-start.16 = (f32[2,512]{1,0:T(2,128)S(1)}, f32[2,512]{1,0:T(2,128)}, u32[]{:S(2)}) copy-start(f32[2,512]{1,0:T(2,128)} %param.17) | copy-start | bytes 12292
  0.7 10.3 %slice-start = ((f32[1,2,4096]{2,1,0:T(2,128)}), f32[1,1,4096]{2,1,0:T(1,128)S(1)}, s32[]{:S(2)}) async-start(f32[1,2,4096]{2,1,0:T(2,128)} %param.23), calls=%async_computation.1 | async-start | bytes 32768 | tf_op jit(solution)/shard_map/slice | solution.py:146
  3.8 50.1 %collective-permute-start = (f32[2,1,4,128,256]{4,3,2,0,1:T(8,128)}, f32[2,1,4,128,256]{4,3,2,0,1:T(8,128)}, u32[]{:S(2)}, u32[]{:S(2)}) collective-permute-start(f32[2,1,4,128,256]{4,3,2,0,1:T(8,128)} %get-tuple-element.44), channel_id=1, source_target_pairs={{0,1},{1,2},{2,3},{3,4},{4,5},{5,6},{6,7},{8,9},{9,10},{10,11},{11... | collective-permute-start | bytes 3145736 | tf_op jit(solution)/shard_map/ppermute | solution.py:80
  9.6 49.1 %collective-permute-start.1 = (f32[2,1,4,128,256]{4,3,2,0,1:T(8,128)}, f32[2,1,4,128,256]{4,3,2,0,1:T(8,128)S(1)}, u32[]{:S(2)}, u32[]{:S(2)}) collective-permute-start(f32[2,1,4,128,256]{4,3,2,0,1:T(8,128)} %get-tuple-element.43), channel_id=1, source_target_pairs={{1,0},{2,1},{3,2},{4,3},{5,4},{6,5},{7,6},{9,8},{10,9},{11,10},{12... | collective-permute-start | bytes 3145736 | tf_op jit(solution)/shard_map/ppermute | solution.py:81
  34.5 6.7 %copy-start = (f32[1,8,128,256]{3,2,1,0:T(8,128)S(1)}, f32[1,8,128,256]{3,2,1,0:T(8,128)}, u32[]{:S(2)}) copy-start(f32[1,8,128,256]{3,2,1,0:T(8,128)} %param.15) | copy-start | bytes 3145732
  34.5 6.7 %copy-start.1 = (f32[1,8,128,256]{3,2,1,0:T(8,128)S(1)}, f32[1,8,128,256]{3,2,1,0:T(8,128)}, u32[]{:S(2)}) copy-start(f32[1,8,128,256]{3,2,1,0:T(8,128)} %param.13) | copy-start | bytes 3145732
  53.8 5.2 %copy-start.11 = (f32[1,8,128,256]{3,2,1,0:T(8,128)S(1)}, f32[1,8,128,256]{3,2,1,0:T(8,128)}, u32[]{:S(2)}) copy-start(f32[1,8,128,256]{3,2,1,0:T(8,128)} %param.12) | copy-start | bytes 3145732
  55.2 3.8 %copy-start.10 = (f32[1,8,128,256]{3,2,1,0:T(8,128)S(1)}, f32[1,8,128,256]{3,2,1,0:T(8,128)}, u32[]{:S(2)}) copy-start(f32[1,8,128,256]{3,2,1,0:T(8,128)} %param.14) | copy-start | bytes 3145732
  57.5 1.5 copy-start.2
  57.6 1.6 copy-start.7
  57.6 1.9 %copy-start.8 = (f32[1,1,8,128,256]{4,3,2,0,1:T(8,128)S(1)}, f32[1,1,8,128,256]{4,3,2,0,1:T(8,128)}, u32[]{:S(2)}) copy-start(f32[1,1,8,128,256]{4,3,2,0,1:T(8,128)} %stack_reshape.13) | copy-start | bytes 3145732
  57.6 2.2 %copy-start.9 = (f32[1,1,8,128,256]{4,3,2,0,1:T(8,128)S(1)}, f32[1,1,8,128,256]{4,3,2,0,1:T(8,128)}, u32[]{:S(2)}) copy-start(f32[1,1,8,128,256]{4,3,2,0,1:T(8,128)} %stack_reshape.12) | copy-start | bytes 3145732
  71.4 48.7 %collective-permute-start.2 = (f32[2,1,4,128,256]{4,3,2,0,1:T(8,128)}, f32[2,1,4,128,256]{4,3,2,0,1:T(8,128)}, u32[]{:S(2)}, u32[]{:S(2)}) collective-permute-start(f32[2,1,4,128,256]{4,3,2,0,1:T(8,128)} %get-tuple-element.36), channel_id=1, source_target_pairs={{0,1},{1,2},{2,3},{3,4},{4,5},{5,6},{6,7},{8,9},{9,10},{10,11},{11... | collective-permute-start | bytes 3145736 | tf_op jit(solution)/shard_map/ppermute | solution.py:80
  76.7 48.3 %collective-permute-start.3 = (f32[2,1,4,128,256]{4,3,2,0,1:T(8,128)}, f32[2,1,4,128,256]{4,3,2,0,1:T(8,128)}, u32[]{:S(2)}, u32[]{:S(2)}) collective-permute-start(f32[2,1,4,128,256]{4,3,2,0,1:T(8,128)} %get-tuple-element.35), channel_id=1, source_target_pairs={{1,0},{2,1},{3,2},{4,3},{5,4},{6,5},{7,6},{9,8},{10,9},{11,10},{12... | collective-permute-start | bytes 3145736 | tf_op jit(solution)/shard_map/ppermute | solution.py:81
  82.5 6.7 %copy-start.12 = (f32[1,2,4096]{2,1,0:T(2,128)S(1)}, f32[1,2,4096]{2,1,0:T(2,128)}, u32[]{:S(2)}) copy-start(f32[1,2,4096]{2,1,0:T(2,128)} %param.23) | copy-start | bytes 98308
  120.1 9.5 %copy-start.6 = (f32[2,1,7,128,256]{4,3,2,0,1:T(8,128)S(1)}, f32[2,1,7,128,256]{4,3,2,0,1:T(8,128)}, u32[]{:S(2)}) copy-start(f32[2,1,7,128,256]{4,3,2,0,1:T(8,128)} %get-tuple-element.30) | copy-start | bytes 5505028
  122.7 6.9 %copy-start.5 = (f32[2,1,7,128,256]{4,3,2,0,1:T(8,128)S(1)}, f32[2,1,7,128,256]{4,3,2,0,1:T(8,128)}, u32[]{:S(2)}) copy-start(f32[2,1,7,128,256]{4,3,2,0,1:T(8,128)} %get-tuple-element.29) | copy-start | bytes 5505028
  123.9 5.7 %copy-start.3 = (f32[1,8,128,256]{3,2,1,0:T(8,128)S(1)}, f32[1,8,128,256]{3,2,1,0:T(8,128)}, u32[]{:S(2)}) copy-start(f32[1,8,128,256]{3,2,1,0:T(8,128)} %param.13) | copy-start | bytes 3145732
  123.9 5.7 %copy-start.4 = (f32[128,2,8,256]{3,0,2,1:T(8,128)S(1)}, f32[128,2,8,256]{3,0,2,1:T(8,128)}, u32[]{:S(2)}) copy-start(f32[128,2,8,256]{3,0,2,1:T(8,128)} %fusion.19) | copy-start | bytes 6291460
  140.7 2.0 %collective-permute-start.4 = (f32[8,2,32,256]{3,0,2,1:T(8,128)S(1)}, f32[8,2,32,256]{3,0,2,1:T(8,128)S(1)}, u32[]{:S(2)}, u32[]{:S(2)}) collective-permute-start(f32[8,2,32,256]{3,0,2,1:T(8,128)S(1)} %bitcast.127), channel_id=1, source_target_pairs={{0,8},{8,0},{16,24},{24,16},{1,9},{9,1},{17,25},{25,17},{2,10},{10... | collective-permute-start | bytes 1572872 | tf_op jit(solution)/shard_map/ppermute | solution.py:108
  143.1 8.4 %collective-permute-start.5 = (f32[8,1,32,256]{3,0,2,1:T(8,128)S(1)}, f32[8,1,32,256]{3,0,2,1:T(8,128)S(1)}, u32[]{:S(2)}, u32[]{:S(2)}) collective-permute-start(f32[8,1,32,256]{3,0,2,1:T(8,128)S(1)} %constant_dynamic-slice_fusion), channel_id=1, source_target_pairs={{0,16},{8,24},{16,0},{24,8},{1,17},{9,25},{17,1},{25,9},{2,18},{10... | collective-permute-start | bytes 786440 | tf_op jit(solution)/shard_map/ppermute | solution.py:108

commit v4 on v3

--- a/solution.py
+++ b/solution.py
@@ -33,34 +33,24 @@
     return matrix
 
 
-def local_laplace(core, zaxis):
+def lateral_laplace(core, zaxis):
     rows, cols = core.shape[zaxis + 1], core.shape[zaxis + 2]
     high = lax.Precision.HIGHEST
     along_y = jnp.einsum("...xy,yk->...xk", core, band(cols), precision=high)
     along_x = jnp.einsum("...xy,kx->...ky", core, band(rows), precision=high)
-    total = 3.0 * COEFFS[0] * core + (along_x + along_y)
-    for k in range(1, 5):
-        near = shifted(core, zaxis, k) + shifted(core, zaxis, -k)
-        total = total + COEFFS[k] * near
-    return total
+    return 3.0 * COEFFS[0] * core + (along_x + along_y)
 
 
-def halo_laplace(below, above, planes, zaxis):
-    parts = []
-    for p in range(planes):
-        term = None
-        for k in range(1, 5):
-            for q in (p - k, p + k):
-                if q < 0:
-                    piece = lax.index_in_dim(below, HALO + q, axis=zaxis, keepdims=True)
-                elif q >= planes:
-                    piece = lax.index_in_dim(above, q - planes, axis=zaxis, keepdims=True)
-                else:
-                    continue
-                piece = COEFFS[k] * piece
-                term = piece if term is None else term + piece
-        parts.append(term)
-    return jnp.concatenate(parts, axis=zaxis)
+def depth_laplace(below, core, above, zaxis):
+    planes = core.shape[zaxis]
+    extended = jnp.concatenate([below, core, above], axis=zaxis)
+    total = None
+    for k in range(1, 5):
+        near = lax.slice_in_dim(extended, HALO + k, HALO + k + planes, axis=zaxis) + lax.slice_in_dim(
+            extended, HALO - k, HALO - k + planes, axis=zaxis
+        )
+        total = COEFFS[k] * near if total is None else total + COEFFS[k] * near
+    return total
 
 
 def smooth(values, axis):
@@ -145,8 +135,13 @@
         forward_part = spread(source_flat, signs * wavelet[step][None, :], first_plane, planes, rows, cols)
         adjoint_part = spread(receiver_flat, residual_traces[:, step, :], first_plane, planes, rows, cols)
         terms = jnp.stack([forward_part, adjoint_part])
-        base = 2.0 * current - earlier + courant * local_laplace(current, zaxis) + terms
-        fresh = base + courant * halo_laplace(below, above, planes, zaxis)
+        lateral_part = lateral_laplace(current, zaxis)
+        fresh = (
+            2.0 * current
+            - earlier
+            + courant * (lateral_part + depth_laplace(below, current, above, zaxis))
+            + terms
+        )
         if step + 1 < STEPS:
             below, above = exchange(fresh, zaxis)
             gate = fresh

time: 167 us -> 149 us (0.89)
  other arithmetic: 76 us -> 62.1 us
  local copies, waits for them, and re-layouts: 19.7 us -> 11.6 us
  waiting for transfers between devices: 23.7 us -> 30.5 us
  matrix products: 16.4 us -> 12.6 us
    unnamed x14 -> x0, other arithmetic: 13.1 us -> none
    ppermute x2, waiting for transfers between devices: 15 us -> 21.7 us  [exchange(): below = lax.ppermute(last, 'depth', up)]
    slice x9 -> x6, local copies, waits for them, and re-layouts: 7.21 us -> 1.14 us  [shifted(): kept = lax.slice_in_dim(values, offset, size, axis=axis)]
    dot_general x4, matrix products: 16.4 us -> 12.6 us  [the longest x2 7.41 us: lateral_laplace(): along_y = jnp.einsum('...xy,yk->...xk', core, band(cols), precision=high)]
    another operation x4 -> x1, other arithmetic: 4.05 us -> 3.03 us  [on_device(): current = jnp.stack([forward_now, adjoint_now])]
  transfers between devices with their start and end apart: 6 -> 6, of which waited for: 4 -> 4; matrix products, arithmetic and copies ran while one was open for 48% -> 43% of each run, Pallas kernels for 0% -> 0%
where the time goes in v4:
time: 149 us; the launch traced here: 148 us
  other arithmetic  62.1 us (42%)
  waiting for transfers between devices  30.5 us (20%)
  starting transfers between devices  16.2 us (11%)
  blocking collectives  14.1 us (9%)
  matrix products  12.6 us (8%)
  local copies, waits for them, and re-layouts  11.6 us (8%)
    scatter-add x4, other arithmetic, spread(): jnp.zeros((values.shape[0], limit), jnp.float32).at[:, local]  52.8 us
    ppermute x2, waiting for transfers between devices, exchange(): below = lax.ppermute(last, 'depth', up)  21.7 us
    all_to_all x1, blocking collectives, on_device(): lax.all_to_all(reduced, 'depth', split_axis=1, concat_axis=0, tiled=True)  14.1 us
    ppermute x2, starting transfers between devices, exchange(): below = lax.ppermute(last, 'depth', up)  11.9 us
    ppermute x2, waiting for transfers between devices, reduce_shots(): blocks = keep + lax.ppermute(send, 'shots', pairs)  8.72 us
    another operation x4, local copies, waits for them, and re-layouts, on_device(): terms = jnp.stack([forward_part, adjoint_part])  7.52 us
    dot_general x2, matrix products, lateral_laplace(): along_y = jnp.einsum('...xy,yk->...xk', core, band(cols), precision=high)  7.41 us
    dot_general x2, matrix products, lateral_laplace(): along_x = jnp.einsum('...xy,kx->...ky', core, band(rows), precision=high)  5.22 us
  transfers between devices with their start and end apart: 6, of which 4 were waited for; matrix products, arithmetic and copies ran while one was open for 43% of the time, Pallas kernels for 0%

profile of v4, /device:TPU:0, one launch (start us, length us, event | category | flops | bytes accessed | tf_op | source)
XLA Modules:
  0.0 148.2 jit_solution(1000114654574230278)
XLA Ops:
  0.7 3.0 %fusion.44 = (f32[2,1,4,128,256]{4,3,2,0,1:T(8,128)}, f32[2,1,4,128,256]{4,3,2,0,1:T(8,128)}) fusion(f32[1,1,8,128,256]{4,3,2,0,1:T(8,128)} %bitcast.84, f32[1,1,8,128,256]{4,3,2,0,1:T(8,128)} %bitcast.89), kind=kLoop, calls=%fused_computation.74 | loop fusion | flops 524288 | bytes 4194304 | tf_op jit(solution)/shard_map/stack | solution.py:124
  3.7 1.4 collective-permute-start
  5.1 6.5 %collective-permute-start.1 = (f32[2,1,4,128,256]{4,3,2,0,1:T(8,128)}, f32[2,1,4,128,256]{4,3,2,0,1:T(8,128)}, u32[]{:S(2)}, u32[]{:S(2)}) collective-permute-start(f32[2,1,4,128,256]{4,3,2,0,1:T(8,128)} %get-tuple-element.34), channel_id=1, source_target_pairs={{0,1},{1,2},{2,3},{3,4},{4,5},{5,6},{6,7},{8,9},{9,10},{10,11},{11... | collective-permute-start | bytes 3145736 | tf_op jit(solution)/shard_map/ppermute | solution.py:70
  11.6 22.2 %scatter_custom_fusion.1 = f32[262144]{0:T(1024)S(1)} fusion(s32[4096]{0:T(1024)S(1)} %get-tuple-element.22, f32[4096]{0:T(1024)S(1)} %bitcast.100, f32[]{:T(128)} %constant.104.clone.1), kind=kCustom, calls=%fused_computation.89 | custom fusion | flops 4096 | bytes 1048580 | tf_op jit(solution)/shard_map/scatter-add | solution.py:80
  33.8 1.3 stack_reshape.13
  35.1 3.5 %scatter_custom_fusion = f32[262144]{0:T(1024)S(1)} fusion(s32[512]{0:T(512)S(1)} %get-tuple-element.20, f32[512]{0:T(512)S(1)} %bitcast.103, f32[]{:T(128)} %constant.104.clone.1), kind=kCustom, calls=%fused_computation.91 | custom fusion | flops 512 | bytes 1048580 | tf_op jit(solution)/shard_map/scatter-add | solution.py:80
  38.7 1.3 stack_reshape.12
  39.9 1.9 %fusion.38 = f32[2,8,128,256]{3,2,1,0:T(8,128)S(1)} fusion(f32[1,1,8,128,256]{4,3,2,0,1:T(8,128)S(1)} %bitcast.90, f32[1,1,8,128,256]{4,3,2,0,1:T(8,128)S(1)} %bitcast.85), kind=kOutput, calls=%fused_computation.70 | convolution fusion | flops 1611792384 | bytes 4194304 | tf_op jit(solution)/shard_map/...xy,yk->...xk/dot_general | solution.py:39
  42.0 12.8 %collective-permute-done.1 = f32[2,1,4,128,256]{4,3,2,0,1:T(8,128)} collective-permute-done((f32[2,1,4,128,256]{4,3,2,0,1:T(8,128)}, f32[2,1,4,128,256]{4,3,2,0,1:T(8,128)}, u32[]{:S(2)}, u32[]{:S(2)}) %collective-permute-start.1) | collective-permute-done | bytes 1048608 | tf_op jit(solution)/shard_map/ppermute | solution.py:70
  54.8 2.3 %pad_maximum_fusion = (f32[2,1,12,128,256]{4,3,2,0,1:T(8,128)S(1)}, f32[2,1,12,128,256]{4,3,2,0,1:T(8,128)S(1)}) fusion(f32[2,1,4,128,256]{4,3,2,0,1:T(8,128)} %collective-permute-done, f32[1,1,8,128,256]{4,3,2,0,1:T(8,128)S(1)} %bitcast.91, f32[1,1,8,128,256]{4,3,2,0,1:T(8,128)S(1)} %bitcast.86, f32[2,1,4,128,256]{4,3,2,0,1:T(8,128)} %collective-permute-done.1), kind=kLoop, calls=%fused_computation.16 | loop fusion | flops 3145728 | bytes 10485760 | tf_op jit(solution)/shard_map/concatenate | solution.py:46
  57.1 3.3 %fusion.26 = f32[2,1,8,128,256]{4,3,2,0,1:T(8,128)S(1)} fusion(f32[2,1,12,128,256]{4,3,2,0,1:T(8,128)S(1)} %get-tuple-element.32, f32[2,1,12,128,256]{4,3,2,0,1:T(8,128)S(1)} %get-tuple-element.31, f32[1,1,8,128,256]{4,3,2,0,1:T(8,128)S(1)} %bitcast.104, f32[1,1,8,128,256]{4,3,2,0,1:T(8,128)S(1)} %bitcast.105, f32[1,1,8,128,256]{4,3,2,0,1:T(8,128)S(1)} %copy-done.4, ...), kind=kOutput, calls=%fused_computation.52 | convolution fusion | flops 818053120 | bytes 30408704 | tf_op jit(solution)/shard_map/...xy,kx->...ky/dot_general | solution.py:40
  60.5 1.5 %fusion.144 = (f32[2,1,4,128,256]{4,3,2,0,1:T(8,128)}, f32[2,1,4,128,256]{4,3,2,0,1:T(8,128)}) fusion(f32[2,1,8,128,256]{4,3,2,0,1:T(8,128)S(1)} %fusion.26), kind=kLoop, calls=%fused_computation.198 | loop fusion | bytes 4194304 | tf_op jit(solution)/shard_map/slice | solution.py:69
  62.0 5.4 %collective-permute-start.3 = (f32[2,1,4,128,256]{4,3,2,0,1:T(8,128)}, f32[2,1,4,128,256]{4,3,2,0,1:T(8,128)}, u32[]{:S(2)}, u32[]{:S(2)}) collective-permute-start(f32[2,1,4,128,256]{4,3,2,0,1:T(8,128)} %get-tuple-element.30), channel_id=1, source_target_pairs={{0,1},{1,2},{2,3},{3,4},{4,5},{5,6},{6,7},{8,9},{9,10},{10,11},{11... | collective-permute-start | bytes 3145736 | tf_op jit(solution)/shard_map/ppermute | solution.py:70
  67.4 1.3 collective-permute-start.2
  68.8 22.9 %scatter_custom_fusion.3 = f32[262144]{0:T(1024)} fusion(s32[4096]{0:T(1024)S(1)} %compare_select_fusion, f32[4096]{0:T(1024)S(1)} %bitcast.101, f32[]{:T(128)} %constant.104.clone.1), kind=kCustom, calls=%fused_computation.85 | custom fusion | flops 4096 | bytes 1048580 | tf_op jit(solution)/shard_map/scatter-add | solution.py:80
  91.7 2.5 %stack_reshape.15 = f32[1,1,8,128,256]{4,3,2,0,1:T(8,128)} reshape(f32[262144]{0:T(1024)} %scatter_custom_fusion.3) | data formatting | bytes 2097152 | tf_op jit(solution)/shard_map/stack;reshape | solution.py:137
  94.2 4.3 %scatter_custom_fusion.2 = f32[262144]{0:T(1024)} fusion(s32[512]{0:T(512)S(1)} %compare_select_fusion.2, f32[512]{0:T(512)S(1)} %bitcast.102, f32[]{:T(128)} %constant.104.clone.1), kind=kCustom, calls=%fused_computation.87 | custom fusion | flops 512 | bytes 1048580 | tf_op jit(solution)/shard_map/scatter-add | solution.py:80
  98.4 2.5 %stack_reshape.14 = f32[1,1,8,128,256]{4,3,2,0,1:T(8,128)} reshape(f32[262144]{0:T(1024)} %scatter_custom_fusion.2) | data formatting | bytes 2097152 | tf_op jit(solution)/shard_map/stack;reshape | solution.py:137
  101.0 1.9 %fusion.36 = f32[128,2,8,256]{3,0,2,1:T(8,128)S(1)} fusion(f32[2,1,8,128,256]{4,3,2,0,1:T(8,128)S(1)} %fusion.26), kind=kOutput, calls=%fused_computation.68 | convolution fusion | flops 805470208 | bytes 4194304 | tf_op jit(solution)/shard_map/...xy,kx->...ky/dot_general | solution.py:40
  102.9 8.9 %collective-permute-done.3 = f32[2,1,4,128,256]{4,3,2,0,1:T(8,128)} collective-permute-done((f32[2,1,4,128,256]{4,3,2,0,1:T(8,128)}, f32[2,1,4,128,256]{4,3,2,0,1:T(8,128)}, u32[]{:S(2)}, u32[]{:S(2)}) %collective-permute-start.3) | collective-permute-done | bytes 1048608 | tf_op jit(solution)/shard_map/ppermute | solution.py:70
  111.8 5.5 %fusion.8 = f32[2,1,8,128,256]{4,3,2,0,1:T(8,128)S(1)} fusion(f32[2,1,8,128,256]{4,3,2,0,1:T(8,128)S(1)} %fusion.26, f32[2,1,4,128,256]{4,3,2,0,1:T(8,128)} %collective-permute-done.3, f32[2,1,4,128,256]{4,3,2,0,1:T(8,128)} %collective-permute-done.2, f32[1,1,8,128,256]{4,3,2,0,1:T(8,128)S(1)} %copy-done.5, f32[1,1,8,128,256]{4,3,2,0,1:T(8,128)S(1)} %copy-done.7, ...), kind=kOutput, calls=%fused_computation.31 | convolution fusion | flops 1626996736 | bytes 15728640 | tf_op jit(solution)/shard_map/...xy,yk->...xk/dot_general | solution.py:39
  117.3 2.4 %add_bitcast_fusion = (f32[8,128,256]{2,1,0:T(8,128)S(1)}, f32[1,8,128,256]{3,2,1,0:T(8,128)}, f32[1,8,128,256]{3,2,1,0:T(8,128)}, f32[1,8,128,256]{3,2,1,0:T(8,128)}, f32[1,8,128,256]{3,2,1,0:T(8,128)}) fusion(f32[2,1,8,128,256]{4,3,2,0,1:T(8,128)S(1)} %fusion.8, f32[2,1,8,128,256]{4,3,2,0,1:T(8,128)S(1)} %fusion.26), kind=kLoop, calls=%fused_computation.78 | loop fusion | flops 786432 | bytes 9437184 | tf_op jit(solution)/shard_map/add | solution.py:149
  120.0 0.4 multiply_add_fusion.1
  120.4 0.4 fusion.146
  120.8 0.4 fusion.145
  121.2 0.6 multiply_add_fusion
  122.3 1.9 %collective-permute-done.4 = f32[8,2,32,256]{3,0,2,1:T(8,128)S(1)} collective-permute-done((f32[8,2,32,256]{3,0,2,1:T(8,128)S(1)}, f32[8,2,32,256]{3,0,2,1:T(8,128)S(1)}, u32[]{:S(2)}, u32[]{:S(2)}) %collective-permute-start.4) | collective-permute-done | bytes 524320 | tf_op jit(solution)/shard_map/ppermute | solution.py:98
  124.2 0.3 bitcast_add_fusion.2
  124.5 1.6 %collective-permute-start.5 = (f32[8,1,32,256]{3,0,2,1:T(8,128)S(1)}, f32[8,1,32,256]{3,0,2,1:T(8,128)S(1)}, u32[]{:S(2)}, u32[]{:S(2)}) collective-permute-start(f32[8,1,32,256]{3,0,2,1:T(8,128)S(1)} %constant_dynamic-slice_fusion), channel_id=1, source_target_pairs={{0,16},{8,24},{16,0},{24,8},{1,17},{9,25},{17,1},{25,9},{2,18},{10... | collective-permute-start | bytes 786440 | tf_op jit(solution)/shard_map/ppermute | solution.py:98
  126.1 6.9 %collective-permute-done.5 = f32[8,1,32,256]{3,0,2,1:T(8,128)S(1)} collective-permute-done((f32[8,1,32,256]{3,0,2,1:T(8,128)S(1)}, f32[8,1,32,256]{3,0,2,1:T(8,128)S(1)}, u32[]{:S(2)}, u32[]{:S(2)}) %collective-permute-start.5) | collective-permute-done | bytes 262176 | tf_op jit(solution)/shard_map/ppermute | solution.py:98
  133.0 14.1 %all_to_all.18 = f32[8,32,256]{2,0,1:T(8,128)S(1)} all-to-all(f32[8,32,256]{2,0,1:T(8,128)S(1)} %add_bitcast_fusion.1), channel_id=1, replica_groups=mesh['shots'=4,'depth'=8] {'depth'}, dimensions={1} | all-to-all | bytes 524288 | tf_op jit(solution)/shard_map/all_to_all | solution.py:153
  147.3 0.9 copy.22
  (61 shorter events, 1.3 us)
Async XLA Ops:
  0.6 11.0 %copy-start.9 = (s32[4096]{0:T(1024)S(1)}, s32[4096]{0:T(1024)}, u32[]{:S(2)}) copy-start(s32[4096]{0:T(1024)} %param.22) | copy-start | bytes 49156
  0.6 11.0 %copy-start.10 = (s32[4096]{0:T(1024)S(1)}, s32[4096]{0:T(1024)}, u32[]{:S(2)}) copy-start(s32[4096]{0:T(1024)} %param.21) | copy-start | bytes 49156
  0.7 11.0 %slice-start = ((f32[1,2,4096]{2,1,0:T(2,128)}), f32[1,1,4096]{2,1,0:T(1,128)S(1)}, s32[]{:S(2)}) async-start(f32[1,2,4096]{2,1,0:T(2,128)} %param.23), calls=%async_computation.1 | async-start | bytes 32768 | tf_op jit(solution)/shard_map/slice | solution.py:136
  3.7 31.4 %copy-start.13 = (s32[512]{0:T(512)S(1)}, s32[512]{0:T(512)}, u32[]{:S(2)}) copy-start(s32[512]{0:T(512)} %param.20) | copy-start | bytes 6148
  3.7 31.4 %copy-start.14 = (s32[512]{0:T(512)S(1)}, s32[512]{0:T(512)}, u32[]{:S(2)}) copy-start(s32[512]{0:T(512)} %param.19) | copy-start | bytes 6148
  3.7 31.4 %copy-start.11 = (s32[1,512]{1,0:T(1,128)S(1)}, s32[1,512]{1,0:T(1,128)}, u32[]{:S(2)}) copy-start(s32[1,512]{1,0:T(1,128)} %param.18) | copy-start | bytes 6148
  3.7 31.4 %copy-start.12 = (f32[2,512]{1,0:T(2,128)S(1)}, f32[2,512]{1,0:T(2,128)}, u32[]{:S(2)}) copy-start(f32[2,512]{1,0:T(2,128)} %param.17) | copy-start | bytes 12292
  3.7 38.3 %collective-permute-start = (f32[2,1,4,128,256]{4,3,2,0,1:T(8,128)}, f32[2,1,4,128,256]{4,3,2,0,1:T(8,128)}, u32[]{:S(2)}, u32[]{:S(2)}) collective-permute-start(f32[2,1,4,128,256]{4,3,2,0,1:T(8,128)} %get-tuple-element.33), channel_id=1, source_target_pairs={{1,0},{2,1},{3,2},{4,3},{5,4},{6,5},{7,6},{9,8},{10,9},{11,10},{12... | collective-permute-start | bytes 3145736 | tf_op jit(solution)/shard_map/ppermute | solution.py:71
  5.1 49.7 %collective-permute-start.1 = (f32[2,1,4,128,256]{4,3,2,0,1:T(8,128)}, f32[2,1,4,128,256]{4,3,2,0,1:T(8,128)}, u32[]{:S(2)}, u32[]{:S(2)}) collective-permute-start(f32[2,1,4,128,256]{4,3,2,0,1:T(8,128)} %get-tuple-element.34), channel_id=1, source_target_pairs={{0,1},{1,2},{2,3},{3,4},{4,5},{5,6},{6,7},{8,9},{9,10},{10,11},{11... | collective-permute-start | bytes 3145736 | tf_op jit(solution)/shard_map/ppermute | solution.py:70
  35.1 4.9 %copy-start = (f32[1,8,128,256]{3,2,1,0:T(8,128)S(1)}, f32[1,8,128,256]{3,2,1,0:T(8,128)}, u32[]{:S(2)}) copy-start(f32[1,8,128,256]{3,2,1,0:T(8,128)} %param.13) | copy-start | bytes 3145732
  35.1 4.9 %copy-start.1 = (f32[1,8,128,256]{3,2,1,0:T(8,128)S(1)}, f32[1,8,128,256]{3,2,1,0:T(8,128)}, u32[]{:S(2)}) copy-start(f32[1,8,128,256]{3,2,1,0:T(8,128)} %param.15) | copy-start | bytes 3145732
  41.9 15.2 %copy-start.2 = (f32[1,8,128,256]{3,2,1,0:T(8,128)S(1)}, f32[1,8,128,256]{3,2,1,0:T(8,128)}, u32[]{:S(2)}) copy-start(f32[1,8,128,256]{3,2,1,0:T(8,128)} %param.15) | copy-start | bytes 3145732
  41.9 15.2 %copy-start.4 = (f32[1,1,8,128,256]{4,3,2,0,1:T(8,128)S(1)}, f32[1,1,8,128,256]{4,3,2,0,1:T(8,128)}, u32[]{:S(2)}) copy-start(f32[1,1,8,128,256]{4,3,2,0,1:T(8,128)} %stack_reshape.13) | copy-start | bytes 3145732
  41.9 15.2 %copy-start.6 = (f32[1,1,8,128,256]{4,3,2,0,1:T(8,128)S(1)}, f32[1,1,8,128,256]{4,3,2,0,1:T(8,128)}, u32[]{:S(2)}) copy-start(f32[1,1,8,128,256]{4,3,2,0,1:T(8,128)} %stack_reshape.12) | copy-start | bytes 3145732
  41.9 15.2 %copy-start.15 = (f32[1,8,128,256]{3,2,1,0:T(8,128)S(1)}, f32[1,8,128,256]{3,2,1,0:T(8,128)}, u32[]{:S(2)}) copy-start(f32[1,8,128,256]{3,2,1,0:T(8,128)} %param.14) | copy-start | bytes 3145732
  41.9 15.2 %copy-start.16 = (f32[1,8,128,256]{3,2,1,0:T(8,128)S(1)}, f32[1,8,128,256]{3,2,1,0:T(8,128)}, u32[]{:S(2)}) copy-start(f32[1,8,128,256]{3,2,1,0:T(8,128)} %param.12) | copy-start | bytes 3145732
  42.0 15.2 %copy-start.17 = (f32[8,128,256]{2,1,0:T(8,128)S(1)}, f32[8,128,256]{2,1,0:T(8,128)}, u32[]{:S(2)}) copy-start(f32[8,128,256]{2,1,0:T(8,128)} %param.16) | copy-start | bytes 3145732
  60.5 8.3 %copy-start.8 = (f32[1,2,4096]{2,1,0:T(2,128)S(1)}, f32[1,2,4096]{2,1,0:T(2,128)}, u32[]{:S(2)}) copy-start(f32[1,2,4096]{2,1,0:T(2,128)} %param.23) | copy-start | bytes 98308
  62.0 49.8 %collective-permute-start.3 = (f32[2,1,4,128,256]{4,3,2,0,1:T(8,128)}, f32[2,1,4,128,256]{4,3,2,0,1:T(8,128)}, u32[]{:S(2)}, u32[]{:S(2)}) collective-permute-start(f32[2,1,4,128,256]{4,3,2,0,1:T(8,128)} %get-tuple-element.30), channel_id=1, source_target_pairs={{0,1},{1,2},{2,3},{3,4},{4,5},{5,6},{6,7},{8,9},{9,10},{10,11},{11... | collective-permute-start | bytes 3145736 | tf_op jit(solution)/shard_map/ppermute | solution.py:70
  67.4 44.4 %collective-permute-start.2 = (f32[2,1,4,128,256]{4,3,2,0,1:T(8,128)}, f32[2,1,4,128,256]{4,3,2,0,1:T(8,128)}, u32[]{:S(2)}, u32[]{:S(2)}) collective-permute-start(f32[2,1,4,128,256]{4,3,2,0,1:T(8,128)} %get-tuple-element.29), channel_id=1, source_target_pairs={{1,0},{2,1},{3,2},{4,3},{5,4},{6,5},{7,6},{9,8},{10,9},{11,10},{12... | collective-permute-start | bytes 3145736 | tf_op jit(solution)/shard_map/ppermute | solution.py:71
  101.0 10.8 %copy-start.3 = (f32[1,8,128,256]{3,2,1,0:T(8,128)S(1)}, f32[1,8,128,256]{3,2,1,0:T(8,128)}, u32[]{:S(2)}) copy-start(f32[1,8,128,256]{3,2,1,0:T(8,128)} %param.15) | copy-start | bytes 3145732
  101.0 10.8 %copy-start.5 = (f32[1,1,8,128,256]{4,3,2,0,1:T(8,128)S(1)}, f32[1,1,8,128,256]{4,3,2,0,1:T(8,128)}, u32[]{:S(2)}) copy-start(f32[1,1,8,128,256]{4,3,2,0,1:T(8,128)} %stack_reshape.15) | copy-start | bytes 3145732
  101.0 10.8 %copy-start.7 = (f32[1,1,8,128,256]{4,3,2,0,1:T(8,128)S(1)}, f32[1,1,8,128,256]{4,3,2,0,1:T(8,128)}, u32[]{:S(2)}) copy-start(f32[1,1,8,128,256]{4,3,2,0,1:T(8,128)} %stack_reshape.14) | copy-start | bytes 3145732
  101.0 10.8 %copy-start.18 = (f32[8,128,256]{2,1,0:T(8,128)S(1)}, f32[8,128,256]{2,1,0:T(8,128)}, u32[]{:S(2)}) copy-start(f32[8,128,256]{2,1,0:T(8,128)} %param.16) | copy-start | bytes 3145732
  122.2 2.0 %collective-permute-start.4 = (f32[8,2,32,256]{3,0,2,1:T(8,128)S(1)}, f32[8,2,32,256]{3,0,2,1:T(8,128)S(1)}, u32[]{:S(2)}, u32[]{:S(2)}) collective-permute-start(f32[8,2,32,256]{3,0,2,1:T(8,128)S(1)} %bitcast.99), channel_id=1, source_target_pairs={{0,8},{8,0},{16,24},{24,16},{1,9},{9,1},{17,25},{25,17},{2,10},{10... | collective-permute-start | bytes 1572872 | tf_op jit(solution)/shard_map/ppermute | solution.py:98
  124.5 8.4 %collective-permute-start.5 = (f32[8,1,32,256]{3,0,2,1:T(8,128)S(1)}, f32[8,1,32,256]{3,0,2,1:T(8,128)S(1)}, u32[]{:S(2)}, u32[]{:S(2)}) collective-permute-start(f32[8,1,32,256]{3,0,2,1:T(8,128)S(1)} %constant_dynamic-slice_fusion), channel_id=1, source_target_pairs={{0,16},{8,24},{16,0},{24,8},{1,17},{9,25},{17,1},{25,9},{2,18},{10... | collective-permute-start | bytes 786440 | tf_op jit(solution)/shard_map/ppermute | solution.py:98

commit v5 on v4

--- a/solution.py
+++ b/solution.py
@@ -100,6 +100,22 @@
     return blocks.reshape(shape[:dim] + (length // devices,) + shape[dim + 1 :])
 
 
+def transpose_depth(values, dim):
+    devices = lax.axis_size("depth")
+    me = lax.axis_index("depth")
+    shape = values.shape
+    length = shape[dim] // devices
+    chunks = values.reshape(shape[:dim] + (devices, length) + shape[dim + 1 :])
+    parts = [None] * devices
+    parts[0] = lax.dynamic_index_in_dim(chunks, me, axis=dim, keepdims=False)
+    for offset in range(1, devices):
+        send = lax.dynamic_index_in_dim(chunks, (me + offset) % devices, axis=dim, keepdims=False)
+        pairs = [(i, (i + offset) % devices) for i in range(devices)]
+        parts[devices - offset] = lax.ppermute(send, "depth", pairs)
+    ordered = jnp.roll(jnp.stack(parts), me, axis=0)
+    return ordered.reshape((devices * shape[0],) + ordered.shape[2:])
+
+
 def on_device(
     forward_prev,
     forward_now,
@@ -150,7 +166,7 @@
         earlier, current = (current, fresh)
     lateral_smooth = smooth(smooth(correlation, 1), 2)
     reduced = reduce_shots(lateral_smooth, 1)
-    columns = lax.all_to_all(reduced, "depth", split_axis=1, concat_axis=0, tiled=True)
+    columns = transpose_depth(reduced, 1)
     gradient = smooth(columns, 0)
     return (earlier[0], current[0], earlier[1], current[1], gradient)
 

time: 149 us -> 154 us (1.034)
  blocking collectives: 14.1 us -> 0 us
  starting transfers between devices: 16.2 us -> 28 us
  waiting for transfers between devices: 30.5 us -> 37.2 us
    all_to_all x1 -> x0, blocking collectives: 14.1 us -> none  [on_device(): lax.all_to_all(reduced, 'depth', split_axis=1, concat_axis=0, tiled=True)]
    ppermute x0 -> x7, starting transfers between devices: none -> 11.1 us  [transpose_depth(): parts[devices - offset] = lax.ppermute(send, 'depth', pairs)]
    ppermute x0 -> x7, waiting for transfers between devices: none -> 6.39 us  [transpose_depth(): parts[devices - offset] = lax.ppermute(send, 'depth', pairs)]
  transfers between devices with their start and end apart: 6 -> 13, of which waited for: 4 -> 8; matrix products, arithmetic and copies ran while one was open for 43% -> 42% of each run, Pallas kernels for 0% -> 0%
where the time goes in v5:
time: 154 us; the launch traced here: 153 us
  other arithmetic  62.9 us (41%)
  waiting for transfers between devices  37.2 us (24%)
  starting transfers between devices  28 us (18%)
  matrix products  12.8 us (8%)
  local copies, waits for them, and re-layouts  11 us (7%)
    scatter-add x4, other arithmetic, spread(): jnp.zeros((values.shape[0], limit), jnp.float32).at[:, local]  52.8 us
    ppermute x2, waiting for transfers between devices, exchange(): below = lax.ppermute(last, 'depth', up)  22.1 us
    ppermute x2, starting transfers between devices, exchange(): below = lax.ppermute(last, 'depth', up)  12.5 us
    ppermute x7, starting transfers between devices, transpose_depth(): parts[devices - offset] = lax.ppermute(send, 'depth', pairs)  11.1 us
    ppermute x2, waiting for transfers between devices, reduce_shots(): blocks = keep + lax.ppermute(send, 'shots', pairs)  8.72 us
    dot_general x2, matrix products, lateral_laplace(): along_y = jnp.einsum('...xy,yk->...xk', core, band(cols), precision=high)  7.6 us
    another operation x4, local copies, waits for them, and re-layouts, on_device(): terms = jnp.stack([forward_part, adjoint_part])  7.51 us
    ppermute x7, waiting for transfers between devices, transpose_depth(): parts[devices - offset] = lax.ppermute(send, 'depth', pairs)  6.39 us
  transfers between devices with their start and end apart: 13, of which 8 were waited for; matrix products, arithmetic and copies ran while one was open for 42% of the time, Pallas kernels for 0%

profile of v5, /device:TPU:0, one launch (start us, length us, event | category | flops | bytes accessed | tf_op | source)
XLA Modules:
  0.0 153.1 jit_solution(7387637665146658664)
XLA Ops:
  0.7 3.0 %fusion.44 = (f32[2,1,4,128,256]{4,3,2,0,1:T(8,128)}, f32[2,1,4,128,256]{4,3,2,0,1:T(8,128)}) fusion(f32[1,1,8,128,256]{4,3,2,0,1:T(8,128)} %bitcast.115, f32[1,1,8,128,256]{4,3,2,0,1:T(8,128)} %bitcast.120), kind=kLoop, calls=%fused_computation.74 | loop fusion | flops 524288 | bytes 4194304 | tf_op jit(solution)/shard_map/stack | solution.py:140
  3.7 1.4 collective-permute-start
  5.1 6.5 %collective-permute-start.1 = (f32[2,1,4,128,256]{4,3,2,0,1:T(8,128)}, f32[2,1,4,128,256]{4,3,2,0,1:T(8,128)}, u32[]{:S(2)}, u32[]{:S(2)}) collective-permute-start(f32[2,1,4,128,256]{4,3,2,0,1:T(8,128)} %get-tuple-element.29), channel_id=1, source_target_pairs={{0,1},{1,2},{2,3},{3,4},{4,5},{5,6},{6,7},{8,9},{9,10},{10,11},{11... | collective-permute-start | bytes 3145736 | tf_op jit(solution)/shard_map/ppermute | solution.py:70
  11.6 22.2 %scatter_custom_fusion.1 = f32[262144]{0:T(1024)S(1)} fusion(s32[4096]{0:T(1024)S(1)} %get-tuple-element.17, f32[4096]{0:T(1024)S(1)} %bitcast.132, f32[]{:T(128)} %constant.173.clone.1), kind=kCustom, calls=%fused_computation.89 | custom fusion | flops 4096 | bytes 1048580 | tf_op jit(solution)/shard_map/scatter-add | solution.py:80
  33.8 1.3 stack_reshape.13
  35.1 3.5 %scatter_custom_fusion = f32[262144]{0:T(1024)S(1)} fusion(s32[512]{0:T(512)S(1)} %get-tuple-element.15, f32[512]{0:T(512)S(1)} %bitcast.135, f32[]{:T(128)} %constant.173.clone.1), kind=kCustom, calls=%fused_computation.91 | custom fusion | flops 512 | bytes 1048580 | tf_op jit(solution)/shard_map/scatter-add | solution.py:80
  38.7 1.3 stack_reshape.12
  39.9 1.9 %fusion.38 = f32[2,8,128,256]{3,2,1,0:T(8,128)S(1)} fusion(f32[1,1,8,128,256]{4,3,2,0,1:T(8,128)S(1)} %bitcast.121, f32[1,1,8,128,256]{4,3,2,0,1:T(8,128)S(1)} %bitcast.116), kind=kOutput, calls=%fused_computation.70 | convolution fusion | flops 1611792384 | bytes 4194304 | tf_op jit(solution)/shard_map/...xy,yk->...xk/dot_general | solution.py:39
  42.0 12.8 %collective-permute-done.1 = f32[2,1,4,128,256]{4,3,2,0,1:T(8,128)} collective-permute-done((f32[2,1,4,128,256]{4,3,2,0,1:T(8,128)}, f32[2,1,4,128,256]{4,3,2,0,1:T(8,128)}, u32[]{:S(2)}, u32[]{:S(2)}) %collective-permute-start.1) | collective-permute-done | bytes 1048608 | tf_op jit(solution)/shard_map/ppermute | solution.py:70
  54.8 2.3 %pad_maximum_fusion = (f32[2,1,12,128,256]{4,3,2,0,1:T(8,128)S(1)}, f32[2,1,12,128,256]{4,3,2,0,1:T(8,128)S(1)}) fusion(f32[2,1,4,128,256]{4,3,2,0,1:T(8,128)} %collective-permute-done, f32[1,1,8,128,256]{4,3,2,0,1:T(8,128)S(1)} %bitcast.122, f32[1,1,8,128,256]{4,3,2,0,1:T(8,128)S(1)} %bitcast.117, f32[2,1,4,128,256]{4,3,2,0,1:T(8,128)} %collective-permute-done.1), kind=kLoop, calls=%fused_computation.16 | loop fusion | flops 3145728 | bytes 10485760 | tf_op jit(solution)/shard_map/concatenate | solution.py:46
  57.1 3.3 %fusion.26 = f32[2,1,8,128,256]{4,3,2,0,1:T(8,128)S(1)} fusion(f32[2,1,12,128,256]{4,3,2,0,1:T(8,128)S(1)} %get-tuple-element.27, f32[2,1,12,128,256]{4,3,2,0,1:T(8,128)S(1)} %get-tuple-element.26, f32[1,1,8,128,256]{4,3,2,0,1:T(8,128)S(1)} %bitcast.136, f32[1,1,8,128,256]{4,3,2,0,1:T(8,128)S(1)} %bitcast.137, f32[1,1,8,128,256]{4,3,2,0,1:T(8,128)S(1)} %copy-done.4, ...), kind=kOutput, calls=%fused_computation.52 | convolution fusion | flops 818053120 | bytes 30408704 | tf_op jit(solution)/shard_map/...xy,kx->...ky/dot_general | solution.py:40
  60.5 1.5 %fusion.144 = (f32[2,1,4,128,256]{4,3,2,0,1:T(8,128)}, f32[2,1,4,128,256]{4,3,2,0,1:T(8,128)}) fusion(f32[2,1,8,128,256]{4,3,2,0,1:T(8,128)S(1)} %fusion.26), kind=kLoop, calls=%fused_computation.221 | loop fusion | bytes 4194304 | tf_op jit(solution)/shard_map/slice | solution.py:69
  62.0 1.4 collective-permute-start.2
  63.4 6.0 %collective-permute-start.3 = (f32[2,1,4,128,256]{4,3,2,0,1:T(8,128)}, f32[2,1,4,128,256]{4,3,2,0,1:T(8,128)}, u32[]{:S(2)}, u32[]{:S(2)}) collective-permute-start(f32[2,1,4,128,256]{4,3,2,0,1:T(8,128)} %get-tuple-element.25), channel_id=1, source_target_pairs={{0,1},{1,2},{2,3},{3,4},{4,5},{5,6},{6,7},{8,9},{9,10},{10,11},{11... | collective-permute-start | bytes 3145736 | tf_op jit(solution)/shard_map/ppermute | solution.py:70
  69.5 4.3 %scatter_custom_fusion.2 = f32[262144]{0:T(1024)} fusion(s32[512]{0:T(512)S(1)} %compare_select_fusion.2, f32[512]{0:T(512)S(1)} %bitcast.134, f32[]{:T(128)} %constant.173.clone.1), kind=kCustom, calls=%fused_computation.87 | custom fusion | flops 512 | bytes 1048580 | tf_op jit(solution)/shard_map/scatter-add | solution.py:80
  73.7 2.5 %stack_reshape.14 = f32[1,1,8,128,256]{4,3,2,0,1:T(8,128)} reshape(f32[262144]{0:T(1024)} %scatter_custom_fusion.2) | data formatting | bytes 2097152 | tf_op jit(solution)/shard_map/stack;reshape | solution.py:153
  76.3 22.9 %scatter_custom_fusion.3 = f32[262144]{0:T(1024)} fusion(s32[4096]{0:T(1024)S(1)} %compare_select_fusion, f32[4096]{0:T(1024)S(1)} %bitcast.133, f32[]{:T(128)} %constant.173.clone.1), kind=kCustom, calls=%fused_computation.85 | custom fusion | flops 4096 | bytes 1048580 | tf_op jit(solution)/shard_map/scatter-add | solution.py:80
  99.2 2.5 %stack_reshape.15 = f32[1,1,8,128,256]{4,3,2,0,1:T(8,128)} reshape(f32[262144]{0:T(1024)} %scatter_custom_fusion.3) | data formatting | bytes 2097152 | tf_op jit(solution)/shard_map/stack;reshape | solution.py:153
  101.7 1.9 %fusion.36 = f32[128,2,8,256]{3,0,2,1:T(8,128)S(1)} fusion(f32[2,1,8,128,256]{4,3,2,0,1:T(8,128)S(1)} %fusion.26), kind=kOutput, calls=%fused_computation.68 | convolution fusion | flops 805470208 | bytes 4194304 | tf_op jit(solution)/shard_map/...xy,kx->...ky/dot_general | solution.py:40
  103.6 9.2 %collective-permute-done.3 = f32[2,1,4,128,256]{4,3,2,0,1:T(8,128)} collective-permute-done((f32[2,1,4,128,256]{4,3,2,0,1:T(8,128)}, f32[2,1,4,128,256]{4,3,2,0,1:T(8,128)}, u32[]{:S(2)}, u32[]{:S(2)}) %collective-permute-start.3) | collective-permute-done | bytes 1048608 | tf_op jit(solution)/shard_map/ppermute | solution.py:70
  112.8 5.7 %fusion.8 = f32[2,1,8,128,256]{4,3,2,0,1:T(8,128)S(1)} fusion(f32[2,1,8,128,256]{4,3,2,0,1:T(8,128)S(1)} %fusion.26, f32[2,1,4,128,256]{4,3,2,0,1:T(8,128)} %collective-permute-done.3, f32[2,1,4,128,256]{4,3,2,0,1:T(8,128)} %collective-permute-done.2, f32[1,1,8,128,256]{4,3,2,0,1:T(8,128)S(1)} %copy-done.7, f32[1,1,8,128,256]{4,3,2,0,1:T(8,128)S(1)} %copy-done.5, ...), kind=kOutput, calls=%fused_computation.31 | convolution fusion | flops 1626996736 | bytes 15728640 | tf_op jit(solution)/shard_map/...xy,yk->...xk/dot_general | solution.py:39
  118.5 2.4 %add_bitcast_fusion = (f32[8,128,256]{2,1,0:T(8,128)S(1)}, f32[1,8,128,256]{3,2,1,0:T(8,128)}, f32[1,8,128,256]{3,2,1,0:T(8,128)}, f32[1,8,128,256]{3,2,1,0:T(8,128)}, f32[1,8,128,256]{3,2,1,0:T(8,128)}) fusion(f32[2,1,8,128,256]{4,3,2,0,1:T(8,128)S(1)} %fusion.8, f32[2,1,8,128,256]{4,3,2,0,1:T(8,128)S(1)} %fusion.26), kind=kLoop, calls=%fused_computation.78 | loop fusion | flops 786432 | bytes 9437184 | tf_op jit(solution)/shard_map/add | solution.py:165
  123.5 1.9 %collective-permute-done.4 = f32[8,2,32,256]{3,0,2,1:T(8,128)S(1)} collective-permute-done((f32[8,2,32,256]{3,0,2,1:T(8,128)S(1)}, f32[8,2,32,256]{3,0,2,1:T(8,128)S(1)}, u32[]{:S(2)}, u32[]{:S(2)}) %collective-permute-start.4) | collective-permute-done | bytes 524320 | tf_op jit(solution)/shard_map/ppermute | solution.py:98
  125.7 1.6 %collective-permute-start.5 = (f32[8,1,32,256]{3,0,2,1:T(8,128)S(1)}, f32[8,1,32,256]{3,0,2,1:T(8,128)S(1)}, u32[]{:S(2)}, u32[]{:S(2)}) collective-permute-start(f32[8,1,32,256]{3,0,2,1:T(8,128)S(1)} %constant_dynamic-slice_fusion.1), channel_id=1, source_target_pairs={{0,16},{8,24},{16,0},{24,8},{1,17},{9,25},{17,1},{25,9},{2,18},{10... | collective-permute-start | bytes 786440 | tf_op jit(solution)/shard_map/ppermute | solution.py:98
  127.3 6.9 %collective-permute-done.5 = f32[8,1,32,256]{3,0,2,1:T(8,128)S(1)} collective-permute-done((f32[8,1,32,256]{3,0,2,1:T(8,128)S(1)}, f32[8,1,32,256]{3,0,2,1:T(8,128)S(1)}, u32[]{:S(2)}, u32[]{:S(2)}) %collective-permute-start.5) | collective-permute-done | bytes 262176 | tf_op jit(solution)/shard_map/ppermute | solution.py:98
  135.0 5.3 %collective-permute-start.7 = (f32[8,4,256]{2,0,1:T(8,128)S(1)}, f32[8,4,256]{2,0,1:T(8,128)S(1)}, u32[]{:S(2)}, u32[]{:S(2)}) collective-permute-start(f32[8,4,256]{2,0,1:T(8,128)S(1)} %get-tuple-element.49), channel_id=1, source_target_pairs={{0,6},{1,7},{2,0},{3,1},{4,2},{5,3},{6,4},{7,5},{8,14},{9,15},{10,... | collective-permute-start | bytes 98312 | tf_op jit(solution)/shard_map/ppermute | solution.py:114
  140.4 2.8 %collective-permute-start.10 = (f32[8,4,256]{2,0,1:T(8,128)S(1)}, f32[8,4,256]{2,0,1:T(8,128)S(1)}, u32[]{:S(2)}, u32[]{:S(2)}) collective-permute-start(f32[8,4,256]{2,0,1:T(8,128)S(1)} %get-tuple-element.46), channel_id=1, source_target_pairs={{0,3},{1,4},{2,5},{3,6},{4,7},{5,0},{6,1},{7,2},{8,11},{9,12},{10,... | collective-permute-start | bytes 98312 | tf_op jit(solution)/shard_map/ppermute | solution.py:114
  143.2 1.9 %collective-permute-start.11 = (f32[8,4,256]{2,0,1:T(8,128)S(1)}, f32[8,4,256]{2,0,1:T(8,128)S(1)}, u32[]{:S(2)}, u32[]{:S(2)}) collective-permute-start(f32[8,4,256]{2,0,1:T(8,128)S(1)} %get-tuple-element.45), channel_id=1, source_target_pairs={{0,2},{1,3},{2,4},{3,5},{4,6},{5,7},{6,0},{7,1},{8,10},{9,11},{10,... | collective-permute-start | bytes 98312 | tf_op jit(solution)/shard_map/ppermute | solution.py:114
  145.5 1.3 collective-permute-done.10
  146.8 2.1 %collective-permute-done.11 = f32[8,4,256]{2,0,1:T(8,128)S(1)} collective-permute-done((f32[8,4,256]{2,0,1:T(8,128)S(1)}, f32[8,4,256]{2,0,1:T(8,128)S(1)}, u32[]{:S(2)}, u32[]{:S(2)}) %collective-permute-start.11) | collective-permute-done | bytes 32800 | tf_op jit(solution)/shard_map/ppermute | solution.py:114
  148.9 2.8 %collective-permute-done.12 = f32[8,4,256]{2,0,1:T(8,128)S(1)} collective-permute-done((f32[8,4,256]{2,0,1:T(8,128)S(1)}, f32[8,4,256]{2,0,1:T(8,128)S(1)}, u32[]{:S(2)}, u32[]{:S(2)}) %collective-permute-start.12) | collective-permute-done | bytes 32800 | tf_op jit(solution)/shard_map/ppermute | solution.py:114
  152.1 1.0 multiply_add_fusion.2
  (91 shorter events, 4.8 us)
Async XLA Ops:
  0.6 11.0 %copy-start.9 = (s32[4096]{0:T(1024)S(1)}, s32[4096]{0:T(1024)}, u32[]{:S(2)}) copy-start(s32[4096]{0:T(1024)} %param.22) | copy-start | bytes 49156
  0.6 11.0 %copy-start.10 = (s32[4096]{0:T(1024)S(1)}, s32[4096]{0:T(1024)}, u32[]{:S(2)}) copy-start(s32[4096]{0:T(1024)} %param.21) | copy-start | bytes 49156
  0.7 11.0 %slice-start = ((f32[1,2,4096]{2,1,0:T(2,128)}), f32[1,1,4096]{2,1,0:T(1,128)S(1)}, s32[]{:S(2)}) async-start(f32[1,2,4096]{2,1,0:T(2,128)} %param.23), calls=%async_computation | async-start | bytes 32768 | tf_op jit(solution)/shard_map/slice | solution.py:152
  3.7 31.4 %copy-start.13 = (s32[512]{0:T(512)S(1)}, s32[512]{0:T(512)}, u32[]{:S(2)}) copy-start(s32[512]{0:T(512)} %param.20) | copy-start | bytes 6148
  3.7 31.4 %copy-start.14 = (s32[512]{0:T(512)S(1)}, s32[512]{0:T(512)}, u32[]{:S(2)}) copy-start(s32[512]{0:T(512)} %param.19) | copy-start | bytes 6148
  3.7 31.4 %copy-start.11 = (s32[1,512]{1,0:T(1,128)S(1)}, s32[1,512]{1,0:T(1,128)}, u32[]{:S(2)}) copy-start(s32[1,512]{1,0:T(1,128)} %param.18) | copy-start | bytes 6148
  3.7 31.4 %copy-start.12 = (f32[2,512]{1,0:T(2,128)S(1)}, f32[2,512]{1,0:T(2,128)}, u32[]{:S(2)}) copy-start(f32[2,512]{1,0:T(2,128)} %param.17) | copy-start | bytes 12292
  3.7 38.2 %collective-permute-start = (f32[2,1,4,128,256]{4,3,2,0,1:T(8,128)}, f32[2,1,4,128,256]{4,3,2,0,1:T(8,128)}, u32[]{:S(2)}, u32[]{:S(2)}) collective-permute-start(f32[2,1,4,128,256]{4,3,2,0,1:T(8,128)} %get-tuple-element.28), channel_id=1, source_target_pairs={{1,0},{2,1},{3,2},{4,3},{5,4},{6,5},{7,6},{9,8},{10,9},{11,10},{12... | collective-permute-start | bytes 3145736 | tf_op jit(solution)/shard_map/ppermute | solution.py:71
  5.1 49.7 %collective-permute-start.1 = (f32[2,1,4,128,256]{4,3,2,0,1:T(8,128)}, f32[2,1,4,128,256]{4,3,2,0,1:T(8,128)}, u32[]{:S(2)}, u32[]{:S(2)}) collective-permute-start(f32[2,1,4,128,256]{4,3,2,0,1:T(8,128)} %get-tuple-element.29), channel_id=1, source_target_pairs={{0,1},{1,2},{2,3},{3,4},{4,5},{5,6},{6,7},{8,9},{9,10},{10,11},{11... | collective-permute-start | bytes 3145736 | tf_op jit(solution)/shard_map/ppermute | solution.py:70
  35.1 4.9 %copy-start.1 = (f32[1,8,128,256]{3,2,1,0:T(8,128)S(1)}, f32[1,8,128,256]{3,2,1,0:T(8,128)}, u32[]{:S(2)}) copy-start(f32[1,8,128,256]{3,2,1,0:T(8,128)} %param.15) | copy-start | bytes 3145732
  41.9 15.2 %copy-start.2 = (f32[1,8,128,256]{3,2,1,0:T(8,128)S(1)}, f32[1,8,128,256]{3,2,1,0:T(8,128)}, u32[]{:S(2)}) copy-start(f32[1,8,128,256]{3,2,1,0:T(8,128)} %param.15) | copy-start | bytes 3145732
  41.9 15.2 %copy-start.4 = (f32[1,1,8,128,256]{4,3,2,0,1:T(8,128)S(1)}, f32[1,1,8,128,256]{4,3,2,0,1:T(8,128)}, u32[]{:S(2)}) copy-start(f32[1,1,8,128,256]{4,3,2,0,1:T(8,128)} %stack_reshape.13) | copy-start | bytes 3145732
  41.9 15.2 %copy-start.6 = (f32[1,1,8,128,256]{4,3,2,0,1:T(8,128)S(1)}, f32[1,1,8,128,256]{4,3,2,0,1:T(8,128)}, u32[]{:S(2)}) copy-start(f32[1,1,8,128,256]{4,3,2,0,1:T(8,128)} %stack_reshape.12) | copy-start | bytes 3145732
  41.9 15.2 %copy-start.15 = (f32[1,8,128,256]{3,2,1,0:T(8,128)S(1)}, f32[1,8,128,256]{3,2,1,0:T(8,128)}, u32[]{:S(2)}) copy-start(f32[1,8,128,256]{3,2,1,0:T(8,128)} %param.14) | copy-start | bytes 3145732
  41.9 15.2 %copy-start.16 = (f32[1,8,128,256]{3,2,1,0:T(8,128)S(1)}, f32[1,8,128,256]{3,2,1,0:T(8,128)}, u32[]{:S(2)}) copy-start(f32[1,8,128,256]{3,2,1,0:T(8,128)} %param.12) | copy-start | bytes 3145732
  41.9 15.2 %copy-start.17 = (f32[8,128,256]{2,1,0:T(8,128)S(1)}, f32[8,128,256]{2,1,0:T(8,128)}, u32[]{:S(2)}) copy-start(f32[8,128,256]{2,1,0:T(8,128)} %param.16) | copy-start | bytes 3145732
  62.0 14.2 %copy-start.8 = (f32[1,2,4096]{2,1,0:T(2,128)S(1)}, f32[1,2,4096]{2,1,0:T(2,128)}, u32[]{:S(2)}) copy-start(f32[1,2,4096]{2,1,0:T(2,128)} %param.23) | copy-start | bytes 98308
  62.0 41.5 %collective-permute-start.2 = (f32[2,1,4,128,256]{4,3,2,0,1:T(8,128)}, f32[2,1,4,128,256]{4,3,2,0,1:T(8,128)}, u32[]{:S(2)}, u32[]{:S(2)}) collective-permute-start(f32[2,1,4,128,256]{4,3,2,0,1:T(8,128)} %get-tuple-element.24), channel_id=1, source_target_pairs={{1,0},{2,1},{3,2},{4,3},{5,4},{6,5},{7,6},{9,8},{10,9},{11,10},{12... | collective-permute-start | bytes 3145736 | tf_op jit(solution)/shard_map/ppermute | solution.py:71
  63.4 49.4 %collective-permute-start.3 = (f32[2,1,4,128,256]{4,3,2,0,1:T(8,128)}, f32[2,1,4,128,256]{4,3,2,0,1:T(8,128)}, u32[]{:S(2)}, u32[]{:S(2)}) collective-permute-start(f32[2,1,4,128,256]{4,3,2,0,1:T(8,128)} %get-tuple-element.25), channel_id=1, source_target_pairs={{0,1},{1,2},{2,3},{3,4},{4,5},{5,6},{6,7},{8,9},{9,10},{10,11},{11... | collective-permute-start | bytes 3145736 | tf_op jit(solution)/shard_map/ppermute | solution.py:70
  101.6 11.2 %copy-start.3 = (f32[1,8,128,256]{3,2,1,0:T(8,128)S(1)}, f32[1,8,128,256]{3,2,1,0:T(8,128)}, u32[]{:S(2)}) copy-start(f32[1,8,128,256]{3,2,1,0:T(8,128)} %param.15) | copy-start | bytes 3145732
  101.6 11.2 %copy-start.5 = (f32[1,1,8,128,256]{4,3,2,0,1:T(8,128)S(1)}, f32[1,1,8,128,256]{4,3,2,0,1:T(8,128)}, u32[]{:S(2)}) copy-start(f32[1,1,8,128,256]{4,3,2,0,1:T(8,128)} %stack_reshape.14) | copy-start | bytes 3145732
  101.6 11.2 %copy-start.7 = (f32[1,1,8,128,256]{4,3,2,0,1:T(8,128)S(1)}, f32[1,1,8,128,256]{4,3,2,0,1:T(8,128)}, u32[]{:S(2)}) copy-start(f32[1,1,8,128,256]{4,3,2,0,1:T(8,128)} %stack_reshape.15) | copy-start | bytes 3145732
  101.7 11.2 %copy-start.18 = (f32[8,128,256]{2,1,0:T(8,128)S(1)}, f32[8,128,256]{2,1,0:T(8,128)}, u32[]{:S(2)}) copy-start(f32[8,128,256]{2,1,0:T(8,128)} %param.16) | copy-start | bytes 3145732
  123.4 2.0 %collective-permute-start.4 = (f32[8,2,32,256]{3,0,2,1:T(8,128)S(1)}, f32[8,2,32,256]{3,0,2,1:T(8,128)S(1)}, u32[]{:S(2)}, u32[]{:S(2)}) collective-permute-start(f32[8,2,32,256]{3,0,2,1:T(8,128)S(1)} %bitcast.131), channel_id=1, source_target_pairs={{0,8},{8,0},{16,24},{24,16},{1,9},{9,1},{17,25},{25,17},{2,10},{10... | collective-permute-start | bytes 1572872 | tf_op jit(solution)/shard_map/ppermute | solution.py:98
  125.7 8.4 %collective-permute-start.5 = (f32[8,1,32,256]{3,0,2,1:T(8,128)S(1)}, f32[8,1,32,256]{3,0,2,1:T(8,128)S(1)}, u32[]{:S(2)}, u32[]{:S(2)}) collective-permute-start(f32[8,1,32,256]{3,0,2,1:T(8,128)S(1)} %constant_dynamic-slice_fusion.1), channel_id=1, source_target_pairs={{0,16},{8,24},{16,0},{24,8},{1,17},{9,25},{17,1},{25,9},{2,18},{10... | collective-permute-start | bytes 786440 | tf_op jit(solution)/shard_map/ppermute | solution.py:98
  134.2 9.0 %collective-permute-start.6 = (f32[8,4,256]{2,0,1:T(8,128)S(1)}, f32[8,4,256]{2,0,1:T(8,128)S(1)}, u32[]{:S(2)}, u32[]{:S(2)}) collective-permute-start(f32[8,4,256]{2,0,1:T(8,128)S(1)} %get-tuple-element.50), channel_id=1, source_target_pairs={{0,7},{1,0},{2,1},{3,2},{4,3},{5,4},{6,5},{7,6},{8,15},{9,8},{10,9... | collective-permute-start | bytes 98312 | tf_op jit(solution)/shard_map/ppermute | solution.py:114
  135.0 10.1 %collective-permute-start.7 = (f32[8,4,256]{2,0,1:T(8,128)S(1)}, f32[8,4,256]{2,0,1:T(8,128)S(1)}, u32[]{:S(2)}, u32[]{:S(2)}) collective-permute-start(f32[8,4,256]{2,0,1:T(8,128)S(1)} %get-tuple-element.49), channel_id=1, source_target_pairs={{0,6},{1,7},{2,0},{3,1},{4,2},{5,3},{6,4},{7,5},{8,14},{9,15},{10,... | collective-permute-start | bytes 98312 | tf_op jit(solution)/shard_map/ppermute | solution.py:114
  140.3 5.1 %collective-permute-start.8 = (f32[8,4,256]{2,0,1:T(8,128)S(1)}, f32[8,4,256]{2,0,1:T(8,128)S(1)}, u32[]{:S(2)}, u32[]{:S(2)}) collective-permute-start(f32[8,4,256]{2,0,1:T(8,128)S(1)} %get-tuple-element.48), channel_id=1, source_target_pairs={{0,5},{1,6},{2,7},{3,0},{4,1},{5,2},{6,3},{7,4},{8,13},{9,14},{10,... | collective-permute-start | bytes 98312 | tf_op jit(solution)/shard_map/ppermute | solution.py:114
  140.3 5.3 %collective-permute-start.9 = (f32[8,4,256]{2,0,1:T(8,128)S(1)}, f32[8,4,256]{2,0,1:T(8,128)S(1)}, u32[]{:S(2)}, u32[]{:S(2)}) collective-permute-start(f32[8,4,256]{2,0,1:T(8,128)S(1)} %get-tuple-element.47), channel_id=1, source_target_pairs={{0,4},{1,5},{2,6},{3,7},{4,0},{5,1},{6,2},{7,3},{8,12},{9,13},{10,... | collective-permute-start | bytes 98312 | tf_op jit(solution)/shard_map/ppermute | solution.py:114
  140.4 6.4 %collective-permute-start.10 = (f32[8,4,256]{2,0,1:T(8,128)S(1)}, f32[8,4,256]{2,0,1:T(8,128)S(1)}, u32[]{:S(2)}, u32[]{:S(2)}) collective-permute-start(f32[8,4,256]{2,0,1:T(8,128)S(1)} %get-tuple-element.46), channel_id=1, source_target_pairs={{0,3},{1,4},{2,5},{3,6},{4,7},{5,0},{6,1},{7,2},{8,11},{9,12},{10,... | collective-permute-start | bytes 98312 | tf_op jit(solution)/shard_map/ppermute | solution.py:114
  143.2 5.7 %collective-permute-start.11 = (f32[8,4,256]{2,0,1:T(8,128)S(1)}, f32[8,4,256]{2,0,1:T(8,128)S(1)}, u32[]{:S(2)}, u32[]{:S(2)}) collective-permute-start(f32[8,4,256]{2,0,1:T(8,128)S(1)} %get-tuple-element.45), channel_id=1, source_target_pairs={{0,2},{1,3},{2,4},{3,5},{4,6},{5,7},{6,0},{7,1},{8,10},{9,11},{10,... | collective-permute-start | bytes 98312 | tf_op jit(solution)/shard_map/ppermute | solution.py:114
  145.1 6.6 %collective-permute-start.12 = (f32[8,4,256]{2,0,1:T(8,128)S(1)}, f32[8,4,256]{2,0,1:T(8,128)S(1)}, u32[]{:S(2)}, u32[]{:S(2)}) collective-permute-start(f32[8,4,256]{2,0,1:T(8,128)S(1)} %get-tuple-element.44), channel_id=1, source_target_pairs={{0,1},{1,2},{2,3},{3,4},{4,5},{5,6},{6,7},{7,0},{8,9},{9,10},{10,1... | collective-permute-start | bytes 98312 | tf_op jit(solution)/shard_map/ppermute | solution.py:114
  (1 other events, 4.9 us)

commit v6 on v4

--- a/solution.py
+++ b/solution.py
@@ -81,6 +81,28 @@
     return grid.reshape(values.shape[0], planes, rows, cols)
 
 
+def spread_dense(depth, cell, values, first_plane, planes, rows, cols):
+    steps, count = values.shape
+    local = depth - first_plane
+    inside = (local >= 0) & (local < planes)
+    row_id = jnp.where(inside, local * rows + cell // cols, -1)
+    by_row = (row_id[None, :] == jnp.arange(planes * rows)[:, None]).astype(jnp.bfloat16)
+    by_col = (cell % cols)[:, None] == jnp.arange(cols)[None, :]
+    pieces = []
+    rest = values
+    for _ in range(3):
+        piece = lax.reduce_precision(rest, exponent_bits=8, mantissa_bits=7)
+        rest = rest - piece
+        pieces.append(piece.astype(jnp.bfloat16))
+    stacked = jnp.stack(pieces)
+    right = jnp.where(by_col[None, None], stacked[:, :, :, None], jnp.zeros((), jnp.bfloat16))
+    right = right.transpose(2, 0, 1, 3).reshape(count, 3 * steps * cols)
+    grid = jnp.dot(by_row, right, preferred_element_type=jnp.float32)
+    grid = grid.reshape(planes * rows, 3, steps, cols)
+    grid = grid[:, 0] + grid[:, 1] + grid[:, 2]
+    return grid.transpose(1, 0, 2).reshape(steps, planes, rows, cols)
+
+
 def reduce_shots(values, dim):
     devices = lax.axis_size("shots")
     me = lax.axis_index("shots")
@@ -126,15 +148,10 @@
     below, above = exchange(current, zaxis)
     first_plane = position * planes
     correlation = None
-    gate = ()
+    forward_terms = spread_dense(source_depth, source_cell, signs[0][None, :] * wavelet, first_plane, planes, rows, cols)
+    adjoint_terms = spread_dense(receiver_depth, receiver_cell, residual_traces[0], first_plane, planes, rows, cols)
     for step in range(STEPS):
-        if step > 0:
-            gate, (source_flat, receiver_flat, signs, wavelet, residual_traces) = lax.optimization_barrier(
-                (gate, (source_flat, receiver_flat, signs, wavelet, residual_traces))
-            )
-        forward_part = spread(source_flat, signs * wavelet[step][None, :], first_plane, planes, rows, cols)
-        adjoint_part = spread(receiver_flat, residual_traces[:, step, :], first_plane, planes, rows, cols)
-        terms = jnp.stack([forward_part, adjoint_part])
+        terms = jnp.stack([forward_terms[step : step + 1], adjoint_terms[step : step + 1]])
         lateral_part = lateral_laplace(current, zaxis)
         fresh = (
             2.0 * current
@@ -144,7 +161,6 @@
         )
         if step + 1 < STEPS:
             below, above = exchange(fresh, zaxis)
-            gate = fresh
         part = fresh[0, 0] * fresh[1, 0]
         correlation = part if correlation is None else correlation + part
         earlier, current = (current, fresh)

time: 149 us -> 149 us (level)
  other arithmetic: 62.1 us -> 11.6 us
  waiting for transfers between devices: 30.5 us -> 68.6 us
  matrix products: 12.6 us -> 30.5 us
  local copies, waits for them, and re-layouts: 11.6 us -> 6.28 us
    scatter-add x4 -> x0, other arithmetic: 52.8 us -> none  [spread(): jnp.zeros((values.shape[0], limit), jnp.float32).at[:, local]]
    ppermute x2, waiting for transfers between devices: 21.7 us -> 41.1 us  [exchange(): below = lax.ppermute(last, 'depth', up)]
    ppermute x2, waiting for transfers between devices: 0.01 us -> 18.8 us  [exchange(): above = lax.ppermute(leading, 'depth', down)]
    dot_general x0 -> x2, matrix products: none -> 16.4 us  [spread_dense(): grid = jnp.dot(by_row, right, preferred_element_type=jnp.float32)]
    another operation x4 -> x0, local copies, waits for them, and re-layouts: 7.52 us -> none  [on_device(): terms = jnp.stack([forward_part, adjoint_part])]
    slice x3 -> x2, local copies, waits for them, and re-layouts: 0.03 us -> 2.21 us  [the longest x1 1.11 us: on_device(): adjoint_terms[step:step + 1]]
    eq x0 -> x2, other arithmetic: none -> 1.67 us  [spread_dense(): by_col = (cell % cols)[:, None] == jnp.arange(cols)[None, :]]
  transfers between devices with their start and end apart: 6 -> 6, of which waited for: 4 -> 5; matrix products, arithmetic and copies ran while one was open for 43% -> 18% of each run, Pallas kernels for 0% -> 0%
where the time goes in v6:
time: 149 us
  waiting for transfers between devices  68.6 us (46%)
  matrix products  30.5 us (20%)
  starting transfers between devices  16.7 us (11%)
  blocking collectives  14.1 us (9%)
  other arithmetic  11.6 us (8%)
  local copies, waits for them, and re-layouts  6.28 us (4%)
    ppermute x2, waiting for transfers between devices, exchange(): below = lax.ppermute(last, 'depth', up)  41.1 us
    ppermute x2, waiting for transfers between devices, exchange(): above = lax.ppermute(leading, 'depth', down)  18.8 us
    dot_general x2, matrix products, spread_dense(): grid = jnp.dot(by_row, right, preferred_element_type=jnp.float32)  16.4 us
    all_to_all x1, blocking collectives, on_device(): lax.all_to_all(reduced, 'depth', split_axis=1, concat_axis=0, tiled=True)  14.1 us
    ppermute x2, starting transfers between devices, exchange(): below = lax.ppermute(last, 'depth', up)  12.5 us
    dot_general x2, matrix products, lateral_laplace(): along_y = jnp.einsum('...xy,yk->...xk', core, band(cols), precision=high)  8.88 us
    ppermute x2, waiting for transfers between devices, reduce_shots(): blocks = keep + lax.ppermute(send, 'shots', pairs)  8.72 us
    dot_general x2, matrix products, lateral_laplace(): along_x = jnp.einsum('...xy,kx->...ky', core, band(rows), precision=high)  5.22 us
  transfers between devices with their start and end apart: 6, of which 5 were waited for; matrix products, arithmetic and copies ran while one was open for 18% of the time, Pallas kernels for 0%

profile of v6, /device:TPU:0, one launch (start us, length us, event | category | flops | bytes accessed | tf_op | source)
XLA Modules:
  0.0 148.9 jit_solution(13847850731644957618)
XLA Ops:
  0.7 3.2 %fusion.61 = (f32[2,1,4,128,256]{4,3,2,0,1:T(8,128)}, f32[2,1,4,128,256]{4,3,2,0,1:T(8,128)}) fusion(f32[1,1,8,128,256]{4,3,2,0,1:T(8,128)} %bitcast.127, f32[1,1,8,128,256]{4,3,2,0,1:T(8,128)} %bitcast.132), kind=kLoop, calls=%fused_computation.92 | loop fusion | flops 524288 | bytes 4194304 | tf_op jit(solution)/shard_map/stack | solution.py:146
  3.8 1.3 collective-permute-start
  5.1 6.5 %collective-permute-start.1 = (f32[2,1,4,128,256]{4,3,2,0,1:T(8,128)}, f32[2,1,4,128,256]{4,3,2,0,1:T(8,128)}, u32[]{:S(2)}, u32[]{:S(2)}) collective-permute-start(f32[2,1,4,128,256]{4,3,2,0,1:T(8,128)} %get-tuple-element.24), channel_id=1, source_target_pairs={{0,1},{1,2},{2,3},{3,4},{4,5},{5,6},{6,7},{8,9},{9,10},{10,11},{11... | collective-permute-start | bytes 3145736 | tf_op jit(solution)/shard_map/ppermute | solution.py:70
  11.6 3.2 %fusion.49 = f32[2,8,128,256]{3,2,1,0:T(8,128)} fusion(f32[1,1,8,128,256]{4,3,2,0,1:T(8,128)S(1)} %bitcast.133, f32[1,1,8,128,256]{4,3,2,0,1:T(8,128)S(1)} %bitcast.128), kind=kOutput, calls=%fused_computation.82 | convolution fusion | flops 1611792384 | bytes 4194304 | tf_op jit(solution)/shard_map/...xy,yk->...xk/dot_general | solution.py:39
  14.9 1.6 %iota_compare_fusion.1 = pred[4096,256]{0,1:T(8,128)(4,1)} fusion(s32[4096]{0:T(1024)S(1)} %get-tuple-element.43), kind=kLoop, calls=%fused_computation.15 | loop fusion | flops 1048576 | bytes 1064960 | tf_op jit(solution)/shard_map/eq | solution.py:90
  16.6 14.6 %fusion.1 = f32[1024,3,2,256]{3,0,2,1:T(8,128)S(1)} fusion(pred[4096,256]{0,1:T(8,128)(4,1)} %iota_compare_fusion.1, s32[4096]{0:T(1024)S(1)} %get-tuple-element.42, bf16[4096,3,2]{0,2,1:T(2,128)(2,1)S(1)} %maximum_bitcast_fusion), kind=kOutput, calls=%fused_computation.2 | convolution fusion | flops 12895387648 | bytes 7405568 | tf_op jit(solution)/shard_map/dot_general | solution.py:100
  31.2 0.4 fusion.30
  31.6 1.1 fusion.173
  32.9 1.8 %fusion.54 = f32[1024,3,2,256]{3,0,2,1:T(8,128)S(1)} fusion(pred[512,256]{0,1:T(8,128)(4,1)S(1)} %iota_compare_fusion.3, s32[512]{0:T(512)S(1)} %get-tuple-element.47, bf16[512,3,2]{0,2,1:T(2,128)(2,1)S(1)} %maximum_bitcast_fusion.1), kind=kOutput, calls=%fused_computation.88 | convolution fusion | flops 1611923456 | bytes 6430720 | tf_op jit(solution)/shard_map/dot_general | solution.py:100
  34.8 0.4 fusion.31
  35.2 1.1 fusion.172
  36.3 18.4 %collective-permute-done.1 = f32[2,1,4,128,256]{4,3,2,0,1:T(8,128)} collective-permute-done((f32[2,1,4,128,256]{4,3,2,0,1:T(8,128)}, f32[2,1,4,128,256]{4,3,2,0,1:T(8,128)}, u32[]{:S(2)}, u32[]{:S(2)}) %collective-permute-start.1) | collective-permute-done | bytes 1048608 | tf_op jit(solution)/shard_map/ppermute | solution.py:70
  54.8 2.0 %pad_maximum_fusion = (f32[2,1,12,128,256]{4,3,2,0,1:T(8,128)S(1)}, f32[2,1,12,128,256]{4,3,2,0,1:T(8,128)S(1)}) fusion(f32[2,1,4,128,256]{4,3,2,0,1:T(8,128)S(1)} %collective-permute-done, f32[1,1,8,128,256]{4,3,2,0,1:T(8,128)S(1)} %bitcast.134, f32[1,1,8,128,256]{4,3,2,0,1:T(8,128)S(1)} %bitcast.129, f32[2,1,4,128,256]{4,3,2,0,1:T(8,128)} %collective-permute-done.1), kind=kLoop, calls=%fused_computation.22 | loop fusion | flops 3145728 | bytes 10485760 | tf_op jit(solution)/shard_map/concatenate | solution.py:46
  56.8 3.3 %fusion.37 = f32[2,1,8,128,256]{4,3,2,0,1:T(8,128)S(1)} fusion(f32[2,1,12,128,256]{4,3,2,0,1:T(8,128)S(1)} %get-tuple-element.22, f32[2,1,12,128,256]{4,3,2,0,1:T(8,128)S(1)} %get-tuple-element.21, f32[1,1,8,128,256]{4,3,2,0,1:T(8,128)S(1)} %bitcast.148, f32[1,1,8,128,256]{4,3,2,0,1:T(8,128)S(1)} %bitcast.149, f32[1,1,8,128,256]{4,3,2,0,1:T(8,128)S(1)} %bitcast.144, ...), kind=kOutput, calls=%fused_computation.64 | convolution fusion | flops 818053120 | bytes 30408704 | tf_op jit(solution)/shard_map/...xy,kx->...ky/dot_general | solution.py:40
  60.1 1.5 %fusion.174 = (f32[2,1,4,128,256]{4,3,2,0,1:T(8,128)}, f32[2,1,4,128,256]{4,3,2,0,1:T(8,128)}) fusion(f32[2,1,8,128,256]{4,3,2,0,1:T(8,128)S(1)} %fusion.37), kind=kLoop, calls=%fused_computation.245 | loop fusion | bytes 4194304 | tf_op jit(solution)/shard_map/slice | solution.py:69
  61.6 1.3 collective-permute-start.2
  62.9 6.0 %collective-permute-start.3 = (f32[2,1,4,128,256]{4,3,2,0,1:T(8,128)}, f32[2,1,4,128,256]{4,3,2,0,1:T(8,128)}, u32[]{:S(2)}, u32[]{:S(2)}) collective-permute-start(f32[2,1,4,128,256]{4,3,2,0,1:T(8,128)} %get-tuple-element.20), channel_id=1, source_target_pairs={{0,1},{1,2},{2,3},{3,4},{4,5},{5,6},{6,7},{8,9},{9,10},{10,11},{11... | collective-permute-start | bytes 3145736 | tf_op jit(solution)/shard_map/ppermute | solution.py:70
  68.9 1.9 %fusion.47 = f32[128,2,8,256]{3,0,2,1:T(8,128)S(1)} fusion(f32[2,1,8,128,256]{4,3,2,0,1:T(8,128)S(1)} %fusion.37), kind=kOutput, calls=%fused_computation.80 | convolution fusion | flops 805470208 | bytes 4194304 | tf_op jit(solution)/shard_map/...xy,kx->...ky/dot_general | solution.py:40
  70.8 18.8 %collective-permute-done.2 = f32[2,1,4,128,256]{4,3,2,0,1:T(8,128)} collective-permute-done((f32[2,1,4,128,256]{4,3,2,0,1:T(8,128)}, f32[2,1,4,128,256]{4,3,2,0,1:T(8,128)}, u32[]{:S(2)}, u32[]{:S(2)}) %collective-permute-start.2) | collective-permute-done | bytes 1048608 | tf_op jit(solution)/shard_map/ppermute | solution.py:71
  89.7 22.6 %collective-permute-done.3 = f32[2,1,4,128,256]{4,3,2,0,1:T(8,128)} collective-permute-done((f32[2,1,4,128,256]{4,3,2,0,1:T(8,128)}, f32[2,1,4,128,256]{4,3,2,0,1:T(8,128)}, u32[]{:S(2)}, u32[]{:S(2)}) %collective-permute-start.3) | collective-permute-done | bytes 1048608 | tf_op jit(solution)/shard_map/ppermute | solution.py:70
  112.3 5.7 %fusion.17 = f32[2,1,8,128,256]{4,3,2,0,1:T(8,128)S(1)} fusion(f32[2,1,8,128,256]{4,3,2,0,1:T(8,128)S(1)} %fusion.37, f32[2,1,4,128,256]{4,3,2,0,1:T(8,128)} %collective-permute-done.3, f32[2,1,4,128,256]{4,3,2,0,1:T(8,128)} %collective-permute-done.2, f32[1,1,8,128,256]{4,3,2,0,1:T(8,128)S(1)} %bitcast.142, f32[1,1,8,128,256]{4,3,2,0,1:T(8,128)S(1)} %bitcast.143, ...), kind=kOutput, calls=%fused_computation.37 | convolution fusion | flops 1626996736 | bytes 15728640 | tf_op jit(solution)/shard_map/...xy,yk->...xk/dot_general | solution.py:39
  118.0 2.4 %add_bitcast_fusion = (f32[8,128,256]{2,1,0:T(8,128)S(1)}, f32[1,8,128,256]{3,2,1,0:T(8,128)}, f32[1,8,128,256]{3,2,1,0:T(8,128)}, f32[1,8,128,256]{3,2,1,0:T(8,128)}, f32[1,8,128,256]{3,2,1,0:T(8,128)}) fusion(f32[2,1,8,128,256]{4,3,2,0,1:T(8,128)S(1)} %fusion.17, f32[2,1,8,128,256]{4,3,2,0,1:T(8,128)S(1)} %fusion.37), kind=kLoop, calls=%fused_computation.96 | loop fusion | flops 786432 | bytes 9437184 | tf_op jit(solution)/shard_map/add | solution.py:165
  120.7 0.4 multiply_add_fusion.1
  121.1 0.4 fusion.175
  121.5 0.4 fusion.176
  121.9 0.6 multiply_add_fusion
  123.0 1.9 %collective-permute-done.4 = f32[8,2,32,256]{3,0,2,1:T(8,128)S(1)} collective-permute-done((f32[8,2,32,256]{3,0,2,1:T(8,128)S(1)}, f32[8,2,32,256]{3,0,2,1:T(8,128)S(1)}, u32[]{:S(2)}, u32[]{:S(2)}) %collective-permute-start.4) | collective-permute-done | bytes 524320 | tf_op jit(solution)/shard_map/ppermute | solution.py:120
  124.9 0.3 bitcast_add_fusion.2
  125.2 1.6 %collective-permute-start.5 = (f32[8,1,32,256]{3,0,2,1:T(8,128)S(1)}, f32[8,1,32,256]{3,0,2,1:T(8,128)S(1)}, u32[]{:S(2)}, u32[]{:S(2)}) collective-permute-start(f32[8,1,32,256]{3,0,2,1:T(8,128)S(1)} %constant_dynamic-slice_fusion), channel_id=1, source_target_pairs={{0,16},{8,24},{16,0},{24,8},{1,17},{9,25},{17,1},{25,9},{2,18},{10... | collective-permute-start | bytes 786440 | tf_op jit(solution)/shard_map/ppermute | solution.py:120
  126.8 6.9 %collective-permute-done.5 = f32[8,1,32,256]{3,0,2,1:T(8,128)S(1)} collective-permute-done((f32[8,1,32,256]{3,0,2,1:T(8,128)S(1)}, f32[8,1,32,256]{3,0,2,1:T(8,128)S(1)}, u32[]{:S(2)}, u32[]{:S(2)}) %collective-permute-start.5) | collective-permute-done | bytes 262176 | tf_op jit(solution)/shard_map/ppermute | solution.py:120
  133.7 14.1 %all_to_all.18 = f32[8,32,256]{2,0,1:T(8,128)S(1)} all-to-all(f32[8,32,256]{2,0,1:T(8,128)S(1)} %add_bitcast_fusion.1), channel_id=1, replica_groups=mesh['shots'=4,'depth'=8] {'depth'}, dimensions={1} | all-to-all | bytes 524288 | tf_op jit(solution)/shard_map/all_to_all | solution.py:169
  148.0 0.9 copy.22
  (56 shorter events, 1.4 us)
Async XLA Ops:
  0.6 11.0 %copy-start = (f32[1,8,128,256]{3,2,1,0:T(8,128)S(1)}, f32[1,8,128,256]{3,2,1,0:T(8,128)}, u32[]{:S(2)}) copy-start(f32[1,8,128,256]{3,2,1,0:T(8,128)} %param.13) | copy-start | bytes 3145732
  0.6 11.0 %copy-start.1 = (f32[1,8,128,256]{3,2,1,0:T(8,128)S(1)}, f32[1,8,128,256]{3,2,1,0:T(8,128)}, u32[]{:S(2)}) copy-start(f32[1,8,128,256]{3,2,1,0:T(8,128)} %param.15) | copy-start | bytes 3145732
  3.8 32.5 %collective-permute-start = (f32[2,1,4,128,256]{4,3,2,0,1:T(8,128)}, f32[2,1,4,128,256]{4,3,2,0,1:T(8,128)S(1)}, u32[]{:S(2)}, u32[]{:S(2)}) collective-permute-start(f32[2,1,4,128,256]{4,3,2,0,1:T(8,128)} %get-tuple-element.23), channel_id=1, source_target_pairs={{1,0},{2,1},{3,2},{4,3},{5,4},{6,5},{7,6},{9,8},{10,9},{11,10},{12... | collective-permute-start | bytes 3145736 | tf_op jit(solution)/shard_map/ppermute | solution.py:71
  5.1 49.7 %collective-permute-start.1 = (f32[2,1,4,128,256]{4,3,2,0,1:T(8,128)}, f32[2,1,4,128,256]{4,3,2,0,1:T(8,128)}, u32[]{:S(2)}, u32[]{:S(2)}) collective-permute-start(f32[2,1,4,128,256]{4,3,2,0,1:T(8,128)} %get-tuple-element.24), channel_id=1, source_target_pairs={{0,1},{1,2},{2,3},{3,4},{4,5},{5,6},{6,7},{8,9},{9,10},{10,11},{11... | collective-permute-start | bytes 3145736 | tf_op jit(solution)/shard_map/ppermute | solution.py:70
  11.6 3.2 %copy-start.7 = (f32[1,2,4096]{2,1,0:T(2,128)S(1)}, f32[1,2,4096]{2,1,0:T(2,128)}, u32[]{:S(2)}) copy-start(f32[1,2,4096]{2,1,0:T(2,128)} %param.23) | copy-start | bytes 98308
  11.6 3.3 %copy-start.8 = (s32[4096]{0:T(1024)S(1)}, s32[4096]{0:T(1024)}, u32[]{:S(2)}) copy-start(s32[4096]{0:T(1024)} %param.22) | copy-start | bytes 49156
  11.6 3.3 %copy-start.9 = (s32[4096]{0:T(1024)S(1)}, s32[4096]{0:T(1024)}, u32[]{:S(2)}) copy-start(s32[4096]{0:T(1024)} %param.21) | copy-start | bytes 49156
  31.6 1.2 copy-start.13
  31.6 1.2 copy-start.11
  31.6 1.2 copy-start.12
  31.6 1.3 copy-start.10
  36.3 20.4 %copy-start.2 = (f32[1,8,128,256]{3,2,1,0:T(8,128)S(1)}, f32[1,8,128,256]{3,2,1,0:T(8,128)}, u32[]{:S(2)}) copy-start(f32[1,8,128,256]{3,2,1,0:T(8,128)} %param.15) | copy-start | bytes 3145732
  36.3 20.4 %copy-start.4 = (f32[2,8,128,256]{3,2,1,0:T(8,128)S(1)}, f32[2,8,128,256]{3,2,1,0:T(8,128)}, u32[]{:S(2)}) copy-start(f32[2,8,128,256]{3,2,1,0:T(8,128)} %fusion.49) | copy-start | bytes 6291460
  36.3 20.4 %copy-start.14 = (f32[1,8,128,256]{3,2,1,0:T(8,128)S(1)}, f32[1,8,128,256]{3,2,1,0:T(8,128)}, u32[]{:S(2)}) copy-start(f32[1,8,128,256]{3,2,1,0:T(8,128)} %param.14) | copy-start | bytes 3145732
  36.3 20.4 %copy-start.15 = (f32[1,8,128,256]{3,2,1,0:T(8,128)S(1)}, f32[1,8,128,256]{3,2,1,0:T(8,128)}, u32[]{:S(2)}) copy-start(f32[1,8,128,256]{3,2,1,0:T(8,128)} %param.12) | copy-start | bytes 3145732
  36.3 20.5 %copy-start.16 = (f32[8,128,256]{2,1,0:T(8,128)S(1)}, f32[8,128,256]{2,1,0:T(8,128)}, u32[]{:S(2)}) copy-start(f32[8,128,256]{2,1,0:T(8,128)} %param.16) | copy-start | bytes 3145732
  61.6 28.0 %collective-permute-start.2 = (f32[2,1,4,128,256]{4,3,2,0,1:T(8,128)}, f32[2,1,4,128,256]{4,3,2,0,1:T(8,128)}, u32[]{:S(2)}, u32[]{:S(2)}) collective-permute-start(f32[2,1,4,128,256]{4,3,2,0,1:T(8,128)} %get-tuple-element.19), channel_id=1, source_target_pairs={{1,0},{2,1},{3,2},{4,3},{5,4},{6,5},{7,6},{9,8},{10,9},{11,10},{12... | collective-permute-start | bytes 3145736 | tf_op jit(solution)/shard_map/ppermute | solution.py:71
  62.9 49.4 %collective-permute-start.3 = (f32[2,1,4,128,256]{4,3,2,0,1:T(8,128)}, f32[2,1,4,128,256]{4,3,2,0,1:T(8,128)}, u32[]{:S(2)}, u32[]{:S(2)}) collective-permute-start(f32[2,1,4,128,256]{4,3,2,0,1:T(8,128)} %get-tuple-element.20), channel_id=1, source_target_pairs={{0,1},{1,2},{2,3},{3,4},{4,5},{5,6},{6,7},{8,9},{9,10},{10,11},{11... | collective-permute-start | bytes 3145736 | tf_op jit(solution)/shard_map/ppermute | solution.py:70
  68.9 43.4 %copy-start.3 = (f32[1,8,128,256]{3,2,1,0:T(8,128)S(1)}, f32[1,8,128,256]{3,2,1,0:T(8,128)}, u32[]{:S(2)}) copy-start(f32[1,8,128,256]{3,2,1,0:T(8,128)} %param.15) | copy-start | bytes 3145732
  68.9 43.4 %copy-start.5 = (f32[1,1024,256]{2,1,0:T(8,128)S(1)}, f32[1,1024,256]{2,1,0:T(8,128)}, u32[]{:S(2)}) copy-start(f32[1,1024,256]{2,1,0:T(8,128)} %get-tuple-element.17) | copy-start | bytes 3145732
  68.9 43.4 %copy-start.6 = (f32[1,1024,256]{2,1,0:T(8,128)S(1)}, f32[1,1024,256]{2,1,0:T(8,128)}, u32[]{:S(2)}) copy-start(f32[1,1024,256]{2,1,0:T(8,128)} %get-tuple-element.15) | copy-start | bytes 3145732
  68.9 43.4 %copy-start.17 = (f32[8,128,256]{2,1,0:T(8,128)S(1)}, f32[8,128,256]{2,1,0:T(8,128)}, u32[]{:S(2)}) copy-start(f32[8,128,256]{2,1,0:T(8,128)} %param.16) | copy-start | bytes 3145732
  122.9 2.0 %collective-permute-start.4 = (f32[8,2,32,256]{3,0,2,1:T(8,128)S(1)}, f32[8,2,32,256]{3,0,2,1:T(8,128)S(1)}, u32[]{:S(2)}, u32[]{:S(2)}) collective-permute-start(f32[8,2,32,256]{3,0,2,1:T(8,128)S(1)} %bitcast.146), channel_id=1, source_target_pairs={{0,8},{8,0},{16,24},{24,16},{1,9},{9,1},{17,25},{25,17},{2,10},{10... | collective-permute-start | bytes 1572872 | tf_op jit(solution)/shard_map/ppermute | solution.py:120
  125.2 8.4 %collective-permute-start.5 = (f32[8,1,32,256]{3,0,2,1:T(8,128)S(1)}, f32[8,1,32,256]{3,0,2,1:T(8,128)S(1)}, u32[]{:S(2)}, u32[]{:S(2)}) collective-permute-start(f32[8,1,32,256]{3,0,2,1:T(8,128)S(1)} %constant_dynamic-slice_fusion), channel_id=1, source_target_pairs={{0,16},{8,24},{16,0},{24,8},{1,17},{9,25},{17,1},{25,9},{2,18},{10... | collective-permute-start | bytes 786440 | tf_op jit(solution)/shard_map/ppermute | solution.py:120

commit v7 on v6

--- a/solution.py
+++ b/solution.py
@@ -122,6 +122,50 @@
     return blocks.reshape(shape[:dim] + (length // devices,) + shape[dim + 1 :])
 
 
+def halves(current, earlier, courant, terms, zaxis):
+    planes = current.shape[zaxis]
+    lateral = lateral_laplace(current, zaxis)
+    low = lambda a, lo=0: lax.slice_in_dim(a, lo, lo + HALO, axis=a.ndim - 3)
+    parts = []
+    for first, sign in ((0, 1), (planes - HALO, -1)):
+        inner = None
+        for k in range(1, 5):
+            piece = COEFFS[k] * low(current, first + sign * k)
+            inner = piece if inner is None else inner + piece
+        update = (
+            2.0 * low(current, first)
+            - low(earlier, first)
+            + low(courant, first) * (low(lateral, first) + inner)
+            + low(terms, first)
+        )
+        parts.append(update)
+    return parts
+
+
+def finish_low(partial, current, below, courant, zaxis):
+    extended = jnp.concatenate([below, lax.slice_in_dim(current, 0, HALO, axis=zaxis)], axis=zaxis)
+    outer = None
+    for k in range(1, 5):
+        piece = COEFFS[k] * lax.slice_in_dim(extended, HALO - k, 2 * HALO - k, axis=zaxis)
+        outer = piece if outer is None else outer + piece
+    return partial + courant[:HALO] * outer
+
+
+def finish_high(partial, current, above, courant, zaxis):
+    planes = current.shape[zaxis]
+    extended = jnp.concatenate([lax.slice_in_dim(current, planes - HALO, planes, axis=zaxis), above], axis=zaxis)
+    outer = None
+    for k in range(1, 5):
+        piece = COEFFS[k] * lax.slice_in_dim(extended, k, k + HALO, axis=zaxis)
+        outer = piece if outer is None else outer + piece
+    return partial + courant[planes - HALO :] * outer
+
+
+def gradient_part(correlation):
+    reduced = reduce_shots(smooth(smooth(correlation, 1), 2), 1)
+    return lax.all_to_all(reduced, "depth", split_axis=1, concat_axis=0, tiled=True)
+
+
 def on_device(
     forward_prev,
     forward_now,
@@ -137,38 +181,42 @@
     residual_traces,
 ):
     planes, rows, cols = courant.shape
-    lateral = rows * cols
-    source_flat = source_depth * lateral + source_cell
-    receiver_flat = receiver_depth * lateral + receiver_cell
+    assert planes == 2 * HALO and STEPS == 2
     signs = (2 * sign_bits - 1).astype(jnp.float32)
     position = lax.axis_index("depth")
+    devices = lax.axis_size("depth")
+    up = [(i, i + 1) for i in range(devices - 1)]
+    down = [(i + 1, i) for i in range(devices - 1)]
     earlier = jnp.stack([forward_prev, adjoint_prev])
     current = jnp.stack([forward_now, adjoint_now])
     zaxis = 2
-    below, above = exchange(current, zaxis)
     first_plane = position * planes
-    correlation = None
     forward_terms = spread_dense(source_depth, source_cell, signs[0][None, :] * wavelet, first_plane, planes, rows, cols)
     adjoint_terms = spread_dense(receiver_depth, receiver_cell, residual_traces[0], first_plane, planes, rows, cols)
-    for step in range(STEPS):
-        terms = jnp.stack([forward_terms[step : step + 1], adjoint_terms[step : step + 1]])
-        lateral_part = lateral_laplace(current, zaxis)
-        fresh = (
-            2.0 * current
-            - earlier
-            + courant * (lateral_part + depth_laplace(below, current, above, zaxis))
-            + terms
-        )
-        if step + 1 < STEPS:
-            below, above = exchange(fresh, zaxis)
-        part = fresh[0, 0] * fresh[1, 0]
-        correlation = part if correlation is None else correlation + part
-        earlier, current = (current, fresh)
-    lateral_smooth = smooth(smooth(correlation, 1), 2)
-    reduced = reduce_shots(lateral_smooth, 1)
-    columns = lax.all_to_all(reduced, "depth", split_axis=1, concat_axis=0, tiled=True)
+    terms = [jnp.stack([forward_terms[t : t + 1], adjoint_terms[t : t + 1]]) for t in range(STEPS)]
+
+    below = lax.ppermute(lax.slice_in_dim(current, HALO, planes, axis=zaxis), "depth", up)
+    above = lax.ppermute(lax.slice_in_dim(current, 0, HALO, axis=zaxis), "depth", down)
+    part_low, part_high = lax.optimization_barrier(halves(current, earlier, courant, terms[0], zaxis))
+    first_low = finish_low(part_low, current, below, courant, zaxis)
+    next_above = lax.ppermute(first_low, "depth", down)
+    first_high = finish_high(part_high, current, above, courant, zaxis)
+    next_below = lax.ppermute(first_high, "depth", up)
+    first = jnp.concatenate([first_low, first_high], axis=zaxis)
+
+    part_low, part_high = lax.optimization_barrier(halves(first, current, courant, terms[1], zaxis))
+    second_high = finish_high(part_high, first, next_above, courant, zaxis)
+    high = gradient_part(first_high[0, 0] * first_high[1, 0] + second_high[0, 0] * second_high[1, 0])
+    second_low = finish_low(part_low, first, next_below, courant, zaxis)
+    second = jnp.concatenate([second_low, second_high], axis=zaxis)
+
+    low = gradient_part(first_low[0, 0] * first_low[1, 0] + second_low[0, 0] * second_low[1, 0])
+    width = low.shape[1]
+    columns = jnp.stack(
+        [low.reshape(devices, HALO, width, cols), high.reshape(devices, HALO, width, cols)], axis=1
+    ).reshape(devices * planes, width, cols)
     gradient = smooth(columns, 0)
-    return (earlier[0], current[0], earlier[1], current[1], gradient)
+    return (first[0], second[0], first[1], second[1], gradient)
 
 
 def solution(mesh):

time: 149 us -> 177 us (1.19)
  other arithmetic: 11.6 us -> 26.7 us
  starting transfers between devices: 16.7 us -> 31.5 us
  blocking collectives: 14.1 us -> 0 us
  waiting for transfers between devices: 68.6 us -> 77.1 us
  local copies, waits for them, and re-layouts: 6.28 us -> 11.9 us
  matrix products: 30.5 us -> 27.9 us
    all_to_all x0 -> x2, starting transfers between devices: none -> 14.6 us  [gradient_part(): lax.all_to_all(reduced, 'depth', split_axis=1, concat_axis=0, tiled=True)]
    all_to_all x1 -> x0, blocking collectives: 14.1 us -> none  [on_device(): lax.all_to_all(reduced, 'depth', split_axis=1, concat_axis=0, tiled=True)]
    add x1 -> x10, other arithmetic: 2.36 us -> 14.1 us  [the longest x4 7.1 us: halves(): 2.0 * low(current, first) - low(earlier, first)]
    all_to_all x0 -> x2, waiting for transfers between devices: none -> 9.91 us  [gradient_part(): lax.all_to_all(reduced, 'depth', split_axis=1, concat_axis=0, tiled=True)]
    ppermute x2 -> x4, waiting for transfers between devices: 8.72 us -> 1.86 us  [reduce_shots(): blocks = keep + lax.ppermute(send, 'shots', pairs)]
    ppermute x4, waiting for transfers between devices: 59.9 us -> 65.3 us  [the longest x1 33.7 us: on_device(): next_below = lax.ppermute(first_high, 'depth', up)]
    dot_general x2, matrix products: 8.88 us -> 5.48 us  [lateral_laplace(): along_y = jnp.einsum('...xy,yk->...xk', core, band(cols), precision=high)]
    squeeze x0 -> x2, other arithmetic: none -> 3.09 us  [on_device(): return (first[0], second[0], first[1], second[1], gradient)]
  transfers between devices with their start and end apart: 6 -> 10, of which waited for: 5 -> 7; matrix products, arithmetic and copies ran while one was open for 18% -> 15% of each run, Pallas kernels for 0% -> 0%
where the time goes in v7:
time: 177 us; the launch traced here: 176 us
  waiting for transfers between devices  77.1 us (44%)
  starting transfers between devices  31.5 us (18%)
  matrix products  27.9 us (16%)
  other arithmetic  26.7 us (15%)
  local copies, waits for them, and re-layouts  11.9 us (7%)
    ppermute x1, waiting for transfers between devices, on_device(): next_below = lax.ppermute(first_high, 'depth', up)  33.7 us
    ppermute x1, waiting for transfers between devices, on_device(): lax.ppermute(lax.slice_in_dim(current, 0, HALO, axis=zaxis), 'depth', down)  16.8 us
    dot_general x2, matrix products, spread_dense(): grid = jnp.dot(by_row, right, preferred_element_type=jnp.float32)  16.4 us
    ppermute x1, waiting for transfers between devices, on_device(): lax.ppermute(lax.slice_in_dim(current, HALO, planes, axis=zaxis), 'depth'...  14.9 us
    all_to_all x2, starting transfers between devices, gradient_part(): lax.all_to_all(reduced, 'depth', split_axis=1, concat_axis=0, tiled=True)  14.6 us
    all_to_all x2, waiting for transfers between devices, gradient_part(): lax.all_to_all(reduced, 'depth', split_axis=1, concat_axis=0, tiled=True)  9.91 us
    add x4, other arithmetic, halves(): 2.0 * low(current, first) - low(earlier, first)  7.1 us
    ppermute x1, starting transfers between devices, on_device(): lax.ppermute(lax.slice_in_dim(current, HALO, planes, axis=zaxis), 'depth'...  6.5 us
  transfers between devices with their start and end apart: 10, of which 7 were waited for; matrix products, arithmetic and copies ran while one was open for 15% of the time, Pallas kernels for 0%

profile of v7, /device:TPU:0, one launch (start us, length us, event | category | flops | bytes accessed | tf_op | source)
XLA Modules:
  0.0 176.3 jit_solution(9638097957117569298)
XLA Ops:
  0.7 3.6 %fusion.17 = f32[2,8,128,256]{3,2,1,0:T(8,128)S(1)} fusion(f32[1,1,8,128,256]{4,3,2,0,1:T(8,128)} %bitcast.172, f32[1,1,8,128,256]{4,3,2,0,1:T(8,128)} %bitcast.177), kind=kOutput, calls=%fused_computation.62 | convolution fusion | flops 1611792384 | bytes 4194304 | tf_op jit(solution)/shard_map/...xy,yk->...xk/dot_general | solution.py:39
  4.5 3.7 %fusion.12 = f32[2,1,8,128,256]{4,3,2,1,0:T(8,128)} fusion(f32[2,8,128,256]{3,2,1,0:T(8,128)S(1)} %fusion.17, f32[1,1,8,128,256]{4,3,2,0,1:T(8,128)S(1)} %bitcast.174, f32[1,1,8,128,256]{4,3,2,0,1:T(8,128)S(1)} %bitcast.179), kind=kOutput, calls=%fused_computation.57 | convolution fusion | flops 808091648 | bytes 6291456 | tf_op jit(solution)/shard_map/...xy,kx->...ky/dot_general | solution.py:40
  8.3 1.6 iota_compare_fusion.1
  10.0 14.6 %fusion.1 = f32[1024,3,2,256]{3,0,2,1:T(8,128)S(1)} fusion(pred[4096,256]{0,1:T(8,128)(4,1)} %iota_compare_fusion.1, s32[4096]{0:T(1024)S(1)} %get-tuple-element.53, bf16[4096,3,2]{0,2,1:T(2,128)(2,1)S(1)} %maximum_bitcast_fusion), kind=kOutput, calls=%fused_computation.2 | convolution fusion | flops 12895387648 | bytes 7405568 | tf_op jit(solution)/shard_map/dot_general | solution.py:100
  25.0 1.1 fusion.218
  26.3 1.8 %fusion.22 = f32[1024,3,2,256]{3,0,2,1:T(8,128)S(1)} fusion(pred[512,256]{0,1:T(8,128)(4,1)S(1)} %iota_compare_fusion.3, s32[512]{0:T(512)S(1)} %get-tuple-element.58, bf16[512,3,2]{0,2,1:T(2,128)(2,1)S(1)} %maximum_bitcast_fusion.1), kind=kOutput, calls=%fused_computation.68 | convolution fusion | flops 1611923456 | bytes 6430720 | tf_op jit(solution)/shard_map/dot_general | solution.py:100
  28.6 1.1 fusion.219
  32.7 2.2 %fusion.99 = (f32[2,1,4,128,256]{4,3,2,1,0:T(8,128)}, f32[2,1,4,128,256]{4,3,2,1,0:T(8,128)}, f32[2,1,4,128,256]{4,3,2,1,0:T(8,128)}) fusion(f32[1,1,8,128,256]{4,3,2,1,0:T(8,128)S(1)} %bitcast.187, f32[1,1,8,128,256]{4,3,2,1,0:T(8,128)S(1)} %bitcast.189, f32[2,1,8,128,256]{4,3,2,1,0:T(8,128)S(1)} %copy-done.15, f32[1,1,8,128,256]{4,3,2,1,0:T(8,128)S(1)} %bitcast.196, ...), kind=kLoop, calls=%fused_computation.149 | loop fusion | flops 4194304 | bytes 15204352 | tf_op jit(solution)/shard_map/add | solution.py:136
  34.8 1.3 collective-permute-start.1
  36.1 6.5 %collective-permute-start = (f32[2,1,4,128,256]{4,3,2,1,0:T(8,128)}, f32[2,1,4,128,256]{4,3,2,1,0:T(8,128)}, u32[]{:S(2)}, u32[]{:S(2)}) collective-permute-start(f32[2,1,4,128,256]{4,3,2,1,0:T(8,128)} %get-tuple-element.14), channel_id=1, source_target_pairs={{0,1},{1,2},{2,3},{3,4},{4,5},{5,6},{6,7},{8,9},{9,10},{10,11},{11... | collective-permute-start | bytes 3145736 | tf_op jit(solution)/shard_map/ppermute | solution.py:198
  42.6 3.7 %fusion.37 = f32[2,1,4,128,256]{4,3,2,1,0:T(8,128)} fusion(f32[1,1,8,128,256]{4,3,2,1,0:T(8,128)} %bitcast.190, f32[1,1,8,128,256]{4,3,2,1,0:T(8,128)} %bitcast.188, f32[1,1,8,128,256]{4,3,2,1,0:T(8,128)} %bitcast.193, f32[1,1,8,128,256]{4,3,2,1,0:T(8,128)} %bitcast.195, f32[2,1,8,128,256]{4,3,2,1,0:T(8,128)} %fusion.12, ...), kind=kLoop, calls=%fused_computation.78 | loop fusion | flops 3932160 | bytes 12058624 | tf_op jit(solution)/shard_map/add | solution.py:136
  46.4 16.8 %collective-permute-done.1 = f32[2,1,4,128,256]{4,3,2,1,0:T(8,128)} collective-permute-done((f32[2,1,4,128,256]{4,3,2,1,0:T(8,128)}, f32[2,1,4,128,256]{4,3,2,1,0:T(8,128)}, u32[]{:S(2)}, u32[]{:S(2)}) %collective-permute-start.1) | collective-permute-done | bytes 1048608 | tf_op jit(solution)/shard_map/ppermute | solution.py:199
  63.1 3.1 %fusion.66 = f32[2,1,4,128,256]{4,3,2,1,0:T(8,128)S(1)} fusion(f32[2,1,4,128,256]{4,3,2,1,0:T(8,128)} %get-tuple-element.10, f32[2,1,4,128,256]{4,3,2,1,0:T(8,128)} %get-tuple-element.14, f32[2,1,4,128,256]{4,3,2,1,0:T(8,128)} %collective-permute-done.1, f32[4,128,256]{2,1,0:T(8,128)} %copy-done.7), kind=kLoop, calls=%fused_computation.107 | loop fusion | flops 3145728 | bytes 4718592 | tf_op jit(solution)/shard_map/add | solution.py:161
  66.3 4.7 %collective-permute-start.2 = (f32[2,1,4,128,256]{4,3,2,1,0:T(8,128)S(1)}, f32[2,1,4,128,256]{4,3,2,1,0:T(8,128)S(1)}, u32[]{:S(2)}, u32[]{:S(2)}) collective-permute-start(f32[2,1,4,128,256]{4,3,2,1,0:T(8,128)S(1)} %fusion.66), channel_id=1, source_target_pairs={{0,1},{1,2},{2,3},{3,4},{4,5},{5,6},{6,7},{8,9},{9,10},{10,11},{11... | collective-permute-start | bytes 3145736 | tf_op jit(solution)/shard_map/ppermute | solution.py:204
  71.0 14.9 %collective-permute-done = f32[2,1,4,128,256]{4,3,2,1,0:T(8,128)} collective-permute-done((f32[2,1,4,128,256]{4,3,2,1,0:T(8,128)}, f32[2,1,4,128,256]{4,3,2,1,0:T(8,128)}, u32[]{:S(2)}, u32[]{:S(2)}) %collective-permute-start) | collective-permute-done | bytes 1048608 | tf_op jit(solution)/shard_map/ppermute | solution.py:198
  85.9 2.8 %fusion.75 = f32[2,1,4,128,256]{4,3,2,1,0:T(8,128)S(1)} fusion(f32[2,1,4,128,256]{4,3,2,1,0:T(8,128)S(1)} %copy-done.16, f32[2,1,4,128,256]{4,3,2,1,0:T(8,128)} %collective-permute-done, f32[2,1,4,128,256]{4,3,2,1,0:T(8,128)} %get-tuple-element.23, f32[4,128,256]{2,1,0:T(8,128)S(1)} %copy-done.6), kind=kLoop, calls=%fused_computation.116 | loop fusion | flops 3145728 | bytes 4718592 | tf_op jit(solution)/shard_map/add | solution.py:151
  88.7 1.9 %fusion.13 = f32[2,8,128,256]{3,2,1,0:T(8,128)S(1)} fusion(f32[2,1,4,128,256]{4,3,2,1,0:T(8,128)S(1)} %fusion.66, f32[2,1,4,128,256]{4,3,2,1,0:T(8,128)S(1)} %fusion.75), kind=kOutput, calls=%fused_computation.58 | convolution fusion | flops 1611792384 | bytes 4194304 | tf_op jit(solution)/shard_map/...xy,yk->...xk/dot_general | solution.py:39
  90.6 1.8 %collective-permute-start.3 = (f32[2,1,4,128,256]{4,3,2,1,0:T(8,128)S(1)}, f32[2,1,4,128,256]{4,3,2,1,0:T(8,128)S(1)}, u32[]{:S(2)}, u32[]{:S(2)}) collective-permute-start(f32[2,1,4,128,256]{4,3,2,1,0:T(8,128)S(1)} %fusion.75), channel_id=1, source_target_pairs={{1,0},{2,1},{3,2},{4,3},{5,4},{6,5},{7,6},{9,8},{10,9},{11,10},{12... | collective-permute-start | bytes 3145736 | tf_op jit(solution)/shard_map/ppermute | solution.py:202
  92.4 2.3 %fusion.11 = f32[2,1,8,128,256]{4,3,2,1,0:T(8,128)S(1)} fusion(f32[2,8,128,256]{3,2,1,0:T(8,128)S(1)} %fusion.13, f32[2,1,4,128,256]{4,3,2,1,0:T(8,128)S(1)} %fusion.66, f32[2,1,4,128,256]{4,3,2,1,0:T(8,128)S(1)} %fusion.75), kind=kOutput, calls=%fused_computation.55 | convolution fusion | flops 808091648 | bytes 6291456 | tf_op jit(solution)/shard_map/...xy,kx->...ky/dot_general | solution.py:40
  96.9 33.7 %collective-permute-done.2 = f32[2,1,4,128,256]{4,3,2,1,0:T(8,128)S(1)} collective-permute-done((f32[2,1,4,128,256]{4,3,2,1,0:T(8,128)S(1)}, f32[2,1,4,128,256]{4,3,2,1,0:T(8,128)S(1)}, u32[]{:S(2)}, u32[]{:S(2)}) %collective-permute-start.2) | collective-permute-done | bytes 1048608 | tf_op jit(solution)/shard_map/ppermute | solution.py:204
  136.5 1.1 copy.79
  138.4 1.2 bitcast_add_fusion.3
  139.5 1.6 collective-permute-start.5
  141.1 1.2 bitcast_add_fusion.2
  143.5 1.7 collective-permute-done.5
  145.8 11.2 %all-to-all-start = ((f32[4,32,256]{2,0,1:T(4,128)}), f32[4,32,256]{2,0,1:T(4,128)S(1)}, u32[]{:S(2)}, u32[]{:S(2)}) async-start(f32[4,32,256]{2,0,1:T(4,128)} %add_bitcast_fusion.1), calls=%async_computation | async-start | bytes 262144 | tf_op jit(solution)/shard_map/all_to_all | solution.py:166
  157.1 1.6 add_bitcast_fusion
  158.7 5.7 %all-to-all-done = f32[4,32,256]{2,0,1:T(4,128)S(1)} async-done(((f32[4,32,256]{2,0,1:T(4,128)}), f32[4,32,256]{2,0,1:T(4,128)S(1)}, u32[]{:S(2)}, u32[]{:S(2)}) %all-to-all-start) | async-done | bytes 131104 | tf_op jit(solution)/shard_map/all_to_all | solution.py:166
  164.4 3.4 %all-to-all-start.1 = ((f32[4,32,256]{2,0,1:T(4,128)}), f32[4,32,256]{2,0,1:T(4,128)S(1)}, u32[]{:S(2)}, u32[]{:S(2)}) async-start(f32[4,32,256]{2,0,1:T(4,128)} %add_bitcast_fusion), calls=%async_computation.1 | async-start | bytes 262144 | tf_op jit(solution)/shard_map/all_to_all | solution.py:166
  167.8 1.5 fusion.86
  169.3 1.6 fusion.87
  170.9 4.2 %all-to-all-done.1 = f32[4,32,256]{2,0,1:T(4,128)S(1)} async-done(((f32[4,32,256]{2,0,1:T(4,128)}), f32[4,32,256]{2,0,1:T(4,128)S(1)}, u32[]{:S(2)}, u32[]{:S(2)}) %all-to-all-start.1) | async-done | bytes 131104 | tf_op jit(solution)/shard_map/all_to_all | solution.py:166
  (101 shorter events, 16.2 us)
Async XLA Ops:
  0.6 3.6 %copy-start.2 = (f32[1,8,128,256]{3,2,1,0:T(8,128)S(1)}, f32[1,8,128,256]{3,2,1,0:T(8,128)}, u32[]{:S(2)}) copy-start(f32[1,8,128,256]{3,2,1,0:T(8,128)} %param.15) | copy-start | bytes 3145732
  0.6 3.6 %copy-start.3 = (f32[1,8,128,256]{3,2,1,0:T(8,128)S(1)}, f32[1,8,128,256]{3,2,1,0:T(8,128)}, u32[]{:S(2)}) copy-start(f32[1,8,128,256]{3,2,1,0:T(8,128)} %param.13) | copy-start | bytes 3145732
  4.5 38.1 %copy-start = (f32[2,1,8,128,256]{4,3,2,1,0:T(8,128)}, f32[2,1,8,128,256]{4,3,2,1,0:T(8,128)S(1)}, u32[]{:S(2)}) copy-start(f32[2,1,8,128,256]{4,3,2,1,0:T(8,128)S(1)} %fusion.31) | copy-start | bytes 6291460
  4.5 3.7 %copy-start.20 = (f32[1,2,4096]{2,1,0:T(2,128)S(1)}, f32[1,2,4096]{2,1,0:T(2,128)}, u32[]{:S(2)}) copy-start(f32[1,2,4096]{2,1,0:T(2,128)} %param.23) | copy-start | bytes 98308
  4.5 3.7 %copy-start.21 = (s32[4096]{0:T(1024)S(1)}, s32[4096]{0:T(1024)}, u32[]{:S(2)}) copy-start(s32[4096]{0:T(1024)} %param.22) | copy-start | bytes 49156
  4.5 3.7 %copy-start.22 = (s32[4096]{0:T(1024)S(1)}, s32[4096]{0:T(1024)}, u32[]{:S(2)}) copy-start(s32[4096]{0:T(1024)} %param.21) | copy-start | bytes 49156
  26.1 4.9 %copy-start.13 = (f32[1,1024,256]{2,1,0:T(8,128)}, f32[1,1024,256]{2,1,0:T(8,128)S(1)}, u32[]{:S(2)}) copy-start(f32[1,1024,256]{2,1,0:T(8,128)S(1)} %get-tuple-element.20) | copy-start | bytes 3145732
  28.5 1.6 copy-start.19
  28.6 2.5 %copy-start.15 = (f32[2,1,8,128,256]{4,3,2,1,0:T(8,128)S(1)}, f32[2,1,8,128,256]{4,3,2,1,0:T(8,128)}, u32[]{:S(2)}) copy-start(f32[2,1,8,128,256]{4,3,2,1,0:T(8,128)} %fusion.12) | copy-start | bytes 6291460
  28.6 2.7 %copy-start.18 = (f32[1,8,128,256]{3,2,1,0:T(8,128)S(1)}, f32[1,8,128,256]{3,2,1,0:T(8,128)}, u32[]{:S(2)}) copy-start(f32[1,8,128,256]{3,2,1,0:T(8,128)} %param.14) | copy-start | bytes 3145732
  30.1 4.7 %copy-start.14 = (f32[1,1024,256]{2,1,0:T(8,128)}, f32[1,1024,256]{2,1,0:T(8,128)S(1)}, u32[]{:S(2)}) copy-start(f32[1,1024,256]{2,1,0:T(8,128)S(1)} %get-tuple-element.22) | copy-start | bytes 3145732
  30.1 2.1 %copy-start.4 = (f32[1,8,128,256]{3,2,1,0:T(8,128)S(1)}, f32[1,8,128,256]{3,2,1,0:T(8,128)}, u32[]{:S(2)}) copy-start(f32[1,8,128,256]{3,2,1,0:T(8,128)} %param.13) | copy-start | bytes 3145732
  30.1 2.5 %copy-start.17 = (f32[1,8,128,256]{3,2,1,0:T(8,128)S(1)}, f32[1,8,128,256]{3,2,1,0:T(8,128)}, u32[]{:S(2)}) copy-start(f32[1,8,128,256]{3,2,1,0:T(8,128)} %param.12) | copy-start | bytes 3145732
  31.0 3.8 %copy-start.7 = (f32[4,128,256]{2,1,0:T(8,128)}, f32[4,128,256]{2,1,0:T(8,128)S(1)}, u32[]{:S(2)}) copy-start(f32[4,128,256]{2,1,0:T(8,128)S(1)} %get-tuple-element.25) | copy-start | bytes 1572868
  34.8 28.3 %collective-permute-start.1 = (f32[2,1,4,128,256]{4,3,2,1,0:T(8,128)}, f32[2,1,4,128,256]{4,3,2,1,0:T(8,128)}, u32[]{:S(2)}, u32[]{:S(2)}) collective-permute-start(f32[2,1,4,128,256]{4,3,2,1,0:T(8,128)} %get-tuple-element.23), channel_id=1, source_target_pairs={{1,0},{2,1},{3,2},{4,3},{5,4},{6,5},{7,6},{9,8},{10,9},{11,10},{12... | collective-permute-start | bytes 3145736 | tf_op jit(solution)/shard_map/ppermute | solution.py:199
  36.1 49.8 %collective-permute-start = (f32[2,1,4,128,256]{4,3,2,1,0:T(8,128)}, f32[2,1,4,128,256]{4,3,2,1,0:T(8,128)}, u32[]{:S(2)}, u32[]{:S(2)}) collective-permute-start(f32[2,1,4,128,256]{4,3,2,1,0:T(8,128)} %get-tuple-element.14), channel_id=1, source_target_pairs={{0,1},{1,2},{2,3},{3,4},{4,5},{5,6},{6,7},{8,9},{9,10},{10,11},{11... | collective-permute-start | bytes 3145736 | tf_op jit(solution)/shard_map/ppermute | solution.py:198
  46.4 39.5 %copy-start.6 = (f32[4,128,256]{2,1,0:T(8,128)S(1)}, f32[4,128,256]{2,1,0:T(8,128)}, u32[]{:S(2)}) copy-start(f32[4,128,256]{2,1,0:T(8,128)} %get-tuple-element.24) | copy-start | bytes 1572868
  46.4 39.5 %copy-start.16 = (f32[2,1,4,128,256]{4,3,2,1,0:T(8,128)S(1)}, f32[2,1,4,128,256]{4,3,2,1,0:T(8,128)}, u32[]{:S(2)}) copy-start(f32[2,1,4,128,256]{4,3,2,1,0:T(8,128)} %fusion.37) | copy-start | bytes 3145732
  66.3 64.3 %collective-permute-start.2 = (f32[2,1,4,128,256]{4,3,2,1,0:T(8,128)S(1)}, f32[2,1,4,128,256]{4,3,2,1,0:T(8,128)S(1)}, u32[]{:S(2)}, u32[]{:S(2)}) collective-permute-start(f32[2,1,4,128,256]{4,3,2,1,0:T(8,128)S(1)} %fusion.66), channel_id=1, source_target_pairs={{0,1},{1,2},{2,3},{3,4},{4,5},{5,6},{6,7},{8,9},{9,10},{10,11},{11... | collective-permute-start | bytes 3145736 | tf_op jit(solution)/shard_map/ppermute | solution.py:204
  90.6 4.2 %copy-start.5 = (f32[1,8,128,256]{3,2,1,0:T(8,128)S(1)}, f32[1,8,128,256]{3,2,1,0:T(8,128)}, u32[]{:S(2)}) copy-start(f32[1,8,128,256]{3,2,1,0:T(8,128)} %param.13) | copy-start | bytes 3145732
  90.6 4.2 %copy-start.8 = (f32[4,128,256]{2,1,0:T(8,128)S(1)}, f32[4,128,256]{2,1,0:T(8,128)}, u32[]{:S(2)}) copy-start(f32[4,128,256]{2,1,0:T(8,128)} %copy-done.7) | copy-start | bytes 1572868
  90.6 4.2 %copy-start.9 = (f32[1,1024,256]{2,1,0:T(8,128)S(1)}, f32[1,1024,256]{2,1,0:T(8,128)}, u32[]{:S(2)}) copy-start(f32[1,1024,256]{2,1,0:T(8,128)} %get-tuple-element.19) | copy-start | bytes 3145732
  90.6 4.2 %copy-start.10 = (f32[1,1024,256]{2,1,0:T(8,128)S(1)}, f32[1,1024,256]{2,1,0:T(8,128)}, u32[]{:S(2)}) copy-start(f32[1,1024,256]{2,1,0:T(8,128)} %get-tuple-element.21) | copy-start | bytes 3145732
  90.6 41.3 %collective-permute-start.3 = (f32[2,1,4,128,256]{4,3,2,1,0:T(8,128)S(1)}, f32[2,1,4,128,256]{4,3,2,1,0:T(8,128)S(1)}, u32[]{:S(2)}, u32[]{:S(2)}) collective-permute-start(f32[2,1,4,128,256]{4,3,2,1,0:T(8,128)S(1)} %fusion.75), channel_id=1, source_target_pairs={{1,0},{2,1},{3,2},{4,3},{5,4},{6,5},{7,6},{9,8},{10,9},{11,10},{12... | collective-permute-start | bytes 3145736 | tf_op jit(solution)/shard_map/ppermute | solution.py:202
  94.8 1.6 copy-start.1
  136.5 1.9 %collective-permute-start.4 = (f32[4,2,32,256]{3,0,2,1:T(4,128)}, f32[4,2,32,256]{3,0,2,1:T(4,128)}, u32[]{:S(2)}, u32[]{:S(2)}) collective-permute-start(f32[4,2,32,256]{3,0,2,1:T(4,128)} %bitcast.171), channel_id=1, source_target_pairs={{0,8},{8,0},{16,24},{24,16},{1,9},{9,1},{17,25},{25,17},{2,10},{10... | collective-permute-start | bytes 786440 | tf_op jit(solution)/shard_map/ppermute | solution.py:120
  137.6 3.5 %collective-permute-start.6 = (f32[4,2,32,256]{3,0,2,1:T(4,128)S(1)}, f32[4,2,32,256]{3,0,2,1:T(4,128)S(1)}, u32[]{:S(2)}, u32[]{:S(2)}) collective-permute-start(f32[4,2,32,256]{3,0,2,1:T(4,128)S(1)} %bitcast.201), channel_id=1, source_target_pairs={{0,8},{8,0},{16,24},{24,16},{1,9},{9,1},{17,25},{25,17},{2,10},{10... | collective-permute-start | bytes 786440 | tf_op jit(solution)/shard_map/ppermute | solution.py:120
  139.5 5.6 %collective-permute-start.5 = (f32[4,1,32,256]{3,0,2,1:T(4,128)S(1)}, f32[4,1,32,256]{3,0,2,1:T(4,128)S(1)}, u32[]{:S(2)}, u32[]{:S(2)}) collective-permute-start(f32[4,1,32,256]{3,0,2,1:T(4,128)S(1)} %constant_dynamic-slice_fusion.3), channel_id=1, source_target_pairs={{0,16},{8,24},{16,0},{24,8},{1,17},{9,25},{17,1},{25,9},{2,18},{10... | collective-permute-start | bytes 393224 | tf_op jit(solution)/shard_map/ppermute | solution.py:120
  142.9 14.1 %collective-permute-start.7 = (f32[4,1,32,256]{3,0,2,1:T(4,128)}, f32[4,1,32,256]{3,0,2,1:T(4,128)}, u32[]{:S(2)}, u32[]{:S(2)}) collective-permute-start(f32[4,1,32,256]{3,0,2,1:T(4,128)} %constant_dynamic-slice_fusion), channel_id=1, source_target_pairs={{0,16},{8,24},{16,0},{24,8},{1,17},{9,25},{17,1},{25,9},{2,18},{10... | collective-permute-start | bytes 393224 | tf_op jit(solution)/shard_map/ppermute | solution.py:120
  145.8 18.6 %all-to-all-start = ((f32[4,32,256]{2,0,1:T(4,128)}), f32[4,32,256]{2,0,1:T(4,128)S(1)}, u32[]{:S(2)}, u32[]{:S(2)}) async-start(f32[4,32,256]{2,0,1:T(4,128)} %add_bitcast_fusion.1), calls=%async_computation | async-start | bytes 262144 | tf_op jit(solution)/shard_map/all_to_all | solution.py:166
  164.4 10.7 %all-to-all-start.1 = ((f32[4,32,256]{2,0,1:T(4,128)}), f32[4,32,256]{2,0,1:T(4,128)S(1)}, u32[]{:S(2)}, u32[]{:S(2)}) async-start(f32[4,32,256]{2,0,1:T(4,128)} %add_bitcast_fusion), calls=%async_computation.1 | async-start | bytes 262144 | tf_op jit(solution)/shard_map/all_to_all | solution.py:166
  167.8 1.6 copy-start.12
  (5 other events, 5.7 us)

commit v8 on v6

--- a/solution.py
+++ b/solution.py
@@ -152,13 +152,10 @@
     adjoint_terms = spread_dense(receiver_depth, receiver_cell, residual_traces[0], first_plane, planes, rows, cols)
     for step in range(STEPS):
         terms = jnp.stack([forward_terms[step : step + 1], adjoint_terms[step : step + 1]])
-        lateral_part = lateral_laplace(current, zaxis)
-        fresh = (
-            2.0 * current
-            - earlier
-            + courant * (lateral_part + depth_laplace(below, current, above, zaxis))
-            + terms
+        partial = lax.optimization_barrier(
+            2.0 * current - earlier + courant * lateral_laplace(current, zaxis) + terms
         )
+        fresh = partial + courant * depth_laplace(below, current, above, zaxis)
         if step + 1 < STEPS:
             below, above = exchange(fresh, zaxis)
         part = fresh[0, 0] * fresh[1, 0]

time: 149 us -> 145 us (0.973)
  matrix products: 30.5 us -> 25.1 us
  waiting for transfers between devices: 68.6 us -> 63.4 us
  other arithmetic: 11.6 us -> 16.7 us
  local copies, waits for them, and re-layouts: 6.28 us -> 8.28 us
    ppermute x2, waiting for transfers between devices: 18.8 us -> 0.01 us  [exchange(): above = lax.ppermute(leading, 'depth', down)]
    ppermute x2, waiting for transfers between devices: 41.1 us -> 54.7 us  [exchange(): below = lax.ppermute(last, 'depth', up)]
    add x0 -> x2, other arithmetic: none -> 5.64 us  [on_device(): fresh = partial + courant * depth_laplace(below, current, above, zaxis)]
    dot_general x2, matrix products: 8.88 us -> 5.05 us  [lateral_laplace(): along_y = jnp.einsum('...xy,yk->...xk', core, band(cols), precision=high)]
    unnamed x37 -> x35, local copies, waits for them, and re-layouts: 0.96 us -> 2.96 us
  transfers between devices with their start and end apart: 6 -> 6, of which waited for: 5 -> 4; matrix products, arithmetic and copies ran while one was open for 18% -> 20% of each run, Pallas kernels for 0% -> 0%
where the time goes in v8:
time: 145 us
  waiting for transfers between devices  63.4 us (44%)
  matrix products  25.1 us (17%)
  other arithmetic  16.7 us (12%)
  starting transfers between devices  16.3 us (11%)
  blocking collectives  14.1 us (10%)
  local copies, waits for them, and re-layouts  8.28 us (6%)
    ppermute x2, waiting for transfers between devices, exchange(): below = lax.ppermute(last, 'depth', up)  54.7 us
    dot_general x2, matrix products, spread_dense(): grid = jnp.dot(by_row, right, preferred_element_type=jnp.float32)  15.2 us
    all_to_all x1, blocking collectives, on_device(): lax.all_to_all(reduced, 'depth', split_axis=1, concat_axis=0, tiled=True)  14.1 us
    ppermute x2, starting transfers between devices, exchange(): below = lax.ppermute(last, 'depth', up)  11.9 us
    ppermute x2, waiting for transfers between devices, reduce_shots(): blocks = keep + lax.ppermute(send, 'shots', pairs)  8.72 us
    add x2, other arithmetic, on_device(): fresh = partial + courant * depth_laplace(below, current, above, zaxis)  5.64 us
    dot_general x2, matrix products, lateral_laplace(): along_y = jnp.einsum('...xy,yk->...xk', core, band(cols), precision=high)  5.05 us
    dot_general x2, matrix products, lateral_laplace(): along_x = jnp.einsum('...xy,kx->...ky', core, band(rows), precision=high)  4.85 us
  transfers between devices with their start and end apart: 6, of which 4 were waited for; matrix products, arithmetic and copies ran while one was open for 20% of the time, Pallas kernels for 0%

profile of v8, /device:TPU:0, one launch (start us, length us, event | category | flops | bytes accessed | tf_op | source)
XLA Modules:
  0.0 145.0 jit_solution(11306159083265508823)
XLA Ops:
  0.7 3.2 %fusion.62 = (f32[2,1,4,128,256]{4,3,2,0,1:T(8,128)}, f32[2,1,4,128,256]{4,3,2,0,1:T(8,128)}) fusion(f32[1,1,8,128,256]{4,3,2,0,1:T(8,128)} %bitcast.138, f32[1,1,8,128,256]{4,3,2,0,1:T(8,128)} %bitcast.133), kind=kLoop, calls=%fused_computation.94 | loop fusion | flops 524288 | bytes 4194304 | tf_op jit(solution)/shard_map/stack | solution.py:146
  3.8 1.3 collective-permute-start
  5.1 6.5 %collective-permute-start.1 = (f32[2,1,4,128,256]{4,3,2,0,1:T(8,128)}, f32[2,1,4,128,256]{4,3,2,0,1:T(8,128)}, u32[]{:S(2)}, u32[]{:S(2)}) collective-permute-start(f32[2,1,4,128,256]{4,3,2,0,1:T(8,128)} %get-tuple-element.24), channel_id=1, source_target_pairs={{0,1},{1,2},{2,3},{3,4},{4,5},{5,6},{6,7},{8,9},{9,10},{10,11},{11... | collective-permute-start | bytes 3145736 | tf_op jit(solution)/shard_map/ppermute | solution.py:70
  11.6 3.2 %fusion.50 = f32[2,8,128,256]{3,2,1,0:T(8,128)} fusion(f32[1,1,8,128,256]{4,3,2,0,1:T(8,128)S(1)} %bitcast.134, f32[1,1,8,128,256]{4,3,2,0,1:T(8,128)S(1)} %bitcast.139), kind=kOutput, calls=%fused_computation.84 | convolution fusion | flops 1611792384 | bytes 4194304 | tf_op jit(solution)/shard_map/...xy,yk->...xk/dot_general | solution.py:39
  14.9 0.6 iota_compare_fusion.1
  15.6 13.3 %fusion.1 = f32[1024,3,2,256]{3,0,2,1:T(8,128)S(1)} fusion(pred[4096,256]{0,1:T(8,128)(4,1)S(1)} %iota_compare_fusion.1, s32[4096]{0:T(1024)S(1)} %get-tuple-element.42, bf16[4096,3,2]{0,2,1:T(2,128)(2,1)S(1)} %maximum_bitcast_fusion), kind=kOutput, calls=%fused_computation.2 | convolution fusion | flops 12895387648 | bytes 7405568 | tf_op jit(solution)/shard_map/dot_general | solution.py:100
  29.0 0.4 fusion.37
  29.9 1.8 %fusion.55 = f32[1024,3,2,256]{3,0,2,1:T(8,128)S(1)} fusion(pred[512,256]{0,1:T(8,128)(4,1)S(1)} %iota_compare_fusion.3, s32[512]{0:T(512)S(1)} %get-tuple-element.47, bf16[512,3,2]{0,2,1:T(2,128)(2,1)S(1)} %maximum_bitcast_fusion.1), kind=kOutput, calls=%fused_computation.90 | convolution fusion | flops 1611923456 | bytes 6430720 | tf_op jit(solution)/shard_map/dot_general | solution.py:100
  31.7 0.4 fusion.38
  32.1 1.1 fusion.175
  33.3 1.1 fusion.174
  34.4 0.6 copy-done.3
  34.9 0.7 copy-done.5
  35.9 2.4 %fusion.40 = f32[2,1,8,128,256]{4,3,2,0,1:T(8,128)S(1)} fusion(f32[1,1,8,128,256]{4,3,2,0,1:T(8,128)S(1)} %bitcast.152, f32[1,1,8,128,256]{4,3,2,0,1:T(8,128)S(1)} %bitcast.153, f32[1,1,8,128,256]{4,3,2,0,1:T(8,128)S(1)} %bitcast.148, f32[1,1,8,128,256]{4,3,2,0,1:T(8,128)S(1)} %bitcast.149, f32[2,8,128,256]{3,2,1,0:T(8,128)S(1)} %copy-done.5, ...), kind=kOutput, calls=%fused_computation.71 | convolution fusion | flops 811761664 | bytes 11534336 | tf_op jit(solution)/shard_map/...xy,kx->...ky/dot_general | solution.py:40
  38.3 16.5 %collective-permute-done.1 = f32[2,1,4,128,256]{4,3,2,0,1:T(8,128)} collective-permute-done((f32[2,1,4,128,256]{4,3,2,0,1:T(8,128)}, f32[2,1,4,128,256]{4,3,2,0,1:T(8,128)}, u32[]{:S(2)}, u32[]{:S(2)}) %collective-permute-start.1) | collective-permute-done | bytes 1048608 | tf_op jit(solution)/shard_map/ppermute | solution.py:70
  54.8 2.4 %pad_maximum_fusion = (f32[2,1,12,128,256]{4,3,2,0,1:T(8,128)S(1)}, f32[2,1,12,128,256]{4,3,2,0,1:T(8,128)S(1)}) fusion(f32[2,1,4,128,256]{4,3,2,0,1:T(8,128)} %collective-permute-done, f32[1,1,8,128,256]{4,3,2,0,1:T(8,128)S(1)} %bitcast.136, f32[1,1,8,128,256]{4,3,2,0,1:T(8,128)S(1)} %bitcast.141, f32[2,1,4,128,256]{4,3,2,0,1:T(8,128)} %collective-permute-done.1), kind=kLoop, calls=%fused_computation.22 | loop fusion | flops 3145728 | bytes 10485760 | tf_op jit(solution)/shard_map/concatenate | solution.py:46
  57.2 1.6 %fusion.31 = f32[2,1,8,128,256]{4,3,2,0,1:T(8,128)S(1)} fusion(f32[2,1,8,128,256]{4,3,2,0,1:T(8,128)S(1)} %fusion.40, f32[2,1,12,128,256]{4,3,2,0,1:T(8,128)S(1)} %get-tuple-element.22, f32[2,1,12,128,256]{4,3,2,0,1:T(8,128)S(1)} %get-tuple-element.21, f32[8,128,256]{2,1,0:T(8,128)S(1)} %copy-done.3), kind=kLoop, calls=%fused_computation.54 | loop fusion | flops 6815744 | bytes 22020096 | tf_op jit(solution)/shard_map/add | solution.py:158
  58.8 1.5 %fusion.173 = (f32[2,1,4,128,256]{4,3,2,0,1:T(8,128)}, f32[2,1,4,128,256]{4,3,2,0,1:T(8,128)}) fusion(f32[2,1,8,128,256]{4,3,2,0,1:T(8,128)S(1)} %fusion.31), kind=kLoop, calls=%fused_computation.245 | loop fusion | bytes 4194304 | tf_op jit(solution)/shard_map/slice | solution.py:69
  60.3 5.4 %collective-permute-start.3 = (f32[2,1,4,128,256]{4,3,2,0,1:T(8,128)}, f32[2,1,4,128,256]{4,3,2,0,1:T(8,128)}, u32[]{:S(2)}, u32[]{:S(2)}) collective-permute-start(f32[2,1,4,128,256]{4,3,2,0,1:T(8,128)} %get-tuple-element.16), channel_id=1, source_target_pairs={{0,1},{1,2},{2,3},{3,4},{4,5},{5,6},{6,7},{8,9},{9,10},{10,11},{11... | collective-permute-start | bytes 3145736 | tf_op jit(solution)/shard_map/ppermute | solution.py:70
  65.7 1.5 %collective-permute-start.2 = (f32[2,1,4,128,256]{4,3,2,0,1:T(8,128)}, f32[2,1,4,128,256]{4,3,2,0,1:T(8,128)}, u32[]{:S(2)}, u32[]{:S(2)}) collective-permute-start(f32[2,1,4,128,256]{4,3,2,0,1:T(8,128)} %get-tuple-element.15), channel_id=1, source_target_pairs={{1,0},{2,1},{3,2},{4,3},{5,4},{6,5},{7,6},{9,8},{10,9},{11,10},{12... | collective-permute-start | bytes 3145736 | tf_op jit(solution)/shard_map/ppermute | solution.py:71
  67.3 1.8 %fusion.46 = f32[2,8,128,256]{3,2,1,0:T(8,128)S(1)} fusion(f32[2,1,8,128,256]{4,3,2,0,1:T(8,128)S(1)} %fusion.31), kind=kOutput, calls=%fused_computation.80 | convolution fusion | flops 1611268096 | bytes 4194304 | tf_op jit(solution)/shard_map/...xy,yk->...xk/dot_general | solution.py:39
  69.4 2.4 %maximum_add_fusion = f32[2,1,8,128,256]{4,3,2,0,1:T(8,128)S(1)} fusion(f32[1,1,8,128,256]{4,3,2,0,1:T(8,128)S(1)} %bitcast.146, f32[1,1,8,128,256]{4,3,2,0,1:T(8,128)S(1)} %bitcast.147, f32[2,8,128,256]{3,2,1,0:T(8,128)S(1)} %fusion.46, f32[2,1,8,128,256]{4,3,2,0,1:T(8,128)S(1)} %fusion.31, f32[1,1,8,128,256]{4,3,2,0,1:T(8,128)S(1)} %bitcast.137, ...), kind=kOutput, calls=%fused_computation.72 | convolution fusion | flops 810713088 | bytes 11534336 | tf_op jit(solution)/shard_map/...xy,kx->...ky/dot_general | solution.py:40
  71.8 38.2 %collective-permute-done.3 = f32[2,1,4,128,256]{4,3,2,0,1:T(8,128)} collective-permute-done((f32[2,1,4,128,256]{4,3,2,0,1:T(8,128)}, f32[2,1,4,128,256]{4,3,2,0,1:T(8,128)}, u32[]{:S(2)}, u32[]{:S(2)}) %collective-permute-start.3) | collective-permute-done | bytes 1048608 | tf_op jit(solution)/shard_map/ppermute | solution.py:70
  110.1 4.0 %fusion.15 = f32[2,1,8,128,256]{4,3,2,0,1:T(8,128)S(1)} fusion(f32[2,1,8,128,256]{4,3,2,0,1:T(8,128)S(1)} %maximum_add_fusion, f32[2,1,8,128,256]{4,3,2,0,1:T(8,128)S(1)} %fusion.31, f32[2,1,4,128,256]{4,3,2,0,1:T(8,128)} %collective-permute-done.3, f32[2,1,4,128,256]{4,3,2,0,1:T(8,128)} %collective-permute-done.2, f32[8,128,256]{2,1,0:T(8,128)S(1)} %copy-done.4), kind=kLoop, calls=%fused_computation.35 | loop fusion | flops 11010048 | bytes 9437184 | tf_op jit(solution)/shard_map/add | solution.py:158
  114.1 2.4 %add_bitcast_fusion = (f32[8,128,256]{2,1,0:T(8,128)S(1)}, f32[1,8,128,256]{3,2,1,0:T(8,128)}, f32[1,8,128,256]{3,2,1,0:T(8,128)}, f32[1,8,128,256]{3,2,1,0:T(8,128)}, f32[1,8,128,256]{3,2,1,0:T(8,128)}) fusion(f32[2,1,8,128,256]{4,3,2,0,1:T(8,128)S(1)} %fusion.15, f32[2,1,8,128,256]{4,3,2,0,1:T(8,128)S(1)} %fusion.31), kind=kLoop, calls=%fused_computation.98 | loop fusion | flops 786432 | bytes 9437184 | tf_op jit(solution)/shard_map/add | solution.py:162
  116.8 0.4 multiply_add_fusion.1
  118.0 0.6 multiply_add_fusion
  119.1 1.9 %collective-permute-done.4 = f32[8,2,32,256]{3,0,2,1:T(8,128)S(1)} collective-permute-done((f32[8,2,32,256]{3,0,2,1:T(8,128)S(1)}, f32[8,2,32,256]{3,0,2,1:T(8,128)S(1)}, u32[]{:S(2)}, u32[]{:S(2)}) %collective-permute-start.4) | collective-permute-done | bytes 524320 | tf_op jit(solution)/shard_map/ppermute | solution.py:120
  121.4 1.6 %collective-permute-start.5 = (f32[8,1,32,256]{3,0,2,1:T(8,128)S(1)}, f32[8,1,32,256]{3,0,2,1:T(8,128)S(1)}, u32[]{:S(2)}, u32[]{:S(2)}) collective-permute-start(f32[8,1,32,256]{3,0,2,1:T(8,128)S(1)} %constant_dynamic-slice_fusion), channel_id=1, source_target_pairs={{0,16},{8,24},{16,0},{24,8},{1,17},{9,25},{17,1},{25,9},{2,18},{10... | collective-permute-start | bytes 786440 | tf_op jit(solution)/shard_map/ppermute | solution.py:120
  122.9 6.9 %collective-permute-done.5 = f32[8,1,32,256]{3,0,2,1:T(8,128)S(1)} collective-permute-done((f32[8,1,32,256]{3,0,2,1:T(8,128)S(1)}, f32[8,1,32,256]{3,0,2,1:T(8,128)S(1)}, u32[]{:S(2)}, u32[]{:S(2)}) %collective-permute-start.5) | collective-permute-done | bytes 262176 | tf_op jit(solution)/shard_map/ppermute | solution.py:120
  129.8 14.1 %all_to_all.18 = f32[8,32,256]{2,0,1:T(8,128)S(1)} all-to-all(f32[8,32,256]{2,0,1:T(8,128)S(1)} %add_bitcast_fusion.1), channel_id=1, replica_groups=mesh['shots'=4,'depth'=8] {'depth'}, dimensions={1} | all-to-all | bytes 524288 | tf_op jit(solution)/shard_map/all_to_all | solution.py:166
  144.1 0.9 copy.22
  (56 shorter events, 3.2 us)
Async XLA Ops:
  0.6 11.0 %copy-start = (f32[1,8,128,256]{3,2,1,0:T(8,128)S(1)}, f32[1,8,128,256]{3,2,1,0:T(8,128)}, u32[]{:S(2)}) copy-start(f32[1,8,128,256]{3,2,1,0:T(8,128)} %param.15) | copy-start | bytes 3145732
  0.6 11.0 %copy-start.1 = (f32[1,8,128,256]{3,2,1,0:T(8,128)S(1)}, f32[1,8,128,256]{3,2,1,0:T(8,128)}, u32[]{:S(2)}) copy-start(f32[1,8,128,256]{3,2,1,0:T(8,128)} %param.13) | copy-start | bytes 3145732
  3.8 34.5 %collective-permute-start = (f32[2,1,4,128,256]{4,3,2,0,1:T(8,128)}, f32[2,1,4,128,256]{4,3,2,0,1:T(8,128)}, u32[]{:S(2)}, u32[]{:S(2)}) collective-permute-start(f32[2,1,4,128,256]{4,3,2,0,1:T(8,128)} %get-tuple-element.23), channel_id=1, source_target_pairs={{1,0},{2,1},{3,2},{4,3},{5,4},{6,5},{7,6},{9,8},{10,9},{11,10},{12... | collective-permute-start | bytes 3145736 | tf_op jit(solution)/shard_map/ppermute | solution.py:71
  5.1 49.7 %collective-permute-start.1 = (f32[2,1,4,128,256]{4,3,2,0,1:T(8,128)}, f32[2,1,4,128,256]{4,3,2,0,1:T(8,128)}, u32[]{:S(2)}, u32[]{:S(2)}) collective-permute-start(f32[2,1,4,128,256]{4,3,2,0,1:T(8,128)} %get-tuple-element.24), channel_id=1, source_target_pairs={{0,1},{1,2},{2,3},{3,4},{4,5},{5,6},{6,7},{8,9},{9,10},{10,11},{11... | collective-permute-start | bytes 3145736 | tf_op jit(solution)/shard_map/ppermute | solution.py:70
  11.6 3.2 %copy-start.11 = (s32[4096]{0:T(1024)S(1)}, s32[4096]{0:T(1024)}, u32[]{:S(2)}) copy-start(s32[4096]{0:T(1024)} %param.22) | copy-start | bytes 49156
  11.6 3.2 %copy-start.12 = (s32[4096]{0:T(1024)S(1)}, s32[4096]{0:T(1024)}, u32[]{:S(2)}) copy-start(s32[4096]{0:T(1024)} %param.21) | copy-start | bytes 49156
  11.6 3.9 %copy-start.10 = (f32[1,2,4096]{2,1,0:T(2,128)S(1)}, f32[1,2,4096]{2,1,0:T(2,128)}, u32[]{:S(2)}) copy-start(f32[1,2,4096]{2,1,0:T(2,128)} %param.23) | copy-start | bytes 98308
  29.0 0.7 copy-start.14
  29.0 0.7 copy-start.15
  29.0 0.8 copy-start.16
  29.0 0.8 copy-start.13
  32.1 2.2 %copy-start.9 = (f32[1,8,128,256]{3,2,1,0:T(8,128)S(1)}, f32[1,8,128,256]{3,2,1,0:T(8,128)}, u32[]{:S(2)}) copy-start(f32[1,8,128,256]{3,2,1,0:T(8,128)} %param.12) | copy-start | bytes 3145732
  33.2 1.7 %copy-start.3 = (f32[8,128,256]{2,1,0:T(8,128)S(1)}, f32[8,128,256]{2,1,0:T(8,128)}, u32[]{:S(2)}) copy-start(f32[8,128,256]{2,1,0:T(8,128)} %param.16) | copy-start | bytes 3145732
  33.2 2.4 %copy-start.5 = (f32[2,8,128,256]{3,2,1,0:T(8,128)S(1)}, f32[2,8,128,256]{3,2,1,0:T(8,128)}, u32[]{:S(2)}) copy-start(f32[2,8,128,256]{3,2,1,0:T(8,128)} %fusion.50) | copy-start | bytes 6291460
  33.2 2.6 %copy-start.8 = (f32[1,8,128,256]{3,2,1,0:T(8,128)S(1)}, f32[1,8,128,256]{3,2,1,0:T(8,128)}, u32[]{:S(2)}) copy-start(f32[1,8,128,256]{3,2,1,0:T(8,128)} %param.14) | copy-start | bytes 3145732
  60.3 49.8 %collective-permute-start.3 = (f32[2,1,4,128,256]{4,3,2,0,1:T(8,128)}, f32[2,1,4,128,256]{4,3,2,0,1:T(8,128)}, u32[]{:S(2)}, u32[]{:S(2)}) collective-permute-start(f32[2,1,4,128,256]{4,3,2,0,1:T(8,128)} %get-tuple-element.16), channel_id=1, source_target_pairs={{0,1},{1,2},{2,3},{3,4},{4,5},{5,6},{6,7},{8,9},{9,10},{10,11},{11... | collective-permute-start | bytes 3145736 | tf_op jit(solution)/shard_map/ppermute | solution.py:70
  65.7 44.4 %collective-permute-start.2 = (f32[2,1,4,128,256]{4,3,2,0,1:T(8,128)}, f32[2,1,4,128,256]{4,3,2,0,1:T(8,128)}, u32[]{:S(2)}, u32[]{:S(2)}) collective-permute-start(f32[2,1,4,128,256]{4,3,2,0,1:T(8,128)} %get-tuple-element.15), channel_id=1, source_target_pairs={{1,0},{2,1},{3,2},{4,3},{5,4},{6,5},{7,6},{9,8},{10,9},{11,10},{12... | collective-permute-start | bytes 3145736 | tf_op jit(solution)/shard_map/ppermute | solution.py:71
  67.2 1.9 %copy-start.2 = (f32[1,8,128,256]{3,2,1,0:T(8,128)S(1)}, f32[1,8,128,256]{3,2,1,0:T(8,128)}, u32[]{:S(2)}) copy-start(f32[1,8,128,256]{3,2,1,0:T(8,128)} %param.13) | copy-start | bytes 3145732
  67.2 1.9 %copy-start.4 = (f32[8,128,256]{2,1,0:T(8,128)S(1)}, f32[8,128,256]{2,1,0:T(8,128)}, u32[]{:S(2)}) copy-start(f32[8,128,256]{2,1,0:T(8,128)} %param.16) | copy-start | bytes 3145732
  67.3 1.9 %copy-start.6 = (f32[1,1024,256]{2,1,0:T(8,128)S(1)}, f32[1,1024,256]{2,1,0:T(8,128)}, u32[]{:S(2)}) copy-start(f32[1,1024,256]{2,1,0:T(8,128)} %get-tuple-element.19) | copy-start | bytes 3145732
  67.3 2.1 %copy-start.7 = (f32[1,1024,256]{2,1,0:T(8,128)S(1)}, f32[1,1024,256]{2,1,0:T(8,128)}, u32[]{:S(2)}) copy-start(f32[1,1024,256]{2,1,0:T(8,128)} %get-tuple-element.17) | copy-start | bytes 3145732
  119.0 2.0 %collective-permute-start.4 = (f32[8,2,32,256]{3,0,2,1:T(8,128)S(1)}, f32[8,2,32,256]{3,0,2,1:T(8,128)S(1)}, u32[]{:S(2)}, u32[]{:S(2)}) collective-permute-start(f32[8,2,32,256]{3,0,2,1:T(8,128)S(1)} %bitcast.154), channel_id=1, source_target_pairs={{0,8},{8,0},{16,24},{24,16},{1,9},{9,1},{17,25},{25,17},{2,10},{10... | collective-permute-start | bytes 1572872 | tf_op jit(solution)/shard_map/ppermute | solution.py:120
  121.4 8.4 %collective-permute-start.5 = (f32[8,1,32,256]{3,0,2,1:T(8,128)S(1)}, f32[8,1,32,256]{3,0,2,1:T(8,128)S(1)}, u32[]{:S(2)}, u32[]{:S(2)}) collective-permute-start(f32[8,1,32,256]{3,0,2,1:T(8,128)S(1)} %constant_dynamic-slice_fusion), channel_id=1, source_target_pairs={{0,16},{8,24},{16,0},{24,8},{1,17},{9,25},{17,1},{25,9},{2,18},{10... | collective-permute-start | bytes 786440 | tf_op jit(solution)/shard_map/ppermute | solution.py:120

commit v9 on v8

--- a/solution.py
+++ b/solution.py
@@ -60,13 +60,13 @@
     return total
 
 
-def exchange(current, dim):
+def exchange(fields, dim):
     devices = lax.axis_size("depth")
-    length = current.shape[dim]
+    length = fields[0].shape[dim]
     up = [(i, i + 1) for i in range(devices - 1)]
     down = [(i + 1, i) for i in range(devices - 1)]
-    last = lax.slice_in_dim(current, length - HALO, length, axis=dim)
-    leading = lax.slice_in_dim(current, 0, HALO, axis=dim)
+    last = tuple(lax.slice_in_dim(f, length - HALO, length, axis=dim) for f in fields)
+    leading = tuple(lax.slice_in_dim(f, 0, HALO, axis=dim) for f in fields)
     below = lax.ppermute(last, "depth", up)
     above = lax.ppermute(leading, "depth", down)
     return below, above
@@ -142,23 +142,28 @@
     receiver_flat = receiver_depth * lateral + receiver_cell
     signs = (2 * sign_bits - 1).astype(jnp.float32)
     position = lax.axis_index("depth")
-    earlier = jnp.stack([forward_prev, adjoint_prev])
-    current = jnp.stack([forward_now, adjoint_now])
-    zaxis = 2
+    earlier = [forward_prev, adjoint_prev]
+    current = [forward_now, adjoint_now]
+    zaxis = 1
     below, above = exchange(current, zaxis)
     first_plane = position * planes
     correlation = None
     forward_terms = spread_dense(source_depth, source_cell, signs[0][None, :] * wavelet, first_plane, planes, rows, cols)
     adjoint_terms = spread_dense(receiver_depth, receiver_cell, residual_traces[0], first_plane, planes, rows, cols)
     for step in range(STEPS):
-        terms = jnp.stack([forward_terms[step : step + 1], adjoint_terms[step : step + 1]])
+        terms = [forward_terms[step : step + 1], adjoint_terms[step : step + 1]]
         partial = lax.optimization_barrier(
-            2.0 * current - earlier + courant * lateral_laplace(current, zaxis) + terms
+            [
+                2.0 * current[i] - earlier[i] + courant * lateral_laplace(current[i], zaxis) + terms[i]
+                for i in range(2)
+            ]
         )
-        fresh = partial + courant * depth_laplace(below, current, above, zaxis)
+        fresh = [
+            partial[i] + courant * depth_laplace(below[i], current[i], above[i], zaxis) for i in range(2)
+        ]
         if step + 1 < STEPS:
             below, above = exchange(fresh, zaxis)
-        part = fresh[0, 0] * fresh[1, 0]
+        part = fresh[0][0] * fresh[1][0]
         correlation = part if correlation is None else correlation + part
         earlier, current = (current, fresh)
     lateral_smooth = smooth(smooth(correlation, 1), 2)

time: 145 us -> 141 us (0.972)
  waiting for transfers between devices: 63.4 us -> 46.4 us
  starting transfers between devices: 16.3 us -> 27.3 us
  other arithmetic: 16.7 us -> 8.33 us
  local copies, waits for them, and re-layouts: 8.28 us -> 15.5 us
  matrix products: 25.1 us -> 27.8 us
    ppermute x2 -> x4, waiting for transfers between devices: 54.7 us -> 37.6 us  [exchange(): below = lax.ppermute(last, 'depth', up)]
    ppermute x2 -> x4, starting transfers between devices: 11.9 us -> 20.3 us  [exchange(): below = lax.ppermute(last, 'depth', up)]
    add x2 -> x1, other arithmetic: 5.64 us -> 1.61 us  [on_device(): partial[i] + courant * depth_laplace(below[i], current[i], above[i], zaxis)]
    another operation x1 -> x0, other arithmetic: 3.16 us -> none  [on_device(): current = jnp.stack([forward_now, adjoint_now])]
    dot_general x2 -> x4, matrix products: 4.85 us -> 7.49 us  [lateral_laplace(): along_x = jnp.einsum('...xy,kx->...ky', core, band(rows), precision=high)]
    ppermute x2 -> x4, starting transfers between devices: 2.78 us -> 5.36 us  [exchange(): above = lax.ppermute(leading, 'depth', down)]
    unnamed x35 -> x45, local copies, waits for them, and re-layouts: 2.96 us -> 5.5 us
    slice x3 -> x6, local copies, waits for them, and re-layouts: 3.75 us -> 6.16 us  [the longest x4 3.6 us: exchange(): leading = tuple((lax.slice_in_dim(f, 0, HALO, axis=dim) for f in fields))]
  transfers between devices with their start and end apart: 6 -> 10, of which waited for: 4 -> 5; matrix products, arithmetic and copies ran while one was open for 20% -> 25% of each run, Pallas kernels for 0% -> 0%
where the time goes in v9:
time: 141 us
  waiting for transfers between devices  46.4 us (33%)
  matrix products  27.8 us (20%)
  starting transfers between devices  27.3 us (19%)
  local copies, waits for them, and re-layouts  15.5 us (11%)
  blocking collectives  14.1 us (10%)
  other arithmetic  8.33 us (6%)
    ppermute x4, waiting for transfers between devices, exchange(): below = lax.ppermute(last, 'depth', up)  37.6 us
    ppermute x4, starting transfers between devices, exchange(): below = lax.ppermute(last, 'depth', up)  20.3 us
    dot_general x2, matrix products, spread_dense(): grid = jnp.dot(by_row, right, preferred_element_type=jnp.float32)  15.2 us
    all_to_all x1, blocking collectives, on_device(): lax.all_to_all(reduced, 'depth', split_axis=1, concat_axis=0, tiled=True)  14.1 us
    ppermute x2, waiting for transfers between devices, reduce_shots(): blocks = keep + lax.ppermute(send, 'shots', pairs)  8.72 us
    dot_general x4, matrix products, lateral_laplace(): along_x = jnp.einsum('...xy,kx->...ky', core, band(rows), precision=high)  7.49 us
    unnamed x45, local copies, waits for them, and re-layouts  5.5 us
    ppermute x4, starting transfers between devices, exchange(): above = lax.ppermute(leading, 'depth', down)  5.36 us
  transfers between devices with their start and end apart: 10, of which 5 were waited for; matrix products, arithmetic and copies ran while one was open for 25% of the time, Pallas kernels for 0%

profile of v9, /device:TPU:0, one launch (start us, length us, event | category | flops | bytes accessed | tf_op | source)
XLA Modules:
  0.0 140.6 jit_solution(12888967061071284831)
XLA Ops:
  0.6 2.4 %fusion.218 = (f32[1,4,128,256]{3,2,1,0:T(8,128)}, f32[1,4,128,256]{3,2,1,0:T(8,128)}) fusion(f32[1,8,128,256]{3,2,1,0:T(8,128)} %param.15), kind=kLoop, calls=%fused_computation.314 | loop fusion | bytes 2097152 | tf_op jit(solution)/shard_map/slice | solution.py:69
  3.0 5.7 %collective-permute-start.3 = (f32[1,4,128,256]{3,2,1,0:T(8,128)}, f32[1,4,128,256]{3,2,1,0:T(8,128)}, u32[]{:S(2)}, u32[]{:S(2)}) collective-permute-start(f32[1,4,128,256]{3,2,1,0:T(8,128)} %get-tuple-element.42), channel_id=1, source_target_pairs={{0,1},{1,2},{2,3},{3,4},{4,5},{5,6},{6,7},{8,9},{9,10},{10,11},{11... | collective-permute-start | bytes 1572872 | tf_op jit(solution)/shard_map/ppermute | solution.py:70
  8.7 1.3 collective-permute-start.2
  10.0 1.1 fusion.219
  11.1 5.5 %collective-permute-start.1 = (f32[1,4,128,256]{3,2,1,0:T(8,128)}, f32[1,4,128,256]{3,2,1,0:T(8,128)}, u32[]{:S(2)}, u32[]{:S(2)}) collective-permute-start(f32[1,4,128,256]{3,2,1,0:T(8,128)} %get-tuple-element.46), channel_id=1, source_target_pairs={{0,1},{1,2},{2,3},{3,4},{4,5},{5,6},{6,7},{8,9},{9,10},{10,11},{11... | collective-permute-start | bytes 1572872 | tf_op jit(solution)/shard_map/ppermute | solution.py:70
  16.6 1.3 collective-permute-start
  17.9 2.0 %convolution_bitcast_fusion.6 = f32[1,8,128,256]{3,2,1,0:T(8,128)} fusion(f32[1,8,128,256]{3,2,1,0:T(8,128)S(1)} %copy-done.1), kind=kOutput, calls=%fused_computation.52 | convolution fusion | flops 805961728 | bytes 2097152 | tf_op jit(solution)/shard_map/...xy,yk->...xk/dot_general | solution.py:39
  20.1 1.8 %fusion.12 = f32[1024,3,2,256]{3,0,2,1:T(8,128)S(1)} fusion(pred[512,256]{0,1:T(8,128)(4,1)S(1)} %iota_compare_fusion.3, s32[512]{0:T(512)S(1)} %get-tuple-element.61, bf16[512,3,2]{0,2,1:T(2,128)(2,1)S(1)} %maximum_bitcast_fusion.1), kind=kOutput, calls=%fused_computation.30 | convolution fusion | flops 1611923456 | bytes 6430720 | tf_op jit(solution)/shard_map/dot_general | solution.py:100
  22.4 1.5 %fusion.211 = (f32[1,1024,256]{2,1,0:T(8,128)}, f32[1,1024,256]{2,1,0:T(8,128)}) fusion(f32[2,1024,256]{2,1,0:T(8,128)S(1)} %fusion.10), kind=kLoop, calls=%fused_computation.307 | loop fusion | bytes 4194304 | tf_op jit(solution)/shard_map/slice | solution.py:154
  24.6 13.4 %fusion.1 = f32[1024,3,2,256]{3,0,2,1:T(8,128)S(1)} fusion(pred[4096,256]{0,1:T(8,128)(4,1)S(1)} %iota_compare_fusion.1, s32[4096]{0:T(1024)S(1)} %get-tuple-element.56, bf16[4096,3,2]{0,2,1:T(2,128)(2,1)S(1)} %maximum_bitcast_fusion), kind=kOutput, calls=%fused_computation.2 | convolution fusion | flops 12895387648 | bytes 7405568 | tf_op jit(solution)/shard_map/dot_general | solution.py:100
  38.4 1.1 fusion.210
  40.9 2.3 %fusion.21 = f32[1,8,128,256]{3,2,1,0:T(8,128)} fusion(f32[1,8,128,256]{3,2,1,0:T(8,128)S(1)} %bitcast.193, f32[1,8,128,256]{3,2,1,0:T(8,128)S(1)} %copy-done.5, f32[1,8,128,256]{3,2,1,0:T(8,128)S(1)} %copy-done.1, f32[8,128,256]{2,1,0:T(8,128)S(1)} %copy-done, f32[1,8,128,256]{3,2,1,0:T(8,128)S(1)} %copy-done.11), kind=kOutput, calls=%fused_computation.58 | convolution fusion | flops 404914176 | bytes 6291456 | tf_op jit(solution)/shard_map/...xy,kx->...ky/dot_general | solution.py:40
  44.5 2.3 %fusion.26 = f32[1,8,128,256]{3,2,1,0:T(8,128)} fusion(f32[1,8,128,256]{3,2,1,0:T(8,128)S(1)} %bitcast.194, f32[1,8,128,256]{3,2,1,0:T(8,128)S(1)} %convolution_bitcast_fusion.4, f32[1,8,128,256]{3,2,1,0:T(8,128)S(1)} %copy-done.2, f32[8,128,256]{2,1,0:T(8,128)S(1)} %copy-done, f32[1,8,128,256]{3,2,1,0:T(8,128)S(1)} %copy-done.12), kind=kOutput, calls=%fused_computation.63 | convolution fusion | flops 404914176 | bytes 6291456 | tf_op jit(solution)/shard_map/...xy,kx->...ky/dot_general | solution.py:40
  46.9 1.1 constant_dynamic-update-slice_fusion.7
  47.9 5.1 %collective-permute-done.1 = f32[1,4,128,256]{3,2,1,0:T(8,128)} collective-permute-done((f32[1,4,128,256]{3,2,1,0:T(8,128)}, f32[1,4,128,256]{3,2,1,0:T(8,128)}, u32[]{:S(2)}, u32[]{:S(2)}) %collective-permute-start.1) | collective-permute-done | bytes 524320 | tf_op jit(solution)/shard_map/ppermute | solution.py:70
  53.1 1.1 constant_dynamic-update-slice_fusion.3
  54.4 1.1 constant_dynamic-update-slice_fusion.4
  55.7 1.2 constant_dynamic-update-slice_fusion
  57.1 1.6 %fusion.78 = (f32[1,8,128,256]{3,2,1,0:T(8,128)S(1)}, f32[1,8,128,256]{3,2,1,0:T(8,128)S(1)}) fusion(f32[1,8,128,256]{3,2,1,0:T(8,128)S(1)} %copy-done.10, f32[1,12,128,256]{3,2,1,0:T(8,128)S(1)} %get-tuple-element.44, f32[1,12,128,256]{3,2,1,0:T(8,128)S(1)} %constant_dynamic-update-slice_fusion.4, f32[8,128,256]{2,1,0:T(8,128)S(1)} %copy-done, ...), kind=kLoop, calls=%fused_computation.120 | loop fusion | flops 6815744 | bytes 22020096 | tf_op jit(solution)/shard_map/add | solution.py:162
  60.0 4.6 %collective-permute-start.7 = (f32[1,4,128,256]{3,2,1,0:T(8,128)S(1)}, f32[1,4,128,256]{3,2,1,0:T(8,128)S(1)}, u32[]{:S(2)}, u32[]{:S(2)}) collective-permute-start(f32[1,4,128,256]{3,2,1,0:T(8,128)S(1)} %get-tuple-element.38), channel_id=1, source_target_pairs={{0,1},{1,2},{2,3},{3,4},{4,5},{5,6},{6,7},{8,9},{9,10},{10,11},{11... | collective-permute-start | bytes 1572872 | tf_op jit(solution)/shard_map/ppermute | solution.py:70
  64.6 1.3 collective-permute-start.6
  65.9 4.6 %collective-permute-start.5 = (f32[1,4,128,256]{3,2,1,0:T(8,128)S(1)}, f32[1,4,128,256]{3,2,1,0:T(8,128)S(1)}, u32[]{:S(2)}, u32[]{:S(2)}) collective-permute-start(f32[1,4,128,256]{3,2,1,0:T(8,128)S(1)} %get-tuple-element.36), channel_id=1, source_target_pairs={{0,1},{1,2},{2,3},{3,4},{4,5},{5,6},{6,7},{8,9},{9,10},{10,11},{11... | collective-permute-start | bytes 1572872 | tf_op jit(solution)/shard_map/ppermute | solution.py:70
  70.5 1.5 %collective-permute-start.4 = (f32[1,4,128,256]{3,2,1,0:T(8,128)S(1)}, f32[1,4,128,256]{3,2,1,0:T(8,128)S(1)}, u32[]{:S(2)}, u32[]{:S(2)}) collective-permute-start(f32[1,4,128,256]{3,2,1,0:T(8,128)S(1)} %get-tuple-element.35), channel_id=1, source_target_pairs={{1,0},{2,1},{3,2},{4,3},{5,4},{6,5},{7,6},{9,8},{10,9},{11,10},{12... | collective-permute-start | bytes 1572872 | tf_op jit(solution)/shard_map/ppermute | solution.py:71
  72.0 1.4 %fusion.31 = f32[1,8,128,256]{3,2,1,0:T(8,128)S(1)} fusion(f32[1,8,128,256]{3,2,1,0:T(8,128)S(1)} %bitcast.191, f32[1,8,128,256]{3,2,1,0:T(8,128)S(1)} %convolution_bitcast_fusion.2, f32[1,8,128,256]{3,2,1,0:T(8,128)S(1)} %get-tuple-element.40, f32[8,128,256]{2,1,0:T(8,128)S(1)} %copy-done, f32[1,8,128,256]{3,2,1,0:T(8,128)S(1)} %copy-done.1), kind=kOutput, calls=%fused_computation.68 | convolution fusion | flops 404914176 | bytes 6291456 | tf_op jit(solution)/shard_map/...xy,kx->...ky/dot_general | solution.py:40
  74.7 1.4 fusion.36
  76.0 23.3 %collective-permute-done.7 = f32[1,4,128,256]{3,2,1,0:T(8,128)S(1)} collective-permute-done((f32[1,4,128,256]{3,2,1,0:T(8,128)S(1)}, f32[1,4,128,256]{3,2,1,0:T(8,128)S(1)}, u32[]{:S(2)}, u32[]{:S(2)}) %collective-permute-start.7) | collective-permute-done | bytes 524320 | tf_op jit(solution)/shard_map/ppermute | solution.py:70
  99.4 9.2 %collective-permute-done.5 = f32[1,4,128,256]{3,2,1,0:T(8,128)S(1)} collective-permute-done((f32[1,4,128,256]{3,2,1,0:T(8,128)S(1)}, f32[1,4,128,256]{3,2,1,0:T(8,128)S(1)}, u32[]{:S(2)}, u32[]{:S(2)}) %collective-permute-start.5) | collective-permute-done | bytes 524320 | tf_op jit(solution)/shard_map/ppermute | solution.py:70
  108.5 3.5 %bitcast_add_fusion = (f32[8,128,256]{2,1,0:T(8,128)S(1)}, f32[1,8,128,256]{3,2,1,0:T(8,128)}, f32[1,8,128,256]{3,2,1,0:T(8,128)}) fusion(f32[1,8,128,256]{3,2,1,0:T(8,128)S(1)} %get-tuple-element.39, f32[1,8,128,256]{3,2,1,0:T(8,128)S(1)} %get-tuple-element.40, f32[1,8,128,256]{3,2,1,0:T(8,128)S(1)} %fusion.36, ...), kind=kLoop, calls=%fused_computation.142 | loop fusion | flops 11796480 | bytes 10485760 | tf_op jit(solution)/shard_map/add | solution.py:167
  114.8 1.9 %collective-permute-done.8 = f32[8,2,32,256]{3,0,2,1:T(8,128)S(1)} collective-permute-done((f32[8,2,32,256]{3,0,2,1:T(8,128)S(1)}, f32[8,2,32,256]{3,0,2,1:T(8,128)S(1)}, u32[]{:S(2)}, u32[]{:S(2)}) %collective-permute-start.8) | collective-permute-done | bytes 524320 | tf_op jit(solution)/shard_map/ppermute | solution.py:120
  117.0 1.6 %collective-permute-start.9 = (f32[8,1,32,256]{3,0,2,1:T(8,128)S(1)}, f32[8,1,32,256]{3,0,2,1:T(8,128)S(1)}, u32[]{:S(2)}, u32[]{:S(2)}) collective-permute-start(f32[8,1,32,256]{3,0,2,1:T(8,128)S(1)} %constant_dynamic-slice_fusion), channel_id=1, source_target_pairs={{0,16},{8,24},{16,0},{24,8},{1,17},{9,25},{17,1},{25,9},{2,18},{10... | collective-permute-start | bytes 786440 | tf_op jit(solution)/shard_map/ppermute | solution.py:120
  118.5 6.9 %collective-permute-done.9 = f32[8,1,32,256]{3,0,2,1:T(8,128)S(1)} collective-permute-done((f32[8,1,32,256]{3,0,2,1:T(8,128)S(1)}, f32[8,1,32,256]{3,0,2,1:T(8,128)S(1)}, u32[]{:S(2)}, u32[]{:S(2)}) %collective-permute-start.9) | collective-permute-done | bytes 262176 | tf_op jit(solution)/shard_map/ppermute | solution.py:120
  125.4 14.1 %all_to_all.18 = f32[8,32,256]{2,0,1:T(8,128)S(1)} all-to-all(f32[8,32,256]{2,0,1:T(8,128)S(1)} %add_bitcast_fusion), channel_id=1, replica_groups=mesh['shots'=4,'depth'=8] {'depth'}, dimensions={1} | all-to-all | bytes 524288 | tf_op jit(solution)/shard_map/all_to_all | solution.py:171
  (80 shorter events, 11.6 us)
Async XLA Ops:
  0.6 9.3 %copy-start.1 = (f32[1,8,128,256]{3,2,1,0:T(8,128)S(1)}, f32[1,8,128,256]{3,2,1,0:T(8,128)}, u32[]{:S(2)}) copy-start(f32[1,8,128,256]{3,2,1,0:T(8,128)} %param.13) | copy-start | bytes 3145732
  3.0 43.8 %collective-permute-start.3 = (f32[1,4,128,256]{3,2,1,0:T(8,128)}, f32[1,4,128,256]{3,2,1,0:T(8,128)}, u32[]{:S(2)}, u32[]{:S(2)}) collective-permute-start(f32[1,4,128,256]{3,2,1,0:T(8,128)} %get-tuple-element.42), channel_id=1, source_target_pairs={{0,1},{1,2},{2,3},{3,4},{4,5},{5,6},{6,7},{8,9},{9,10},{10,11},{11... | collective-permute-start | bytes 1572872 | tf_op jit(solution)/shard_map/ppermute | solution.py:70
  8.7 45.7 %collective-permute-start.2 = (f32[1,4,128,256]{3,2,1,0:T(8,128)}, f32[1,4,128,256]{3,2,1,0:T(8,128)}, u32[]{:S(2)}, u32[]{:S(2)}) collective-permute-start(f32[1,4,128,256]{3,2,1,0:T(8,128)} %get-tuple-element.41), channel_id=1, source_target_pairs={{1,0},{2,1},{3,2},{4,3},{5,4},{6,5},{7,6},{9,8},{10,9},{11,10},{12... | collective-permute-start | bytes 1572872 | tf_op jit(solution)/shard_map/ppermute | solution.py:71
  11.1 8.8 %copy-start.17 = (s32[512]{0:T(512)S(1)}, s32[512]{0:T(512)}, u32[]{:S(2)}) copy-start(s32[512]{0:T(512)} %param.20) | copy-start | bytes 6148
  11.1 8.8 %copy-start.18 = (s32[512]{0:T(512)S(1)}, s32[512]{0:T(512)}, u32[]{:S(2)}) copy-start(s32[512]{0:T(512)} %param.19) | copy-start | bytes 6148
  11.1 8.9 %copy-start.19 = (s32[1,512]{1,0:T(1,128)S(1)}, s32[1,512]{1,0:T(1,128)}, u32[]{:S(2)}) copy-start(s32[1,512]{1,0:T(1,128)} %param.18) | copy-start | bytes 6148
  11.1 8.9 %copy-start.16 = (f32[2,512]{1,0:T(2,128)S(1)}, f32[2,512]{1,0:T(2,128)}, u32[]{:S(2)}) copy-start(f32[2,512]{1,0:T(2,128)} %param.17) | copy-start | bytes 12292
  11.1 42.0 %collective-permute-start.1 = (f32[1,4,128,256]{3,2,1,0:T(8,128)}, f32[1,4,128,256]{3,2,1,0:T(8,128)}, u32[]{:S(2)}, u32[]{:S(2)}) collective-permute-start(f32[1,4,128,256]{3,2,1,0:T(8,128)} %get-tuple-element.46), channel_id=1, source_target_pairs={{0,1},{1,2},{2,3},{3,4},{4,5},{5,6},{6,7},{8,9},{9,10},{10,11},{11... | collective-permute-start | bytes 1572872 | tf_op jit(solution)/shard_map/ppermute | solution.py:70
  16.6 39.1 %collective-permute-start = (f32[1,4,128,256]{3,2,1,0:T(8,128)}, f32[1,4,128,256]{3,2,1,0:T(8,128)}, u32[]{:S(2)}, u32[]{:S(2)}) collective-permute-start(f32[1,4,128,256]{3,2,1,0:T(8,128)} %get-tuple-element.45), channel_id=1, source_target_pairs={{1,0},{2,1},{3,2},{4,3},{5,4},{6,5},{7,6},{9,8},{10,9},{11,10},{12... | collective-permute-start | bytes 1572872 | tf_op jit(solution)/shard_map/ppermute | solution.py:71
  22.3 1.5 %copy-start.14 = (s32[4096]{0:T(1024)S(1)}, s32[4096]{0:T(1024)}, u32[]{:S(2)}) copy-start(s32[4096]{0:T(1024)} %param.22) | copy-start | bytes 49156
  22.3 1.5 %copy-start.15 = (s32[4096]{0:T(1024)S(1)}, s32[4096]{0:T(1024)}, u32[]{:S(2)}) copy-start(s32[4096]{0:T(1024)} %param.21) | copy-start | bytes 49156
  22.3 2.1 %copy-start.13 = (f32[1,2,4096]{2,1,0:T(2,128)S(1)}, f32[1,2,4096]{2,1,0:T(2,128)}, u32[]{:S(2)}) copy-start(f32[1,2,4096]{2,1,0:T(2,128)} %param.23) | copy-start | bytes 98308
  38.4 1.5 %copy-start = (f32[8,128,256]{2,1,0:T(8,128)S(1)}, f32[8,128,256]{2,1,0:T(8,128)}, u32[]{:S(2)}) copy-start(f32[8,128,256]{2,1,0:T(8,128)} %param.16) | copy-start | bytes 3145732
  38.4 1.9 %copy-start.5 = (f32[1,8,128,256]{3,2,1,0:T(8,128)S(1)}, f32[1,8,128,256]{3,2,1,0:T(8,128)}, u32[]{:S(2)}) copy-start(f32[1,8,128,256]{3,2,1,0:T(8,128)} %convolution_bitcast_fusion.6) | copy-start | bytes 3145732
  38.4 2.2 %copy-start.8 = (f32[1,1024,256]{2,1,0:T(8,128)S(1)}, f32[1,1024,256]{2,1,0:T(8,128)}, u32[]{:S(2)}) copy-start(f32[1,1024,256]{2,1,0:T(8,128)} %get-tuple-element.24) | copy-start | bytes 3145732
  38.4 2.5 %copy-start.11 = (f32[1,8,128,256]{3,2,1,0:T(8,128)S(1)}, f32[1,8,128,256]{3,2,1,0:T(8,128)}, u32[]{:S(2)}) copy-start(f32[1,8,128,256]{3,2,1,0:T(8,128)} %param.12) | copy-start | bytes 3145732
  40.9 2.3 %copy-start.2 = (f32[1,8,128,256]{3,2,1,0:T(8,128)S(1)}, f32[1,8,128,256]{3,2,1,0:T(8,128)}, u32[]{:S(2)}) copy-start(f32[1,8,128,256]{3,2,1,0:T(8,128)} %param.15) | copy-start | bytes 3145732
  43.3 1.2 copy-start.12
  55.4 1.4 %copy-start.9 = (f32[1,8,128,256]{3,2,1,0:T(8,128)S(1)}, f32[1,8,128,256]{3,2,1,0:T(8,128)}, u32[]{:S(2)}) copy-start(f32[1,8,128,256]{3,2,1,0:T(8,128)} %fusion.21) | copy-start | bytes 3145732
  55.5 1.7 %copy-start.10 = (f32[1,8,128,256]{3,2,1,0:T(8,128)S(1)}, f32[1,8,128,256]{3,2,1,0:T(8,128)}, u32[]{:S(2)}) copy-start(f32[1,8,128,256]{3,2,1,0:T(8,128)} %fusion.26) | copy-start | bytes 3145732
  58.8 49.8 %copy-start.3 = (f32[1,8,128,256]{3,2,1,0:T(8,128)}, f32[1,8,128,256]{3,2,1,0:T(8,128)S(1)}, u32[]{:S(2)}) copy-start(f32[1,8,128,256]{3,2,1,0:T(8,128)S(1)} %get-tuple-element.39) | copy-start | bytes 3145732
  58.8 49.8 %copy-start.4 = (f32[1,8,128,256]{3,2,1,0:T(8,128)}, f32[1,8,128,256]{3,2,1,0:T(8,128)S(1)}, u32[]{:S(2)}) copy-start(f32[1,8,128,256]{3,2,1,0:T(8,128)S(1)} %get-tuple-element.40) | copy-start | bytes 3145732
  59.9 12.1 %copy-start.6 = (f32[1,1024,256]{2,1,0:T(8,128)S(1)}, f32[1,1024,256]{2,1,0:T(8,128)}, u32[]{:S(2)}) copy-start(f32[1,1024,256]{2,1,0:T(8,128)} %get-tuple-element.23) | copy-start | bytes 3145732
  60.0 39.4 %collective-permute-start.7 = (f32[1,4,128,256]{3,2,1,0:T(8,128)S(1)}, f32[1,4,128,256]{3,2,1,0:T(8,128)S(1)}, u32[]{:S(2)}, u32[]{:S(2)}) collective-permute-start(f32[1,4,128,256]{3,2,1,0:T(8,128)S(1)} %get-tuple-element.38), channel_id=1, source_target_pairs={{0,1},{1,2},{2,3},{3,4},{4,5},{5,6},{6,7},{8,9},{9,10},{10,11},{11... | collective-permute-start | bytes 1572872 | tf_op jit(solution)/shard_map/ppermute | solution.py:70
  64.6 34.8 %collective-permute-start.6 = (f32[1,4,128,256]{3,2,1,0:T(8,128)S(1)}, f32[1,4,128,256]{3,2,1,0:T(8,128)S(1)}, u32[]{:S(2)}, u32[]{:S(2)}) collective-permute-start(f32[1,4,128,256]{3,2,1,0:T(8,128)S(1)} %get-tuple-element.37), channel_id=1, source_target_pairs={{1,0},{2,1},{3,2},{4,3},{5,4},{6,5},{7,6},{9,8},{10,9},{11,10},{12... | collective-permute-start | bytes 1572872 | tf_op jit(solution)/shard_map/ppermute | solution.py:71
  65.9 42.7 %collective-permute-start.5 = (f32[1,4,128,256]{3,2,1,0:T(8,128)S(1)}, f32[1,4,128,256]{3,2,1,0:T(8,128)S(1)}, u32[]{:S(2)}, u32[]{:S(2)}) collective-permute-start(f32[1,4,128,256]{3,2,1,0:T(8,128)S(1)} %get-tuple-element.36), channel_id=1, source_target_pairs={{0,1},{1,2},{2,3},{3,4},{4,5},{5,6},{6,7},{8,9},{9,10},{10,11},{11... | collective-permute-start | bytes 1572872 | tf_op jit(solution)/shard_map/ppermute | solution.py:70
  70.5 38.1 %collective-permute-start.4 = (f32[1,4,128,256]{3,2,1,0:T(8,128)S(1)}, f32[1,4,128,256]{3,2,1,0:T(8,128)S(1)}, u32[]{:S(2)}, u32[]{:S(2)}) collective-permute-start(f32[1,4,128,256]{3,2,1,0:T(8,128)S(1)} %get-tuple-element.35), channel_id=1, source_target_pairs={{1,0},{2,1},{3,2},{4,3},{5,4},{6,5},{7,6},{9,8},{10,9},{11,10},{12... | collective-permute-start | bytes 1572872 | tf_op jit(solution)/shard_map/ppermute | solution.py:71
  73.4 1.2 copy-start.7
  114.6 2.0 %collective-permute-start.8 = (f32[8,2,32,256]{3,0,2,1:T(8,128)S(1)}, f32[8,2,32,256]{3,0,2,1:T(8,128)S(1)}, u32[]{:S(2)}, u32[]{:S(2)}) collective-permute-start(f32[8,2,32,256]{3,0,2,1:T(8,128)S(1)} %bitcast.197), channel_id=1, source_target_pairs={{0,8},{8,0},{16,24},{24,16},{1,9},{9,1},{17,25},{25,17},{2,10},{10... | collective-permute-start | bytes 1572872 | tf_op jit(solution)/shard_map/ppermute | solution.py:120
  117.0 8.4 %collective-permute-start.9 = (f32[8,1,32,256]{3,0,2,1:T(8,128)S(1)}, f32[8,1,32,256]{3,0,2,1:T(8,128)S(1)}, u32[]{:S(2)}, u32[]{:S(2)}) collective-permute-start(f32[8,1,32,256]{3,0,2,1:T(8,128)S(1)} %constant_dynamic-slice_fusion), channel_id=1, source_target_pairs={{0,16},{8,24},{16,0},{24,8},{1,17},{9,25},{17,1},{25,9},{2,18},{10... | collective-permute-start | bytes 786440 | tf_op jit(solution)/shard_map/ppermute | solution.py:120

commit v10 on v9

--- a/solution.py
+++ b/solution.py
@@ -167,8 +167,12 @@
         correlation = part if correlation is None else correlation + part
         earlier, current = (current, fresh)
     lateral_smooth = smooth(smooth(correlation, 1), 2)
-    reduced = reduce_shots(lateral_smooth, 1)
-    columns = lax.all_to_all(reduced, "depth", split_axis=1, concat_axis=0, tiled=True)
+    moved = lax.all_to_all(lateral_smooth, ("shots", "depth"), split_axis=1, concat_axis=0, tiled=True)
+    groups = lax.axis_size("shots")
+    moved = moved.reshape((groups, moved.shape[0] // groups) + moved.shape[1:])
+    columns = moved[0]
+    for g in range(1, groups):
+        columns = columns + moved[g]
     gradient = smooth(columns, 0)
     return (earlier[0], current[0], earlier[1], current[1], gradient)
 

time: 141 us -> 150 us (1.064)
  blocking collectives: 14.1 us -> 33.5 us
  waiting for transfers between devices: 46.4 us -> 39.6 us
  local copies, waits for them, and re-layouts: 15.5 us -> 13.5 us
  starting transfers between devices: 27.3 us -> 25.5 us
  matrix products: 27.8 us -> 26.1 us
  other arithmetic: 8.33 us -> 9.89 us
    all_to_all x1, blocking collectives: 14.1 us -> 33.5 us  [on_device(): lax.all_to_all(lateral_smooth, ('shots', 'depth'), split_axis=1, concat_a...]
    ppermute x2 -> x0, waiting for transfers between devices: 8.72 us -> none  [reduce_shots(): blocks = keep + lax.ppermute(send, 'shots', pairs)]
    dot_general x4, matrix products: 7.49 us -> 5.45 us  [lateral_laplace(): along_x = jnp.einsum('...xy,kx->...ky', core, band(rows), precision=high)]
    ppermute x4, waiting for transfers between devices: 37.6 us -> 39.6 us  [exchange(): below = lax.ppermute(last, 'depth', up)]
    ppermute x2 -> x0, starting transfers between devices: 1.62 us -> none  [reduce_shots(): blocks = keep + lax.ppermute(send, 'shots', pairs)]
    unnamed x45 -> x34, local copies, waits for them, and re-layouts: 5.5 us -> 4.46 us
  transfers between devices with their start and end apart: 10 -> 8, of which waited for: 5 -> 3; matrix products, arithmetic and copies ran while one was open for 25% -> 23% of each run, Pallas kernels for 0% -> 0%
where the time goes in v10:
time: 150 us; the launch traced here: 149 us
  waiting for transfers between devices  39.6 us (26%)
  blocking collectives  33.5 us (22%)
  matrix products  26.1 us (17%)
  starting transfers between devices  25.5 us (17%)
  local copies, waits for them, and re-layouts  13.5 us (9%)
  other arithmetic  9.89 us (7%)
    ppermute x4, waiting for transfers between devices, exchange(): below = lax.ppermute(last, 'depth', up)  39.6 us
    all_to_all x1, blocking collectives, on_device(): lax.all_to_all(lateral_smooth, ('shots', 'depth'), split_axis=1, concat_a...  33.5 us
    ppermute x4, starting transfers between devices, exchange(): below = lax.ppermute(last, 'depth', up)  20.2 us
    dot_general x2, matrix products, spread_dense(): grid = jnp.dot(by_row, right, preferred_element_type=jnp.float32)  16.4 us
    dot_general x4, matrix products, lateral_laplace(): along_x = jnp.einsum('...xy,kx->...ky', core, band(rows), precision=high)  5.45 us
    ppermute x4, starting transfers between devices, exchange(): above = lax.ppermute(leading, 'depth', down)  5.36 us
    unnamed x34, local copies, waits for them, and re-layouts  4.46 us
    dot_general x4, matrix products, lateral_laplace(): along_y = jnp.einsum('...xy,yk->...xk', core, band(cols), precision=high)  4.19 us
  transfers between devices with their start and end apart: 8, of which 3 were waited for; matrix products, arithmetic and copies ran while one was open for 23% of the time, Pallas kernels for 0%

profile of v10, /device:TPU:0, one launch (start us, length us, event | category | flops | bytes accessed | tf_op | source)
XLA Modules:
  0.0 149.2 jit_solution(10102055186150693823)
XLA Ops:
  0.6 2.3 %fusion.218 = (f32[1,4,128,256]{3,2,1,0:T(8,128)}, f32[1,4,128,256]{3,2,1,0:T(8,128)}) fusion(f32[1,8,128,256]{3,2,1,0:T(8,128)} %param.15), kind=kLoop, calls=%fused_computation.310 | loop fusion | bytes 2097152 | tf_op jit(solution)/shard_map/slice | solution.py:69
  3.0 5.7 %collective-permute-start.3 = (f32[1,4,128,256]{3,2,1,0:T(8,128)}, f32[1,4,128,256]{3,2,1,0:T(8,128)}, u32[]{:S(2)}, u32[]{:S(2)}) collective-permute-start(f32[1,4,128,256]{3,2,1,0:T(8,128)} %get-tuple-element.35), channel_id=1, source_target_pairs={{0,1},{1,2},{2,3},{3,4},{4,5},{5,6},{6,7},{8,9},{9,10},{10,11},{11... | collective-permute-start | bytes 1572872 | tf_op jit(solution)/shard_map/ppermute | solution.py:70
  8.6 1.3 collective-permute-start.2
  9.9 1.1 fusion.219
  11.1 5.5 %collective-permute-start.1 = (f32[1,4,128,256]{3,2,1,0:T(8,128)}, f32[1,4,128,256]{3,2,1,0:T(8,128)}, u32[]{:S(2)}, u32[]{:S(2)}) collective-permute-start(f32[1,4,128,256]{3,2,1,0:T(8,128)} %get-tuple-element.39), channel_id=1, source_target_pairs={{0,1},{1,2},{2,3},{3,4},{4,5},{5,6},{6,7},{8,9},{9,10},{10,11},{11... | collective-permute-start | bytes 1572872 | tf_op jit(solution)/shard_map/ppermute | solution.py:70
  16.6 1.3 collective-permute-start
  17.8 1.0 convolution_bitcast_fusion.6
  19.1 1.8 %fusion.12 = f32[1024,3,2,256]{3,0,2,1:T(8,128)S(1)} fusion(pred[512,256]{0,1:T(8,128)(4,1)S(1)} %iota_compare_fusion.3, s32[512]{0:T(512)S(1)} %get-tuple-element.54, bf16[512,3,2]{0,2,1:T(2,128)(2,1)S(1)} %maximum_bitcast_fusion.1), kind=kOutput, calls=%fused_computation.30 | convolution fusion | flops 1611923456 | bytes 6430720 | tf_op jit(solution)/shard_map/dot_general | solution.py:100
  21.4 1.1 fusion.211
  22.5 1.6 %iota_compare_fusion.1 = pred[4096,256]{0,1:T(8,128)(4,1)} fusion(s32[4096]{0:T(1024)S(1)} %get-tuple-element.50), kind=kLoop, calls=%fused_computation.9 | loop fusion | flops 1048576 | bytes 1064960 | tf_op jit(solution)/shard_map/eq | solution.py:90
  24.3 14.6 %fusion.1 = f32[1024,3,2,256]{3,0,2,1:T(8,128)S(1)} fusion(pred[4096,256]{0,1:T(8,128)(4,1)} %iota_compare_fusion.1, s32[4096]{0:T(1024)S(1)} %get-tuple-element.49, bf16[4096,3,2]{0,2,1:T(2,128)(2,1)S(1)} %maximum_bitcast_fusion), kind=kOutput, calls=%fused_computation.2 | convolution fusion | flops 12895387648 | bytes 7405568 | tf_op jit(solution)/shard_map/dot_general | solution.py:100
  39.4 1.0 copy-done
  41.1 1.3 fusion.21
  42.5 1.1 convolution_bitcast_fusion.4
  43.7 1.4 fusion.26
  45.1 1.1 constant_dynamic-update-slice_fusion.7
  46.2 6.8 %collective-permute-done.1 = f32[1,4,128,256]{3,2,1,0:T(8,128)} collective-permute-done((f32[1,4,128,256]{3,2,1,0:T(8,128)}, f32[1,4,128,256]{3,2,1,0:T(8,128)}, u32[]{:S(2)}, u32[]{:S(2)}) %collective-permute-start.1) | collective-permute-done | bytes 524320 | tf_op jit(solution)/shard_map/ppermute | solution.py:70
  53.0 1.1 constant_dynamic-update-slice_fusion.3
  54.3 1.1 constant_dynamic-update-slice_fusion.4
  55.6 1.1 constant_dynamic-update-slice_fusion
  56.7 1.6 %fusion.78 = (f32[1,8,128,256]{3,2,1,0:T(8,128)S(1)}, f32[1,8,128,256]{3,2,1,0:T(8,128)S(1)}) fusion(f32[1,8,128,256]{3,2,1,0:T(8,128)S(1)} %fusion.26, f32[1,12,128,256]{3,2,1,0:T(8,128)S(1)} %get-tuple-element.37, f32[1,12,128,256]{3,2,1,0:T(8,128)S(1)} %constant_dynamic-update-slice_fusion.4, f32[8,128,256]{2,1,0:T(8,128)S(1)} %copy-done, ...), kind=kLoop, calls=%fused_computation.120 | loop fusion | flops 6815744 | bytes 22020096 | tf_op jit(solution)/shard_map/add | solution.py:162
  58.4 1.0 convolution_bitcast_fusion.2
  59.7 4.4 %collective-permute-start.7 = (f32[1,4,128,256]{3,2,1,0:T(8,128)S(1)}, f32[1,4,128,256]{3,2,1,0:T(8,128)S(1)}, u32[]{:S(2)}, u32[]{:S(2)}) collective-permute-start(f32[1,4,128,256]{3,2,1,0:T(8,128)S(1)} %get-tuple-element.31), channel_id=1, source_target_pairs={{0,1},{1,2},{2,3},{3,4},{4,5},{5,6},{6,7},{8,9},{9,10},{10,11},{11... | collective-permute-start | bytes 1572872 | tf_op jit(solution)/shard_map/ppermute | solution.py:70
  64.1 1.3 collective-permute-start.6
  65.4 4.6 %collective-permute-start.5 = (f32[1,4,128,256]{3,2,1,0:T(8,128)S(1)}, f32[1,4,128,256]{3,2,1,0:T(8,128)S(1)}, u32[]{:S(2)}, u32[]{:S(2)}) collective-permute-start(f32[1,4,128,256]{3,2,1,0:T(8,128)S(1)} %get-tuple-element.29), channel_id=1, source_target_pairs={{0,1},{1,2},{2,3},{3,4},{4,5},{5,6},{6,7},{8,9},{9,10},{10,11},{11... | collective-permute-start | bytes 1572872 | tf_op jit(solution)/shard_map/ppermute | solution.py:70
  70.0 1.5 %collective-permute-start.4 = (f32[1,4,128,256]{3,2,1,0:T(8,128)S(1)}, f32[1,4,128,256]{3,2,1,0:T(8,128)S(1)}, u32[]{:S(2)}, u32[]{:S(2)}) collective-permute-start(f32[1,4,128,256]{3,2,1,0:T(8,128)S(1)} %get-tuple-element.28), channel_id=1, source_target_pairs={{1,0},{2,1},{3,2},{4,3},{5,4},{6,5},{7,6},{9,8},{10,9},{11,10},{12... | collective-permute-start | bytes 1572872 | tf_op jit(solution)/shard_map/ppermute | solution.py:71
  71.5 1.4 fusion.31
  74.0 1.3 fusion.36
  75.3 23.6 %collective-permute-done.7 = f32[1,4,128,256]{3,2,1,0:T(8,128)S(1)} collective-permute-done((f32[1,4,128,256]{3,2,1,0:T(8,128)S(1)}, f32[1,4,128,256]{3,2,1,0:T(8,128)S(1)}, u32[]{:S(2)}, u32[]{:S(2)}) %collective-permute-start.7) | collective-permute-done | bytes 524320 | tf_op jit(solution)/shard_map/ppermute | solution.py:70
  98.9 9.2 %collective-permute-done.5 = f32[1,4,128,256]{3,2,1,0:T(8,128)S(1)} collective-permute-done((f32[1,4,128,256]{3,2,1,0:T(8,128)S(1)}, f32[1,4,128,256]{3,2,1,0:T(8,128)S(1)}, u32[]{:S(2)}, u32[]{:S(2)}) %collective-permute-start.5) | collective-permute-done | bytes 524320 | tf_op jit(solution)/shard_map/ppermute | solution.py:70
  108.1 3.5 %bitcast_add_fusion = (f32[8,128,256]{2,1,0:T(8,128)S(1)}, f32[1,8,128,256]{3,2,1,0:T(8,128)}, f32[1,8,128,256]{3,2,1,0:T(8,128)}) fusion(f32[1,8,128,256]{3,2,1,0:T(8,128)S(1)} %get-tuple-element.32, f32[1,8,128,256]{3,2,1,0:T(8,128)S(1)} %get-tuple-element.33, f32[1,8,128,256]{3,2,1,0:T(8,128)S(1)} %fusion.36, ...), kind=kLoop, calls=%fused_computation.142 | loop fusion | flops 11796480 | bytes 10485760 | tf_op jit(solution)/shard_map/add | solution.py:167
  114.4 33.5 %all_to_all.15 = f32[8,128,256]{2,0,1:T(8,128)S(1)} all-to-all(f32[8,128,256]{2,0,1:T(8,128)S(1)} %copy.26), channel_id=1, replica_groups=mesh['shots'=4,'depth'=8] {'shots','depth'}, dimensions={1} | all-to-all | bytes 2097152 | tf_op jit(solution)/shard_map/all_to_all | solution.py:170
  (62 shorter events, 7.8 us)
Async XLA Ops:
  0.6 9.3 %copy-start.1 = (f32[1,8,128,256]{3,2,1,0:T(8,128)S(1)}, f32[1,8,128,256]{3,2,1,0:T(8,128)}, u32[]{:S(2)}) copy-start(f32[1,8,128,256]{3,2,1,0:T(8,128)} %param.13) | copy-start | bytes 3145732
  3.0 42.1 %collective-permute-start.3 = (f32[1,4,128,256]{3,2,1,0:T(8,128)}, f32[1,4,128,256]{3,2,1,0:T(8,128)}, u32[]{:S(2)}, u32[]{:S(2)}) collective-permute-start(f32[1,4,128,256]{3,2,1,0:T(8,128)} %get-tuple-element.35), channel_id=1, source_target_pairs={{0,1},{1,2},{2,3},{3,4},{4,5},{5,6},{6,7},{8,9},{9,10},{10,11},{11... | collective-permute-start | bytes 1572872 | tf_op jit(solution)/shard_map/ppermute | solution.py:70
  8.6 45.7 %collective-permute-start.2 = (f32[1,4,128,256]{3,2,1,0:T(8,128)}, f32[1,4,128,256]{3,2,1,0:T(8,128)}, u32[]{:S(2)}, u32[]{:S(2)}) collective-permute-start(f32[1,4,128,256]{3,2,1,0:T(8,128)} %get-tuple-element.34), channel_id=1, source_target_pairs={{1,0},{2,1},{3,2},{4,3},{5,4},{6,5},{7,6},{9,8},{10,9},{11,10},{12... | collective-permute-start | bytes 1572872 | tf_op jit(solution)/shard_map/ppermute | solution.py:71
  11.1 7.9 %copy-start.12 = (s32[512]{0:T(512)S(1)}, s32[512]{0:T(512)}, u32[]{:S(2)}) copy-start(s32[512]{0:T(512)} %param.20) | copy-start | bytes 6148
  11.1 7.9 %copy-start.13 = (s32[512]{0:T(512)S(1)}, s32[512]{0:T(512)}, u32[]{:S(2)}) copy-start(s32[512]{0:T(512)} %param.19) | copy-start | bytes 6148
  11.1 8.0 %copy-start.14 = (s32[1,512]{1,0:T(1,128)S(1)}, s32[1,512]{1,0:T(1,128)}, u32[]{:S(2)}) copy-start(s32[1,512]{1,0:T(1,128)} %param.18) | copy-start | bytes 6148
  11.1 8.0 %copy-start.11 = (f32[2,512]{1,0:T(2,128)S(1)}, f32[2,512]{1,0:T(2,128)}, u32[]{:S(2)}) copy-start(f32[2,512]{1,0:T(2,128)} %param.17) | copy-start | bytes 12292
  11.1 42.0 %collective-permute-start.1 = (f32[1,4,128,256]{3,2,1,0:T(8,128)}, f32[1,4,128,256]{3,2,1,0:T(8,128)}, u32[]{:S(2)}, u32[]{:S(2)}) collective-permute-start(f32[1,4,128,256]{3,2,1,0:T(8,128)} %get-tuple-element.39), channel_id=1, source_target_pairs={{0,1},{1,2},{2,3},{3,4},{4,5},{5,6},{6,7},{8,9},{9,10},{10,11},{11... | collective-permute-start | bytes 1572872 | tf_op jit(solution)/shard_map/ppermute | solution.py:70
  16.6 39.1 %collective-permute-start = (f32[1,4,128,256]{3,2,1,0:T(8,128)}, f32[1,4,128,256]{3,2,1,0:T(8,128)}, u32[]{:S(2)}, u32[]{:S(2)}) collective-permute-start(f32[1,4,128,256]{3,2,1,0:T(8,128)} %get-tuple-element.38), channel_id=1, source_target_pairs={{1,0},{2,1},{3,2},{4,3},{5,4},{6,5},{7,6},{9,8},{10,9},{11,10},{12... | collective-permute-start | bytes 1572872 | tf_op jit(solution)/shard_map/ppermute | solution.py:71
  21.4 1.1 copy-start.9
  21.4 1.1 copy-start.10
  21.4 2.7 %copy-start.8 = (f32[1,2,4096]{2,1,0:T(2,128)S(1)}, f32[1,2,4096]{2,1,0:T(2,128)}, u32[]{:S(2)}) copy-start(f32[1,2,4096]{2,1,0:T(2,128)} %param.23) | copy-start | bytes 98308
  39.3 1.2 copy-start
  39.3 1.5 %copy-start.5 = (f32[1,1024,256]{2,1,0:T(8,128)S(1)}, f32[1,1024,256]{2,1,0:T(8,128)}, u32[]{:S(2)}) copy-start(f32[1,1024,256]{2,1,0:T(8,128)} %get-tuple-element.19) | copy-start | bytes 3145732
  39.3 1.8 %copy-start.6 = (f32[1,8,128,256]{3,2,1,0:T(8,128)S(1)}, f32[1,8,128,256]{3,2,1,0:T(8,128)}, u32[]{:S(2)}) copy-start(f32[1,8,128,256]{3,2,1,0:T(8,128)} %param.12) | copy-start | bytes 3145732
  41.1 1.4 copy-start.2
  42.5 1.2 copy-start.7
  58.4 49.7 %copy-start.3 = (f32[1,8,128,256]{3,2,1,0:T(8,128)}, f32[1,8,128,256]{3,2,1,0:T(8,128)S(1)}, u32[]{:S(2)}) copy-start(f32[1,8,128,256]{3,2,1,0:T(8,128)S(1)} %get-tuple-element.32) | copy-start | bytes 3145732
  58.4 49.7 %copy-start.4 = (f32[1,8,128,256]{3,2,1,0:T(8,128)}, f32[1,8,128,256]{3,2,1,0:T(8,128)S(1)}, u32[]{:S(2)}) copy-start(f32[1,8,128,256]{3,2,1,0:T(8,128)S(1)} %get-tuple-element.33) | copy-start | bytes 3145732
  59.7 39.2 %collective-permute-start.7 = (f32[1,4,128,256]{3,2,1,0:T(8,128)S(1)}, f32[1,4,128,256]{3,2,1,0:T(8,128)S(1)}, u32[]{:S(2)}, u32[]{:S(2)}) collective-permute-start(f32[1,4,128,256]{3,2,1,0:T(8,128)S(1)} %get-tuple-element.31), channel_id=1, source_target_pairs={{0,1},{1,2},{2,3},{3,4},{4,5},{5,6},{6,7},{8,9},{9,10},{10,11},{11... | collective-permute-start | bytes 1572872 | tf_op jit(solution)/shard_map/ppermute | solution.py:70
  64.1 34.8 %collective-permute-start.6 = (f32[1,4,128,256]{3,2,1,0:T(8,128)S(1)}, f32[1,4,128,256]{3,2,1,0:T(8,128)S(1)}, u32[]{:S(2)}, u32[]{:S(2)}) collective-permute-start(f32[1,4,128,256]{3,2,1,0:T(8,128)S(1)} %get-tuple-element.30), channel_id=1, source_target_pairs={{1,0},{2,1},{3,2},{4,3},{5,4},{6,5},{7,6},{9,8},{10,9},{11,10},{12... | collective-permute-start | bytes 1572872 | tf_op jit(solution)/shard_map/ppermute | solution.py:71
  65.4 42.7 %collective-permute-start.5 = (f32[1,4,128,256]{3,2,1,0:T(8,128)S(1)}, f32[1,4,128,256]{3,2,1,0:T(8,128)S(1)}, u32[]{:S(2)}, u32[]{:S(2)}) collective-permute-start(f32[1,4,128,256]{3,2,1,0:T(8,128)S(1)} %get-tuple-element.29), channel_id=1, source_target_pairs={{0,1},{1,2},{2,3},{3,4},{4,5},{5,6},{6,7},{8,9},{9,10},{10,11},{11... | collective-permute-start | bytes 1572872 | tf_op jit(solution)/shard_map/ppermute | solution.py:70
  70.0 38.1 %collective-permute-start.4 = (f32[1,4,128,256]{3,2,1,0:T(8,128)S(1)}, f32[1,4,128,256]{3,2,1,0:T(8,128)S(1)}, u32[]{:S(2)}, u32[]{:S(2)}) collective-permute-start(f32[1,4,128,256]{3,2,1,0:T(8,128)S(1)} %get-tuple-element.28), channel_id=1, source_target_pairs={{1,0},{2,1},{3,2},{4,3},{5,4},{6,5},{7,6},{9,8},{10,9},{11,10},{12... | collective-permute-start | bytes 1572872 | tf_op jit(solution)/shard_map/ppermute | solution.py:71

commit v11 on v9

--- a/solution.py
+++ b/solution.py
@@ -51,6 +51,22 @@
         )
         total = COEFFS[k] * near if total is None else total + COEFFS[k] * near
     return total
+
+
+def smooth_matrix(size):
+    index = jnp.arange(size)
+    gap = index[:, None] - index[None, :]
+    matrix = jnp.zeros((size, size), jnp.float32)
+    for k in range(-2, 3):
+        matrix = jnp.where(gap == k, jnp.float32(KERNEL[2 + k]), matrix)
+    return matrix
+
+
+def smooth_lateral(values):
+    high = lax.Precision.HIGHEST
+    rows, cols = values.shape[-2], values.shape[-1]
+    along_y = jnp.einsum("...xy,yk->...xk", values, smooth_matrix(cols), precision=high)
+    return jnp.einsum("...xy,kx->...ky", along_y, smooth_matrix(rows), precision=high)
 
 
 def smooth(values, axis):
@@ -166,7 +182,7 @@
         part = fresh[0][0] * fresh[1][0]
         correlation = part if correlation is None else correlation + part
         earlier, current = (current, fresh)
-    lateral_smooth = smooth(smooth(correlation, 1), 2)
+    lateral_smooth = smooth_lateral(correlation)
     reduced = reduce_shots(lateral_smooth, 1)
     columns = lax.all_to_all(reduced, "depth", split_axis=1, concat_axis=0, tiled=True)
     gradient = smooth(columns, 0)

time: 141 us -> 140 us (level)
  other arithmetic: 8.33 us -> 6.08 us
  matrix products: 27.8 us -> 29.7 us
    add x1 -> x0, other arithmetic: 3.46 us -> none  [on_device(): correlation = part if correlation is None else correlation + part]
    add x1 -> x2, other arithmetic: 1.61 us -> 3.93 us  [on_device(): partial[i] + courant * depth_laplace(below[i], current[i], above[i], zaxis)]
    dot_general x0 -> x2, matrix products: none -> 2.05 us  [the longest x1 1.04 us: smooth_lateral(): jnp.einsum('...xy,yk->...xk', values, smooth_matrix(cols), precision=high)]
    unnamed x45 -> x53, local copies, waits for them, and re-layouts: 5.5 us -> 6.05 us
where the time goes in v11:
time: 140 us
  waiting for transfers between devices  46.2 us (33%)
  matrix products  29.7 us (21%)
  starting transfers between devices  27.3 us (20%)
  local copies, waits for them, and re-layouts  15 us (11%)
  blocking collectives  14.1 us (10%)
  other arithmetic  6.08 us (4%)
    ppermute x4, waiting for transfers between devices, exchange(): below = lax.ppermute(last, 'depth', up)  37.5 us
    ppermute x4, starting transfers between devices, exchange(): below = lax.ppermute(last, 'depth', up)  20.3 us
    dot_general x2, matrix products, spread_dense(): grid = jnp.dot(by_row, right, preferred_element_type=jnp.float32)  15.2 us
    all_to_all x1, blocking collectives, on_device(): lax.all_to_all(reduced, 'depth', split_axis=1, concat_axis=0, tiled=True)  14.1 us
    ppermute x2, waiting for transfers between devices, reduce_shots(): blocks = keep + lax.ppermute(send, 'shots', pairs)  8.72 us
    dot_general x4, matrix products, lateral_laplace(): along_x = jnp.einsum('...xy,kx->...ky', core, band(rows), precision=high)  7.32 us
    unnamed x53, local copies, waits for them, and re-layouts  6.05 us
    ppermute x4, starting transfers between devices, exchange(): above = lax.ppermute(leading, 'depth', down)  5.36 us
  transfers between devices with their start and end apart: 10, of which 5 were waited for; matrix products, arithmetic and copies ran while one was open for 25% of the time, Pallas kernels for 0%

profile of v11, /device:TPU:0, one launch (start us, length us, event | category | flops | bytes accessed | tf_op | source)
XLA Modules:
  0.0 139.6 jit_solution(3933308958666211615)
XLA Ops:
  0.6 2.4 %fusion.286 = (f32[1,4,128,256]{3,2,1,0:T(8,128)}, f32[1,4,128,256]{3,2,1,0:T(8,128)}) fusion(f32[1,8,128,256]{3,2,1,0:T(8,128)} %param.15), kind=kLoop, calls=%fused_computation.372 | loop fusion | bytes 2097152 | tf_op jit(solution)/shard_map/slice | solution.py:85
  3.0 5.7 %collective-permute-start.3 = (f32[1,4,128,256]{3,2,1,0:T(8,128)}, f32[1,4,128,256]{3,2,1,0:T(8,128)}, u32[]{:S(2)}, u32[]{:S(2)}) collective-permute-start(f32[1,4,128,256]{3,2,1,0:T(8,128)} %get-tuple-element.33), channel_id=1, source_target_pairs={{0,1},{1,2},{2,3},{3,4},{4,5},{5,6},{6,7},{8,9},{9,10},{10,11},{11... | collective-permute-start | bytes 1572872 | tf_op jit(solution)/shard_map/ppermute | solution.py:86
  8.7 1.3 collective-permute-start.2
  10.0 1.1 fusion.287
  11.1 5.5 %collective-permute-start.1 = (f32[1,4,128,256]{3,2,1,0:T(8,128)}, f32[1,4,128,256]{3,2,1,0:T(8,128)}, u32[]{:S(2)}, u32[]{:S(2)}) collective-permute-start(f32[1,4,128,256]{3,2,1,0:T(8,128)} %get-tuple-element.37), channel_id=1, source_target_pairs={{0,1},{1,2},{2,3},{3,4},{4,5},{5,6},{6,7},{8,9},{9,10},{10,11},{11... | collective-permute-start | bytes 1572872 | tf_op jit(solution)/shard_map/ppermute | solution.py:86
  16.6 1.3 collective-permute-start
  17.9 2.0 %convolution_bitcast_fusion.6 = f32[1,8,128,256]{3,2,1,0:T(8,128)} fusion(f32[1,8,128,256]{3,2,1,0:T(8,128)S(1)} %copy-done.3), kind=kOutput, calls=%fused_computation.52 | convolution fusion | flops 805961728 | bytes 2097152 | tf_op jit(solution)/shard_map/...xy,yk->...xk/dot_general | solution.py:39
  20.1 1.8 %fusion.12 = f32[1024,3,2,256]{3,0,2,1:T(8,128)S(1)} fusion(pred[512,256]{0,1:T(8,128)(4,1)S(1)} %iota_compare_fusion.3, s32[512]{0:T(512)S(1)} %get-tuple-element.52, bf16[512,3,2]{0,2,1:T(2,128)(2,1)S(1)} %maximum_bitcast_fusion.1), kind=kOutput, calls=%fused_computation.30 | convolution fusion | flops 1611923456 | bytes 6430720 | tf_op jit(solution)/shard_map/dot_general | solution.py:116
  22.4 1.5 %fusion.283 = (f32[1,1024,256]{2,1,0:T(8,128)}, f32[1,1024,256]{2,1,0:T(8,128)}) fusion(f32[2,1024,256]{2,1,0:T(8,128)S(1)} %fusion.10), kind=kLoop, calls=%fused_computation.369 | loop fusion | bytes 4194304 | tf_op jit(solution)/shard_map/slice | solution.py:170
  24.6 13.4 %fusion.1 = f32[1024,3,2,256]{3,0,2,1:T(8,128)S(1)} fusion(pred[4096,256]{0,1:T(8,128)(4,1)S(1)} %iota_compare_fusion.1, s32[4096]{0:T(1024)S(1)} %get-tuple-element.47, bf16[4096,3,2]{0,2,1:T(2,128)(2,1)S(1)} %maximum_bitcast_fusion), kind=kOutput, calls=%fused_computation.2 | convolution fusion | flops 12895387648 | bytes 7405568 | tf_op jit(solution)/shard_map/dot_general | solution.py:116
  38.4 1.1 fusion.282
  40.9 2.3 %fusion.21 = f32[1,8,128,256]{3,2,1,0:T(8,128)} fusion(f32[1,8,128,256]{3,2,1,0:T(8,128)S(1)} %bitcast.205, f32[1,8,128,256]{3,2,1,0:T(8,128)S(1)} %copy-done.9, f32[1,8,128,256]{3,2,1,0:T(8,128)S(1)} %copy-done.3, f32[8,128,256]{2,1,0:T(8,128)S(1)} %copy-done.2, f32[1,8,128,256]{3,2,1,0:T(8,128)S(1)} %copy-done.15), kind=kOutput, calls=%fused_computation.58 | convolution fusion | flops 404914176 | bytes 6291456 | tf_op jit(solution)/shard_map/...xy,kx->...ky/dot_general | solution.py:40
  44.5 2.3 %fusion.26 = f32[1,8,128,256]{3,2,1,0:T(8,128)} fusion(f32[1,8,128,256]{3,2,1,0:T(8,128)S(1)} %bitcast.206, f32[1,8,128,256]{3,2,1,0:T(8,128)S(1)} %convolution_bitcast_fusion.4, f32[1,8,128,256]{3,2,1,0:T(8,128)S(1)} %copy-done.5, f32[8,128,256]{2,1,0:T(8,128)S(1)} %copy-done.2, f32[1,8,128,256]{3,2,1,0:T(8,128)S(1)} %copy-done.16), kind=kOutput, calls=%fused_computation.63 | convolution fusion | flops 404914176 | bytes 6291456 | tf_op jit(solution)/shard_map/...xy,kx->...ky/dot_general | solution.py:40
  46.9 1.1 constant_dynamic-update-slice_fusion.7
  47.9 5.1 %collective-permute-done.1 = f32[1,4,128,256]{3,2,1,0:T(8,128)} collective-permute-done((f32[1,4,128,256]{3,2,1,0:T(8,128)}, f32[1,4,128,256]{3,2,1,0:T(8,128)}, u32[]{:S(2)}, u32[]{:S(2)}) %collective-permute-start.1) | collective-permute-done | bytes 524320 | tf_op jit(solution)/shard_map/ppermute | solution.py:86
  53.1 1.1 constant_dynamic-update-slice_fusion.3
  54.4 1.1 constant_dynamic-update-slice_fusion.4
  55.7 1.2 constant_dynamic-update-slice_fusion
  57.1 1.6 %fusion.78 = (f32[1,8,128,256]{3,2,1,0:T(8,128)S(1)}, f32[1,8,128,256]{3,2,1,0:T(8,128)S(1)}) fusion(f32[1,8,128,256]{3,2,1,0:T(8,128)S(1)} %copy-done.14, f32[1,12,128,256]{3,2,1,0:T(8,128)S(1)} %get-tuple-element.35, f32[1,12,128,256]{3,2,1,0:T(8,128)S(1)} %constant_dynamic-update-slice_fusion.4, f32[8,128,256]{2,1,0:T(8,128)S(1)} %copy-done.2, ...), kind=kLoop, calls=%fused_computation.120 | loop fusion | flops 6815744 | bytes 22020096 | tf_op jit(solution)/shard_map/add | solution.py:178
  60.0 4.6 %collective-permute-start.7 = (f32[1,4,128,256]{3,2,1,0:T(8,128)S(1)}, f32[1,4,128,256]{3,2,1,0:T(8,128)S(1)}, u32[]{:S(2)}, u32[]{:S(2)}) collective-permute-start(f32[1,4,128,256]{3,2,1,0:T(8,128)S(1)} %get-tuple-element.27), channel_id=1, source_target_pairs={{0,1},{1,2},{2,3},{3,4},{4,5},{5,6},{6,7},{8,9},{9,10},{10,11},{11... | collective-permute-start | bytes 1572872 | tf_op jit(solution)/shard_map/ppermute | solution.py:86
  64.6 1.3 collective-permute-start.6
  65.9 4.6 %collective-permute-start.5 = (f32[1,4,128,256]{3,2,1,0:T(8,128)S(1)}, f32[1,4,128,256]{3,2,1,0:T(8,128)S(1)}, u32[]{:S(2)}, u32[]{:S(2)}) collective-permute-start(f32[1,4,128,256]{3,2,1,0:T(8,128)S(1)} %get-tuple-element.29), channel_id=1, source_target_pairs={{0,1},{1,2},{2,3},{3,4},{4,5},{5,6},{6,7},{8,9},{9,10},{10,11},{11... | collective-permute-start | bytes 1572872 | tf_op jit(solution)/shard_map/ppermute | solution.py:86
  70.5 1.5 %collective-permute-start.4 = (f32[1,4,128,256]{3,2,1,0:T(8,128)S(1)}, f32[1,4,128,256]{3,2,1,0:T(8,128)S(1)}, u32[]{:S(2)}, u32[]{:S(2)}) collective-permute-start(f32[1,4,128,256]{3,2,1,0:T(8,128)S(1)} %get-tuple-element.28), channel_id=1, source_target_pairs={{1,0},{2,1},{3,2},{4,3},{5,4},{6,5},{7,6},{9,8},{10,9},{11,10},{12... | collective-permute-start | bytes 1572872 | tf_op jit(solution)/shard_map/ppermute | solution.py:87
  72.0 1.3 fusion.31
  74.9 1.3 fusion.36
  76.2 23.2 %collective-permute-done.7 = f32[1,4,128,256]{3,2,1,0:T(8,128)S(1)} collective-permute-done((f32[1,4,128,256]{3,2,1,0:T(8,128)S(1)}, f32[1,4,128,256]{3,2,1,0:T(8,128)S(1)}, u32[]{:S(2)}, u32[]{:S(2)}) %collective-permute-start.7) | collective-permute-done | bytes 524320 | tf_op jit(solution)/shard_map/ppermute | solution.py:86
  99.4 9.2 %collective-permute-done.5 = f32[1,4,128,256]{3,2,1,0:T(8,128)S(1)} collective-permute-done((f32[1,4,128,256]{3,2,1,0:T(8,128)S(1)}, f32[1,4,128,256]{3,2,1,0:T(8,128)S(1)}, u32[]{:S(2)}, u32[]{:S(2)}) %collective-permute-start.5) | collective-permute-done | bytes 524320 | tf_op jit(solution)/shard_map/ppermute | solution.py:86
  108.5 2.3 %fusion.43 = (f32[1,8,128,256]{3,2,1,0:T(8,128)S(1)}, f32[1,8,128,256]{3,2,1,0:T(8,128)S(1)}) fusion(f32[1,8,128,256]{3,2,1,0:T(8,128)S(1)} %fusion.36, f32[1,8,128,256]{3,2,1,0:T(8,128)S(1)} %get-tuple-element.30, f32[1,4,128,256]{3,2,1,0:T(8,128)S(1)} %collective-permute-done.7, f32[1,4,128,256]{3,2,1,0:T(8,128)S(1)} %collective-permute-done.6, ...), kind=kLoop, calls=%fused_computation.80 | loop fusion | flops 11010048 | bytes 9437184 | tf_op jit(solution)/shard_map/add | solution.py:178
  113.7 1.9 %collective-permute-done.8 = f32[8,2,32,256]{3,0,2,1:T(8,128)S(1)} collective-permute-done((f32[8,2,32,256]{3,0,2,1:T(8,128)S(1)}, f32[8,2,32,256]{3,0,2,1:T(8,128)S(1)}, u32[]{:S(2)}, u32[]{:S(2)}) %collective-permute-start.8) | collective-permute-done | bytes 524320 | tf_op jit(solution)/shard_map/ppermute | solution.py:136
  115.9 1.6 %collective-permute-start.9 = (f32[8,1,32,256]{3,0,2,1:T(8,128)S(1)}, f32[8,1,32,256]{3,0,2,1:T(8,128)S(1)}, u32[]{:S(2)}, u32[]{:S(2)}) collective-permute-start(f32[8,1,32,256]{3,0,2,1:T(8,128)S(1)} %constant_dynamic-slice_fusion), channel_id=1, source_target_pairs={{0,16},{8,24},{16,0},{24,8},{1,17},{9,25},{17,1},{25,9},{2,18},{10... | collective-permute-start | bytes 786440 | tf_op jit(solution)/shard_map/ppermute | solution.py:136
  117.5 6.9 %collective-permute-done.9 = f32[8,1,32,256]{3,0,2,1:T(8,128)S(1)} collective-permute-done((f32[8,1,32,256]{3,0,2,1:T(8,128)S(1)}, f32[8,1,32,256]{3,0,2,1:T(8,128)S(1)}, u32[]{:S(2)}, u32[]{:S(2)}) %collective-permute-start.9) | collective-permute-done | bytes 262176 | tf_op jit(solution)/shard_map/ppermute | solution.py:136
  124.4 14.1 %all_to_all.18 = f32[8,32,256]{2,0,1:T(8,128)S(1)} all-to-all(f32[8,32,256]{2,0,1:T(8,128)S(1)} %add_bitcast_fusion), channel_id=1, replica_groups=mesh['shots'=4,'depth'=8] {'depth'}, dimensions={1} | all-to-all | bytes 524288 | tf_op jit(solution)/shard_map/all_to_all | solution.py:187
  (84 shorter events, 12.0 us)
Async XLA Ops:
  0.6 9.3 %copy-start.3 = (f32[1,8,128,256]{3,2,1,0:T(8,128)S(1)}, f32[1,8,128,256]{3,2,1,0:T(8,128)}, u32[]{:S(2)}) copy-start(f32[1,8,128,256]{3,2,1,0:T(8,128)} %param.13) | copy-start | bytes 3145732
  3.0 43.8 %collective-permute-start.3 = (f32[1,4,128,256]{3,2,1,0:T(8,128)}, f32[1,4,128,256]{3,2,1,0:T(8,128)}, u32[]{:S(2)}, u32[]{:S(2)}) collective-permute-start(f32[1,4,128,256]{3,2,1,0:T(8,128)} %get-tuple-element.33), channel_id=1, source_target_pairs={{0,1},{1,2},{2,3},{3,4},{4,5},{5,6},{6,7},{8,9},{9,10},{10,11},{11... | collective-permute-start | bytes 1572872 | tf_op jit(solution)/shard_map/ppermute | solution.py:86
  8.7 45.7 %collective-permute-start.2 = (f32[1,4,128,256]{3,2,1,0:T(8,128)}, f32[1,4,128,256]{3,2,1,0:T(8,128)}, u32[]{:S(2)}, u32[]{:S(2)}) collective-permute-start(f32[1,4,128,256]{3,2,1,0:T(8,128)} %get-tuple-element.32), channel_id=1, source_target_pairs={{1,0},{2,1},{3,2},{4,3},{5,4},{6,5},{7,6},{9,8},{10,9},{11,10},{12... | collective-permute-start | bytes 1572872 | tf_op jit(solution)/shard_map/ppermute | solution.py:87
  11.1 8.8 %copy-start.21 = (s32[512]{0:T(512)S(1)}, s32[512]{0:T(512)}, u32[]{:S(2)}) copy-start(s32[512]{0:T(512)} %param.20) | copy-start | bytes 6148
  11.1 8.8 %copy-start.22 = (s32[512]{0:T(512)S(1)}, s32[512]{0:T(512)}, u32[]{:S(2)}) copy-start(s32[512]{0:T(512)} %param.19) | copy-start | bytes 6148
  11.1 8.9 %copy-start.23 = (s32[1,512]{1,0:T(1,128)S(1)}, s32[1,512]{1,0:T(1,128)}, u32[]{:S(2)}) copy-start(s32[1,512]{1,0:T(1,128)} %param.18) | copy-start | bytes 6148
  11.1 8.9 %copy-start.20 = (f32[2,512]{1,0:T(2,128)S(1)}, f32[2,512]{1,0:T(2,128)}, u32[]{:S(2)}) copy-start(f32[2,512]{1,0:T(2,128)} %param.17) | copy-start | bytes 12292
  11.1 42.0 %collective-permute-start.1 = (f32[1,4,128,256]{3,2,1,0:T(8,128)}, f32[1,4,128,256]{3,2,1,0:T(8,128)}, u32[]{:S(2)}, u32[]{:S(2)}) collective-permute-start(f32[1,4,128,256]{3,2,1,0:T(8,128)} %get-tuple-element.37), channel_id=1, source_target_pairs={{0,1},{1,2},{2,3},{3,4},{4,5},{5,6},{6,7},{8,9},{9,10},{10,11},{11... | collective-permute-start | bytes 1572872 | tf_op jit(solution)/shard_map/ppermute | solution.py:86
  16.6 39.1 %collective-permute-start = (f32[1,4,128,256]{3,2,1,0:T(8,128)}, f32[1,4,128,256]{3,2,1,0:T(8,128)}, u32[]{:S(2)}, u32[]{:S(2)}) collective-permute-start(f32[1,4,128,256]{3,2,1,0:T(8,128)} %get-tuple-element.36), channel_id=1, source_target_pairs={{1,0},{2,1},{3,2},{4,3},{5,4},{6,5},{7,6},{9,8},{10,9},{11,10},{12... | collective-permute-start | bytes 1572872 | tf_op jit(solution)/shard_map/ppermute | solution.py:87
  22.3 1.5 %copy-start.18 = (s32[4096]{0:T(1024)S(1)}, s32[4096]{0:T(1024)}, u32[]{:S(2)}) copy-start(s32[4096]{0:T(1024)} %param.22) | copy-start | bytes 49156
  22.3 1.5 %copy-start.19 = (s32[4096]{0:T(1024)S(1)}, s32[4096]{0:T(1024)}, u32[]{:S(2)}) copy-start(s32[4096]{0:T(1024)} %param.21) | copy-start | bytes 49156
  22.3 2.1 %copy-start.17 = (f32[1,2,4096]{2,1,0:T(2,128)S(1)}, f32[1,2,4096]{2,1,0:T(2,128)}, u32[]{:S(2)}) copy-start(f32[1,2,4096]{2,1,0:T(2,128)} %param.23) | copy-start | bytes 98308
  38.4 1.5 %copy-start.2 = (f32[8,128,256]{2,1,0:T(8,128)S(1)}, f32[8,128,256]{2,1,0:T(8,128)}, u32[]{:S(2)}) copy-start(f32[8,128,256]{2,1,0:T(8,128)} %param.16) | copy-start | bytes 3145732
  38.4 1.9 %copy-start.9 = (f32[1,8,128,256]{3,2,1,0:T(8,128)S(1)}, f32[1,8,128,256]{3,2,1,0:T(8,128)}, u32[]{:S(2)}) copy-start(f32[1,8,128,256]{3,2,1,0:T(8,128)} %convolution_bitcast_fusion.6) | copy-start | bytes 3145732
  38.4 2.2 %copy-start.12 = (f32[1,1024,256]{2,1,0:T(8,128)S(1)}, f32[1,1024,256]{2,1,0:T(8,128)}, u32[]{:S(2)}) copy-start(f32[1,1024,256]{2,1,0:T(8,128)} %get-tuple-element.21) | copy-start | bytes 3145732
  38.4 2.5 %copy-start.15 = (f32[1,8,128,256]{3,2,1,0:T(8,128)S(1)}, f32[1,8,128,256]{3,2,1,0:T(8,128)}, u32[]{:S(2)}) copy-start(f32[1,8,128,256]{3,2,1,0:T(8,128)} %param.12) | copy-start | bytes 3145732
  40.9 2.3 %copy-start.5 = (f32[1,8,128,256]{3,2,1,0:T(8,128)S(1)}, f32[1,8,128,256]{3,2,1,0:T(8,128)}, u32[]{:S(2)}) copy-start(f32[1,8,128,256]{3,2,1,0:T(8,128)} %param.15) | copy-start | bytes 3145732
  55.4 1.4 %copy-start.13 = (f32[1,8,128,256]{3,2,1,0:T(8,128)S(1)}, f32[1,8,128,256]{3,2,1,0:T(8,128)}, u32[]{:S(2)}) copy-start(f32[1,8,128,256]{3,2,1,0:T(8,128)} %fusion.21) | copy-start | bytes 3145732
  55.5 1.7 %copy-start.14 = (f32[1,8,128,256]{3,2,1,0:T(8,128)S(1)}, f32[1,8,128,256]{3,2,1,0:T(8,128)}, u32[]{:S(2)}) copy-start(f32[1,8,128,256]{3,2,1,0:T(8,128)} %fusion.26) | copy-start | bytes 3145732
  58.8 52.1 %copy-start = (f32[1,8,128,256]{3,2,1,0:T(8,128)}, f32[1,8,128,256]{3,2,1,0:T(8,128)S(1)}, u32[]{:S(2)}) copy-start(f32[1,8,128,256]{3,2,1,0:T(8,128)S(1)} %get-tuple-element.30) | copy-start | bytes 3145732
  58.8 52.1 %copy-start.1 = (f32[1,8,128,256]{3,2,1,0:T(8,128)}, f32[1,8,128,256]{3,2,1,0:T(8,128)S(1)}, u32[]{:S(2)}) copy-start(f32[1,8,128,256]{3,2,1,0:T(8,128)S(1)} %get-tuple-element.31) | copy-start | bytes 3145732
  59.9 12.1 %copy-start.4 = (f32[1,8,128,256]{3,2,1,0:T(8,128)S(1)}, f32[1,8,128,256]{3,2,1,0:T(8,128)}, u32[]{:S(2)}) copy-start(f32[1,8,128,256]{3,2,1,0:T(8,128)} %param.13) | copy-start | bytes 3145732
  59.9 12.1 %copy-start.10 = (f32[1,1024,256]{2,1,0:T(8,128)S(1)}, f32[1,1024,256]{2,1,0:T(8,128)}, u32[]{:S(2)}) copy-start(f32[1,1024,256]{2,1,0:T(8,128)} %get-tuple-element.20) | copy-start | bytes 3145732
  60.0 39.4 %collective-permute-start.7 = (f32[1,4,128,256]{3,2,1,0:T(8,128)S(1)}, f32[1,4,128,256]{3,2,1,0:T(8,128)S(1)}, u32[]{:S(2)}, u32[]{:S(2)}) collective-permute-start(f32[1,4,128,256]{3,2,1,0:T(8,128)S(1)} %get-tuple-element.27), channel_id=1, source_target_pairs={{0,1},{1,2},{2,3},{3,4},{4,5},{5,6},{6,7},{8,9},{9,10},{10,11},{11... | collective-permute-start | bytes 1572872 | tf_op jit(solution)/shard_map/ppermute | solution.py:86
  64.6 34.8 %collective-permute-start.6 = (f32[1,4,128,256]{3,2,1,0:T(8,128)S(1)}, f32[1,4,128,256]{3,2,1,0:T(8,128)S(1)}, u32[]{:S(2)}, u32[]{:S(2)}) collective-permute-start(f32[1,4,128,256]{3,2,1,0:T(8,128)S(1)} %get-tuple-element.26), channel_id=1, source_target_pairs={{1,0},{2,1},{3,2},{4,3},{5,4},{6,5},{7,6},{9,8},{10,9},{11,10},{12... | collective-permute-start | bytes 1572872 | tf_op jit(solution)/shard_map/ppermute | solution.py:87
  65.9 42.7 %collective-permute-start.5 = (f32[1,4,128,256]{3,2,1,0:T(8,128)S(1)}, f32[1,4,128,256]{3,2,1,0:T(8,128)S(1)}, u32[]{:S(2)}, u32[]{:S(2)}) collective-permute-start(f32[1,4,128,256]{3,2,1,0:T(8,128)S(1)} %get-tuple-element.29), channel_id=1, source_target_pairs={{0,1},{1,2},{2,3},{3,4},{4,5},{5,6},{6,7},{8,9},{9,10},{10,11},{11... | collective-permute-start | bytes 1572872 | tf_op jit(solution)/shard_map/ppermute | solution.py:86
  70.5 38.1 %collective-permute-start.4 = (f32[1,4,128,256]{3,2,1,0:T(8,128)S(1)}, f32[1,4,128,256]{3,2,1,0:T(8,128)S(1)}, u32[]{:S(2)}, u32[]{:S(2)}) collective-permute-start(f32[1,4,128,256]{3,2,1,0:T(8,128)S(1)} %get-tuple-element.28), channel_id=1, source_target_pairs={{1,0},{2,1},{3,2},{4,3},{5,4},{6,5},{7,6},{9,8},{10,9},{11,10},{12... | collective-permute-start | bytes 1572872 | tf_op jit(solution)/shard_map/ppermute | solution.py:87
  73.3 1.2 copy-start.6
  73.3 1.5 %copy-start.11 = (f32[1,1024,256]{2,1,0:T(8,128)S(1)}, f32[1,1024,256]{2,1,0:T(8,128)}, u32[]{:S(2)}) copy-start(f32[1,1024,256]{2,1,0:T(8,128)} %get-tuple-element.18) | copy-start | bytes 3145732
  110.9 1.3 copy-start.8
  113.6 2.0 %collective-permute-start.8 = (f32[8,2,32,256]{3,0,2,1:T(8,128)S(1)}, f32[8,2,32,256]{3,0,2,1:T(8,128)S(1)}, u32[]{:S(2)}, u32[]{:S(2)}) collective-permute-start(f32[8,2,32,256]{3,0,2,1:T(8,128)S(1)} %bitcast.209), channel_id=1, source_target_pairs={{0,8},{8,0},{16,24},{24,16},{1,9},{9,1},{17,25},{25,17},{2,10},{10... | collective-permute-start | bytes 1572872 | tf_op jit(solution)/shard_map/ppermute | solution.py:136
  115.9 8.4 %collective-permute-start.9 = (f32[8,1,32,256]{3,0,2,1:T(8,128)S(1)}, f32[8,1,32,256]{3,0,2,1:T(8,128)S(1)}, u32[]{:S(2)}, u32[]{:S(2)}) collective-permute-start(f32[8,1,32,256]{3,0,2,1:T(8,128)S(1)} %constant_dynamic-slice_fusion), channel_id=1, source_target_pairs={{0,16},{8,24},{16,0},{24,8},{1,17},{9,25},{17,1},{25,9},{2,18},{10... | collective-permute-start | bytes 786440 | tf_op jit(solution)/shard_map/ppermute | solution.py:136
  (2 other events, 2.3 us)

commit v12 on v11

--- a/solution.py
+++ b/solution.py
@@ -81,10 +81,10 @@
     length = fields[0].shape[dim]
     up = [(i, i + 1) for i in range(devices - 1)]
     down = [(i + 1, i) for i in range(devices - 1)]
-    last = tuple(lax.slice_in_dim(f, length - HALO, length, axis=dim) for f in fields)
-    leading = tuple(lax.slice_in_dim(f, 0, HALO, axis=dim) for f in fields)
-    below = lax.ppermute(last, "depth", up)
-    above = lax.ppermute(leading, "depth", down)
+    below, above = [], []
+    for f in fields:
+        below.append(lax.ppermute(lax.slice_in_dim(f, length - HALO, length, axis=dim), "depth", up))
+        above.append(lax.ppermute(lax.slice_in_dim(f, 0, HALO, axis=dim), "depth", down))
     return below, above
 
 
@@ -174,11 +174,18 @@
                 for i in range(2)
             ]
         )
-        fresh = [
-            partial[i] + courant * depth_laplace(below[i], current[i], above[i], zaxis) for i in range(2)
-        ]
+        fresh = []
+        halos = ([], [])
+        for i in range(2):
+            if i > 0 and step + 1 < STEPS:
+                _, below[i], above[i] = lax.optimization_barrier((halos[0][-1], below[i], above[i]))
+            fresh.append(partial[i] + courant * depth_laplace(below[i], current[i], above[i], zaxis))
+            if step + 1 < STEPS:
+                sent = exchange([fresh[i]], zaxis)
+                halos[0].append(sent[0][0])
+                halos[1].append(sent[1][0])
         if step + 1 < STEPS:
-            below, above = exchange(fresh, zaxis)
+            below, above = halos
         part = fresh[0][0] * fresh[1][0]
         correlation = part if correlation is None else correlation + part
         earlier, current = (current, fresh)

time: 140 us -> 136 us (0.971)
  waiting for transfers between devices: 46.2 us -> 42.7 us
    ppermute x8, waiting for transfers between devices: 37.5 us -> 34 us  [the longest x4 34 us: exchange(): lax.ppermute(lax.slice_in_dim(f, length - HALO, length, axis=dim), 'depth...]
    unnamed x53 -> x51, local copies, waits for them, and re-layouts: 6.05 us -> 5.28 us
    add x2 -> x3, other arithmetic: 3.93 us -> 3.34 us  [on_device(): partial[i] + courant * depth_laplace(below[i], current[i], above[i], zaxis)]
  transfers between devices with their start and end apart: 10 -> 10, of which waited for: 5 -> 4; matrix products, arithmetic and copies ran while one was open for 25% -> 29% of each run, Pallas kernels for 0% -> 0%
where the time goes in v12:
time: 136 us; the launch traced here: 135 us
  waiting for transfers between devices  42.7 us (31%)
  matrix products  29.7 us (22%)
  starting transfers between devices  27.5 us (20%)
  local copies, waits for them, and re-layouts  14.4 us (11%)
  blocking collectives  14.1 us (10%)
  other arithmetic  5.49 us (4%)
    ppermute x4, waiting for transfers between devices, exchange(): lax.ppermute(lax.slice_in_dim(f, length - HALO, length, axis=dim), 'depth...  34 us
    ppermute x4, starting transfers between devices, exchange(): lax.ppermute(lax.slice_in_dim(f, length - HALO, length, axis=dim), 'depth...  20.6 us
    dot_general x2, matrix products, spread_dense(): grid = jnp.dot(by_row, right, preferred_element_type=jnp.float32)  15.2 us
    all_to_all x1, blocking collectives, on_device(): lax.all_to_all(reduced, 'depth', split_axis=1, concat_axis=0, tiled=True)  14.1 us
    ppermute x2, waiting for transfers between devices, reduce_shots(): blocks = keep + lax.ppermute(send, 'shots', pairs)  8.74 us
    dot_general x4, matrix products, lateral_laplace(): along_x = jnp.einsum('...xy,kx->...ky', core, band(rows), precision=high)  7.29 us
    ppermute x4, starting transfers between devices, exchange(): lax.ppermute(lax.slice_in_dim(f, 0, HALO, axis=dim), 'depth', down)  5.36 us
    unnamed x51, local copies, waits for them, and re-layouts  5.28 us
  transfers between devices with their start and end apart: 10, of which 4 were waited for; matrix products, arithmetic and copies ran while one was open for 29% of the time, Pallas kernels for 0%

profile of v12, /device:TPU:0, one launch (start us, length us, event | category | flops | bytes accessed | tf_op | source)
XLA Modules:
  0.0 135.3 jit_solution(2040995116804922652)
XLA Ops:
  0.6 2.4 %fusion.287 = (f32[1,4,128,256]{3,2,1,0:T(8,128)}, f32[1,4,128,256]{3,2,1,0:T(8,128)}) fusion(f32[1,8,128,256]{3,2,1,0:T(8,128)} %param.13), kind=kLoop, calls=%fused_computation.373 | loop fusion | bytes 2097152 | tf_op jit(solution)/shard_map/slice | solution.py:87
  3.0 5.8 %collective-permute-start.1 = (f32[1,4,128,256]{3,2,1,0:T(8,128)}, f32[1,4,128,256]{3,2,1,0:T(8,128)}, u32[]{:S(2)}, u32[]{:S(2)}) collective-permute-start(f32[1,4,128,256]{3,2,1,0:T(8,128)} %get-tuple-element.39), channel_id=1, source_target_pairs={{0,1},{1,2},{2,3},{3,4},{4,5},{5,6},{6,7},{8,9},{9,10},{10,11},{11... | collective-permute-start | bytes 1572872 | tf_op jit(solution)/shard_map/ppermute | solution.py:86
  8.8 1.3 collective-permute-start
  10.1 1.1 fusion.286
  11.3 5.5 %collective-permute-start.3 = (f32[1,4,128,256]{3,2,1,0:T(8,128)}, f32[1,4,128,256]{3,2,1,0:T(8,128)}, u32[]{:S(2)}, u32[]{:S(2)}) collective-permute-start(f32[1,4,128,256]{3,2,1,0:T(8,128)} %get-tuple-element.37), channel_id=1, source_target_pairs={{0,1},{1,2},{2,3},{3,4},{4,5},{5,6},{6,7},{8,9},{9,10},{10,11},{11... | collective-permute-start | bytes 1572872 | tf_op jit(solution)/shard_map/ppermute | solution.py:86
  16.8 1.3 collective-permute-start.4
  18.1 2.0 %convolution_bitcast_fusion.6 = f32[1,8,128,256]{3,2,1,0:T(8,128)} fusion(f32[1,8,128,256]{3,2,1,0:T(8,128)S(1)} %copy-done.3), kind=kOutput, calls=%fused_computation.52 | convolution fusion | flops 805961728 | bytes 2097152 | tf_op jit(solution)/shard_map/...xy,yk->...xk/dot_general | solution.py:39
  20.3 1.8 %fusion.12 = f32[1024,3,2,256]{3,0,2,1:T(8,128)S(1)} fusion(pred[512,256]{0,1:T(8,128)(4,1)S(1)} %iota_compare_fusion.3, s32[512]{0:T(512)S(1)} %get-tuple-element.54, bf16[512,3,2]{0,2,1:T(2,128)(2,1)S(1)} %maximum_bitcast_fusion.1), kind=kOutput, calls=%fused_computation.30 | convolution fusion | flops 1611923456 | bytes 6430720 | tf_op jit(solution)/shard_map/dot_general | solution.py:116
  22.5 1.5 %fusion.283 = (f32[1,1024,256]{2,1,0:T(8,128)}, f32[1,1024,256]{2,1,0:T(8,128)}) fusion(f32[2,1024,256]{2,1,0:T(8,128)S(1)} %fusion.10), kind=kLoop, calls=%fused_computation.369 | loop fusion | bytes 4194304 | tf_op jit(solution)/shard_map/slice | solution.py:170
  24.8 13.4 %fusion.1 = f32[1024,3,2,256]{3,0,2,1:T(8,128)S(1)} fusion(pred[4096,256]{0,1:T(8,128)(4,1)S(1)} %iota_compare_fusion.1, s32[4096]{0:T(1024)S(1)} %get-tuple-element.49, bf16[4096,3,2]{0,2,1:T(2,128)(2,1)S(1)} %maximum_bitcast_fusion), kind=kOutput, calls=%fused_computation.2 | convolution fusion | flops 12895387648 | bytes 7405568 | tf_op jit(solution)/shard_map/dot_general | solution.py:116
  38.6 1.1 fusion.282
  41.1 2.3 %fusion.21 = f32[1,8,128,256]{3,2,1,0:T(8,128)} fusion(f32[1,8,128,256]{3,2,1,0:T(8,128)S(1)} %bitcast.205, f32[1,8,128,256]{3,2,1,0:T(8,128)S(1)} %copy-done.8, f32[1,8,128,256]{3,2,1,0:T(8,128)S(1)} %copy-done.3, f32[8,128,256]{2,1,0:T(8,128)S(1)} %copy-done, f32[1,8,128,256]{3,2,1,0:T(8,128)S(1)} %copy-done.14), kind=kOutput, calls=%fused_computation.58 | convolution fusion | flops 404914176 | bytes 6291456 | tf_op jit(solution)/shard_map/...xy,kx->...ky/dot_general | solution.py:40
  43.5 1.1 convolution_bitcast_fusion.4
  44.7 2.3 %fusion.26 = f32[1,8,128,256]{3,2,1,0:T(8,128)} fusion(f32[1,8,128,256]{3,2,1,0:T(8,128)S(1)} %bitcast.206, f32[1,8,128,256]{3,2,1,0:T(8,128)S(1)} %convolution_bitcast_fusion.4, f32[1,8,128,256]{3,2,1,0:T(8,128)S(1)} %copy-done.4, f32[8,128,256]{2,1,0:T(8,128)S(1)} %copy-done, f32[1,8,128,256]{3,2,1,0:T(8,128)S(1)} %copy-done.15), kind=kOutput, calls=%fused_computation.63 | convolution fusion | flops 404914176 | bytes 6291456 | tf_op jit(solution)/shard_map/...xy,kx->...ky/dot_general | solution.py:40
  47.0 1.1 constant_dynamic-update-slice_fusion.3
  48.3 1.2 constant_dynamic-update-slice_fusion
  50.2 4.7 %collective-permute-start.2 = (f32[1,4,128,256]{3,2,1,0:T(8,128)S(1)}, f32[1,4,128,256]{3,2,1,0:T(8,128)S(1)}, u32[]{:S(2)}, u32[]{:S(2)}) collective-permute-start(f32[1,4,128,256]{3,2,1,0:T(8,128)S(1)} %get-tuple-element.33), channel_id=1, source_target_pairs={{0,1},{1,2},{2,3},{3,4},{4,5},{5,6},{6,7},{8,9},{9,10},{10,11},{11... | collective-permute-start | bytes 1572872 | tf_op jit(solution)/shard_map/ppermute | solution.py:86
  54.9 1.3 collective-permute-start.5
  57.2 1.3 fusion.31
  58.5 17.6 %collective-permute-done.2 = f32[1,4,128,256]{3,2,1,0:T(8,128)S(1)} collective-permute-done((f32[1,4,128,256]{3,2,1,0:T(8,128)S(1)}, f32[1,4,128,256]{3,2,1,0:T(8,128)S(1)}, u32[]{:S(2)}, u32[]{:S(2)}) %collective-permute-start.2) | collective-permute-done | bytes 524320 | tf_op jit(solution)/shard_map/ppermute | solution.py:86
  76.1 1.1 constant_dynamic-update-slice_fusion.7
  77.5 1.2 constant_dynamic-update-slice_fusion.4
  79.3 4.5 %collective-permute-start.7 = (f32[1,4,128,256]{3,2,1,0:T(8,128)S(1)}, f32[1,4,128,256]{3,2,1,0:T(8,128)S(1)}, u32[]{:S(2)}, u32[]{:S(2)}) collective-permute-start(f32[1,4,128,256]{3,2,1,0:T(8,128)S(1)} %get-tuple-element.31), channel_id=1, source_target_pairs={{0,1},{1,2},{2,3},{3,4},{4,5},{5,6},{6,7},{8,9},{9,10},{10,11},{11... | collective-permute-start | bytes 1572872 | tf_op jit(solution)/shard_map/ppermute | solution.py:86
  83.8 1.5 %collective-permute-start.6 = (f32[1,4,128,256]{3,2,1,0:T(8,128)S(1)}, f32[1,4,128,256]{3,2,1,0:T(8,128)S(1)}, u32[]{:S(2)}, u32[]{:S(2)}) collective-permute-start(f32[1,4,128,256]{3,2,1,0:T(8,128)S(1)} %get-tuple-element.30), channel_id=1, source_target_pairs={{1,0},{2,1},{3,2},{4,3},{5,4},{6,5},{7,6},{9,8},{10,9},{11,10},{12... | collective-permute-start | bytes 1572872 | tf_op jit(solution)/shard_map/ppermute | solution.py:87
  85.4 1.0 convolution_bitcast_fusion
  86.4 1.4 %fusion.36 = f32[1,8,128,256]{3,2,1,0:T(8,128)S(1)} fusion(f32[1,8,128,256]{3,2,1,0:T(8,128)S(1)} %bitcast.203, f32[1,8,128,256]{3,2,1,0:T(8,128)S(1)} %convolution_bitcast_fusion, f32[1,8,128,256]{3,2,1,0:T(8,128)S(1)} %fusion.78, f32[8,128,256]{2,1,0:T(8,128)S(1)} %copy-done, f32[1,8,128,256]{3,2,1,0:T(8,128)S(1)} %copy-done.5), kind=kOutput, calls=%fused_computation.73 | convolution fusion | flops 404914176 | bytes 6291456 | tf_op jit(solution)/shard_map/...xy,kx->...ky/dot_general | solution.py:40
  87.8 16.4 %collective-permute-done.7 = f32[1,4,128,256]{3,2,1,0:T(8,128)S(1)} collective-permute-done((f32[1,4,128,256]{3,2,1,0:T(8,128)S(1)}, f32[1,4,128,256]{3,2,1,0:T(8,128)S(1)}, u32[]{:S(2)}, u32[]{:S(2)}) %collective-permute-start.7) | collective-permute-done | bytes 524320 | tf_op jit(solution)/shard_map/ppermute | solution.py:86
  104.2 2.3 %fusion.43 = (f32[1,8,128,256]{3,2,1,0:T(8,128)S(1)}, f32[1,8,128,256]{3,2,1,0:T(8,128)S(1)}) fusion(f32[1,8,128,256]{3,2,1,0:T(8,128)S(1)} %fusion.36, f32[1,8,128,256]{3,2,1,0:T(8,128)S(1)} %fusion.78, f32[1,4,128,256]{3,2,1,0:T(8,128)S(1)} %collective-permute-done.7, f32[1,4,128,256]{3,2,1,0:T(8,128)S(1)} %collective-permute-done.6, ...), kind=kLoop, calls=%fused_computation.80 | loop fusion | flops 11010048 | bytes 9437184 | tf_op jit(solution)/shard_map/add | solution.py:182
  109.4 1.9 %collective-permute-done.8 = f32[8,2,32,256]{3,0,2,1:T(8,128)S(1)} collective-permute-done((f32[8,2,32,256]{3,0,2,1:T(8,128)S(1)}, f32[8,2,32,256]{3,0,2,1:T(8,128)S(1)}, u32[]{:S(2)}, u32[]{:S(2)}) %collective-permute-start.8) | collective-permute-done | bytes 524320 | tf_op jit(solution)/shard_map/ppermute | solution.py:136
  111.6 1.5 %collective-permute-start.9 = (f32[8,1,32,256]{3,0,2,1:T(8,128)S(1)}, f32[8,1,32,256]{3,0,2,1:T(8,128)S(1)}, u32[]{:S(2)}, u32[]{:S(2)}) collective-permute-start(f32[8,1,32,256]{3,0,2,1:T(8,128)S(1)} %constant_dynamic-slice_fusion), channel_id=1, source_target_pairs={{0,16},{8,24},{16,0},{24,8},{1,17},{9,25},{17,1},{25,9},{2,18},{10... | collective-permute-start | bytes 786440 | tf_op jit(solution)/shard_map/ppermute | solution.py:136
  113.1 6.9 %collective-permute-done.9 = f32[8,1,32,256]{3,0,2,1:T(8,128)S(1)} collective-permute-done((f32[8,1,32,256]{3,0,2,1:T(8,128)S(1)}, f32[8,1,32,256]{3,0,2,1:T(8,128)S(1)}, u32[]{:S(2)}, u32[]{:S(2)}) %collective-permute-start.9) | collective-permute-done | bytes 262176 | tf_op jit(solution)/shard_map/ppermute | solution.py:136
  120.0 14.1 %all_to_all.18 = f32[8,32,256]{2,0,1:T(8,128)S(1)} all-to-all(f32[8,32,256]{2,0,1:T(8,128)S(1)} %add_bitcast_fusion), channel_id=1, replica_groups=mesh['shots'=4,'depth'=8] {'depth'}, dimensions={1} | all-to-all | bytes 524288 | tf_op jit(solution)/shard_map/all_to_all | solution.py:194
  (83 shorter events, 10.2 us)
Async XLA Ops:
  0.6 9.5 %copy-start.4 = (f32[1,8,128,256]{3,2,1,0:T(8,128)S(1)}, f32[1,8,128,256]{3,2,1,0:T(8,128)}, u32[]{:S(2)}) copy-start(f32[1,8,128,256]{3,2,1,0:T(8,128)} %param.15) | copy-start | bytes 3145732
  3.0 15.0 %copy-start.3 = (f32[1,8,128,256]{3,2,1,0:T(8,128)S(1)}, f32[1,8,128,256]{3,2,1,0:T(8,128)}, u32[]{:S(2)}) copy-start(f32[1,8,128,256]{3,2,1,0:T(8,128)} %param.13) | copy-start | bytes 3145732
  3.0 44.0 %collective-permute-start.1 = (f32[1,4,128,256]{3,2,1,0:T(8,128)}, f32[1,4,128,256]{3,2,1,0:T(8,128)}, u32[]{:S(2)}, u32[]{:S(2)}) collective-permute-start(f32[1,4,128,256]{3,2,1,0:T(8,128)} %get-tuple-element.39), channel_id=1, source_target_pairs={{0,1},{1,2},{2,3},{3,4},{4,5},{5,6},{6,7},{8,9},{9,10},{10,11},{11... | collective-permute-start | bytes 1572872 | tf_op jit(solution)/shard_map/ppermute | solution.py:86
  8.8 39.5 %collective-permute-start = (f32[1,4,128,256]{3,2,1,0:T(8,128)}, f32[1,4,128,256]{3,2,1,0:T(8,128)}, u32[]{:S(2)}, u32[]{:S(2)}) collective-permute-start(f32[1,4,128,256]{3,2,1,0:T(8,128)} %get-tuple-element.38), channel_id=1, source_target_pairs={{1,0},{2,1},{3,2},{4,3},{5,4},{6,5},{7,6},{9,8},{10,9},{11,10},{12... | collective-permute-start | bytes 1572872 | tf_op jit(solution)/shard_map/ppermute | solution.py:87
  11.2 8.8 %copy-start.20 = (s32[512]{0:T(512)S(1)}, s32[512]{0:T(512)}, u32[]{:S(2)}) copy-start(s32[512]{0:T(512)} %param.20) | copy-start | bytes 6148
  11.2 8.8 %copy-start.21 = (s32[512]{0:T(512)S(1)}, s32[512]{0:T(512)}, u32[]{:S(2)}) copy-start(s32[512]{0:T(512)} %param.19) | copy-start | bytes 6148
  11.3 8.9 %copy-start.22 = (s32[1,512]{1,0:T(1,128)S(1)}, s32[1,512]{1,0:T(1,128)}, u32[]{:S(2)}) copy-start(s32[1,512]{1,0:T(1,128)} %param.18) | copy-start | bytes 6148
  11.3 9.0 %copy-start.19 = (f32[2,512]{1,0:T(2,128)S(1)}, f32[2,512]{1,0:T(2,128)}, u32[]{:S(2)}) copy-start(f32[2,512]{1,0:T(2,128)} %param.17) | copy-start | bytes 12292
  11.3 47.3 %collective-permute-start.3 = (f32[1,4,128,256]{3,2,1,0:T(8,128)}, f32[1,4,128,256]{3,2,1,0:T(8,128)}, u32[]{:S(2)}, u32[]{:S(2)}) collective-permute-start(f32[1,4,128,256]{3,2,1,0:T(8,128)} %get-tuple-element.37), channel_id=1, source_target_pairs={{0,1},{1,2},{2,3},{3,4},{4,5},{5,6},{6,7},{8,9},{9,10},{10,11},{11... | collective-permute-start | bytes 1572872 | tf_op jit(solution)/shard_map/ppermute | solution.py:86
  16.8 41.8 %collective-permute-start.4 = (f32[1,4,128,256]{3,2,1,0:T(8,128)}, f32[1,4,128,256]{3,2,1,0:T(8,128)}, u32[]{:S(2)}, u32[]{:S(2)}) collective-permute-start(f32[1,4,128,256]{3,2,1,0:T(8,128)} %get-tuple-element.36), channel_id=1, source_target_pairs={{1,0},{2,1},{3,2},{4,3},{5,4},{6,5},{7,6},{9,8},{10,9},{11,10},{12... | collective-permute-start | bytes 1572872 | tf_op jit(solution)/shard_map/ppermute | solution.py:87
  22.5 1.5 %copy-start.17 = (s32[4096]{0:T(1024)S(1)}, s32[4096]{0:T(1024)}, u32[]{:S(2)}) copy-start(s32[4096]{0:T(1024)} %param.22) | copy-start | bytes 49156
  22.5 1.5 %copy-start.18 = (s32[4096]{0:T(1024)S(1)}, s32[4096]{0:T(1024)}, u32[]{:S(2)}) copy-start(s32[4096]{0:T(1024)} %param.21) | copy-start | bytes 49156
  22.5 2.1 %copy-start.16 = (f32[1,2,4096]{2,1,0:T(2,128)S(1)}, f32[1,2,4096]{2,1,0:T(2,128)}, u32[]{:S(2)}) copy-start(f32[1,2,4096]{2,1,0:T(2,128)} %param.23) | copy-start | bytes 98308
  38.6 1.5 %copy-start = (f32[8,128,256]{2,1,0:T(8,128)S(1)}, f32[8,128,256]{2,1,0:T(8,128)}, u32[]{:S(2)}) copy-start(f32[8,128,256]{2,1,0:T(8,128)} %param.16) | copy-start | bytes 3145732
  38.6 1.9 %copy-start.8 = (f32[1,8,128,256]{3,2,1,0:T(8,128)S(1)}, f32[1,8,128,256]{3,2,1,0:T(8,128)}, u32[]{:S(2)}) copy-start(f32[1,8,128,256]{3,2,1,0:T(8,128)} %convolution_bitcast_fusion.6) | copy-start | bytes 3145732
  38.6 2.2 %copy-start.11 = (f32[1,1024,256]{2,1,0:T(8,128)S(1)}, f32[1,1024,256]{2,1,0:T(8,128)}, u32[]{:S(2)}) copy-start(f32[1,1024,256]{2,1,0:T(8,128)} %get-tuple-element.25) | copy-start | bytes 3145732
  38.6 2.5 %copy-start.14 = (f32[1,8,128,256]{3,2,1,0:T(8,128)S(1)}, f32[1,8,128,256]{3,2,1,0:T(8,128)}, u32[]{:S(2)}) copy-start(f32[1,8,128,256]{3,2,1,0:T(8,128)} %param.12) | copy-start | bytes 3145732
  43.5 1.2 copy-start.15
  48.1 1.4 %copy-start.13 = (f32[1,8,128,256]{3,2,1,0:T(8,128)S(1)}, f32[1,8,128,256]{3,2,1,0:T(8,128)}, u32[]{:S(2)}) copy-start(f32[1,8,128,256]{3,2,1,0:T(8,128)} %fusion.21) | copy-start | bytes 3145732
  50.0 56.5 %copy-start.1 = (f32[1,8,128,256]{3,2,1,0:T(8,128)}, f32[1,8,128,256]{3,2,1,0:T(8,128)S(1)}, u32[]{:S(2)}) copy-start(f32[1,8,128,256]{3,2,1,0:T(8,128)S(1)} %fusion.87) | copy-start | bytes 3145732
  50.2 7.1 %copy-start.10 = (f32[1,1024,256]{2,1,0:T(8,128)S(1)}, f32[1,1024,256]{2,1,0:T(8,128)}, u32[]{:S(2)}) copy-start(f32[1,1024,256]{2,1,0:T(8,128)} %get-tuple-element.24) | copy-start | bytes 3145732
  50.2 26.0 %collective-permute-start.2 = (f32[1,4,128,256]{3,2,1,0:T(8,128)S(1)}, f32[1,4,128,256]{3,2,1,0:T(8,128)S(1)}, u32[]{:S(2)}, u32[]{:S(2)}) collective-permute-start(f32[1,4,128,256]{3,2,1,0:T(8,128)S(1)} %get-tuple-element.33), channel_id=1, source_target_pairs={{0,1},{1,2},{2,3},{3,4},{4,5},{5,6},{6,7},{8,9},{9,10},{10,11},{11... | collective-permute-start | bytes 1572872 | tf_op jit(solution)/shard_map/ppermute | solution.py:86
  54.9 32.9 %collective-permute-start.5 = (f32[1,4,128,256]{3,2,1,0:T(8,128)S(1)}, f32[1,4,128,256]{3,2,1,0:T(8,128)S(1)}, u32[]{:S(2)}, u32[]{:S(2)}) collective-permute-start(f32[1,4,128,256]{3,2,1,0:T(8,128)S(1)} %get-tuple-element.32), channel_id=1, source_target_pairs={{1,0},{2,1},{3,2},{4,3},{5,4},{6,5},{7,6},{9,8},{10,9},{11,10},{12... | collective-permute-start | bytes 1572872 | tf_op jit(solution)/shard_map/ppermute | solution.py:87
  58.5 18.7 %copy-start.5 = (f32[1,8,128,256]{3,2,1,0:T(8,128)S(1)}, f32[1,8,128,256]{3,2,1,0:T(8,128)}, u32[]{:S(2)}) copy-start(f32[1,8,128,256]{3,2,1,0:T(8,128)} %param.15) | copy-start | bytes 3145732
  77.2 1.4 %copy-start.12 = (f32[1,8,128,256]{3,2,1,0:T(8,128)S(1)}, f32[1,8,128,256]{3,2,1,0:T(8,128)}, u32[]{:S(2)}) copy-start(f32[1,8,128,256]{3,2,1,0:T(8,128)} %fusion.26) | copy-start | bytes 3145732
  79.2 27.4 %copy-start.2 = (f32[1,8,128,256]{3,2,1,0:T(8,128)}, f32[1,8,128,256]{3,2,1,0:T(8,128)S(1)}, u32[]{:S(2)}) copy-start(f32[1,8,128,256]{3,2,1,0:T(8,128)S(1)} %fusion.78) | copy-start | bytes 3145732
  79.3 7.1 %copy-start.9 = (f32[1,1024,256]{2,1,0:T(8,128)S(1)}, f32[1,1024,256]{2,1,0:T(8,128)}, u32[]{:S(2)}) copy-start(f32[1,1024,256]{2,1,0:T(8,128)} %get-tuple-element.22) | copy-start | bytes 3145732
  79.3 24.9 %collective-permute-start.7 = (f32[1,4,128,256]{3,2,1,0:T(8,128)S(1)}, f32[1,4,128,256]{3,2,1,0:T(8,128)S(1)}, u32[]{:S(2)}, u32[]{:S(2)}) collective-permute-start(f32[1,4,128,256]{3,2,1,0:T(8,128)S(1)} %get-tuple-element.31), channel_id=1, source_target_pairs={{0,1},{1,2},{2,3},{3,4},{4,5},{5,6},{6,7},{8,9},{9,10},{10,11},{11... | collective-permute-start | bytes 1572872 | tf_op jit(solution)/shard_map/ppermute | solution.py:86
  83.8 20.3 %collective-permute-start.6 = (f32[1,4,128,256]{3,2,1,0:T(8,128)S(1)}, f32[1,4,128,256]{3,2,1,0:T(8,128)S(1)}, u32[]{:S(2)}, u32[]{:S(2)}) collective-permute-start(f32[1,4,128,256]{3,2,1,0:T(8,128)S(1)} %get-tuple-element.30), channel_id=1, source_target_pairs={{1,0},{2,1},{3,2},{4,3},{5,4},{6,5},{7,6},{9,8},{10,9},{11,10},{12... | collective-permute-start | bytes 1572872 | tf_op jit(solution)/shard_map/ppermute | solution.py:87
  106.5 1.3 copy-start.7
  109.3 2.0 %collective-permute-start.8 = (f32[8,2,32,256]{3,0,2,1:T(8,128)S(1)}, f32[8,2,32,256]{3,0,2,1:T(8,128)S(1)}, u32[]{:S(2)}, u32[]{:S(2)}) collective-permute-start(f32[8,2,32,256]{3,0,2,1:T(8,128)S(1)} %bitcast.209), channel_id=1, source_target_pairs={{0,8},{8,0},{16,24},{24,16},{1,9},{9,1},{17,25},{25,17},{2,10},{10... | collective-permute-start | bytes 1572872 | tf_op jit(solution)/shard_map/ppermute | solution.py:136
  111.6 8.4 %collective-permute-start.9 = (f32[8,1,32,256]{3,0,2,1:T(8,128)S(1)}, f32[8,1,32,256]{3,0,2,1:T(8,128)S(1)}, u32[]{:S(2)}, u32[]{:S(2)}) collective-permute-start(f32[8,1,32,256]{3,0,2,1:T(8,128)S(1)} %constant_dynamic-slice_fusion), channel_id=1, source_target_pairs={{0,16},{8,24},{16,0},{24,8},{1,17},{9,25},{17,1},{25,9},{2,18},{10... | collective-permute-start | bytes 786440 | tf_op jit(solution)/shard_map/ppermute | solution.py:136
  (1 other events, 1.1 us)

commit v13 on v12

--- a/solution.py
+++ b/solution.py
@@ -178,12 +178,33 @@
         halos = ([], [])
         for i in range(2):
             if i > 0 and step + 1 < STEPS:
-                _, below[i], above[i] = lax.optimization_barrier((halos[0][-1], below[i], above[i]))
+                _, below[i], above[i] = lax.optimization_barrier((marker, below[i], above[i]))
             fresh.append(partial[i] + courant * depth_laplace(below[i], current[i], above[i], zaxis))
             if step + 1 < STEPS:
-                sent = exchange([fresh[i]], zaxis)
-                halos[0].append(sent[0][0])
-                halos[1].append(sent[1][0])
+                if i == 0:
+                    devices = lax.axis_size("depth")
+                    length = fresh[i].shape[zaxis]
+                    marker = lax.ppermute(
+                        lax.slice_in_dim(fresh[i], length - 1, length, axis=zaxis),
+                        "depth",
+                        [(j, j + 1) for j in range(devices - 1)],
+                    )
+                    rest = lax.ppermute(
+                        lax.slice_in_dim(fresh[i], length - HALO, length - 1, axis=zaxis),
+                        "depth",
+                        [(j, j + 1) for j in range(devices - 1)],
+                    )
+                    leading = lax.ppermute(
+                        lax.slice_in_dim(fresh[i], 0, HALO, axis=zaxis),
+                        "depth",
+                        [(j + 1, j) for j in range(devices - 1)],
+                    )
+                    halos[0].append(jnp.concatenate([rest, marker], axis=zaxis))
+                    halos[1].append(leading)
+                else:
+                    sent = exchange([fresh[i]], zaxis)
+                    halos[0].append(sent[0][0])
+                    halos[1].append(sent[1][0])
         if step + 1 < STEPS:
             below, above = halos
         part = fresh[0][0] * fresh[1][0]

time: 136 us -> 130 us (0.956)
  waiting for transfers between devices: 42.7 us -> 32.3 us
  starting transfers between devices: 27.5 us -> 31.7 us
    ppermute x4 -> x3, waiting for transfers between devices: 34 us -> 8.29 us  [exchange(): lax.ppermute(lax.slice_in_dim(f, length - HALO, length, axis=dim), 'depth...]
    ppermute x0 -> x3, waiting for transfers between devices: none -> 15.3 us  [the longest x1 15.3 us: on_device(): lax.ppermute(lax.slice_in_dim(fresh[i], length - HALO, length - 1, axis=z...]
    ppermute x0 -> x3, starting transfers between devices: none -> 9.87 us  [the longest x1 4.68 us: on_device(): lax.ppermute(lax.slice_in_dim(fresh[i], length - 1, length, axis=zaxis),...]
    ppermute x4 -> x3, starting transfers between devices: 20.6 us -> 16.3 us  [exchange(): lax.ppermute(lax.slice_in_dim(f, length - HALO, length, axis=dim), 'depth...]
    ppermute x4 -> x3, starting transfers between devices: 5.36 us -> 3.85 us  [exchange(): lax.ppermute(lax.slice_in_dim(f, 0, HALO, axis=dim), 'depth', down)]
    add x3 -> x4, other arithmetic: 3.34 us -> 2.35 us  [on_device(): partial[i] + courant * depth_laplace(below[i], current[i], above[i], zaxis)]
    unnamed x51 -> x49, local copies, waits for them, and re-layouts: 5.28 us -> 5.61 us
    slice x4 -> x3, local copies, waits for them, and re-layouts: 3.7 us -> 3.54 us  [exchange(): lax.slice_in_dim(f, 0, HALO, axis=dim)]
  transfers between devices with their start and end apart: 10 -> 11, of which waited for: 4 -> 4; matrix products, arithmetic and copies ran while one was open for 29% -> 30% of each run, Pallas kernels for 0% -> 0%
where the time goes in v13:
time: 130 us; the launch traced here: 129 us
  waiting for transfers between devices  32.3 us (25%)
  starting transfers between devices  31.7 us (24%)
  matrix products  29.5 us (23%)
  blocking collectives  15.3 us (12%)
  local copies, waits for them, and re-layouts  14.3 us (11%)
  other arithmetic  4.81 us (4%)
  between operations  1.32 us (1%)
    ppermute x3, starting transfers between devices, exchange(): lax.ppermute(lax.slice_in_dim(f, length - HALO, length, axis=dim), 'depth...  16.3 us
    all_to_all x1, blocking collectives, on_device(): lax.all_to_all(reduced, 'depth', split_axis=1, concat_axis=0, tiled=True)  15.3 us
    ppermute x1, waiting for transfers between devices, on_device(): lax.ppermute(lax.slice_in_dim(fresh[i], length - HALO, length - 1, axis=z...  15.3 us
    dot_general x2, matrix products, spread_dense(): grid = jnp.dot(by_row, right, preferred_element_type=jnp.float32)  15 us
    ppermute x2, waiting for transfers between devices, reduce_shots(): blocks = keep + lax.ppermute(send, 'shots', pairs)  8.71 us
    ppermute x3, waiting for transfers between devices, exchange(): lax.ppermute(lax.slice_in_dim(f, length - HALO, length, axis=dim), 'depth...  8.29 us
    dot_general x4, matrix products, lateral_laplace(): along_x = jnp.einsum('...xy,kx->...ky', core, band(rows), precision=high)  7.28 us
    unnamed x49, local copies, waits for them, and re-layouts  5.61 us
  transfers between devices with their start and end apart: 11, of which 4 were waited for; matrix products, arithmetic and copies ran while one was open for 30% of the time, Pallas kernels for 0%

profile of v13, /device:TPU:0, one launch (start us, length us, event | category | flops | bytes accessed | tf_op | source)
XLA Modules:
  0.0 129.2 jit_solution(15323081464364907197)
XLA Ops:
  0.6 2.3 %fusion.282 = (f32[1,4,128,256]{3,2,1,0:T(8,128)}, f32[1,4,128,256]{3,2,1,0:T(8,128)}) fusion(f32[1,8,128,256]{3,2,1,0:T(8,128)} %param.13), kind=kLoop, calls=%fused_computation.364 | loop fusion | bytes 2097152 | tf_op jit(solution)/shard_map/slice | solution.py:87
  3.0 5.7 %collective-permute-start.1 = (f32[1,4,128,256]{3,2,1,0:T(8,128)}, f32[1,4,128,256]{3,2,1,0:T(8,128)}, u32[]{:S(2)}, u32[]{:S(2)}) collective-permute-start(f32[1,4,128,256]{3,2,1,0:T(8,128)} %get-tuple-element.35), channel_id=1, source_target_pairs={{0,1},{1,2},{2,3},{3,4},{4,5},{5,6},{6,7},{8,9},{9,10},{10,11},{11... | collective-permute-start | bytes 1572872 | tf_op jit(solution)/shard_map/ppermute | solution.py:86
  8.6 1.3 collective-permute-start
  9.9 1.1 fusion.281
  11.0 5.5 %collective-permute-start.3 = (f32[1,4,128,256]{3,2,1,0:T(8,128)}, f32[1,4,128,256]{3,2,1,0:T(8,128)}, u32[]{:S(2)}, u32[]{:S(2)}) collective-permute-start(f32[1,4,128,256]{3,2,1,0:T(8,128)} %get-tuple-element.33), channel_id=1, source_target_pairs={{0,1},{1,2},{2,3},{3,4},{4,5},{5,6},{6,7},{8,9},{9,10},{10,11},{11... | collective-permute-start | bytes 1572872 | tf_op jit(solution)/shard_map/ppermute | solution.py:86
  16.5 1.3 collective-permute-start.4
  17.8 2.0 %convolution_bitcast_fusion.4 = f32[1,8,128,256]{3,2,1,0:T(8,128)} fusion(f32[1,8,128,256]{3,2,1,0:T(8,128)S(1)} %copy-done.4), kind=kOutput, calls=%fused_computation.45 | convolution fusion | flops 805961728 | bytes 2097152 | tf_op jit(solution)/shard_map/...xy,yk->...xk/dot_general | solution.py:39
  20.6 13.2 %fusion.1 = f32[1024,3,2,256]{3,0,2,1:T(8,128)S(1)} fusion(pred[4096,256]{0,1:T(8,128)(4,1)S(1)} %iota_compare_fusion.1, s32[4096]{0:T(1024)S(1)} %get-tuple-element.45, bf16[4096,3,2]{0,2,1:T(2,128)(2,1)S(1)} %maximum_bitcast_fusion), kind=kOutput, calls=%fused_computation.2 | convolution fusion | flops 12895387648 | bytes 7405568 | tf_op jit(solution)/shard_map/dot_general | solution.py:116
  34.5 1.1 fusion.278
  35.7 1.8 %fusion.12 = f32[1024,3,2,256]{3,0,2,1:T(8,128)S(1)} fusion(pred[512,256]{0,1:T(8,128)(4,1)S(1)} %iota_compare_fusion.3, s32[512]{0:T(512)S(1)} %get-tuple-element.50, bf16[512,3,2]{0,2,1:T(2,128)(2,1)S(1)} %maximum_bitcast_fusion.1), kind=kOutput, calls=%fused_computation.27 | convolution fusion | flops 1611923456 | bytes 6430720 | tf_op jit(solution)/shard_map/dot_general | solution.py:116
  38.0 1.1 fusion.279
  40.2 2.4 %fusion.26 = f32[1,8,128,256]{3,2,1,0:T(8,128)} fusion(f32[1,8,128,256]{3,2,1,0:T(8,128)S(1)} %bitcast.205, f32[1,8,128,256]{3,2,1,0:T(8,128)S(1)} %copy-done.8, f32[1,8,128,256]{3,2,1,0:T(8,128)S(1)} %copy-done.4, f32[8,128,256]{2,1,0:T(8,128)S(1)} %copy-done, f32[1,8,128,256]{3,2,1,0:T(8,128)S(1)} %copy-done.13), kind=kOutput, calls=%fused_computation.58 | convolution fusion | flops 404914176 | bytes 6291456 | tf_op jit(solution)/shard_map/...xy,kx->...ky/dot_general | solution.py:40
  42.6 1.0 convolution_bitcast_fusion.6
  43.8 2.3 %fusion.21 = f32[1,8,128,256]{3,2,1,0:T(8,128)} fusion(f32[1,8,128,256]{3,2,1,0:T(8,128)S(1)} %bitcast.206, f32[1,8,128,256]{3,2,1,0:T(8,128)S(1)} %convolution_bitcast_fusion.6, f32[1,8,128,256]{3,2,1,0:T(8,128)S(1)} %copy-done.3, f32[8,128,256]{2,1,0:T(8,128)S(1)} %copy-done, f32[1,8,128,256]{3,2,1,0:T(8,128)S(1)} %copy-done.14), kind=kOutput, calls=%fused_computation.53 | convolution fusion | flops 404914176 | bytes 6291456 | tf_op jit(solution)/shard_map/...xy,kx->...ky/dot_general | solution.py:40
  46.1 1.1 constant_dynamic-update-slice_fusion.3
  47.5 1.2 constant_dynamic-update-slice_fusion
  49.3 4.7 %collective-permute-start.2 = (f32[1,1,128,256]{3,2,1,0:T(8,128)S(1)}, f32[1,1,128,256]{3,2,1,0:T(8,128)S(1)}, u32[]{:S(2)}, u32[]{:S(2)}) collective-permute-start(f32[1,1,128,256]{3,2,1,0:T(8,128)S(1)} %slice.285), channel_id=1, source_target_pairs={{0,1},{1,2},{2,3},{3,4},{4,5},{5,6},{6,7},{8,9},{9,10},{10,11},{11... | collective-permute-start | bytes 393224 | tf_op jit(solution)/shard_map/ppermute | solution.py:187
  54.0 3.7 %collective-permute-start.6 = (f32[1,3,128,256]{3,2,1,0:T(8,128)S(1)}, f32[1,3,128,256]{3,2,1,0:T(8,128)S(1)}, u32[]{:S(2)}, u32[]{:S(2)}) collective-permute-start(f32[1,3,128,256]{3,2,1,0:T(8,128)S(1)} %slice.300), channel_id=1, source_target_pairs={{0,1},{1,2},{2,3},{3,4},{4,5},{5,6},{6,7},{8,9},{9,10},{10,11},{11... | collective-permute-start | bytes 1179656 | tf_op jit(solution)/shard_map/ppermute | solution.py:192
  57.6 1.5 %collective-permute-start.5 = (f32[1,4,128,256]{3,2,1,0:T(8,128)S(1)}, f32[1,4,128,256]{3,2,1,0:T(8,128)S(1)}, u32[]{:S(2)}, u32[]{:S(2)}) collective-permute-start(f32[1,4,128,256]{3,2,1,0:T(8,128)S(1)} %slice.295), channel_id=1, source_target_pairs={{1,0},{2,1},{3,2},{4,3},{5,4},{6,5},{7,6},{9,8},{10,9},{11,10},{12... | collective-permute-start | bytes 1572872 | tf_op jit(solution)/shard_map/ppermute | solution.py:197
  60.2 1.3 fusion.31
  61.5 1.2 constant_dynamic-update-slice_fusion.7
  63.1 1.2 constant_dynamic-update-slice_fusion.4
  66.4 1.4 %fusion.36 = f32[1,8,128,256]{3,2,1,0:T(8,128)S(1)} fusion(f32[1,8,128,256]{3,2,1,0:T(8,128)S(1)} %bitcast.203, f32[1,8,128,256]{3,2,1,0:T(8,128)S(1)} %convolution_bitcast_fusion, f32[1,8,128,256]{3,2,1,0:T(8,128)S(1)} %fusion.74, f32[8,128,256]{2,1,0:T(8,128)S(1)} %copy-done, f32[1,8,128,256]{3,2,1,0:T(8,128)S(1)} %copy-done.5), kind=kOutput, calls=%fused_computation.68 | convolution fusion | flops 404914176 | bytes 6291456 | tf_op jit(solution)/shard_map/...xy,kx->...ky/dot_general | solution.py:40
  67.9 1.3 %collective-permute-start.7 = (f32[1,4,128,256]{3,2,1,0:T(8,128)S(1)}, f32[1,4,128,256]{3,2,1,0:T(8,128)S(1)}, u32[]{:S(2)}, u32[]{:S(2)}) collective-permute-start(f32[1,4,128,256]{3,2,1,0:T(8,128)S(1)} %get-tuple-element.28), channel_id=1, source_target_pairs={{1,0},{2,1},{3,2},{4,3},{5,4},{6,5},{7,6},{9,8},{10,9},{11,10},{12... | collective-permute-start | bytes 1572872 | tf_op jit(solution)/shard_map/ppermute | solution.py:87
  69.2 5.2 %collective-permute-start.8 = (f32[1,4,128,256]{3,2,1,0:T(8,128)S(1)}, f32[1,4,128,256]{3,2,1,0:T(8,128)S(1)}, u32[]{:S(2)}, u32[]{:S(2)}) collective-permute-start(f32[1,4,128,256]{3,2,1,0:T(8,128)S(1)} %get-tuple-element.29), channel_id=1, source_target_pairs={{0,1},{1,2},{2,3},{3,4},{4,5},{5,6},{6,7},{8,9},{9,10},{10,11},{11... | collective-permute-start | bytes 1572872 | tf_op jit(solution)/shard_map/ppermute | solution.py:86
  74.4 15.3 %collective-permute-done.6 = f32[1,3,128,256]{3,2,1,0:T(8,128)S(1)} collective-permute-done((f32[1,3,128,256]{3,2,1,0:T(8,128)S(1)}, f32[1,3,128,256]{3,2,1,0:T(8,128)S(1)}, u32[]{:S(2)}, u32[]{:S(2)}) %collective-permute-start.6) | collective-permute-done | bytes 393248 | tf_op jit(solution)/shard_map/ppermute | solution.py:192
  90.3 8.3 %collective-permute-done.8 = f32[1,4,128,256]{3,2,1,0:T(8,128)S(1)} collective-permute-done((f32[1,4,128,256]{3,2,1,0:T(8,128)S(1)}, f32[1,4,128,256]{3,2,1,0:T(8,128)S(1)}, u32[]{:S(2)}, u32[]{:S(2)}) %collective-permute-start.8) | collective-permute-done | bytes 524320 | tf_op jit(solution)/shard_map/ppermute | solution.py:86
  99.5 1.1 fusion.89
  102.1 1.9 %collective-permute-done.9 = f32[8,2,32,256]{3,0,2,1:T(8,128)S(1)} collective-permute-done((f32[8,2,32,256]{3,0,2,1:T(8,128)S(1)}, f32[8,2,32,256]{3,0,2,1:T(8,128)S(1)}, u32[]{:S(2)}, u32[]{:S(2)}) %collective-permute-start.9) | collective-permute-done | bytes 524320 | tf_op jit(solution)/shard_map/ppermute | solution.py:136
  104.3 1.6 %collective-permute-start.10 = (f32[8,1,32,256]{3,0,2,1:T(8,128)S(1)}, f32[8,1,32,256]{3,0,2,1:T(8,128)S(1)}, u32[]{:S(2)}, u32[]{:S(2)}) collective-permute-start(f32[8,1,32,256]{3,0,2,1:T(8,128)S(1)} %constant_dynamic-slice_fusion), channel_id=1, source_target_pairs={{0,16},{8,24},{16,0},{24,8},{1,17},{9,25},{17,1},{25,9},{2,18},{10... | collective-permute-start | bytes 786440 | tf_op jit(solution)/shard_map/ppermute | solution.py:136
  105.9 6.9 %collective-permute-done.10 = f32[8,1,32,256]{3,0,2,1:T(8,128)S(1)} collective-permute-done((f32[8,1,32,256]{3,0,2,1:T(8,128)S(1)}, f32[8,1,32,256]{3,0,2,1:T(8,128)S(1)}, u32[]{:S(2)}, u32[]{:S(2)}) %collective-permute-start.10) | collective-permute-done | bytes 262176 | tf_op jit(solution)/shard_map/ppermute | solution.py:136
  112.8 15.3 %all_to_all.18 = f32[8,32,256]{2,0,1:T(8,128)S(1)} all-to-all(f32[8,32,256]{2,0,1:T(8,128)S(1)} %add_bitcast_fusion), channel_id=1, replica_groups=mesh['shots'=4,'depth'=8] {'depth'}, dimensions={1} | all-to-all | bytes 524288 | tf_op jit(solution)/shard_map/all_to_all | solution.py:215
  (87 shorter events, 12.1 us)
Async XLA Ops:
  0.6 9.3 %copy-start.4 = (f32[1,8,128,256]{3,2,1,0:T(8,128)S(1)}, f32[1,8,128,256]{3,2,1,0:T(8,128)}, u32[]{:S(2)}) copy-start(f32[1,8,128,256]{3,2,1,0:T(8,128)} %param.15) | copy-start | bytes 3145732
  3.0 43.2 %collective-permute-start.1 = (f32[1,4,128,256]{3,2,1,0:T(8,128)}, f32[1,4,128,256]{3,2,1,0:T(8,128)}, u32[]{:S(2)}, u32[]{:S(2)}) collective-permute-start(f32[1,4,128,256]{3,2,1,0:T(8,128)} %get-tuple-element.35), channel_id=1, source_target_pairs={{0,1},{1,2},{2,3},{3,4},{4,5},{5,6},{6,7},{8,9},{9,10},{10,11},{11... | collective-permute-start | bytes 1572872 | tf_op jit(solution)/shard_map/ppermute | solution.py:86
  8.6 38.8 %collective-permute-start = (f32[1,4,128,256]{3,2,1,0:T(8,128)}, f32[1,4,128,256]{3,2,1,0:T(8,128)}, u32[]{:S(2)}, u32[]{:S(2)}) collective-permute-start(f32[1,4,128,256]{3,2,1,0:T(8,128)} %get-tuple-element.34), channel_id=1, source_target_pairs={{1,0},{2,1},{3,2},{4,3},{5,4},{6,5},{7,6},{9,8},{10,9},{11,10},{12... | collective-permute-start | bytes 1572872 | tf_op jit(solution)/shard_map/ppermute | solution.py:87
  11.0 8.8 %copy-start.15 = (f32[1,2,4096]{2,1,0:T(2,128)S(1)}, f32[1,2,4096]{2,1,0:T(2,128)}, u32[]{:S(2)}) copy-start(f32[1,2,4096]{2,1,0:T(2,128)} %param.23) | copy-start | bytes 98308
  11.0 8.8 %copy-start.16 = (s32[4096]{0:T(1024)S(1)}, s32[4096]{0:T(1024)}, u32[]{:S(2)}) copy-start(s32[4096]{0:T(1024)} %param.22) | copy-start | bytes 49156
  11.0 8.9 %copy-start.17 = (s32[4096]{0:T(1024)S(1)}, s32[4096]{0:T(1024)}, u32[]{:S(2)}) copy-start(s32[4096]{0:T(1024)} %param.21) | copy-start | bytes 49156
  11.0 50.4 %collective-permute-start.3 = (f32[1,4,128,256]{3,2,1,0:T(8,128)}, f32[1,4,128,256]{3,2,1,0:T(8,128)}, u32[]{:S(2)}, u32[]{:S(2)}) collective-permute-start(f32[1,4,128,256]{3,2,1,0:T(8,128)} %get-tuple-element.33), channel_id=1, source_target_pairs={{0,1},{1,2},{2,3},{3,4},{4,5},{5,6},{6,7},{8,9},{9,10},{10,11},{11... | collective-permute-start | bytes 1572872 | tf_op jit(solution)/shard_map/ppermute | solution.py:86
  16.5 45.0 %collective-permute-start.4 = (f32[1,4,128,256]{3,2,1,0:T(8,128)}, f32[1,4,128,256]{3,2,1,0:T(8,128)}, u32[]{:S(2)}, u32[]{:S(2)}) collective-permute-start(f32[1,4,128,256]{3,2,1,0:T(8,128)} %get-tuple-element.32), channel_id=1, source_target_pairs={{1,0},{2,1},{3,2},{4,3},{5,4},{6,5},{7,6},{9,8},{10,9},{11,10},{12... | collective-permute-start | bytes 1572872 | tf_op jit(solution)/shard_map/ppermute | solution.py:87
  34.4 1.2 copy-start.21
  34.4 1.2 copy-start.19
  34.4 1.2 copy-start.20
  34.4 1.3 copy-start.18
  38.0 1.5 %copy-start = (f32[8,128,256]{2,1,0:T(8,128)S(1)}, f32[8,128,256]{2,1,0:T(8,128)}, u32[]{:S(2)}) copy-start(f32[8,128,256]{2,1,0:T(8,128)} %param.16) | copy-start | bytes 3145732
  38.0 1.9 %copy-start.8 = (f32[1,8,128,256]{3,2,1,0:T(8,128)S(1)}, f32[1,8,128,256]{3,2,1,0:T(8,128)}, u32[]{:S(2)}) copy-start(f32[1,8,128,256]{3,2,1,0:T(8,128)} %convolution_bitcast_fusion.4) | copy-start | bytes 3145732
  38.0 2.2 %copy-start.13 = (f32[1,8,128,256]{3,2,1,0:T(8,128)S(1)}, f32[1,8,128,256]{3,2,1,0:T(8,128)}, u32[]{:S(2)}) copy-start(f32[1,8,128,256]{3,2,1,0:T(8,128)} %param.14) | copy-start | bytes 3145732
  40.2 2.4 %copy-start.3 = (f32[1,8,128,256]{3,2,1,0:T(8,128)S(1)}, f32[1,8,128,256]{3,2,1,0:T(8,128)}, u32[]{:S(2)}) copy-start(f32[1,8,128,256]{3,2,1,0:T(8,128)} %param.13) | copy-start | bytes 3145732
  42.6 1.2 copy-start.14
  47.2 1.4 %copy-start.12 = (f32[1,8,128,256]{3,2,1,0:T(8,128)S(1)}, f32[1,8,128,256]{3,2,1,0:T(8,128)}, u32[]{:S(2)}) copy-start(f32[1,8,128,256]{3,2,1,0:T(8,128)} %fusion.21) | copy-start | bytes 3145732
  49.1 50.3 %copy-start.1 = (f32[1,8,128,256]{3,2,1,0:T(8,128)}, f32[1,8,128,256]{3,2,1,0:T(8,128)S(1)}, u32[]{:S(2)}) copy-start(f32[1,8,128,256]{3,2,1,0:T(8,128)S(1)} %fusion.83) | copy-start | bytes 3145732
  49.2 11.0 %copy-start.10 = (f32[1,1024,256]{2,1,0:T(8,128)S(1)}, f32[1,1024,256]{2,1,0:T(8,128)}, u32[]{:S(2)}) copy-start(f32[1,1024,256]{2,1,0:T(8,128)} %get-tuple-element.24) | copy-start | bytes 3145732
  49.3 12.2 %collective-permute-start.2 = (f32[1,1,128,256]{3,2,1,0:T(8,128)S(1)}, f32[1,1,128,256]{3,2,1,0:T(8,128)S(1)}, u32[]{:S(2)}, u32[]{:S(2)}) collective-permute-start(f32[1,1,128,256]{3,2,1,0:T(8,128)S(1)} %slice.285), channel_id=1, source_target_pairs={{0,1},{1,2},{2,3},{3,4},{4,5},{5,6},{6,7},{8,9},{9,10},{10,11},{11... | collective-permute-start | bytes 393224 | tf_op jit(solution)/shard_map/ppermute | solution.py:187
  54.0 35.7 %collective-permute-start.6 = (f32[1,3,128,256]{3,2,1,0:T(8,128)S(1)}, f32[1,3,128,256]{3,2,1,0:T(8,128)S(1)}, u32[]{:S(2)}, u32[]{:S(2)}) collective-permute-start(f32[1,3,128,256]{3,2,1,0:T(8,128)S(1)} %slice.300), channel_id=1, source_target_pairs={{0,1},{1,2},{2,3},{3,4},{4,5},{5,6},{6,7},{8,9},{9,10},{10,11},{11... | collective-permute-start | bytes 1179656 | tf_op jit(solution)/shard_map/ppermute | solution.py:192
  57.6 32.1 %collective-permute-start.5 = (f32[1,4,128,256]{3,2,1,0:T(8,128)S(1)}, f32[1,4,128,256]{3,2,1,0:T(8,128)S(1)}, u32[]{:S(2)}, u32[]{:S(2)}) collective-permute-start(f32[1,4,128,256]{3,2,1,0:T(8,128)S(1)} %slice.295), channel_id=1, source_target_pairs={{1,0},{2,1},{3,2},{4,3},{5,4},{6,5},{7,6},{9,8},{10,9},{11,10},{12... | collective-permute-start | bytes 1572872 | tf_op jit(solution)/shard_map/ppermute | solution.py:197
  61.5 1.4 %copy-start.5 = (f32[1,8,128,256]{3,2,1,0:T(8,128)S(1)}, f32[1,8,128,256]{3,2,1,0:T(8,128)}, u32[]{:S(2)}) copy-start(f32[1,8,128,256]{3,2,1,0:T(8,128)} %param.15) | copy-start | bytes 3145732
  62.9 1.4 %copy-start.11 = (f32[1,8,128,256]{3,2,1,0:T(8,128)S(1)}, f32[1,8,128,256]{3,2,1,0:T(8,128)}, u32[]{:S(2)}) copy-start(f32[1,8,128,256]{3,2,1,0:T(8,128)} %fusion.26) | copy-start | bytes 3145732
  64.8 34.7 %copy-start.2 = (f32[1,8,128,256]{3,2,1,0:T(8,128)}, f32[1,8,128,256]{3,2,1,0:T(8,128)S(1)}, u32[]{:S(2)}) copy-start(f32[1,8,128,256]{3,2,1,0:T(8,128)S(1)} %fusion.74) | copy-start | bytes 3145732
  64.8 1.6 %copy-start.9 = (f32[1,1024,256]{2,1,0:T(8,128)S(1)}, f32[1,1024,256]{2,1,0:T(8,128)}, u32[]{:S(2)}) copy-start(f32[1,1024,256]{2,1,0:T(8,128)} %get-tuple-element.22) | copy-start | bytes 3145732
  67.9 22.4 %collective-permute-start.7 = (f32[1,4,128,256]{3,2,1,0:T(8,128)S(1)}, f32[1,4,128,256]{3,2,1,0:T(8,128)S(1)}, u32[]{:S(2)}, u32[]{:S(2)}) collective-permute-start(f32[1,4,128,256]{3,2,1,0:T(8,128)S(1)} %get-tuple-element.28), channel_id=1, source_target_pairs={{1,0},{2,1},{3,2},{4,3},{5,4},{6,5},{7,6},{9,8},{10,9},{11,10},{12... | collective-permute-start | bytes 1572872 | tf_op jit(solution)/shard_map/ppermute | solution.py:87
  69.2 29.4 %collective-permute-start.8 = (f32[1,4,128,256]{3,2,1,0:T(8,128)S(1)}, f32[1,4,128,256]{3,2,1,0:T(8,128)S(1)}, u32[]{:S(2)}, u32[]{:S(2)}) collective-permute-start(f32[1,4,128,256]{3,2,1,0:T(8,128)S(1)} %get-tuple-element.29), channel_id=1, source_target_pairs={{0,1},{1,2},{2,3},{3,4},{4,5},{5,6},{6,7},{8,9},{9,10},{10,11},{11... | collective-permute-start | bytes 1572872 | tf_op jit(solution)/shard_map/ppermute | solution.py:86
  90.2 9.2 %copy-start.6 = (f32[1,8,128,256]{3,2,1,0:T(8,128)}, f32[1,8,128,256]{3,2,1,0:T(8,128)S(1)}, u32[]{:S(2)}) copy-start(f32[1,8,128,256]{3,2,1,0:T(8,128)S(1)} %fusion.60) | copy-start | bytes 3145732
  102.0 2.0 %collective-permute-start.9 = (f32[8,2,32,256]{3,0,2,1:T(8,128)S(1)}, f32[8,2,32,256]{3,0,2,1:T(8,128)S(1)}, u32[]{:S(2)}, u32[]{:S(2)}) collective-permute-start(f32[8,2,32,256]{3,0,2,1:T(8,128)S(1)} %bitcast.209), channel_id=1, source_target_pairs={{0,8},{8,0},{16,24},{24,16},{1,9},{9,1},{17,25},{25,17},{2,10},{10... | collective-permute-start | bytes 1572872 | tf_op jit(solution)/shard_map/ppermute | solution.py:136
  104.3 8.4 %collective-permute-start.10 = (f32[8,1,32,256]{3,0,2,1:T(8,128)S(1)}, f32[8,1,32,256]{3,0,2,1:T(8,128)S(1)}, u32[]{:S(2)}, u32[]{:S(2)}) collective-permute-start(f32[8,1,32,256]{3,0,2,1:T(8,128)S(1)} %constant_dynamic-slice_fusion), channel_id=1, source_target_pairs={{0,16},{8,24},{16,0},{24,8},{1,17},{9,25},{17,1},{25,9},{2,18},{10... | collective-permute-start | bytes 786440 | tf_op jit(solution)/shard_map/ppermute | solution.py:136
  (1 other events, 1.1 us)

commit v14 on v12

--- a/solution.py
+++ b/solution.py
@@ -166,8 +166,11 @@
     correlation = None
     forward_terms = spread_dense(source_depth, source_cell, signs[0][None, :] * wavelet, first_plane, planes, rows, cols)
     adjoint_terms = spread_dense(receiver_depth, receiver_cell, residual_traces[0], first_plane, planes, rows, cols)
+    markers = []
     for step in range(STEPS):
         terms = [forward_terms[step : step + 1], adjoint_terms[step : step + 1]]
+        if markers:
+            _, current[1] = lax.optimization_barrier((markers[1], current[1]))
         partial = lax.optimization_barrier(
             [
                 2.0 * current[i] - earlier[i] + courant * lateral_laplace(current[i], zaxis) + terms[i]
@@ -176,14 +179,32 @@
         )
         fresh = []
         halos = ([], [])
+        markers = []
         for i in range(2):
             if i > 0 and step + 1 < STEPS:
-                _, below[i], above[i] = lax.optimization_barrier((halos[0][-1], below[i], above[i]))
+                _, below[i], above[i] = lax.optimization_barrier((markers[0], below[i], above[i]))
             fresh.append(partial[i] + courant * depth_laplace(below[i], current[i], above[i], zaxis))
             if step + 1 < STEPS:
-                sent = exchange([fresh[i]], zaxis)
-                halos[0].append(sent[0][0])
-                halos[1].append(sent[1][0])
+                devices = lax.axis_size("depth")
+                length = fresh[i].shape[zaxis]
+                marker = lax.ppermute(
+                    lax.slice_in_dim(fresh[i], length - 1, length, axis=zaxis),
+                    "depth",
+                    [(j, j + 1) for j in range(devices - 1)],
+                )
+                rest = lax.ppermute(
+                    lax.slice_in_dim(fresh[i], length - HALO, length - 1, axis=zaxis),
+                    "depth",
+                    [(j, j + 1) for j in range(devices - 1)],
+                )
+                leading = lax.ppermute(
+                    lax.slice_in_dim(fresh[i], 0, HALO, axis=zaxis),
+                    "depth",
+                    [(j + 1, j) for j in range(devices - 1)],
+                )
+                halos[0].append(jnp.concatenate([rest, marker], axis=zaxis))
+                halos[1].append(leading)
+                markers.append(marker)
         if step + 1 < STEPS:
             below, above = halos
         part = fresh[0][0] * fresh[1][0]

time: 136 us -> 130 us (0.956)
  waiting for transfers between devices: 42.7 us -> 30.9 us
  starting transfers between devices: 27.5 us -> 34.3 us
    ppermute x4 -> x2, waiting for transfers between devices: 34 us -> 0.01 us  [exchange(): lax.ppermute(lax.slice_in_dim(f, length - HALO, length, axis=dim), 'depth...]
    ppermute x0 -> x6, waiting for transfers between devices: none -> 22.2 us  [the longest x2 18.6 us: on_device(): lax.ppermute(lax.slice_in_dim(fresh[i], length - 1, length, axis=zaxis),...]
    ppermute x0 -> x6, starting transfers between devices: none -> 18.9 us  [the longest x2 9.38 us: on_device(): lax.ppermute(lax.slice_in_dim(fresh[i], length - 1, length, axis=zaxis),...]
    ppermute x4 -> x2, starting transfers between devices: 20.6 us -> 11.2 us  [exchange(): lax.ppermute(lax.slice_in_dim(f, length - HALO, length, axis=dim), 'depth...]
    ppermute x4 -> x2, starting transfers between devices: 5.36 us -> 2.56 us  [exchange(): lax.ppermute(lax.slice_in_dim(f, 0, HALO, axis=dim), 'depth', down)]
    add x3 -> x4, other arithmetic: 3.34 us -> 1.95 us  [on_device(): partial[i] + courant * depth_laplace(below[i], current[i], above[i], zaxis)]
    slice x4 -> x2, local copies, waits for them, and re-layouts: 3.7 us -> 3.49 us  [exchange(): lax.slice_in_dim(f, 0, HALO, axis=dim)]
    unnamed x51 -> x54, local copies, waits for them, and re-layouts: 5.28 us -> 5.44 us
  transfers between devices with their start and end apart: 10 -> 12, of which waited for: 4 -> 4; matrix products, arithmetic and copies ran while one was open for 29% -> 31% of each run, Pallas kernels for 0% -> 0%
where the time goes in v14:
time: 130 us; the launch traced here: 129 us
  starting transfers between devices  34.3 us (26%)
  waiting for transfers between devices  30.9 us (24%)
  matrix products  29.6 us (23%)
  local copies, waits for them, and re-layouts  14.2 us (11%)
  blocking collectives  14.1 us (11%)
  other arithmetic  4.42 us (3%)
  between operations  1.4 us (1%)
    ppermute x2, waiting for transfers between devices, on_device(): lax.ppermute(lax.slice_in_dim(fresh[i], length - 1, length, axis=zaxis),...  18.6 us
    dot_general x2, matrix products, spread_dense(): grid = jnp.dot(by_row, right, preferred_element_type=jnp.float32)  15 us
    all_to_all x1, blocking collectives, on_device(): lax.all_to_all(reduced, 'depth', split_axis=1, concat_axis=0, tiled=True)  14.1 us
    ppermute x2, starting transfers between devices, exchange(): lax.ppermute(lax.slice_in_dim(f, length - HALO, length, axis=dim), 'depth...  11.2 us
    ppermute x2, starting transfers between devices, on_device(): lax.ppermute(lax.slice_in_dim(fresh[i], length - 1, length, axis=zaxis),...  9.38 us
    ppermute x2, waiting for transfers between devices, reduce_shots(): blocks = keep + lax.ppermute(send, 'shots', pairs)  8.71 us
    dot_general x4, matrix products, lateral_laplace(): along_x = jnp.einsum('...xy,kx->...ky', core, band(rows), precision=high)  7.44 us
    ppermute x2, starting transfers between devices, on_device(): lax.ppermute(lax.slice_in_dim(fresh[i], length - HALO, length - 1, axis=z...  6.72 us
  transfers between devices with their start and end apart: 12, of which 4 were waited for; matrix products, arithmetic and copies ran while one was open for 31% of the time, Pallas kernels for 0%

profile of v14, /device:TPU:0, one launch (start us, length us, event | category | flops | bytes accessed | tf_op | source)
XLA Modules:
  0.0 128.9 jit_solution(12188059574222061292)
XLA Ops:
  0.6 2.4 %fusion.274 = (f32[1,4,128,256]{3,2,1,0:T(8,128)}, f32[1,4,128,256]{3,2,1,0:T(8,128)}) fusion(f32[1,8,128,256]{3,2,1,0:T(8,128)} %param.13), kind=kLoop, calls=%fused_computation.348 | loop fusion | bytes 2097152 | tf_op jit(solution)/shard_map/slice | solution.py:87
  3.0 5.7 %collective-permute-start.1 = (f32[1,4,128,256]{3,2,1,0:T(8,128)}, f32[1,4,128,256]{3,2,1,0:T(8,128)}, u32[]{:S(2)}, u32[]{:S(2)}) collective-permute-start(f32[1,4,128,256]{3,2,1,0:T(8,128)} %get-tuple-element.37), channel_id=1, source_target_pairs={{0,1},{1,2},{2,3},{3,4},{4,5},{5,6},{6,7},{8,9},{9,10},{10,11},{11... | collective-permute-start | bytes 1572872 | tf_op jit(solution)/shard_map/ppermute | solution.py:86
  8.7 1.3 collective-permute-start
  10.0 1.1 fusion.273
  11.1 5.5 %collective-permute-start.3 = (f32[1,4,128,256]{3,2,1,0:T(8,128)}, f32[1,4,128,256]{3,2,1,0:T(8,128)}, u32[]{:S(2)}, u32[]{:S(2)}) collective-permute-start(f32[1,4,128,256]{3,2,1,0:T(8,128)} %get-tuple-element.35), channel_id=1, source_target_pairs={{0,1},{1,2},{2,3},{3,4},{4,5},{5,6},{6,7},{8,9},{9,10},{10,11},{11... | collective-permute-start | bytes 1572872 | tf_op jit(solution)/shard_map/ppermute | solution.py:86
  16.6 1.3 collective-permute-start.4
  17.9 2.0 %convolution_bitcast_fusion.4 = f32[1,8,128,256]{3,2,1,0:T(8,128)} fusion(f32[1,8,128,256]{3,2,1,0:T(8,128)S(1)} %copy-done.5), kind=kOutput, calls=%fused_computation.33 | convolution fusion | flops 805961728 | bytes 2097152 | tf_op jit(solution)/shard_map/...xy,yk->...xk/dot_general | solution.py:39
  20.7 13.2 %fusion.1 = f32[1024,3,2,256]{3,0,2,1:T(8,128)S(1)} fusion(pred[4096,256]{0,1:T(8,128)(4,1)S(1)} %iota_compare_fusion.1, s32[4096]{0:T(1024)S(1)} %get-tuple-element.47, bf16[4096,3,2]{0,2,1:T(2,128)(2,1)S(1)} %maximum_bitcast_fusion), kind=kOutput, calls=%fused_computation.2 | convolution fusion | flops 12895387648 | bytes 7405568 | tf_op jit(solution)/shard_map/dot_general | solution.py:116
  34.5 1.1 fusion.271
  35.8 1.8 %fusion.12 = f32[1024,3,2,256]{3,0,2,1:T(8,128)S(1)} fusion(pred[512,256]{0,1:T(8,128)(4,1)S(1)} %iota_compare_fusion.3, s32[512]{0:T(512)S(1)} %get-tuple-element.52, bf16[512,3,2]{0,2,1:T(2,128)(2,1)S(1)} %maximum_bitcast_fusion.1), kind=kOutput, calls=%fused_computation.21 | convolution fusion | flops 1611923456 | bytes 6430720 | tf_op jit(solution)/shard_map/dot_general | solution.py:116
  38.1 1.1 fusion.272
  40.3 2.4 %fusion.26 = f32[1,8,128,256]{3,2,1,0:T(8,128)} fusion(f32[1,8,128,256]{3,2,1,0:T(8,128)S(1)} %bitcast.208, f32[1,8,128,256]{3,2,1,0:T(8,128)S(1)} %copy-done.9, f32[1,8,128,256]{3,2,1,0:T(8,128)S(1)} %copy-done.5, f32[8,128,256]{2,1,0:T(8,128)S(1)} %copy-done, f32[1,8,128,256]{3,2,1,0:T(8,128)S(1)} %copy-done.14), kind=kOutput, calls=%fused_computation.46 | convolution fusion | flops 404914176 | bytes 6291456 | tf_op jit(solution)/shard_map/...xy,kx->...ky/dot_general | solution.py:40
  42.7 1.1 convolution_bitcast_fusion.6
  43.9 2.4 %fusion.21 = f32[1,8,128,256]{3,2,1,0:T(8,128)} fusion(f32[1,8,128,256]{3,2,1,0:T(8,128)S(1)} %bitcast.209, f32[1,8,128,256]{3,2,1,0:T(8,128)S(1)} %convolution_bitcast_fusion.6, f32[1,8,128,256]{3,2,1,0:T(8,128)S(1)} %copy-done.3, f32[8,128,256]{2,1,0:T(8,128)S(1)} %copy-done, f32[1,8,128,256]{3,2,1,0:T(8,128)S(1)} %copy-done.15), kind=kOutput, calls=%fused_computation.41 | convolution fusion | flops 404914176 | bytes 6291456 | tf_op jit(solution)/shard_map/...xy,kx->...ky/dot_general | solution.py:40
  46.3 1.1 constant_dynamic-update-slice_fusion.3
  47.6 1.2 constant_dynamic-update-slice_fusion
  49.4 4.7 %collective-permute-start.2 = (f32[1,1,128,256]{3,2,1,0:T(8,128)S(1)}, f32[1,1,128,256]{3,2,1,0:T(8,128)S(1)}, u32[]{:S(2)}, u32[]{:S(2)}) collective-permute-start(f32[1,1,128,256]{3,2,1,0:T(8,128)S(1)} %slice.289), channel_id=1, source_target_pairs={{0,1},{1,2},{2,3},{3,4},{4,5},{5,6},{6,7},{8,9},{9,10},{10,11},{11... | collective-permute-start | bytes 393224 | tf_op jit(solution)/shard_map/ppermute | solution.py:190
  54.1 3.7 %collective-permute-start.7 = (f32[1,3,128,256]{3,2,1,0:T(8,128)S(1)}, f32[1,3,128,256]{3,2,1,0:T(8,128)S(1)}, u32[]{:S(2)}, u32[]{:S(2)}) collective-permute-start(f32[1,3,128,256]{3,2,1,0:T(8,128)S(1)} %slice.305), channel_id=1, source_target_pairs={{0,1},{1,2},{2,3},{3,4},{4,5},{5,6},{6,7},{8,9},{9,10},{10,11},{11... | collective-permute-start | bytes 1179656 | tf_op jit(solution)/shard_map/ppermute | solution.py:195
  57.8 1.3 %collective-permute-start.6 = (f32[1,4,128,256]{3,2,1,0:T(8,128)S(1)}, f32[1,4,128,256]{3,2,1,0:T(8,128)S(1)}, u32[]{:S(2)}, u32[]{:S(2)}) collective-permute-start(f32[1,4,128,256]{3,2,1,0:T(8,128)S(1)} %slice.300), channel_id=1, source_target_pairs={{1,0},{2,1},{3,2},{4,3},{5,4},{6,5},{7,6},{9,8},{10,9},{11,10},{12... | collective-permute-start | bytes 1572872 | tf_op jit(solution)/shard_map/ppermute | solution.py:200
  60.1 1.1 constant_dynamic-update-slice_fusion.7
  61.5 1.2 constant_dynamic-update-slice_fusion.4
  63.2 4.7 %collective-permute-start.5 = (f32[1,1,128,256]{3,2,1,0:T(8,128)S(1)}, f32[1,1,128,256]{3,2,1,0:T(8,128)S(1)}, u32[]{:S(2)}, u32[]{:S(2)}) collective-permute-start(f32[1,1,128,256]{3,2,1,0:T(8,128)S(1)} %slice.298), channel_id=1, source_target_pairs={{0,1},{1,2},{2,3},{3,4},{4,5},{5,6},{6,7},{8,9},{9,10},{10,11},{11... | collective-permute-start | bytes 393224 | tf_op jit(solution)/shard_map/ppermute | solution.py:190
  67.9 1.4 %fusion.31 = f32[1,8,128,256]{3,2,1,0:T(8,128)S(1)} fusion(f32[1,8,128,256]{3,2,1,0:T(8,128)S(1)} %bitcast.207, f32[1,8,128,256]{3,2,1,0:T(8,128)S(1)} %convolution_bitcast_fusion.2, f32[1,8,128,256]{3,2,1,0:T(8,128)S(1)} %fusion.70, f32[8,128,256]{2,1,0:T(8,128)S(1)} %copy-done, f32[1,8,128,256]{3,2,1,0:T(8,128)S(1)} %copy-done.4), kind=kOutput, calls=%fused_computation.51 | convolution fusion | flops 404914176 | bytes 6291456 | tf_op jit(solution)/shard_map/...xy,kx->...ky/dot_general | solution.py:40
  69.4 3.1 %collective-permute-start.9 = (f32[1,3,128,256]{3,2,1,0:T(8,128)S(1)}, f32[1,3,128,256]{3,2,1,0:T(8,128)S(1)}, u32[]{:S(2)}, u32[]{:S(2)}) collective-permute-start(f32[1,3,128,256]{3,2,1,0:T(8,128)S(1)} %slice.314), channel_id=1, source_target_pairs={{0,1},{1,2},{2,3},{3,4},{4,5},{5,6},{6,7},{8,9},{9,10},{10,11},{11... | collective-permute-start | bytes 1179656 | tf_op jit(solution)/shard_map/ppermute | solution.py:195
  72.4 1.5 %collective-permute-start.8 = (f32[1,4,128,256]{3,2,1,0:T(8,128)S(1)}, f32[1,4,128,256]{3,2,1,0:T(8,128)S(1)}, u32[]{:S(2)}, u32[]{:S(2)}) collective-permute-start(f32[1,4,128,256]{3,2,1,0:T(8,128)S(1)} %slice.311), channel_id=1, source_target_pairs={{1,0},{2,1},{3,2},{4,3},{5,4},{6,5},{7,6},{9,8},{10,9},{11,10},{12... | collective-permute-start | bytes 1572872 | tf_op jit(solution)/shard_map/ppermute | solution.py:200
  74.0 18.6 %collective-permute-done.5 = f32[1,1,128,256]{3,2,1,0:T(8,128)S(1)} collective-permute-done((f32[1,1,128,256]{3,2,1,0:T(8,128)S(1)}, f32[1,1,128,256]{3,2,1,0:T(8,128)S(1)}, u32[]{:S(2)}, u32[]{:S(2)}) %collective-permute-start.5) | collective-permute-done | bytes 131104 | tf_op jit(solution)/shard_map/ppermute | solution.py:190
  93.6 1.4 %fusion.87 = f32[1,8,128,256]{3,2,1,0:T(8,128)S(1)} fusion(f32[1,8,128,256]{3,2,1,0:T(8,128)S(1)} %bitcast.206, f32[8,128,256]{2,1,0:T(8,128)S(1)} %copy-done, f32[1,8,128,256]{3,2,1,0:T(8,128)S(1)} %fusion.61, f32[1,8,128,256]{3,2,1,0:T(8,128)S(1)} %copy-done.6, f32[1,8,128,256]{3,2,1,0:T(8,128)S(1)} %convolution_bitcast_fusion), kind=kOutput, calls=%fused_computation.125 | convolution fusion | flops 404914176 | bytes 6291456 | tf_op jit(solution)/shard_map/...xy,kx->...ky/dot_general | solution.py:40
  95.1 3.5 %collective-permute-done.9 = f32[1,3,128,256]{3,2,1,0:T(8,128)S(1)} collective-permute-done((f32[1,3,128,256]{3,2,1,0:T(8,128)S(1)}, f32[1,3,128,256]{3,2,1,0:T(8,128)S(1)}, u32[]{:S(2)}, u32[]{:S(2)}) %collective-permute-start.9) | collective-permute-done | bytes 393248 | tf_op jit(solution)/shard_map/ppermute | solution.py:195
  103.0 1.9 %collective-permute-done.10 = f32[8,2,32,256]{3,0,2,1:T(8,128)S(1)} collective-permute-done((f32[8,2,32,256]{3,0,2,1:T(8,128)S(1)}, f32[8,2,32,256]{3,0,2,1:T(8,128)S(1)}, u32[]{:S(2)}, u32[]{:S(2)}) %collective-permute-start.10) | collective-permute-done | bytes 524320 | tf_op jit(solution)/shard_map/ppermute | solution.py:136
  105.2 1.6 %collective-permute-start.11 = (f32[8,1,32,256]{3,0,2,1:T(8,128)S(1)}, f32[8,1,32,256]{3,0,2,1:T(8,128)S(1)}, u32[]{:S(2)}, u32[]{:S(2)}) collective-permute-start(f32[8,1,32,256]{3,0,2,1:T(8,128)S(1)} %constant_dynamic-slice_fusion), channel_id=1, source_target_pairs={{0,16},{8,24},{16,0},{24,8},{1,17},{9,25},{17,1},{25,9},{2,18},{10... | collective-permute-start | bytes 786440 | tf_op jit(solution)/shard_map/ppermute | solution.py:136
  106.8 6.9 %collective-permute-done.11 = f32[8,1,32,256]{3,0,2,1:T(8,128)S(1)} collective-permute-done((f32[8,1,32,256]{3,0,2,1:T(8,128)S(1)}, f32[8,1,32,256]{3,0,2,1:T(8,128)S(1)}, u32[]{:S(2)}, u32[]{:S(2)}) %collective-permute-start.11) | collective-permute-done | bytes 262176 | tf_op jit(solution)/shard_map/ppermute | solution.py:136
  113.7 14.1 %all_to_all.18 = f32[8,32,256]{2,0,1:T(8,128)S(1)} all-to-all(f32[8,32,256]{2,0,1:T(8,128)S(1)} %add_bitcast_fusion), channel_id=1, replica_groups=mesh['shots'=4,'depth'=8] {'depth'}, dimensions={1} | all-to-all | bytes 524288 | tf_op jit(solution)/shard_map/all_to_all | solution.py:215
  (97 shorter events, 12.6 us)
Async XLA Ops:
  0.6 9.3 %copy-start.5 = (f32[1,8,128,256]{3,2,1,0:T(8,128)S(1)}, f32[1,8,128,256]{3,2,1,0:T(8,128)}, u32[]{:S(2)}) copy-start(f32[1,8,128,256]{3,2,1,0:T(8,128)} %param.15) | copy-start | bytes 3145732
  3.0 43.3 %collective-permute-start.1 = (f32[1,4,128,256]{3,2,1,0:T(8,128)}, f32[1,4,128,256]{3,2,1,0:T(8,128)}, u32[]{:S(2)}, u32[]{:S(2)}) collective-permute-start(f32[1,4,128,256]{3,2,1,0:T(8,128)} %get-tuple-element.37), channel_id=1, source_target_pairs={{0,1},{1,2},{2,3},{3,4},{4,5},{5,6},{6,7},{8,9},{9,10},{10,11},{11... | collective-permute-start | bytes 1572872 | tf_op jit(solution)/shard_map/ppermute | solution.py:86
  8.7 38.9 %collective-permute-start = (f32[1,4,128,256]{3,2,1,0:T(8,128)}, f32[1,4,128,256]{3,2,1,0:T(8,128)}, u32[]{:S(2)}, u32[]{:S(2)}) collective-permute-start(f32[1,4,128,256]{3,2,1,0:T(8,128)} %get-tuple-element.36), channel_id=1, source_target_pairs={{1,0},{2,1},{3,2},{4,3},{5,4},{6,5},{7,6},{9,8},{10,9},{11,10},{12... | collective-permute-start | bytes 1572872 | tf_op jit(solution)/shard_map/ppermute | solution.py:87
  11.1 8.8 %copy-start.16 = (f32[1,2,4096]{2,1,0:T(2,128)S(1)}, f32[1,2,4096]{2,1,0:T(2,128)}, u32[]{:S(2)}) copy-start(f32[1,2,4096]{2,1,0:T(2,128)} %param.23) | copy-start | bytes 98308
  11.1 8.8 %copy-start.17 = (s32[4096]{0:T(1024)S(1)}, s32[4096]{0:T(1024)}, u32[]{:S(2)}) copy-start(s32[4096]{0:T(1024)} %param.22) | copy-start | bytes 49156
  11.1 8.8 %copy-start.18 = (s32[4096]{0:T(1024)S(1)}, s32[4096]{0:T(1024)}, u32[]{:S(2)}) copy-start(s32[4096]{0:T(1024)} %param.21) | copy-start | bytes 49156
  11.1 49.0 %collective-permute-start.3 = (f32[1,4,128,256]{3,2,1,0:T(8,128)}, f32[1,4,128,256]{3,2,1,0:T(8,128)}, u32[]{:S(2)}, u32[]{:S(2)}) collective-permute-start(f32[1,4,128,256]{3,2,1,0:T(8,128)} %get-tuple-element.35), channel_id=1, source_target_pairs={{0,1},{1,2},{2,3},{3,4},{4,5},{5,6},{6,7},{8,9},{9,10},{10,11},{11... | collective-permute-start | bytes 1572872 | tf_op jit(solution)/shard_map/ppermute | solution.py:86
  16.6 43.5 %collective-permute-start.4 = (f32[1,4,128,256]{3,2,1,0:T(8,128)}, f32[1,4,128,256]{3,2,1,0:T(8,128)}, u32[]{:S(2)}, u32[]{:S(2)}) collective-permute-start(f32[1,4,128,256]{3,2,1,0:T(8,128)} %get-tuple-element.34), channel_id=1, source_target_pairs={{1,0},{2,1},{3,2},{4,3},{5,4},{6,5},{7,6},{9,8},{10,9},{11,10},{12... | collective-permute-start | bytes 1572872 | tf_op jit(solution)/shard_map/ppermute | solution.py:87
  34.5 1.2 copy-start.22
  34.5 1.2 copy-start.20
  34.5 1.3 copy-start.19
  38.1 1.5 %copy-start = (f32[8,128,256]{2,1,0:T(8,128)S(1)}, f32[8,128,256]{2,1,0:T(8,128)}, u32[]{:S(2)}) copy-start(f32[8,128,256]{2,1,0:T(8,128)} %param.16) | copy-start | bytes 3145732
  38.1 1.9 %copy-start.9 = (f32[1,8,128,256]{3,2,1,0:T(8,128)S(1)}, f32[1,8,128,256]{3,2,1,0:T(8,128)}, u32[]{:S(2)}) copy-start(f32[1,8,128,256]{3,2,1,0:T(8,128)} %convolution_bitcast_fusion.4) | copy-start | bytes 3145732
  38.1 2.2 %copy-start.14 = (f32[1,8,128,256]{3,2,1,0:T(8,128)S(1)}, f32[1,8,128,256]{3,2,1,0:T(8,128)}, u32[]{:S(2)}) copy-start(f32[1,8,128,256]{3,2,1,0:T(8,128)} %param.14) | copy-start | bytes 3145732
  40.3 2.4 %copy-start.3 = (f32[1,8,128,256]{3,2,1,0:T(8,128)S(1)}, f32[1,8,128,256]{3,2,1,0:T(8,128)}, u32[]{:S(2)}) copy-start(f32[1,8,128,256]{3,2,1,0:T(8,128)} %param.13) | copy-start | bytes 3145732
  42.7 1.2 copy-start.15
  47.4 1.4 %copy-start.13 = (f32[1,8,128,256]{3,2,1,0:T(8,128)S(1)}, f32[1,8,128,256]{3,2,1,0:T(8,128)}, u32[]{:S(2)}) copy-start(f32[1,8,128,256]{3,2,1,0:T(8,128)} %fusion.21) | copy-start | bytes 3145732
  49.3 50.7 %copy-start.2 = (f32[1,8,128,256]{3,2,1,0:T(8,128)}, f32[1,8,128,256]{3,2,1,0:T(8,128)S(1)}, u32[]{:S(2)}) copy-start(f32[1,8,128,256]{3,2,1,0:T(8,128)S(1)} %fusion.70) | copy-start | bytes 3145732
  49.4 11.8 %copy-start.6 = (f32[1,8,128,256]{3,2,1,0:T(8,128)S(1)}, f32[1,8,128,256]{3,2,1,0:T(8,128)}, u32[]{:S(2)}) copy-start(f32[1,8,128,256]{3,2,1,0:T(8,128)} %param.15) | copy-start | bytes 3145732
  49.4 10.7 %collective-permute-start.2 = (f32[1,1,128,256]{3,2,1,0:T(8,128)S(1)}, f32[1,1,128,256]{3,2,1,0:T(8,128)S(1)}, u32[]{:S(2)}, u32[]{:S(2)}) collective-permute-start(f32[1,1,128,256]{3,2,1,0:T(8,128)S(1)} %slice.289), channel_id=1, source_target_pairs={{0,1},{1,2},{2,3},{3,4},{4,5},{5,6},{6,7},{8,9},{9,10},{10,11},{11... | collective-permute-start | bytes 393224 | tf_op jit(solution)/shard_map/ppermute | solution.py:190
  54.1 40.9 %collective-permute-start.7 = (f32[1,3,128,256]{3,2,1,0:T(8,128)S(1)}, f32[1,3,128,256]{3,2,1,0:T(8,128)S(1)}, u32[]{:S(2)}, u32[]{:S(2)}) collective-permute-start(f32[1,3,128,256]{3,2,1,0:T(8,128)S(1)} %slice.305), channel_id=1, source_target_pairs={{0,1},{1,2},{2,3},{3,4},{4,5},{5,6},{6,7},{8,9},{9,10},{10,11},{11... | collective-permute-start | bytes 1179656 | tf_op jit(solution)/shard_map/ppermute | solution.py:195
  57.8 41.2 %collective-permute-start.6 = (f32[1,4,128,256]{3,2,1,0:T(8,128)S(1)}, f32[1,4,128,256]{3,2,1,0:T(8,128)S(1)}, u32[]{:S(2)}, u32[]{:S(2)}) collective-permute-start(f32[1,4,128,256]{3,2,1,0:T(8,128)S(1)} %slice.300), channel_id=1, source_target_pairs={{1,0},{2,1},{3,2},{4,3},{5,4},{6,5},{7,6},{9,8},{10,9},{11,10},{12... | collective-permute-start | bytes 1572872 | tf_op jit(solution)/shard_map/ppermute | solution.py:200
  61.2 1.4 %copy-start.12 = (f32[1,8,128,256]{3,2,1,0:T(8,128)S(1)}, f32[1,8,128,256]{3,2,1,0:T(8,128)}, u32[]{:S(2)}) copy-start(f32[1,8,128,256]{3,2,1,0:T(8,128)} %fusion.26) | copy-start | bytes 3145732
  62.6 5.3 %copy-start.4 = (f32[1,8,128,256]{3,2,1,0:T(8,128)S(1)}, f32[1,8,128,256]{3,2,1,0:T(8,128)}, u32[]{:S(2)}) copy-start(f32[1,8,128,256]{3,2,1,0:T(8,128)} %param.13) | copy-start | bytes 3145732
  62.6 5.3 %copy-start.11 = (f32[1,1024,256]{2,1,0:T(8,128)S(1)}, f32[1,1024,256]{2,1,0:T(8,128)}, u32[]{:S(2)}) copy-start(f32[1,1024,256]{2,1,0:T(8,128)} %get-tuple-element.26) | copy-start | bytes 3145732
  63.2 36.8 %copy-start.1 = (f32[1,8,128,256]{3,2,1,0:T(8,128)}, f32[1,8,128,256]{3,2,1,0:T(8,128)S(1)}, u32[]{:S(2)}) copy-start(f32[1,8,128,256]{3,2,1,0:T(8,128)S(1)} %fusion.61) | copy-start | bytes 3145732
  63.2 29.4 %collective-permute-start.5 = (f32[1,1,128,256]{3,2,1,0:T(8,128)S(1)}, f32[1,1,128,256]{3,2,1,0:T(8,128)S(1)}, u32[]{:S(2)}, u32[]{:S(2)}) collective-permute-start(f32[1,1,128,256]{3,2,1,0:T(8,128)S(1)} %slice.298), channel_id=1, source_target_pairs={{0,1},{1,2},{2,3},{3,4},{4,5},{5,6},{6,7},{8,9},{9,10},{10,11},{11... | collective-permute-start | bytes 393224 | tf_op jit(solution)/shard_map/ppermute | solution.py:190
  69.3 24.3 %copy-start.10 = (f32[1,1024,256]{2,1,0:T(8,128)S(1)}, f32[1,1024,256]{2,1,0:T(8,128)}, u32[]{:S(2)}) copy-start(f32[1,1024,256]{2,1,0:T(8,128)} %get-tuple-element.24) | copy-start | bytes 3145732
  69.4 29.3 %collective-permute-start.9 = (f32[1,3,128,256]{3,2,1,0:T(8,128)S(1)}, f32[1,3,128,256]{3,2,1,0:T(8,128)S(1)}, u32[]{:S(2)}, u32[]{:S(2)}) collective-permute-start(f32[1,3,128,256]{3,2,1,0:T(8,128)S(1)} %slice.314), channel_id=1, source_target_pairs={{0,1},{1,2},{2,3},{3,4},{4,5},{5,6},{6,7},{8,9},{9,10},{10,11},{11... | collective-permute-start | bytes 1179656 | tf_op jit(solution)/shard_map/ppermute | solution.py:195
  72.4 27.0 %collective-permute-start.8 = (f32[1,4,128,256]{3,2,1,0:T(8,128)S(1)}, f32[1,4,128,256]{3,2,1,0:T(8,128)S(1)}, u32[]{:S(2)}, u32[]{:S(2)}) collective-permute-start(f32[1,4,128,256]{3,2,1,0:T(8,128)S(1)} %slice.311), channel_id=1, source_target_pairs={{1,0},{2,1},{3,2},{4,3},{5,4},{6,5},{7,6},{9,8},{10,9},{11,10},{12... | collective-permute-start | bytes 1572872 | tf_op jit(solution)/shard_map/ppermute | solution.py:200
  102.9 2.0 %collective-permute-start.10 = (f32[8,2,32,256]{3,0,2,1:T(8,128)S(1)}, f32[8,2,32,256]{3,0,2,1:T(8,128)S(1)}, u32[]{:S(2)}, u32[]{:S(2)}) collective-permute-start(f32[8,2,32,256]{3,0,2,1:T(8,128)S(1)} %bitcast.212), channel_id=1, source_target_pairs={{0,8},{8,0},{16,24},{24,16},{1,9},{9,1},{17,25},{25,17},{2,10},{10... | collective-permute-start | bytes 1572872 | tf_op jit(solution)/shard_map/ppermute | solution.py:136
  105.2 8.4 %collective-permute-start.11 = (f32[8,1,32,256]{3,0,2,1:T(8,128)S(1)}, f32[8,1,32,256]{3,0,2,1:T(8,128)S(1)}, u32[]{:S(2)}, u32[]{:S(2)}) collective-permute-start(f32[8,1,32,256]{3,0,2,1:T(8,128)S(1)} %constant_dynamic-slice_fusion), channel_id=1, source_target_pairs={{0,16},{8,24},{16,0},{24,8},{1,17},{9,25},{17,1},{25,9},{2,18},{10... | collective-permute-start | bytes 786440 | tf_op jit(solution)/shard_map/ppermute | solution.py:136
  (3 other events, 3.2 us)

commit v15 on v13

--- a/solution.py
+++ b/solution.py
@@ -213,7 +213,7 @@
     lateral_smooth = smooth_lateral(correlation)
     reduced = reduce_shots(lateral_smooth, 1)
     columns = lax.all_to_all(reduced, "depth", split_axis=1, concat_axis=0, tiled=True)
-    gradient = smooth(columns, 0)
+    gradient = jnp.einsum("zw,wxy->zxy", smooth_matrix(columns.shape[0]), columns, precision=lax.Precision.HIGHEST)
     return (earlier[0], current[0], earlier[1], current[1], gradient)
 
 

time: 130 us -> 130 us (level)
  no operation moved by 1% of the time
where the time goes in v15:
time: 130 us; the launch traced here: 129 us
  waiting for transfers between devices  32.3 us (25%)
  starting transfers between devices  31.7 us (24%)
  matrix products  29.8 us (23%)
  blocking collectives  15.3 us (12%)
  local copies, waits for them, and re-layouts  14.2 us (11%)
  other arithmetic  4.71 us (4%)
  between operations  1.3 us (1%)
    ppermute x3, starting transfers between devices, exchange(): lax.ppermute(lax.slice_in_dim(f, length - HALO, length, axis=dim), 'depth...  16.4 us
    all_to_all x1, blocking collectives, on_device(): lax.all_to_all(reduced, 'depth', split_axis=1, concat_axis=0, tiled=True)  15.3 us
    ppermute x1, waiting for transfers between devices, on_device(): lax.ppermute(lax.slice_in_dim(fresh[i], length - HALO, length - 1, axis=z...  15.3 us
    dot_general x2, matrix products, spread_dense(): grid = jnp.dot(by_row, right, preferred_element_type=jnp.float32)  15 us
    ppermute x2, waiting for transfers between devices, reduce_shots(): blocks = keep + lax.ppermute(send, 'shots', pairs)  8.71 us
    ppermute x3, waiting for transfers between devices, exchange(): lax.ppermute(lax.slice_in_dim(f, length - HALO, length, axis=dim), 'depth...  8.29 us
    dot_general x4, matrix products, lateral_laplace(): along_x = jnp.einsum('...xy,kx->...ky', core, band(rows), precision=high)  7.26 us
    unnamed x49, local copies, waits for them, and re-layouts  5.61 us
  transfers between devices with their start and end apart: 11, of which 4 were waited for; matrix products, arithmetic and copies ran while one was open for 30% of the time, Pallas kernels for 0%

profile of v15, /device:TPU:0, one launch (start us, length us, event | category | flops | bytes accessed | tf_op | source)
XLA Modules:
  0.0 129.3 jit_solution(17660374185626759292)
XLA Ops:
  0.6 2.3 %fusion.319 = (f32[1,4,128,256]{3,2,1,0:T(8,128)}, f32[1,4,128,256]{3,2,1,0:T(8,128)}) fusion(f32[1,8,128,256]{3,2,1,0:T(8,128)} %param.13), kind=kLoop, calls=%fused_computation.395 | loop fusion | bytes 2097152 | tf_op jit(solution)/shard_map/slice | solution.py:87
  3.0 5.7 %collective-permute-start.1 = (f32[1,4,128,256]{3,2,1,0:T(8,128)}, f32[1,4,128,256]{3,2,1,0:T(8,128)}, u32[]{:S(2)}, u32[]{:S(2)}) collective-permute-start(f32[1,4,128,256]{3,2,1,0:T(8,128)} %get-tuple-element.40), channel_id=1, source_target_pairs={{0,1},{1,2},{2,3},{3,4},{4,5},{5,6},{6,7},{8,9},{9,10},{10,11},{11... | collective-permute-start | bytes 1572872 | tf_op jit(solution)/shard_map/ppermute | solution.py:86
  8.7 1.3 collective-permute-start
  10.0 1.1 fusion.318
  11.1 5.5 %collective-permute-start.3 = (f32[1,4,128,256]{3,2,1,0:T(8,128)}, f32[1,4,128,256]{3,2,1,0:T(8,128)}, u32[]{:S(2)}, u32[]{:S(2)}) collective-permute-start(f32[1,4,128,256]{3,2,1,0:T(8,128)} %get-tuple-element.38), channel_id=1, source_target_pairs={{0,1},{1,2},{2,3},{3,4},{4,5},{5,6},{6,7},{8,9},{9,10},{10,11},{11... | collective-permute-start | bytes 1572872 | tf_op jit(solution)/shard_map/ppermute | solution.py:86
  16.6 1.3 collective-permute-start.4
  17.8 2.0 %convolution_bitcast_fusion.4 = f32[1,8,128,256]{3,2,1,0:T(8,128)} fusion(f32[1,8,128,256]{3,2,1,0:T(8,128)S(1)} %copy-done.4), kind=kOutput, calls=%fused_computation.45 | convolution fusion | flops 805961728 | bytes 2097152 | tf_op jit(solution)/shard_map/...xy,yk->...xk/dot_general | solution.py:39
  20.7 13.2 %fusion.1 = f32[1024,3,2,256]{3,0,2,1:T(8,128)S(1)} fusion(pred[4096,256]{0,1:T(8,128)(4,1)S(1)} %iota_compare_fusion.1, s32[4096]{0:T(1024)S(1)} %get-tuple-element.46, bf16[4096,3,2]{0,2,1:T(2,128)(2,1)S(1)} %maximum_bitcast_fusion), kind=kOutput, calls=%fused_computation.2 | convolution fusion | flops 12895387648 | bytes 7405568 | tf_op jit(solution)/shard_map/dot_general | solution.py:116
  34.5 1.1 fusion.315
  35.8 1.8 %fusion.12 = f32[1024,3,2,256]{3,0,2,1:T(8,128)S(1)} fusion(pred[512,256]{0,1:T(8,128)(4,1)S(1)} %iota_compare_fusion.3, s32[512]{0:T(512)S(1)} %get-tuple-element.51, bf16[512,3,2]{0,2,1:T(2,128)(2,1)S(1)} %maximum_bitcast_fusion.1), kind=kOutput, calls=%fused_computation.27 | convolution fusion | flops 1611923456 | bytes 6430720 | tf_op jit(solution)/shard_map/dot_general | solution.py:116
  38.1 1.1 fusion.316
  40.3 2.3 %fusion.26 = f32[1,8,128,256]{3,2,1,0:T(8,128)} fusion(f32[1,8,128,256]{3,2,1,0:T(8,128)S(1)} %bitcast.204, f32[1,8,128,256]{3,2,1,0:T(8,128)S(1)} %copy-done.8, f32[1,8,128,256]{3,2,1,0:T(8,128)S(1)} %copy-done.4, f32[8,128,256]{2,1,0:T(8,128)S(1)} %copy-done, f32[1,8,128,256]{3,2,1,0:T(8,128)S(1)} %copy-done.13), kind=kOutput, calls=%fused_computation.58 | convolution fusion | flops 404914176 | bytes 6291456 | tf_op jit(solution)/shard_map/...xy,kx->...ky/dot_general | solution.py:40
  43.8 2.3 %fusion.21 = f32[1,8,128,256]{3,2,1,0:T(8,128)} fusion(f32[1,8,128,256]{3,2,1,0:T(8,128)S(1)} %bitcast.205, f32[1,8,128,256]{3,2,1,0:T(8,128)S(1)} %convolution_bitcast_fusion.6, f32[1,8,128,256]{3,2,1,0:T(8,128)S(1)} %copy-done.3, f32[8,128,256]{2,1,0:T(8,128)S(1)} %copy-done, f32[1,8,128,256]{3,2,1,0:T(8,128)S(1)} %copy-done.14), kind=kOutput, calls=%fused_computation.53 | convolution fusion | flops 404914176 | bytes 6291456 | tf_op jit(solution)/shard_map/...xy,kx->...ky/dot_general | solution.py:40
  46.1 1.1 constant_dynamic-update-slice_fusion.3
  47.5 1.2 constant_dynamic-update-slice_fusion
  49.3 4.7 %collective-permute-start.2 = (f32[1,1,128,256]{3,2,1,0:T(8,128)S(1)}, f32[1,1,128,256]{3,2,1,0:T(8,128)S(1)}, u32[]{:S(2)}, u32[]{:S(2)}) collective-permute-start(f32[1,1,128,256]{3,2,1,0:T(8,128)S(1)} %slice.269), channel_id=1, source_target_pairs={{0,1},{1,2},{2,3},{3,4},{4,5},{5,6},{6,7},{8,9},{9,10},{10,11},{11... | collective-permute-start | bytes 393224 | tf_op jit(solution)/shard_map/ppermute | solution.py:187
  54.0 3.7 %collective-permute-start.6 = (f32[1,3,128,256]{3,2,1,0:T(8,128)S(1)}, f32[1,3,128,256]{3,2,1,0:T(8,128)S(1)}, u32[]{:S(2)}, u32[]{:S(2)}) collective-permute-start(f32[1,3,128,256]{3,2,1,0:T(8,128)S(1)} %slice.284), channel_id=1, source_target_pairs={{0,1},{1,2},{2,3},{3,4},{4,5},{5,6},{6,7},{8,9},{9,10},{10,11},{11... | collective-permute-start | bytes 1179656 | tf_op jit(solution)/shard_map/ppermute | solution.py:192
  57.6 1.5 %collective-permute-start.5 = (f32[1,4,128,256]{3,2,1,0:T(8,128)S(1)}, f32[1,4,128,256]{3,2,1,0:T(8,128)S(1)}, u32[]{:S(2)}, u32[]{:S(2)}) collective-permute-start(f32[1,4,128,256]{3,2,1,0:T(8,128)S(1)} %slice.279), channel_id=1, source_target_pairs={{1,0},{2,1},{3,2},{4,3},{5,4},{6,5},{7,6},{9,8},{10,9},{11,10},{12... | collective-permute-start | bytes 1572872 | tf_op jit(solution)/shard_map/ppermute | solution.py:197
  60.2 1.3 fusion.31
  61.5 1.2 constant_dynamic-update-slice_fusion.7
  63.1 1.2 constant_dynamic-update-slice_fusion.4
  64.8 1.0 convolution_bitcast_fusion
  66.4 1.4 %fusion.36 = f32[1,8,128,256]{3,2,1,0:T(8,128)S(1)} fusion(f32[1,8,128,256]{3,2,1,0:T(8,128)S(1)} %bitcast.202, f32[1,8,128,256]{3,2,1,0:T(8,128)S(1)} %convolution_bitcast_fusion, f32[1,8,128,256]{3,2,1,0:T(8,128)S(1)} %fusion.74, f32[8,128,256]{2,1,0:T(8,128)S(1)} %copy-done, f32[1,8,128,256]{3,2,1,0:T(8,128)S(1)} %copy-done.5), kind=kOutput, calls=%fused_computation.68 | convolution fusion | flops 404914176 | bytes 6291456 | tf_op jit(solution)/shard_map/...xy,kx->...ky/dot_general | solution.py:40
  67.9 1.3 collective-permute-start.7
  69.2 5.2 %collective-permute-start.8 = (f32[1,4,128,256]{3,2,1,0:T(8,128)S(1)}, f32[1,4,128,256]{3,2,1,0:T(8,128)S(1)}, u32[]{:S(2)}, u32[]{:S(2)}) collective-permute-start(f32[1,4,128,256]{3,2,1,0:T(8,128)S(1)} %get-tuple-element.34), channel_id=1, source_target_pairs={{0,1},{1,2},{2,3},{3,4},{4,5},{5,6},{6,7},{8,9},{9,10},{10,11},{11... | collective-permute-start | bytes 1572872 | tf_op jit(solution)/shard_map/ppermute | solution.py:86
  74.4 15.3 %collective-permute-done.6 = f32[1,3,128,256]{3,2,1,0:T(8,128)S(1)} collective-permute-done((f32[1,3,128,256]{3,2,1,0:T(8,128)S(1)}, f32[1,3,128,256]{3,2,1,0:T(8,128)S(1)}, u32[]{:S(2)}, u32[]{:S(2)}) %collective-permute-start.6) | collective-permute-done | bytes 393248 | tf_op jit(solution)/shard_map/ppermute | solution.py:192
  90.3 8.3 %collective-permute-done.8 = f32[1,4,128,256]{3,2,1,0:T(8,128)S(1)} collective-permute-done((f32[1,4,128,256]{3,2,1,0:T(8,128)S(1)}, f32[1,4,128,256]{3,2,1,0:T(8,128)S(1)}, u32[]{:S(2)}, u32[]{:S(2)}) %collective-permute-start.8) | collective-permute-done | bytes 524320 | tf_op jit(solution)/shard_map/ppermute | solution.py:86
  99.5 1.1 fusion.89
  102.1 1.9 %collective-permute-done.9 = f32[8,2,32,256]{3,0,2,1:T(8,128)S(1)} collective-permute-done((f32[8,2,32,256]{3,0,2,1:T(8,128)S(1)}, f32[8,2,32,256]{3,0,2,1:T(8,128)S(1)}, u32[]{:S(2)}, u32[]{:S(2)}) %collective-permute-start.9) | collective-permute-done | bytes 524320 | tf_op jit(solution)/shard_map/ppermute | solution.py:136
  104.3 1.6 %collective-permute-start.10 = (f32[8,1,32,256]{3,0,2,1:T(8,128)S(1)}, f32[8,1,32,256]{3,0,2,1:T(8,128)S(1)}, u32[]{:S(2)}, u32[]{:S(2)}) collective-permute-start(f32[8,1,32,256]{3,0,2,1:T(8,128)S(1)} %constant_dynamic-slice_fusion), channel_id=1, source_target_pairs={{0,16},{8,24},{16,0},{24,8},{1,17},{9,25},{17,1},{25,9},{2,18},{10... | collective-permute-start | bytes 786440 | tf_op jit(solution)/shard_map/ppermute | solution.py:136
  105.9 6.8 %collective-permute-done.10 = f32[8,1,32,256]{3,0,2,1:T(8,128)S(1)} collective-permute-done((f32[8,1,32,256]{3,0,2,1:T(8,128)S(1)}, f32[8,1,32,256]{3,0,2,1:T(8,128)S(1)}, u32[]{:S(2)}, u32[]{:S(2)}) %collective-permute-start.10) | collective-permute-done | bytes 262176 | tf_op jit(solution)/shard_map/ppermute | solution.py:136
  112.8 15.3 %all_to_all.18 = f32[8,32,256]{2,0,1:T(8,128)S(1)} all-to-all(f32[8,32,256]{2,0,1:T(8,128)S(1)} %add_bitcast_fusion), channel_id=1, replica_groups=mesh['shots'=4,'depth'=8] {'depth'}, dimensions={1} | all-to-all | bytes 524288 | tf_op jit(solution)/shard_map/all_to_all | solution.py:215
  (84 shorter events, 12.2 us)
Async XLA Ops:
  0.6 9.3 %copy-start.4 = (f32[1,8,128,256]{3,2,1,0:T(8,128)S(1)}, f32[1,8,128,256]{3,2,1,0:T(8,128)}, u32[]{:S(2)}) copy-start(f32[1,8,128,256]{3,2,1,0:T(8,128)} %param.15) | copy-start | bytes 3145732
  3.0 43.2 %collective-permute-start.1 = (f32[1,4,128,256]{3,2,1,0:T(8,128)}, f32[1,4,128,256]{3,2,1,0:T(8,128)}, u32[]{:S(2)}, u32[]{:S(2)}) collective-permute-start(f32[1,4,128,256]{3,2,1,0:T(8,128)} %get-tuple-element.40), channel_id=1, source_target_pairs={{0,1},{1,2},{2,3},{3,4},{4,5},{5,6},{6,7},{8,9},{9,10},{10,11},{11... | collective-permute-start | bytes 1572872 | tf_op jit(solution)/shard_map/ppermute | solution.py:86
  8.7 38.8 %collective-permute-start = (f32[1,4,128,256]{3,2,1,0:T(8,128)}, f32[1,4,128,256]{3,2,1,0:T(8,128)}, u32[]{:S(2)}, u32[]{:S(2)}) collective-permute-start(f32[1,4,128,256]{3,2,1,0:T(8,128)} %get-tuple-element.39), channel_id=1, source_target_pairs={{1,0},{2,1},{3,2},{4,3},{5,4},{6,5},{7,6},{9,8},{10,9},{11,10},{12... | collective-permute-start | bytes 1572872 | tf_op jit(solution)/shard_map/ppermute | solution.py:87
  11.1 8.8 %copy-start.15 = (f32[1,2,4096]{2,1,0:T(2,128)S(1)}, f32[1,2,4096]{2,1,0:T(2,128)}, u32[]{:S(2)}) copy-start(f32[1,2,4096]{2,1,0:T(2,128)} %param.23) | copy-start | bytes 98308
  11.1 8.8 %copy-start.16 = (s32[4096]{0:T(1024)S(1)}, s32[4096]{0:T(1024)}, u32[]{:S(2)}) copy-start(s32[4096]{0:T(1024)} %param.22) | copy-start | bytes 49156
  11.1 8.9 %copy-start.17 = (s32[4096]{0:T(1024)S(1)}, s32[4096]{0:T(1024)}, u32[]{:S(2)}) copy-start(s32[4096]{0:T(1024)} %param.21) | copy-start | bytes 49156
  11.1 50.4 %collective-permute-start.3 = (f32[1,4,128,256]{3,2,1,0:T(8,128)}, f32[1,4,128,256]{3,2,1,0:T(8,128)}, u32[]{:S(2)}, u32[]{:S(2)}) collective-permute-start(f32[1,4,128,256]{3,2,1,0:T(8,128)} %get-tuple-element.38), channel_id=1, source_target_pairs={{0,1},{1,2},{2,3},{3,4},{4,5},{5,6},{6,7},{8,9},{9,10},{10,11},{11... | collective-permute-start | bytes 1572872 | tf_op jit(solution)/shard_map/ppermute | solution.py:86
  16.6 44.9 %collective-permute-start.4 = (f32[1,4,128,256]{3,2,1,0:T(8,128)}, f32[1,4,128,256]{3,2,1,0:T(8,128)}, u32[]{:S(2)}, u32[]{:S(2)}) collective-permute-start(f32[1,4,128,256]{3,2,1,0:T(8,128)} %get-tuple-element.37), channel_id=1, source_target_pairs={{1,0},{2,1},{3,2},{4,3},{5,4},{6,5},{7,6},{9,8},{10,9},{11,10},{12... | collective-permute-start | bytes 1572872 | tf_op jit(solution)/shard_map/ppermute | solution.py:87
  34.4 1.2 copy-start.21
  34.4 1.2 copy-start.19
  34.5 1.2 copy-start.20
  34.5 1.3 copy-start.18
  38.0 1.5 %copy-start = (f32[8,128,256]{2,1,0:T(8,128)S(1)}, f32[8,128,256]{2,1,0:T(8,128)}, u32[]{:S(2)}) copy-start(f32[8,128,256]{2,1,0:T(8,128)} %param.16) | copy-start | bytes 3145732
  38.0 1.9 %copy-start.8 = (f32[1,8,128,256]{3,2,1,0:T(8,128)S(1)}, f32[1,8,128,256]{3,2,1,0:T(8,128)}, u32[]{:S(2)}) copy-start(f32[1,8,128,256]{3,2,1,0:T(8,128)} %convolution_bitcast_fusion.4) | copy-start | bytes 3145732
  38.1 2.2 %copy-start.13 = (f32[1,8,128,256]{3,2,1,0:T(8,128)S(1)}, f32[1,8,128,256]{3,2,1,0:T(8,128)}, u32[]{:S(2)}) copy-start(f32[1,8,128,256]{3,2,1,0:T(8,128)} %param.14) | copy-start | bytes 3145732
  40.3 2.3 %copy-start.3 = (f32[1,8,128,256]{3,2,1,0:T(8,128)S(1)}, f32[1,8,128,256]{3,2,1,0:T(8,128)}, u32[]{:S(2)}) copy-start(f32[1,8,128,256]{3,2,1,0:T(8,128)} %param.13) | copy-start | bytes 3145732
  42.6 1.2 copy-start.14
  47.2 1.4 %copy-start.12 = (f32[1,8,128,256]{3,2,1,0:T(8,128)S(1)}, f32[1,8,128,256]{3,2,1,0:T(8,128)}, u32[]{:S(2)}) copy-start(f32[1,8,128,256]{3,2,1,0:T(8,128)} %fusion.21) | copy-start | bytes 3145732
  49.1 50.3 %copy-start.1 = (f32[1,8,128,256]{3,2,1,0:T(8,128)}, f32[1,8,128,256]{3,2,1,0:T(8,128)S(1)}, u32[]{:S(2)}) copy-start(f32[1,8,128,256]{3,2,1,0:T(8,128)S(1)} %fusion.83) | copy-start | bytes 3145732
  49.2 11.0 %copy-start.10 = (f32[1,1024,256]{2,1,0:T(8,128)S(1)}, f32[1,1024,256]{2,1,0:T(8,128)}, u32[]{:S(2)}) copy-start(f32[1,1024,256]{2,1,0:T(8,128)} %get-tuple-element.29) | copy-start | bytes 3145732
  49.3 12.2 %collective-permute-start.2 = (f32[1,1,128,256]{3,2,1,0:T(8,128)S(1)}, f32[1,1,128,256]{3,2,1,0:T(8,128)S(1)}, u32[]{:S(2)}, u32[]{:S(2)}) collective-permute-start(f32[1,1,128,256]{3,2,1,0:T(8,128)S(1)} %slice.269), channel_id=1, source_target_pairs={{0,1},{1,2},{2,3},{3,4},{4,5},{5,6},{6,7},{8,9},{9,10},{10,11},{11... | collective-permute-start | bytes 393224 | tf_op jit(solution)/shard_map/ppermute | solution.py:187
  54.0 35.7 %collective-permute-start.6 = (f32[1,3,128,256]{3,2,1,0:T(8,128)S(1)}, f32[1,3,128,256]{3,2,1,0:T(8,128)S(1)}, u32[]{:S(2)}, u32[]{:S(2)}) collective-permute-start(f32[1,3,128,256]{3,2,1,0:T(8,128)S(1)} %slice.284), channel_id=1, source_target_pairs={{0,1},{1,2},{2,3},{3,4},{4,5},{5,6},{6,7},{8,9},{9,10},{10,11},{11... | collective-permute-start | bytes 1179656 | tf_op jit(solution)/shard_map/ppermute | solution.py:192
  57.6 32.1 %collective-permute-start.5 = (f32[1,4,128,256]{3,2,1,0:T(8,128)S(1)}, f32[1,4,128,256]{3,2,1,0:T(8,128)S(1)}, u32[]{:S(2)}, u32[]{:S(2)}) collective-permute-start(f32[1,4,128,256]{3,2,1,0:T(8,128)S(1)} %slice.279), channel_id=1, source_target_pairs={{1,0},{2,1},{3,2},{4,3},{5,4},{6,5},{7,6},{9,8},{10,9},{11,10},{12... | collective-permute-start | bytes 1572872 | tf_op jit(solution)/shard_map/ppermute | solution.py:197
  61.5 1.4 %copy-start.5 = (f32[1,8,128,256]{3,2,1,0:T(8,128)S(1)}, f32[1,8,128,256]{3,2,1,0:T(8,128)}, u32[]{:S(2)}) copy-start(f32[1,8,128,256]{3,2,1,0:T(8,128)} %param.15) | copy-start | bytes 3145732
  62.9 1.4 %copy-start.11 = (f32[1,8,128,256]{3,2,1,0:T(8,128)S(1)}, f32[1,8,128,256]{3,2,1,0:T(8,128)}, u32[]{:S(2)}) copy-start(f32[1,8,128,256]{3,2,1,0:T(8,128)} %fusion.26) | copy-start | bytes 3145732
  64.8 34.7 %copy-start.2 = (f32[1,8,128,256]{3,2,1,0:T(8,128)}, f32[1,8,128,256]{3,2,1,0:T(8,128)S(1)}, u32[]{:S(2)}) copy-start(f32[1,8,128,256]{3,2,1,0:T(8,128)S(1)} %fusion.74) | copy-start | bytes 3145732
  64.8 1.6 %copy-start.9 = (f32[1,1024,256]{2,1,0:T(8,128)S(1)}, f32[1,1024,256]{2,1,0:T(8,128)}, u32[]{:S(2)}) copy-start(f32[1,1024,256]{2,1,0:T(8,128)} %get-tuple-element.27) | copy-start | bytes 3145732
  67.9 22.4 %collective-permute-start.7 = (f32[1,4,128,256]{3,2,1,0:T(8,128)S(1)}, f32[1,4,128,256]{3,2,1,0:T(8,128)S(1)}, u32[]{:S(2)}, u32[]{:S(2)}) collective-permute-start(f32[1,4,128,256]{3,2,1,0:T(8,128)S(1)} %get-tuple-element.33), channel_id=1, source_target_pairs={{1,0},{2,1},{3,2},{4,3},{5,4},{6,5},{7,6},{9,8},{10,9},{11,10},{12... | collective-permute-start | bytes 1572872 | tf_op jit(solution)/shard_map/ppermute | solution.py:87
  69.2 29.4 %collective-permute-start.8 = (f32[1,4,128,256]{3,2,1,0:T(8,128)S(1)}, f32[1,4,128,256]{3,2,1,0:T(8,128)S(1)}, u32[]{:S(2)}, u32[]{:S(2)}) collective-permute-start(f32[1,4,128,256]{3,2,1,0:T(8,128)S(1)} %get-tuple-element.34), channel_id=1, source_target_pairs={{0,1},{1,2},{2,3},{3,4},{4,5},{5,6},{6,7},{8,9},{9,10},{10,11},{11... | collective-permute-start | bytes 1572872 | tf_op jit(solution)/shard_map/ppermute | solution.py:86
  90.2 9.2 %copy-start.6 = (f32[1,8,128,256]{3,2,1,0:T(8,128)}, f32[1,8,128,256]{3,2,1,0:T(8,128)S(1)}, u32[]{:S(2)}) copy-start(f32[1,8,128,256]{3,2,1,0:T(8,128)S(1)} %fusion.60) | copy-start | bytes 3145732
  102.0 2.0 %collective-permute-start.9 = (f32[8,2,32,256]{3,0,2,1:T(8,128)S(1)}, f32[8,2,32,256]{3,0,2,1:T(8,128)S(1)}, u32[]{:S(2)}, u32[]{:S(2)}) collective-permute-start(f32[8,2,32,256]{3,0,2,1:T(8,128)S(1)} %bitcast.207), channel_id=1, source_target_pairs={{0,8},{8,0},{16,24},{24,16},{1,9},{9,1},{17,25},{25,17},{2,10},{10... | collective-permute-start | bytes 1572872 | tf_op jit(solution)/shard_map/ppermute | solution.py:136
  104.3 8.4 %collective-permute-start.10 = (f32[8,1,32,256]{3,0,2,1:T(8,128)S(1)}, f32[8,1,32,256]{3,0,2,1:T(8,128)S(1)}, u32[]{:S(2)}, u32[]{:S(2)}) collective-permute-start(f32[8,1,32,256]{3,0,2,1:T(8,128)S(1)} %constant_dynamic-slice_fusion), channel_id=1, source_target_pairs={{0,16},{8,24},{16,0},{24,8},{1,17},{9,25},{17,1},{25,9},{2,18},{10... | collective-permute-start | bytes 786440 | tf_op jit(solution)/shard_map/ppermute | solution.py:136
  (1 other events, 1.1 us)

commit v16 on v13

--- a/solution.py
+++ b/solution.py
@@ -83,8 +83,8 @@
     down = [(i + 1, i) for i in range(devices - 1)]
     below, above = [], []
     for f in fields:
+        above.append(lax.ppermute(lax.slice_in_dim(f, 0, HALO, axis=dim), "depth", down))
         below.append(lax.ppermute(lax.slice_in_dim(f, length - HALO, length, axis=dim), "depth", up))
-        above.append(lax.ppermute(lax.slice_in_dim(f, 0, HALO, axis=dim), "depth", down))
     return below, above
 
 

time: 130 us -> 130 us (level)
  no operation moved by 1% of the time
where the time goes in v16:
time: 130 us; the launch traced here: 129 us
  waiting for transfers between devices  32.3 us (25%)
  starting transfers between devices  31.7 us (24%)
  matrix products  29.5 us (23%)
  blocking collectives  15.3 us (12%)
  local copies, waits for them, and re-layouts  14.3 us (11%)
  other arithmetic  4.81 us (4%)
  between operations  1.32 us (1%)
    ppermute x3, starting transfers between devices, exchange(): lax.ppermute(lax.slice_in_dim(f, length - HALO, length, axis=dim), 'depth...  16.3 us
    all_to_all x1, blocking collectives, on_device(): lax.all_to_all(reduced, 'depth', split_axis=1, concat_axis=0, tiled=True)  15.3 us
    ppermute x1, waiting for transfers between devices, on_device(): lax.ppermute(lax.slice_in_dim(fresh[i], length - HALO, length - 1, axis=z...  15.3 us
    dot_general x2, matrix products, spread_dense(): grid = jnp.dot(by_row, right, preferred_element_type=jnp.float32)  15 us
    ppermute x2, waiting for transfers between devices, reduce_shots(): blocks = keep + lax.ppermute(send, 'shots', pairs)  8.71 us
    ppermute x3, waiting for transfers between devices, exchange(): lax.ppermute(lax.slice_in_dim(f, length - HALO, length, axis=dim), 'depth...  8.29 us
    dot_general x4, matrix products, lateral_laplace(): along_x = jnp.einsum('...xy,kx->...ky', core, band(rows), precision=high)  7.28 us
    unnamed x49, local copies, waits for them, and re-layouts  5.61 us
  transfers between devices with their start and end apart: 11, of which 4 were waited for; matrix products, arithmetic and copies ran while one was open for 30% of the time, Pallas kernels for 0%

profile of v16, /device:TPU:0, one launch (start us, length us, event | category | flops | bytes accessed | tf_op | source)
XLA Modules:
  0.0 129.2 jit_solution(15323081464364907197)
XLA Ops:
  0.6 2.3 %fusion.282 = (f32[1,4,128,256]{3,2,1,0:T(8,128)}, f32[1,4,128,256]{3,2,1,0:T(8,128)}) fusion(f32[1,8,128,256]{3,2,1,0:T(8,128)} %param.13), kind=kLoop, calls=%fused_computation.364 | loop fusion | bytes 2097152 | tf_op jit(solution)/shard_map/slice | solution.py:86
  3.0 5.7 %collective-permute-start.1 = (f32[1,4,128,256]{3,2,1,0:T(8,128)}, f32[1,4,128,256]{3,2,1,0:T(8,128)}, u32[]{:S(2)}, u32[]{:S(2)}) collective-permute-start(f32[1,4,128,256]{3,2,1,0:T(8,128)} %get-tuple-element.35), channel_id=1, source_target_pairs={{0,1},{1,2},{2,3},{3,4},{4,5},{5,6},{6,7},{8,9},{9,10},{10,11},{11... | collective-permute-start | bytes 1572872 | tf_op jit(solution)/shard_map/ppermute | solution.py:87
  8.6 1.3 collective-permute-start
  9.9 1.1 fusion.281
  11.0 5.5 %collective-permute-start.3 = (f32[1,4,128,256]{3,2,1,0:T(8,128)}, f32[1,4,128,256]{3,2,1,0:T(8,128)}, u32[]{:S(2)}, u32[]{:S(2)}) collective-permute-start(f32[1,4,128,256]{3,2,1,0:T(8,128)} %get-tuple-element.33), channel_id=1, source_target_pairs={{0,1},{1,2},{2,3},{3,4},{4,5},{5,6},{6,7},{8,9},{9,10},{10,11},{11... | collective-permute-start | bytes 1572872 | tf_op jit(solution)/shard_map/ppermute | solution.py:87
  16.5 1.3 collective-permute-start.4
  17.8 2.0 %convolution_bitcast_fusion.4 = f32[1,8,128,256]{3,2,1,0:T(8,128)} fusion(f32[1,8,128,256]{3,2,1,0:T(8,128)S(1)} %copy-done.4), kind=kOutput, calls=%fused_computation.45 | convolution fusion | flops 805961728 | bytes 2097152 | tf_op jit(solution)/shard_map/...xy,yk->...xk/dot_general | solution.py:39
  20.6 13.2 %fusion.1 = f32[1024,3,2,256]{3,0,2,1:T(8,128)S(1)} fusion(pred[4096,256]{0,1:T(8,128)(4,1)S(1)} %iota_compare_fusion.1, s32[4096]{0:T(1024)S(1)} %get-tuple-element.45, bf16[4096,3,2]{0,2,1:T(2,128)(2,1)S(1)} %maximum_bitcast_fusion), kind=kOutput, calls=%fused_computation.2 | convolution fusion | flops 12895387648 | bytes 7405568 | tf_op jit(solution)/shard_map/dot_general | solution.py:116
  34.5 1.1 fusion.278
  35.7 1.8 %fusion.12 = f32[1024,3,2,256]{3,0,2,1:T(8,128)S(1)} fusion(pred[512,256]{0,1:T(8,128)(4,1)S(1)} %iota_compare_fusion.3, s32[512]{0:T(512)S(1)} %get-tuple-element.50, bf16[512,3,2]{0,2,1:T(2,128)(2,1)S(1)} %maximum_bitcast_fusion.1), kind=kOutput, calls=%fused_computation.27 | convolution fusion | flops 1611923456 | bytes 6430720 | tf_op jit(solution)/shard_map/dot_general | solution.py:116
  38.0 1.1 fusion.279
  40.2 2.4 %fusion.26 = f32[1,8,128,256]{3,2,1,0:T(8,128)} fusion(f32[1,8,128,256]{3,2,1,0:T(8,128)S(1)} %bitcast.205, f32[1,8,128,256]{3,2,1,0:T(8,128)S(1)} %copy-done.8, f32[1,8,128,256]{3,2,1,0:T(8,128)S(1)} %copy-done.4, f32[8,128,256]{2,1,0:T(8,128)S(1)} %copy-done, f32[1,8,128,256]{3,2,1,0:T(8,128)S(1)} %copy-done.13), kind=kOutput, calls=%fused_computation.58 | convolution fusion | flops 404914176 | bytes 6291456 | tf_op jit(solution)/shard_map/...xy,kx->...ky/dot_general | solution.py:40
  42.6 1.0 convolution_bitcast_fusion.6
  43.8 2.3 %fusion.21 = f32[1,8,128,256]{3,2,1,0:T(8,128)} fusion(f32[1,8,128,256]{3,2,1,0:T(8,128)S(1)} %bitcast.206, f32[1,8,128,256]{3,2,1,0:T(8,128)S(1)} %convolution_bitcast_fusion.6, f32[1,8,128,256]{3,2,1,0:T(8,128)S(1)} %copy-done.3, f32[8,128,256]{2,1,0:T(8,128)S(1)} %copy-done, f32[1,8,128,256]{3,2,1,0:T(8,128)S(1)} %copy-done.14), kind=kOutput, calls=%fused_computation.53 | convolution fusion | flops 404914176 | bytes 6291456 | tf_op jit(solution)/shard_map/...xy,kx->...ky/dot_general | solution.py:40
  46.1 1.1 constant_dynamic-update-slice_fusion.3
  47.5 1.2 constant_dynamic-update-slice_fusion
  49.3 4.7 %collective-permute-start.2 = (f32[1,1,128,256]{3,2,1,0:T(8,128)S(1)}, f32[1,1,128,256]{3,2,1,0:T(8,128)S(1)}, u32[]{:S(2)}, u32[]{:S(2)}) collective-permute-start(f32[1,1,128,256]{3,2,1,0:T(8,128)S(1)} %slice.285), channel_id=1, source_target_pairs={{0,1},{1,2},{2,3},{3,4},{4,5},{5,6},{6,7},{8,9},{9,10},{10,11},{11... | collective-permute-start | bytes 393224 | tf_op jit(solution)/shard_map/ppermute | solution.py:187
  54.0 3.7 %collective-permute-start.6 = (f32[1,3,128,256]{3,2,1,0:T(8,128)S(1)}, f32[1,3,128,256]{3,2,1,0:T(8,128)S(1)}, u32[]{:S(2)}, u32[]{:S(2)}) collective-permute-start(f32[1,3,128,256]{3,2,1,0:T(8,128)S(1)} %slice.300), channel_id=1, source_target_pairs={{0,1},{1,2},{2,3},{3,4},{4,5},{5,6},{6,7},{8,9},{9,10},{10,11},{11... | collective-permute-start | bytes 1179656 | tf_op jit(solution)/shard_map/ppermute | solution.py:192
  57.6 1.5 %collective-permute-start.5 = (f32[1,4,128,256]{3,2,1,0:T(8,128)S(1)}, f32[1,4,128,256]{3,2,1,0:T(8,128)S(1)}, u32[]{:S(2)}, u32[]{:S(2)}) collective-permute-start(f32[1,4,128,256]{3,2,1,0:T(8,128)S(1)} %slice.295), channel_id=1, source_target_pairs={{1,0},{2,1},{3,2},{4,3},{5,4},{6,5},{7,6},{9,8},{10,9},{11,10},{12... | collective-permute-start | bytes 1572872 | tf_op jit(solution)/shard_map/ppermute | solution.py:197
  60.2 1.3 fusion.31
  61.5 1.2 constant_dynamic-update-slice_fusion.7
  63.1 1.2 constant_dynamic-update-slice_fusion.4
  66.4 1.4 %fusion.36 = f32[1,8,128,256]{3,2,1,0:T(8,128)S(1)} fusion(f32[1,8,128,256]{3,2,1,0:T(8,128)S(1)} %bitcast.203, f32[1,8,128,256]{3,2,1,0:T(8,128)S(1)} %convolution_bitcast_fusion, f32[1,8,128,256]{3,2,1,0:T(8,128)S(1)} %fusion.74, f32[8,128,256]{2,1,0:T(8,128)S(1)} %copy-done, f32[1,8,128,256]{3,2,1,0:T(8,128)S(1)} %copy-done.5), kind=kOutput, calls=%fused_computation.68 | convolution fusion | flops 404914176 | bytes 6291456 | tf_op jit(solution)/shard_map/...xy,kx->...ky/dot_general | solution.py:40
  67.9 1.3 %collective-permute-start.7 = (f32[1,4,128,256]{3,2,1,0:T(8,128)S(1)}, f32[1,4,128,256]{3,2,1,0:T(8,128)S(1)}, u32[]{:S(2)}, u32[]{:S(2)}) collective-permute-start(f32[1,4,128,256]{3,2,1,0:T(8,128)S(1)} %get-tuple-element.28), channel_id=1, source_target_pairs={{1,0},{2,1},{3,2},{4,3},{5,4},{6,5},{7,6},{9,8},{10,9},{11,10},{12... | collective-permute-start | bytes 1572872 | tf_op jit(solution)/shard_map/ppermute | solution.py:86
  69.2 5.2 %collective-permute-start.8 = (f32[1,4,128,256]{3,2,1,0:T(8,128)S(1)}, f32[1,4,128,256]{3,2,1,0:T(8,128)S(1)}, u32[]{:S(2)}, u32[]{:S(2)}) collective-permute-start(f32[1,4,128,256]{3,2,1,0:T(8,128)S(1)} %get-tuple-element.29), channel_id=1, source_target_pairs={{0,1},{1,2},{2,3},{3,4},{4,5},{5,6},{6,7},{8,9},{9,10},{10,11},{11... | collective-permute-start | bytes 1572872 | tf_op jit(solution)/shard_map/ppermute | solution.py:87
  74.4 15.3 %collective-permute-done.6 = f32[1,3,128,256]{3,2,1,0:T(8,128)S(1)} collective-permute-done((f32[1,3,128,256]{3,2,1,0:T(8,128)S(1)}, f32[1,3,128,256]{3,2,1,0:T(8,128)S(1)}, u32[]{:S(2)}, u32[]{:S(2)}) %collective-permute-start.6) | collective-permute-done | bytes 393248 | tf_op jit(solution)/shard_map/ppermute | solution.py:192
  90.3 8.3 %collective-permute-done.8 = f32[1,4,128,256]{3,2,1,0:T(8,128)S(1)} collective-permute-done((f32[1,4,128,256]{3,2,1,0:T(8,128)S(1)}, f32[1,4,128,256]{3,2,1,0:T(8,128)S(1)}, u32[]{:S(2)}, u32[]{:S(2)}) %collective-permute-start.8) | collective-permute-done | bytes 524320 | tf_op jit(solution)/shard_map/ppermute | solution.py:87
  99.5 1.1 fusion.89
  102.1 1.9 %collective-permute-done.9 = f32[8,2,32,256]{3,0,2,1:T(8,128)S(1)} collective-permute-done((f32[8,2,32,256]{3,0,2,1:T(8,128)S(1)}, f32[8,2,32,256]{3,0,2,1:T(8,128)S(1)}, u32[]{:S(2)}, u32[]{:S(2)}) %collective-permute-start.9) | collective-permute-done | bytes 524320 | tf_op jit(solution)/shard_map/ppermute | solution.py:136
  104.3 1.6 %collective-permute-start.10 = (f32[8,1,32,256]{3,0,2,1:T(8,128)S(1)}, f32[8,1,32,256]{3,0,2,1:T(8,128)S(1)}, u32[]{:S(2)}, u32[]{:S(2)}) collective-permute-start(f32[8,1,32,256]{3,0,2,1:T(8,128)S(1)} %constant_dynamic-slice_fusion), channel_id=1, source_target_pairs={{0,16},{8,24},{16,0},{24,8},{1,17},{9,25},{17,1},{25,9},{2,18},{10... | collective-permute-start | bytes 786440 | tf_op jit(solution)/shard_map/ppermute | solution.py:136
  105.9 6.9 %collective-permute-done.10 = f32[8,1,32,256]{3,0,2,1:T(8,128)S(1)} collective-permute-done((f32[8,1,32,256]{3,0,2,1:T(8,128)S(1)}, f32[8,1,32,256]{3,0,2,1:T(8,128)S(1)}, u32[]{:S(2)}, u32[]{:S(2)}) %collective-permute-start.10) | collective-permute-done | bytes 262176 | tf_op jit(solution)/shard_map/ppermute | solution.py:136
  112.8 15.3 %all_to_all.18 = f32[8,32,256]{2,0,1:T(8,128)S(1)} all-to-all(f32[8,32,256]{2,0,1:T(8,128)S(1)} %add_bitcast_fusion), channel_id=1, replica_groups=mesh['shots'=4,'depth'=8] {'depth'}, dimensions={1} | all-to-all | bytes 524288 | tf_op jit(solution)/shard_map/all_to_all | solution.py:215
  (87 shorter events, 12.1 us)
Async XLA Ops:
  0.6 9.3 %copy-start.4 = (f32[1,8,128,256]{3,2,1,0:T(8,128)S(1)}, f32[1,8,128,256]{3,2,1,0:T(8,128)}, u32[]{:S(2)}) copy-start(f32[1,8,128,256]{3,2,1,0:T(8,128)} %param.15) | copy-start | bytes 3145732
  3.0 43.2 %collective-permute-start.1 = (f32[1,4,128,256]{3,2,1,0:T(8,128)}, f32[1,4,128,256]{3,2,1,0:T(8,128)}, u32[]{:S(2)}, u32[]{:S(2)}) collective-permute-start(f32[1,4,128,256]{3,2,1,0:T(8,128)} %get-tuple-element.35), channel_id=1, source_target_pairs={{0,1},{1,2},{2,3},{3,4},{4,5},{5,6},{6,7},{8,9},{9,10},{10,11},{11... | collective-permute-start | bytes 1572872 | tf_op jit(solution)/shard_map/ppermute | solution.py:87
  8.6 38.8 %collective-permute-start = (f32[1,4,128,256]{3,2,1,0:T(8,128)}, f32[1,4,128,256]{3,2,1,0:T(8,128)}, u32[]{:S(2)}, u32[]{:S(2)}) collective-permute-start(f32[1,4,128,256]{3,2,1,0:T(8,128)} %get-tuple-element.34), channel_id=1, source_target_pairs={{1,0},{2,1},{3,2},{4,3},{5,4},{6,5},{7,6},{9,8},{10,9},{11,10},{12... | collective-permute-start | bytes 1572872 | tf_op jit(solution)/shard_map/ppermute | solution.py:86
  11.0 8.8 %copy-start.15 = (f32[1,2,4096]{2,1,0:T(2,128)S(1)}, f32[1,2,4096]{2,1,0:T(2,128)}, u32[]{:S(2)}) copy-start(f32[1,2,4096]{2,1,0:T(2,128)} %param.23) | copy-start | bytes 98308
  11.0 8.8 %copy-start.16 = (s32[4096]{0:T(1024)S(1)}, s32[4096]{0:T(1024)}, u32[]{:S(2)}) copy-start(s32[4096]{0:T(1024)} %param.22) | copy-start | bytes 49156
  11.0 8.9 %copy-start.17 = (s32[4096]{0:T(1024)S(1)}, s32[4096]{0:T(1024)}, u32[]{:S(2)}) copy-start(s32[4096]{0:T(1024)} %param.21) | copy-start | bytes 49156
  11.0 50.4 %collective-permute-start.3 = (f32[1,4,128,256]{3,2,1,0:T(8,128)}, f32[1,4,128,256]{3,2,1,0:T(8,128)}, u32[]{:S(2)}, u32[]{:S(2)}) collective-permute-start(f32[1,4,128,256]{3,2,1,0:T(8,128)} %get-tuple-element.33), channel_id=1, source_target_pairs={{0,1},{1,2},{2,3},{3,4},{4,5},{5,6},{6,7},{8,9},{9,10},{10,11},{11... | collective-permute-start | bytes 1572872 | tf_op jit(solution)/shard_map/ppermute | solution.py:87
  16.5 45.0 %collective-permute-start.4 = (f32[1,4,128,256]{3,2,1,0:T(8,128)}, f32[1,4,128,256]{3,2,1,0:T(8,128)}, u32[]{:S(2)}, u32[]{:S(2)}) collective-permute-start(f32[1,4,128,256]{3,2,1,0:T(8,128)} %get-tuple-element.32), channel_id=1, source_target_pairs={{1,0},{2,1},{3,2},{4,3},{5,4},{6,5},{7,6},{9,8},{10,9},{11,10},{12... | collective-permute-start | bytes 1572872 | tf_op jit(solution)/shard_map/ppermute | solution.py:86
  34.4 1.2 copy-start.21
  34.4 1.2 copy-start.19
  34.4 1.2 copy-start.20
  34.4 1.3 copy-start.18
  38.0 1.5 %copy-start = (f32[8,128,256]{2,1,0:T(8,128)S(1)}, f32[8,128,256]{2,1,0:T(8,128)}, u32[]{:S(2)}) copy-start(f32[8,128,256]{2,1,0:T(8,128)} %param.16) | copy-start | bytes 3145732
  38.0 1.9 %copy-start.8 = (f32[1,8,128,256]{3,2,1,0:T(8,128)S(1)}, f32[1,8,128,256]{3,2,1,0:T(8,128)}, u32[]{:S(2)}) copy-start(f32[1,8,128,256]{3,2,1,0:T(8,128)} %convolution_bitcast_fusion.4) | copy-start | bytes 3145732
  38.0 2.2 %copy-start.13 = (f32[1,8,128,256]{3,2,1,0:T(8,128)S(1)}, f32[1,8,128,256]{3,2,1,0:T(8,128)}, u32[]{:S(2)}) copy-start(f32[1,8,128,256]{3,2,1,0:T(8,128)} %param.14) | copy-start | bytes 3145732
  40.2 2.4 %copy-start.3 = (f32[1,8,128,256]{3,2,1,0:T(8,128)S(1)}, f32[1,8,128,256]{3,2,1,0:T(8,128)}, u32[]{:S(2)}) copy-start(f32[1,8,128,256]{3,2,1,0:T(8,128)} %param.13) | copy-start | bytes 3145732
  42.6 1.2 copy-start.14
  47.2 1.4 %copy-start.12 = (f32[1,8,128,256]{3,2,1,0:T(8,128)S(1)}, f32[1,8,128,256]{3,2,1,0:T(8,128)}, u32[]{:S(2)}) copy-start(f32[1,8,128,256]{3,2,1,0:T(8,128)} %fusion.21) | copy-start | bytes 3145732
  49.1 50.3 %copy-start.1 = (f32[1,8,128,256]{3,2,1,0:T(8,128)}, f32[1,8,128,256]{3,2,1,0:T(8,128)S(1)}, u32[]{:S(2)}) copy-start(f32[1,8,128,256]{3,2,1,0:T(8,128)S(1)} %fusion.83) | copy-start | bytes 3145732
  49.2 11.0 %copy-start.10 = (f32[1,1024,256]{2,1,0:T(8,128)S(1)}, f32[1,1024,256]{2,1,0:T(8,128)}, u32[]{:S(2)}) copy-start(f32[1,1024,256]{2,1,0:T(8,128)} %get-tuple-element.24) | copy-start | bytes 3145732
  49.3 12.2 %collective-permute-start.2 = (f32[1,1,128,256]{3,2,1,0:T(8,128)S(1)}, f32[1,1,128,256]{3,2,1,0:T(8,128)S(1)}, u32[]{:S(2)}, u32[]{:S(2)}) collective-permute-start(f32[1,1,128,256]{3,2,1,0:T(8,128)S(1)} %slice.285), channel_id=1, source_target_pairs={{0,1},{1,2},{2,3},{3,4},{4,5},{5,6},{6,7},{8,9},{9,10},{10,11},{11... | collective-permute-start | bytes 393224 | tf_op jit(solution)/shard_map/ppermute | solution.py:187
  54.0 35.7 %collective-permute-start.6 = (f32[1,3,128,256]{3,2,1,0:T(8,128)S(1)}, f32[1,3,128,256]{3,2,1,0:T(8,128)S(1)}, u32[]{:S(2)}, u32[]{:S(2)}) collective-permute-start(f32[1,3,128,256]{3,2,1,0:T(8,128)S(1)} %slice.300), channel_id=1, source_target_pairs={{0,1},{1,2},{2,3},{3,4},{4,5},{5,6},{6,7},{8,9},{9,10},{10,11},{11... | collective-permute-start | bytes 1179656 | tf_op jit(solution)/shard_map/ppermute | solution.py:192
  57.6 32.1 %collective-permute-start.5 = (f32[1,4,128,256]{3,2,1,0:T(8,128)S(1)}, f32[1,4,128,256]{3,2,1,0:T(8,128)S(1)}, u32[]{:S(2)}, u32[]{:S(2)}) collective-permute-start(f32[1,4,128,256]{3,2,1,0:T(8,128)S(1)} %slice.295), channel_id=1, source_target_pairs={{1,0},{2,1},{3,2},{4,3},{5,4},{6,5},{7,6},{9,8},{10,9},{11,10},{12... | collective-permute-start | bytes 1572872 | tf_op jit(solution)/shard_map/ppermute | solution.py:197
  61.5 1.4 %copy-start.5 = (f32[1,8,128,256]{3,2,1,0:T(8,128)S(1)}, f32[1,8,128,256]{3,2,1,0:T(8,128)}, u32[]{:S(2)}) copy-start(f32[1,8,128,256]{3,2,1,0:T(8,128)} %param.15) | copy-start | bytes 3145732
  62.9 1.4 %copy-start.11 = (f32[1,8,128,256]{3,2,1,0:T(8,128)S(1)}, f32[1,8,128,256]{3,2,1,0:T(8,128)}, u32[]{:S(2)}) copy-start(f32[1,8,128,256]{3,2,1,0:T(8,128)} %fusion.26) | copy-start | bytes 3145732
  64.8 34.7 %copy-start.2 = (f32[1,8,128,256]{3,2,1,0:T(8,128)}, f32[1,8,128,256]{3,2,1,0:T(8,128)S(1)}, u32[]{:S(2)}) copy-start(f32[1,8,128,256]{3,2,1,0:T(8,128)S(1)} %fusion.74) | copy-start | bytes 3145732
  64.8 1.6 %copy-start.9 = (f32[1,1024,256]{2,1,0:T(8,128)S(1)}, f32[1,1024,256]{2,1,0:T(8,128)}, u32[]{:S(2)}) copy-start(f32[1,1024,256]{2,1,0:T(8,128)} %get-tuple-element.22) | copy-start | bytes 3145732
  67.9 22.4 %collective-permute-start.7 = (f32[1,4,128,256]{3,2,1,0:T(8,128)S(1)}, f32[1,4,128,256]{3,2,1,0:T(8,128)S(1)}, u32[]{:S(2)}, u32[]{:S(2)}) collective-permute-start(f32[1,4,128,256]{3,2,1,0:T(8,128)S(1)} %get-tuple-element.28), channel_id=1, source_target_pairs={{1,0},{2,1},{3,2},{4,3},{5,4},{6,5},{7,6},{9,8},{10,9},{11,10},{12... | collective-permute-start | bytes 1572872 | tf_op jit(solution)/shard_map/ppermute | solution.py:86
  69.2 29.4 %collective-permute-start.8 = (f32[1,4,128,256]{3,2,1,0:T(8,128)S(1)}, f32[1,4,128,256]{3,2,1,0:T(8,128)S(1)}, u32[]{:S(2)}, u32[]{:S(2)}) collective-permute-start(f32[1,4,128,256]{3,2,1,0:T(8,128)S(1)} %get-tuple-element.29), channel_id=1, source_target_pairs={{0,1},{1,2},{2,3},{3,4},{4,5},{5,6},{6,7},{8,9},{9,10},{10,11},{11... | collective-permute-start | bytes 1572872 | tf_op jit(solution)/shard_map/ppermute | solution.py:87
  90.2 9.2 %copy-start.6 = (f32[1,8,128,256]{3,2,1,0:T(8,128)}, f32[1,8,128,256]{3,2,1,0:T(8,128)S(1)}, u32[]{:S(2)}) copy-start(f32[1,8,128,256]{3,2,1,0:T(8,128)S(1)} %fusion.60) | copy-start | bytes 3145732
  102.0 2.0 %collective-permute-start.9 = (f32[8,2,32,256]{3,0,2,1:T(8,128)S(1)}, f32[8,2,32,256]{3,0,2,1:T(8,128)S(1)}, u32[]{:S(2)}, u32[]{:S(2)}) collective-permute-start(f32[8,2,32,256]{3,0,2,1:T(8,128)S(1)} %bitcast.209), channel_id=1, source_target_pairs={{0,8},{8,0},{16,24},{24,16},{1,9},{9,1},{17,25},{25,17},{2,10},{10... | collective-permute-start | bytes 1572872 | tf_op jit(solution)/shard_map/ppermute | solution.py:136
  104.3 8.4 %collective-permute-start.10 = (f32[8,1,32,256]{3,0,2,1:T(8,128)S(1)}, f32[8,1,32,256]{3,0,2,1:T(8,128)S(1)}, u32[]{:S(2)}, u32[]{:S(2)}) collective-permute-start(f32[8,1,32,256]{3,0,2,1:T(8,128)S(1)} %constant_dynamic-slice_fusion), channel_id=1, source_target_pairs={{0,16},{8,24},{16,0},{24,8},{1,17},{9,25},{17,1},{25,9},{2,18},{10... | collective-permute-start | bytes 786440 | tf_op jit(solution)/shard_map/ppermute | solution.py:136
  (1 other events, 1.1 us)
